TPU v7x, 32 devices: a whole 2x2x4 slice. The times are simulated.
32 devices in a mesh: groups: 2 (over y), gx: 4 (over z), gz: 2 (over x), vert: 2 (over core).
Axes of the slice: x: 2, y: 2, z: 4, core: 2. Of those that a mesh axis runs over, the one named last changes fastest.
Arguments:
- flow_field: bfloat16 [4, 4, 5, 4, 256, 256], P('groups', 'vert', None, 'gx', None, 'gz'), parts along dimension 0, may hold values from -6 to 6
- test_streams: int32 [4], P('groups'), parts along dimension 0, may hold values from 0 to 999999
- snapshot_ids: int32 [4, 4], P('groups', 'vert'), parts along dimension 0, may hold values from 0 to 65535
Outputs:
- sketch_x: float32 [8, 128], P(('groups', 'gx')), parts along dimension 0
- sketch_y: float32 [512, 128], P(('groups', 'gx', 'gz', 'vert')), parts along dimension 0
- sketch_z: float32 [512, 128], P(('groups', 'gz'), ('gx', 'vert')), parts along dimension 0
- core_sketch: float32 [4608, 2, 48], P(('groups', 'gx')), parts along dimension 0
There are 2 independent parts, one for each index of `groups`. A program takes and returns all parts, laid end to end along the dimension named above; each array names one. Nothing has to cross between parts.
All inputs are finite; a program needn't handle non-finite values.
Results may differ from a plain program's by a relative error of at most 0.007.
Values sent between devices are 32-bit elements; how exact they have to be, the bound alone decides.
No kernel may reach another device: no remote copies, remote signals or barrier semaphores. Data moves between devices by JAX's collectives and lax.ppermute only.
A program may use at most 64 MiB of HBM per device.

v0:
```python
import math

import jax
import jax.numpy as jnp
from jax import lax
from jax.sharding import PartitionSpec as P

K = 128
S = 48
E = 2


def hash_index(index, stream, salt):
    mixed = index * -1640531535 + stream * -2048144777 + salt
    mixed = jnp.bitwise_xor(mixed, lax.shift_right_logical(mixed, jnp.int32(16)))
    mixed = mixed * 739982445
    mixed = jnp.bitwise_xor(mixed, lax.shift_right_logical(mixed, jnp.int32(13)))
    mixed = mixed * 695872825
    return jnp.bitwise_xor(mixed, lax.shift_right_logical(mixed, jnp.int32(16)))


def unit_value(index, stream, salt):
    upper = lax.shift_right_logical(hash_index(index, stream, salt), jnp.int32(9))
    return ((2 * upper + 1).astype(jnp.float32) * 2.0 ** (-24) - 1.0).astype(jnp.bfloat16)


def test_table(row_ids, col_ids, stride, stream, salt):
    return unit_value(row_ids[:, None] * stride + col_ids[None, :], stream, salt)


def shards(flow_field, test_streams, snapshot_ids):
    highest = lax.Precision.HIGHEST
    batches, local_snaps, variables, cells_x, cells_y, cells_z = flow_field.shape
    slabs_x = lax.axis_size("gx")
    total_x = cells_x * slabs_x
    total_z = cells_z * lax.axis_size("gz")
    total_q = variables * batches * local_snaps * lax.axis_size("vert")
    factor_stream = test_streams[0]
    core_stream = test_streams[1]
    rank_ids = jnp.arange(K, dtype=jnp.int32)
    sketch_ids = jnp.arange(S, dtype=jnp.int32)
    x_ids = lax.axis_index("gx") * cells_x + jnp.arange(cells_x, dtype=jnp.int32)
    y_ids = jnp.arange(cells_y, dtype=jnp.int32)
    z_ids = lax.axis_index("gz") * cells_z + jnp.arange(cells_z, dtype=jnp.int32)
    ax_tab = test_table(x_ids, rank_ids, K, factor_stream, 1).astype(jnp.float32)
    ay_low = test_table(y_ids, rank_ids, K, factor_stream, 2)
    az_low = test_table(z_ids, rank_ids, K, factor_stream, 3)
    ay_tab = ay_low.astype(jnp.float32)
    phy_low = test_table(sketch_ids, y_ids, cells_y, core_stream, 6)
    phz_low = test_table(sketch_ids, z_ids, total_z, core_stream, 7)

    def batch_terms(batch_idx):
        blocks = flow_field[batch_idx].reshape(-1, cells_x, cells_y, cells_z)
        pairs = blocks.shape[0]
        q_ids = (
            snapshot_ids[batch_idx][:, None] * variables
            + jnp.arange(variables, dtype=jnp.int32)[None, :]
        ).reshape(-1)
        aq_tab = test_table(q_ids, rank_ids, K, factor_stream, 4).astype(jnp.float32)
        phq_low = test_table(q_ids, jnp.arange(E, dtype=jnp.int32), E, core_stream, 8)
        rows_z = blocks.reshape(-1, cells_z)
        along_z = jnp.dot(rows_z, az_low, preferred_element_type=jnp.float32).reshape(
            pairs, cells_x, cells_y, K
        )
        along_y = jnp.einsum("qxyz,yk->qxzk", blocks, ay_low, preferred_element_type=jnp.float32)
        weights = aq_tab[:, None, :] * ax_tab[None, :, :]
        part_x = jnp.sum(
            jnp.sum(along_z * ay_tab[None, None, :, :], axis=2) * aq_tab[:, None, :], axis=0
        )
        part_y = jnp.sum(along_z * weights[:, :, None, :], axis=(0, 1))
        part_z = jnp.sum(along_y * weights[:, :, None, :], axis=(0, 1))
        first = jnp.dot(rows_z, phz_low.T, preferred_element_type=jnp.float32).reshape(
            pairs, cells_x, cells_y, S
        )
        second = jnp.einsum("qxyc,by->qxbc", first, phy_low.astype(jnp.float32), precision=highest)
        partial_core = jnp.einsum(
            "qxbc,qe->bcex", second, phq_low.astype(jnp.float32), precision=highest
        )
        return (part_x, part_y, part_z, partial_core.reshape(S * S, E, cells_x))

    def finish(part_x, part_y, part_z, partial_core):
        summed, sum_x = lax.psum((partial_core, part_x), ("gz", "vert"))
        phx_whole = test_table(
            sketch_ids, jnp.arange(total_x, dtype=jnp.int32), total_x, core_stream, 5
        ).astype(jnp.float32)
        core = jnp.einsum(
            "rex,ax->rea",
            lax.all_to_all(summed, "gx", split_axis=0, concat_axis=2, tiled=True),
            phx_whole,
            precision=highest,
        )
        sum_z = lax.psum_scatter(part_z, ("gx", "vert"), scatter_dimension=1, tiled=True)
        sum_y = lax.psum_scatter(part_y, ("gx", "gz", "vert"), scatter_dimension=0, tiled=True)
        return (sum_x, sum_y, sum_z, core)

    terms = [batch_terms(batch_idx) for batch_idx in range(batches)]
    totals = finish(terms[0][0], terms[0][1], terms[0][2], terms[0][3])
    for later in terms[1:]:
        latest = finish(later[0], later[1], later[2], later[3])
        totals = tuple((earlier + newer for earlier, newer in zip(totals, latest)))
    scale_x = 3.0**1.5 / math.sqrt(cells_y * total_z * total_q)
    scale_y = 3.0**1.5 / math.sqrt(total_x * total_z * total_q)
    scale_z = 3.0**1.5 / math.sqrt(total_x * cells_y * total_q)
    scale_core = 9.0 / math.sqrt(total_x * cells_y * total_z * total_q)
    return (totals[0] * scale_x, totals[1] * scale_y, totals[2] * scale_z, totals[3] * scale_core)


def solution(mesh):
    in_specs = (P("groups", "vert", None, "gx", None, "gz"), P("groups"), P("groups", "vert"))
    out_specs = (
        P(("groups", "gx"), None),
        P(("groups", "gx", "gz", "vert"), None),
        P(("groups", "gz"), ("gx", "vert")),
        P(("groups", "gx"), None, None),
    )
    return jax.shard_map(shards, mesh=mesh, in_specs=in_specs, out_specs=out_specs, check_vma=False)
```

profile of v0, /device:TPU:0, one launch (start us, length us, event | category | flops | bytes accessed | tf_op | source)
XLA Modules:
  0.0 124.9 jit_solution(1838660358389235373)
XLA Ops:
  7.2 1.3 %fusion.295 = (s32[1]{0:T(128)}, s32[1]{0:T(128)}) fusion(s32[2]{0:T(128)} %param.4), kind=kLoop, calls=%fused_computation.343 | loop fusion | bytes 16 | tf_op jit(solution)/shard_map/slice | solution.py:39
  8.5 0.8 multiply_bitcast_fusion
  9.4 0.1 mul.691
  9.5 0.1 mul.680
  9.6 1.4 %fusion.294 = (bf16[1,2,5,1,256,128]{5,4,3,2,1,0:T(8,128)(2,1)S(1)}, bf16[1,2,5,1,256,128]{5,4,3,2,1,0:T(8,128)(2,1)S(1)}) fusion(bf16[2,2,5,1,256,128]{5,4,3,2,1,0:T(8,128)(2,1)} %param.3), kind=kLoop, calls=%fused_computation.342 | loop fusion | bytes 2621440 | tf_op jit(solution)/shard_map/slice | solution.py:53
  11.7 0.1 convert_multiply_fusion
  11.8 0.3 fusion.2
  12.1 0.3 fusion.3
  12.4 0.6 add.598
  13.8 1.2 fusion.68
  15.0 0.4 fusion.66
  15.4 0.5 convolution_bitcast_fusion
  15.8 1.5 %convolution_bitcast_fusion.1 = f32[2560,128]{0,1:T(8,128)} fusion(bf16[2560,128]{1,0:T(8,128)(2,1)S(1)} %bitcast.111, s32[]{:T(128)} %bitcast, s32[128]{0:T(128)S(1)} %broadcast_multiply_fusion.3), kind=kOutput, calls=%fused_computation.1 | convolution fusion | flops 84197376 | bytes 1966596 | tf_op jit(solution)/shard_map/dot_general | solution.py:62
  17.5 0.1 copy.23
  17.6 0.6 convolution_bitcast_fusion.5
  18.3 0.3 convolution_bitcast_fusion.7
  18.6 0.1 reshape.486
  18.7 0.6 convolution_bitcast_fusion.4
  19.3 0.3 convolution_bitcast_fusion.6
  19.6 0.1 reshape.489
  19.8 1.5 %copy.24 = f32[2560,128]{1,0:T(8,128)} copy(f32[2560,128]{0,1:T(8,128)S(1)} %convolution_bitcast_fusion) | data formatting | bytes 2621440 | tf_op jit(solution)/shard_map/dot_general | solution.py:62
  21.2 1.5 %copy.22 = f32[2560,128]{1,0:T(8,128)} copy(f32[2560,128]{0,1:T(8,128)S(1)} %copy-done) | data formatting | bytes 2621440 | tf_op jit(solution)/shard_map/dot_general | solution.py:62
  22.7 1.7 %multiply_reduce_fusion = (f32[256,128]{1,0:T(8,128)S(1)}, f32[10,128]{1,0:T(8,128)S(1)}, f32[10,128]{1,0:T(8,128)S(1)}, f32[256,128]{1,0:T(8,128)S(1)}) fusion(f32[10,1,256,128]{3,2,0,1:T(8,128)S(1)} %bitcast.115, f32[10,128]{1,0:T(8,128)S(1)} %get-tuple-element.23, f32[256,128]{1,0:T(8,128)S(1)} %copy.23, f32[10,1,256,128]{3,2,0,1:T(8,128)} %bitcast.116, ...), kind=kLoop, calls=%fused_computation.2 | loop fusion | flops 2553344 | bytes 3035136 | tf_op jit(solution)/shard_map/reduce_sum | solution.py:70
  24.4 0.1 fusion.70
  24.6 13.2 %all-reduce = (f32[1,128]{1,0:T(1,128)S(1)}, f32[2304,2,1]{0,1,2:T(2,128)S(1)}, f32[2304,2,1]{0,1,2:T(2,128)S(1)}) all-reduce(f32[1,128]{1,0:T(1,128)S(1)} %add_bitcast_fusion, f32[2304,2,1]{0,1,2:T(2,128)S(1)} %reshape.486, f32[2304,2,1]{0,1,2:T(2,128)S(1)} %reshape.489), channel_id=1, replica_groups=mesh['groups'=2,'gx'=4,'gz'=2,'vert'=2] {'gz','vert'}, use_global_device_ids=true, to_apply=%region_2.0 | all-reduce | flops 9344 | bytes 74752 | tf_op jit(solution)/shard_map/psum | solution.py:82
  37.7 1.5 %copy.28 = f32[2304,2,1]{1,2,0:T(1,128)S(1)} copy(f32[2304,2,1]{0,1,2:T(2,128)S(1)} %get-tuple-element.9) | data formatting | bytes 36864 | tf_op jit(solution)/shard_map/psum | solution.py:82
  39.2 0.5 broadcast.1041
  39.8 10.4 %reduce.10 = f32[2304,2]{1,0:T(8,128)S(1)} reduce(f32[2304,1,2]{2,1,0:T(1,128)S(1)} %bitcast.117, f32[]{:T(128)} %broadcast.1041), dimensions={1}, to_apply=%bitcast.99.reduce_sub_computation | reduce | bytes 36868
  50.2 1.3 %reshape.496 = f32[4,1,1152]{2,1,0:T(1,128)} reshape(f32[2304,2]{1,0:T(8,128)S(1)} %reduce.10) | data formatting | bytes 36864
  51.5 4.9 %all-to-all-start = ((f32[4,1,1152]{2,1,0:T(1,128)}), f32[4,1,1152]{2,1,0:T(1,128)S(1)}, u32[]{:S(2)}, u32[]{:S(2)}) async-start(f32[4,1,1152]{2,1,0:T(1,128)} %reshape.496), calls=%async_computation | async-start | bytes 36864 | tf_op jit(solution)/shard_map/all_to_all | solution.py:88
  56.4 0.7 add.597
  57.1 0.5 broadcast_multiply_fusion.2
  57.6 1.4 %copy.33 = f32[2304,2,1]{1,2,0:T(1,128)S(1)} copy(f32[2304,2,1]{0,1,2:T(2,128)S(1)} %get-tuple-element.10) | data formatting | bytes 36864 | tf_op jit(solution)/shard_map/psum | solution.py:82
  59.1 10.4 %reduce.12 = f32[2304,2]{1,0:T(8,128)S(1)} reduce(f32[2304,1,2]{2,1,0:T(1,128)S(1)} %bitcast.118, f32[]{:T(128)} %broadcast.1041), dimensions={1}, to_apply=%bitcast.101.reduce_sub_computation | reduce | bytes 36868
  69.5 1.3 %reshape.498 = f32[4,1,1152]{2,1,0:T(1,128)} reshape(f32[2304,2]{1,0:T(8,128)S(1)} %reduce.12) | data formatting | bytes 36864
  70.8 5.1 %all-to-all-start.1 = ((f32[4,1,1152]{2,1,0:T(1,128)}), f32[4,1,1152]{2,1,0:T(1,128)S(1)}, u32[]{:S(2)}, u32[]{:S(2)}) async-start(f32[4,1,1152]{2,1,0:T(1,128)} %reshape.498), calls=%async_computation.1 | async-start | bytes 36864 | tf_op jit(solution)/shard_map/all_to_all | solution.py:88
  75.9 0.7 reduce.11
  76.6 1.8 %reshape.497 = f32[2304,1,2]{2,1,0:T(1,128)S(1)} reshape(f32[4,1152]{1,0:T(4,128)S(1)} %reduce.11) | data formatting | bytes 36864
  78.5 0.4 copy.35
  78.9 2.7 %all-to-all-done.1 = f32[4,1,1152]{2,1,0:T(1,128)S(1)} async-done(((f32[4,1,1152]{2,1,0:T(1,128)}), f32[4,1,1152]{2,1,0:T(1,128)S(1)}, u32[]{:S(2)}, u32[]{:S(2)}) %all-to-all-start.1) | async-done | bytes 18464 | tf_op jit(solution)/shard_map/all_to_all | solution.py:88
  81.5 0.7 reduce.13
  82.2 1.8 %reshape.499 = f32[2304,1,2]{2,1,0:T(1,128)S(1)} reshape(f32[4,1152]{1,0:T(4,128)S(1)} %reduce.13) | data formatting | bytes 36864
  84.1 0.4 copy.36
  84.5 0.3 fusion.64
  84.8 1.0 fusion.4
  85.8 1.3 %broadcast_multiply_fusion = f32[128,16]{0,1:T(8,128)} fusion(f32[128,16]{0,1:T(8,128)} %reduce-scatter.5.cloned.1.call-done), kind=kLoop, calls=%fused_computation.117 | loop fusion | flops 2048 | bytes 16384 | tf_op jit(solution)/shard_map/mul | solution.py:105
  87.1 29.7 %reduce-scatter.3.cloned.1.call-done = f32[16,128]{1,0:T(8,128)} async-done(((f32[256,128]{1,0:T(8,128)}), f32[16,128]{1,0:T(8,128)}) %reduce-scatter.3.cloned.1.call-update) | async-done | bytes 8208 | tf_op jit(solution)/shard_map/reduce_scatter | solution.py:93
  116.8 1.3 %broadcast_multiply_fusion.1 = f32[16,128]{1,0:T(8,128)} fusion(f32[16,128]{1,0:T(8,128)} %reduce-scatter.3.cloned.1.call-done), kind=kLoop, calls=%fused_computation.118 | loop fusion | flops 2048 | bytes 16384 | tf_op jit(solution)/shard_map/mul | solution.py:105
  (26 shorter events, 0.6 us)
Async XLA Ops:
  7.2 78.7 %reduce-scatter.5.cloned.1.call-start = ((), (), s32[]{:S(2)}) async-start(), calls=%async_computation.5 | async-start | bytes 73728 | tf_op jit(solution)/shard_map/reduce_scatter | solution.py:92
  15.8 1.8 %copy-start.2 = (f32[48,2560]{1,0:T(8,128)S(1)}, f32[48,2560]{1,0:T(8,128)}, u32[]{:S(2)}) copy-start(f32[48,2560]{1,0:T(8,128)} %fusion.68) | copy-start | bytes 1474564
  19.7 1.5 %copy-start = (f32[2560,128]{0,1:T(8,128)S(1)}, f32[2560,128]{0,1:T(8,128)}, u32[]{:S(2)}) copy-start(f32[2560,128]{0,1:T(8,128)} %convolution_bitcast_fusion.1) | copy-start | bytes 3932164
  21.2 1.5 %copy-start.1 = (f32[2560,128]{1,0:T(8,128)S(1)}, f32[2560,128]{1,0:T(8,128)}, u32[]{:S(2)}) copy-start(f32[2560,128]{1,0:T(8,128)} %copy.24) | copy-start | bytes 3932164
  51.5 19.3 %all-to-all-start = ((f32[4,1,1152]{2,1,0:T(1,128)}), f32[4,1,1152]{2,1,0:T(1,128)S(1)}, u32[]{:S(2)}, u32[]{:S(2)}) async-start(f32[4,1,1152]{2,1,0:T(1,128)} %reshape.496), calls=%async_computation | async-start | bytes 36864 | tf_op jit(solution)/shard_map/all_to_all | solution.py:88
  56.4 60.4 %reduce-scatter.3.cloned.1.call-start = ((), (), s32[]{:S(2)}) async-start(), calls=%async_computation.4 | async-start | bytes 139264 | tf_op jit(solution)/shard_map/reduce_scatter | solution.py:93
  70.8 10.7 %all-to-all-start.1 = ((f32[4,1,1152]{2,1,0:T(1,128)}), f32[4,1,1152]{2,1,0:T(1,128)S(1)}, u32[]{:S(2)}, u32[]{:S(2)}) async-start(f32[4,1,1152]{2,1,0:T(1,128)} %reshape.498), calls=%async_computation.1 | async-start | bytes 36864 | tf_op jit(solution)/shard_map/all_to_all | solution.py:88
Sparse Core Ops, SparseCore 0:
  13.2 32.7 reduce-scatter.4
  61.1 55.6 reduce-scatter.2
where the time goes:
time: 125 us
  waiting for transfers between devices  32.4 us (26%)
  other arithmetic  29.6 us (24%)
  local copies, waits for them, and re-layouts  16.8 us (13%)
  between operations  15.6 us (12%)
  blocking collectives  13.2 us (11%)
  starting transfers between devices  10 us (8%)
  matrix products  7.37 us (6%)
    reduce_scatter x1, waiting for transfers between devices, finish(): lax.psum_scatter(part_y, ('gx', 'gz', 'vert'), scatter_dimension=0, tiled...  29.7 us
    unnamed x2, other arithmetic  20.9 us
    psum x1, blocking collectives, finish(): summed, sum_x = lax.psum((partial_core, part_x), ('gz', 'vert'))  13.2 us
    all_to_all x2, starting transfers between devices, finish(): lax.all_to_all(summed, 'gx', split_axis=0, concat_axis=2, tiled=True)  9.97 us
    unnamed x11, local copies, waits for them, and re-layouts  6.86 us
    dot_general x2, local copies, waits for them, and re-layouts, batch_terms(): jnp.dot(rows_z, az_low, preferred_element_type=jnp.float32)  2.95 us
    psum x2, local copies, waits for them, and re-layouts, finish(): summed, sum_x = lax.psum((partial_core, part_x), ('gz', 'vert'))  2.89 us
    all_to_all x2, waiting for transfers between devices, finish(): lax.all_to_all(summed, 'gx', split_axis=0, concat_axis=2, tiled=True)  2.68 us
  transfers between devices with their start and end apart: 4, of which 2 were waited for; matrix products, arithmetic and copies ran while one was open for 38% of the time, Pallas kernels for 0%

commit v1 on v0

v1 whole, which is shorter than its diff:
```python
import math

import jax
import jax.numpy as jnp
from jax import lax
from jax.sharding import PartitionSpec as P

K = 128
S = 48
E = 2


def hash_index(index, stream, salt):
    mixed = index * -1640531535 + stream * -2048144777 + salt
    mixed = jnp.bitwise_xor(mixed, lax.shift_right_logical(mixed, jnp.int32(16)))
    mixed = mixed * 739982445
    mixed = jnp.bitwise_xor(mixed, lax.shift_right_logical(mixed, jnp.int32(13)))
    mixed = mixed * 695872825
    return jnp.bitwise_xor(mixed, lax.shift_right_logical(mixed, jnp.int32(16)))


def unit_value(index, stream, salt):
    upper = lax.shift_right_logical(hash_index(index, stream, salt), jnp.int32(9))
    return ((2 * upper + 1).astype(jnp.float32) * 2.0 ** (-24) - 1.0).astype(jnp.bfloat16)


def test_table(row_ids, col_ids, stride, stream, salt):
    return unit_value(row_ids[:, None] * stride + col_ids[None, :], stream, salt)


def bit_of(axis, d):
    return (lax.axis_index(axis) // d) % 2


def halve(arr, dim, bit):
    shape = arr.shape
    split = arr.reshape(shape[:dim] + (shape[dim] // 2, 2) + shape[dim + 1 :])
    keep = lax.dynamic_index_in_dim(split, bit, dim + 1, keepdims=False)
    send = lax.dynamic_index_in_dim(split, 1 - bit, dim + 1, keepdims=False)
    return keep, send


def exchange(axis, d, pieces):
    n = lax.axis_size(axis)
    flat = jnp.concatenate([p.reshape(-1) for p in pieces])
    got = lax.ppermute(flat, axis, [(i, i ^ d) for i in range(n)])
    out, at = [], 0
    for p in pieces:
        out.append(got[at : at + p.size].reshape(p.shape))
        at += p.size
    return out


def bits(n):
    d, out = 1, []
    while d < n:
        out.append(d)
        d *= 2
    return out


def shards(flow_field, test_streams, snapshot_ids):
    highest = lax.Precision.HIGHEST
    f32 = jnp.float32
    batches, local_snaps, variables, cells_x, cells_y, cells_z = flow_field.shape
    n_gx = lax.axis_size("gx")
    n_gz = lax.axis_size("gz")
    n_vert = lax.axis_size("vert")
    total_x = cells_x * n_gx
    total_z = cells_z * n_gz
    total_q = variables * batches * local_snaps * n_vert
    factor_stream = test_streams[0]
    core_stream = test_streams[1]
    gx_me = lax.axis_index("gx")
    rank_ids = jnp.arange(K, dtype=jnp.int32)
    sketch_ids = jnp.arange(S, dtype=jnp.int32)
    x_ids = gx_me * cells_x + jnp.arange(cells_x, dtype=jnp.int32)
    y_ids = jnp.arange(cells_y, dtype=jnp.int32)
    z_ids = lax.axis_index("gz") * cells_z + jnp.arange(cells_z, dtype=jnp.int32)
    q_ids = (
        snapshot_ids[:, :, None] * variables + jnp.arange(variables, dtype=jnp.int32)[None, None, :]
    ).reshape(-1)
    ax = test_table(x_ids, rank_ids, K, factor_stream, 1).astype(f32)
    ay = test_table(y_ids, rank_ids, K, factor_stream, 2)
    az = test_table(z_ids, rank_ids, K, factor_stream, 3)
    aq = test_table(q_ids, rank_ids, K, factor_stream, 4).astype(f32)
    phy = test_table(sketch_ids, y_ids, cells_y, core_stream, 6).astype(f32)
    phz = test_table(sketch_ids, z_ids, total_z, core_stream, 7)
    phq = test_table(q_ids, jnp.arange(E, dtype=jnp.int32), E, core_stream, 8).astype(f32)

    n_q = batches * local_snaps * variables
    field = flow_field.reshape(n_q, cells_x, cells_y, cells_z)
    rows_z = field.reshape(-1, cells_z)

    along_z = jnp.dot(rows_z, az, preferred_element_type=f32).reshape(n_q, cells_x, cells_y, K)
    by_q = jnp.sum(along_z * aq[:, None, None, :], axis=0)
    part_y = jnp.sum(by_q * ax[:, None, :], axis=0)
    part_x = jnp.sum(by_q * ay.astype(f32)[None, :, :], axis=1)
    along_y = jnp.einsum("qxyz,yk->qxzk", field, ay, preferred_element_type=f32)
    weights = aq[:, None, :] * ax[None, :, :]
    part_z = jnp.sum(along_y * weights[:, :, None, :], axis=(0, 1))
    first = jnp.dot(rows_z, phz.T, preferred_element_type=f32).reshape(n_q, cells_x, cells_y, S)
    by_e = jnp.einsum("qxyn,qe->xeyn", first, phq, precision=highest)
    part_core = jnp.einsum("my,xeyn->mnex", phy, by_e, precision=highest).reshape(S * S, E, cells_x)

    rows_each = cells_y // (n_gx * n_gz * n_vert)
    cols_each = K // (n_gx * n_vert)
    core_rows = S * S // n_gx
    sy = part_y.reshape(n_gx, n_gz, n_vert, rows_each, K)
    sz = part_z.reshape(cells_z, n_gx, n_vert, cols_each)
    sx = part_x
    core = part_core.reshape(1, n_gx, core_rows, E, cells_x)

    for d in bits(n_vert):
        b = bit_of("vert", d)
        sy_keep, sy_send = halve(sy, 2, b)
        sz_keep, sz_send = halve(sz, 2, b)
        g_sy, g_sz, g_sx, g_core = exchange("vert", d, [sy_send, sz_send, sx, core])
        sy, sz, sx, core = sy_keep + g_sy, sz_keep + g_sz, sx + g_sx, core + g_core
    for d in bits(n_gz):
        b = bit_of("gz", d)
        sy_keep, sy_send = halve(sy, 1, b)
        g_sy, g_sx, g_core = exchange("gz", d, [sy_send, sx, core])
        sy, sx, core = sy_keep + g_sy, sx + g_sx, core + g_core
    for d in bits(n_gx):
        b = bit_of("gx", d)
        sy_keep, sy_send = halve(sy, 0, b)
        sz_keep, sz_send = halve(sz, 1, b)
        core_keep, core_send = halve(core, 1, b)
        g_sy, g_sz, g_core = exchange("gx", d, [sy_send, sz_send, core_send])
        sy, sz = sy_keep + g_sy, sz_keep + g_sz
        core = jnp.concatenate([core_keep, g_core], axis=0)

    src = jnp.bitwise_xor(gx_me, jnp.arange(n_gx, dtype=jnp.int32))
    x_src = (src[:, None] * cells_x + jnp.arange(cells_x, dtype=jnp.int32)[None, :]).reshape(-1)
    phx = test_table(sketch_ids, x_src, total_x, core_stream, 5).astype(f32)
    held = core.reshape(n_gx, core_rows, E, cells_x).transpose(1, 2, 0, 3).reshape(core_rows, E, n_gx * cells_x)
    core_out = jnp.einsum("rej,aj->rea", held, phx, precision=highest)

    scale_x = 3.0**1.5 / math.sqrt(cells_y * total_z * total_q)
    scale_y = 3.0**1.5 / math.sqrt(total_x * total_z * total_q)
    scale_z = 3.0**1.5 / math.sqrt(total_x * cells_y * total_q)
    scale_core = 9.0 / math.sqrt(total_x * cells_y * total_z * total_q)
    return (
        sx * scale_x,
        sy.reshape(rows_each, K) * scale_y,
        sz.reshape(cells_z, cols_each) * scale_z,
        core_out * scale_core,
    )


def solution(mesh):
    in_specs = (P("groups", "vert", None, "gx", None, "gz"), P("groups"), P("groups", "vert"))
    out_specs = (
        P(("groups", "gx"), None),
        P(("groups", "gx", "gz", "vert"), None),
        P(("groups", "gz"), ("gx", "vert")),
        P(("groups", "gx"), None, None),
    )
    return jax.shard_map(shards, mesh=mesh, in_specs=in_specs, out_specs=out_specs, check_vma=False)
```

time: 125 us -> 38.5 us (0.31)
  waiting for transfers between devices: 32.4 us -> 4.43 us
  other arithmetic: 29.6 us -> 4.23 us
  between operations: 15.6 us -> 2.36 us
  blocking collectives: 13.2 us -> 0 us
  local copies, waits for them, and re-layouts: 16.8 us -> 13.8 us
  matrix products: 7.37 us -> 5.24 us
  starting transfers between devices: 10 us -> 8.16 us
    reduce_scatter x2 -> x0, waiting for transfers between devices: 29.7 us -> none  [the longest x1 29.7 us: finish(): lax.psum_scatter(part_y, ('gx', 'gz', 'vert'), scatter_dimension=0, tiled...]
    unnamed x2 -> x0, other arithmetic: 20.9 us -> none
    psum x1 -> x0, blocking collectives: 13.2 us -> none  [finish(): summed, sum_x = lax.psum((partial_core, part_x), ('gz', 'vert'))]
    all_to_all x2 -> x0, starting transfers between devices: 9.97 us -> none  [finish(): lax.all_to_all(summed, 'gx', split_axis=0, concat_axis=2, tiled=True)]
    ppermute x0 -> x4, starting transfers between devices: none -> 8.16 us  [exchange(): got = lax.ppermute(flat, axis, [(i, i ^ d) for i in range(n)])]
    unnamed x11 -> x4, local copies, waits for them, and re-layouts: 6.86 us -> 0.01 us
    reshape x2 -> x20, local copies, waits for them, and re-layouts: 0.2 us -> 6.59 us  [the longest x14 5.51 us: exchange(): out.append(got[at:at + p.size].reshape(p.shape))]
    ppermute x0 -> x4, waiting for transfers between devices: none -> 4.43 us  [exchange(): got = lax.ppermute(flat, axis, [(i, i ^ d) for i in range(n)])]
  transfers between devices with their start and end apart: 4 -> 4, of which waited for: 2 -> 3; matrix products, arithmetic and copies ran while one was open for 38% -> 8% of each run, Pallas kernels for 0% -> 0%
where the time goes in v1:
time: 38.5 us; the launch traced here: 38.2 us
  local copies, waits for them, and re-layouts  13.8 us (36%)
  starting transfers between devices  8.16 us (21%)
  matrix products  5.24 us (14%)
  waiting for transfers between devices  4.43 us (12%)
  other arithmetic  4.23 us (11%)
  between operations  2.36 us (6%)
    ppermute x4, starting transfers between devices, exchange(): got = lax.ppermute(flat, axis, [(i, i ^ d) for i in range(n)])  8.16 us
    reshape x14, local copies, waits for them, and re-layouts, exchange(): out.append(got[at:at + p.size].reshape(p.shape))  5.51 us
    ppermute x4, waiting for transfers between devices, exchange(): got = lax.ppermute(flat, axis, [(i, i ^ d) for i in range(n)])  4.43 us
    dot_general x1, local copies, waits for them, and re-layouts, shards(): jnp.dot(rows_z, az, preferred_element_type=f32)  3.25 us
    dot_general x1, matrix products, shards(): jnp.dot(rows_z, az, preferred_element_type=f32)  2.16 us
    reduce_sum x1, other arithmetic, shards(): by_q = jnp.sum(along_z * aq[:, None, None, :], axis=0)  1.94 us
    slice x1, local copies, waits for them, and re-layouts, shards(): core_stream = test_streams[1]  1.35 us
    dot_general x1, matrix products, shards(): core_out = jnp.einsum('rej,aj->rea', held, phx, precision=highest)  1.1 us
  transfers between devices with their start and end apart: 4, of which 3 were waited for; matrix products, arithmetic and copies ran while one was open for 8% of the time, Pallas kernels for 0%

profile of v1, /device:TPU:0, one launch (start us, length us, event | category | flops | bytes accessed | tf_op | source)
XLA Modules:
  0.0 38.2 jit_solution(3559514348504105740)
XLA Ops:
  0.7 1.4 %fusion.233 = (s32[1]{0:T(128)}, s32[1]{0:T(128)}) fusion(s32[2]{0:T(128)} %param.4), kind=kLoop, calls=%fused_computation.298 | loop fusion | bytes 16 | tf_op jit(solution)/shard_map/slice | solution.py:73
  2.7 2.2 %convolution_bitcast_fusion = f32[5120,128]{0,1:T(8,128)} fusion(bf16[5120,128]{1,0:T(8,128)(2,1)S(1)} %bitcast.103, s32[]{:T(128)} %bitcast, s32[128]{0:T(128)S(1)} %get-tuple-element.25), kind=kOutput, calls=%fused_computation | convolution fusion | flops 168083456 | bytes 3932676 | tf_op jit(solution)/shard_map/dot_general | solution.py:95
  4.9 3.2 %copy.25 = f32[5120,128]{1,0:T(8,128)} copy(f32[5120,128]{0,1:T(8,128)} %convolution_bitcast_fusion) | data formatting | bytes 5242880 | tf_op jit(solution)/shard_map/dot_general | solution.py:95
  8.2 0.1 mul.533
  9.0 0.6 %convolution_bitcast_fusion.1 = f32[5120,48]{0,1:T(8,128)S(1)} fusion(bf16[5120,128]{1,0:T(8,128)(2,1)S(1)} %bitcast.104, s32[]{:T(128)} %bitcast.10, s32[128]{0:T(128)S(1)} %get-tuple-element.24, s32[48]{0:T(128)S(1)} %iota_multiply_fusion.2), kind=kOutput, calls=%fused_computation.1 | convolution fusion | flops 63031296 | bytes 2294468 | tf_op jit(solution)/shard_map/dot_general | solution.py:102
  9.6 0.2 reshape.574
  9.7 0.1 mul.576
  9.8 0.5 %fusion.138 = f32[2,256,48]{1,0,2:T(2,128)S(1)} fusion(f32[20,256,48]{1,0,2:T(8,128)S(1)} %reshape.574, s32[]{:T(128)} %bitcast.10, s32[20]{0:T(128)S(1)} %mul.576), kind=kOutput, calls=%fused_computation.195 | convolution fusion | flops 5899000 | bytes 1081428 | tf_op jit(solution)/shard_map/qxyn,qe->xeyn/dot_general | solution.py:103
  10.4 0.3 convolution_bitcast_fusion.3
  10.6 0.6 %copy.29 = f32[48,48,2,1]{2,1,0,3:T(8,128)S(1)} copy(f32[48,48,2,1]{0,1,2,3:T(8,128)S(1)} %convolution_bitcast_fusion.3) | data formatting | bytes 36864 | tf_op jit(solution)/shard_map/my,xeyn->mnex/transpose | solution.py:104
  11.2 0.6 %reshape_reshape_reshape.3 = f32[4608]{0:T(1024)S(1)} reshape(f32[48,48,2,1]{2,1,0,3:T(8,128)S(1)} %copy.29) | data formatting | bytes 36864 | tf_op jit(solution)/shard_map/reshape;reshape;reshape | solution.py:45
  11.8 0.1 broadcast_multiply_fusion.1
  11.9 1.9 %multiply_reduce_fusion = f32[256,128]{1,0:T(8,128)S(1)} fusion(f32[20,1,256,128]{3,2,0,1:T(8,128)} %bitcast.106, f32[20,128]{1,0:T(8,128)S(1)} %get-tuple-element.21), kind=kLoop, calls=%fused_computation.2 | loop fusion | flops 1277952 | bytes 2762752 | tf_op jit(solution)/shard_map/reduce_sum | solution.py:96
  13.8 0.2 multiply_reduce_fusion.1
  14.0 0.6 %fusion.1 = f32[128,128]{0,1:T(8,128)S(1)} fusion(bf16[20,256,128]{2,1,0:T(8,128)(2,1)S(1)} %bitcast.105, f32[20,128]{1,0:T(8,128)S(1)} %get-tuple-element.20, s32[]{:T(128)} %bitcast, s32[256]{0:T(256)S(1)} %iota_multiply_fusion), kind=kOutput, calls=%fused_computation.5 | convolution fusion | flops 169033728 | bytes 1387524 | tf_op jit(solution)/shard_map/qxyz,yk->qxzk/dot_general | solution.py:99
  14.6 0.1 copy.27
  14.8 0.2 reshape.573
  15.0 0.5 %collective-permute-start = (f32[29312]{0:T(1024)S(1)}, f32[29312]{0:T(1024)S(1)}, u32[]{:S(2)}, u32[]{:S(2)}) collective-permute-start(f32[29312]{0:T(1024)S(1)} %pad_maximum_fusion), channel_id=1, source_target_pairs={{0,1},{1,0},{2,3},{3,2},{4,5},{5,4},{6,7},{7,6},{8,9},{9,8},{10,11... | collective-permute-start | bytes 351752 | tf_op jit(solution)/shard_map/ppermute | solution.py:46
  15.6 0.1 reshape_reshape.12
  15.7 0.8 %collective-permute-done = f32[29312]{0:T(1024)S(1)} collective-permute-done((f32[29312]{0:T(1024)S(1)}, f32[29312]{0:T(1024)S(1)}, u32[]{:S(2)}, u32[]{:S(2)}) %collective-permute-start) | collective-permute-done | bytes 117280 | tf_op jit(solution)/shard_map/ppermute | solution.py:46
  16.6 2.9 %collective-permute-start.1 = (f32[12928]{0:T(1024)S(1)}, f32[12928]{0:T(1024)S(1)}, u32[]{:S(2)}, u32[]{:S(2)}) collective-permute-start(f32[12928]{0:T(1024)S(1)} %pad_maximum_fusion.1), channel_id=1, source_target_pairs={{0,2},{2,0},{1,3},{3,1},{4,6},{6,4},{5,7},{7,5},{8,10},{10,8},{9,1... | collective-permute-start | bytes 155144 | tf_op jit(solution)/shard_map/ppermute | solution.py:46
  19.5 0.4 reshape.580
  19.9 0.2 copy.31
  20.1 1.1 %reshape.582 = f32[1,2,2,576,2,1]{4,3,2,1,5,0:T(8,128)S(1)} reshape(f32[4608]{0:T(1024)S(1)} %get-tuple-element.8) | data formatting | bytes 36864 | tf_op jit(solution)/shard_map/reshape | solution.py:49
  21.2 0.4 %copy.34 = f32[1,2,2,576,2,1]{3,2,1,4,5,0:T(2,128)S(1)} copy(f32[1,2,2,576,2,1]{4,3,2,1,5,0:T(8,128)S(1)} %reshape.582) | data formatting | bytes 36864 | tf_op jit(solution)/shard_map/reshape | solution.py:49
  21.6 0.1 copy.32
  21.7 0.2 reshape.581
  21.9 1.1 %reshape.583 = f32[1,2,2,576,2,1]{4,3,2,1,5,0:T(8,128)S(1)} reshape(f32[4608]{0:T(1024)S(1)} %slice.101) | data formatting | bytes 36864 | tf_op jit(solution)/shard_map/reshape | solution.py:49
  23.1 0.4 %copy.35 = f32[1,2,2,576,2,1]{3,2,1,4,5,0:T(2,128)S(1)} copy(f32[1,2,2,576,2,1]{4,3,2,1,5,0:T(8,128)S(1)} %reshape.583) | data formatting | bytes 36864 | tf_op jit(solution)/shard_map/reshape | solution.py:49
  23.5 0.2 copy.36
  23.8 0.3 reshape.584
  24.2 1.9 %collective-permute-start.2 = (f32[10496]{0:T(1024)S(1)}, f32[10496]{0:T(1024)S(1)}, u32[]{:S(2)}, u32[]{:S(2)}) collective-permute-start(f32[10496]{0:T(1024)S(1)} %pad_maximum_fusion.2), channel_id=1, source_target_pairs={{0,4},{4,0},{8,12},{12,8},{1,5},{5,1},{9,13},{13,9},{2,6},{6,2},{1... | collective-permute-start | bytes 125960 | tf_op jit(solution)/shard_map/ppermute | solution.py:46
  26.0 2.2 %collective-permute-done.2 = f32[10496]{0:T(1024)S(1)} collective-permute-done((f32[10496]{0:T(1024)S(1)}, f32[10496]{0:T(1024)S(1)}, u32[]{:S(2)}, u32[]{:S(2)}) %collective-permute-start.2) | collective-permute-done | bytes 42016 | tf_op jit(solution)/shard_map/ppermute | solution.py:46
  28.3 0.5 %reshape.589 = f32[1,2,576,2,1]{3,2,1,4,0:T(8,128)S(1)} reshape(f32[2304]{0:T(1024)S(1)} %slice.104) | data formatting | bytes 18432 | tf_op jit(solution)/shard_map/reshape | solution.py:49
  28.8 0.2 copy.40
  29.1 0.2 copy.41
  29.3 0.3 reshape.590
  29.6 0.2 reshape.587
  29.9 0.1 copy.38
  30.1 0.1 reshape.588
  30.2 2.9 %collective-permute-start.3 = (f32[6400]{0:T(1024)S(1)}, f32[6400]{0:T(1024)S(1)}, u32[]{:S(2)}, u32[]{:S(2)}) collective-permute-start(f32[6400]{0:T(1024)S(1)} %pad_maximum_fusion.3), channel_id=1, source_target_pairs={{0,8},{4,12},{8,0},{12,4},{1,9},{5,13},{9,1},{13,5},{2,10},{6,14},... | collective-permute-start | bytes 76808 | tf_op jit(solution)/shard_map/ppermute | solution.py:46
  33.1 0.5 %fusion.164 = f32[1,128]{1,0:T(1,128)} fusion(f32[128]{0:T(128)S(1)} %slice_add_fusion.1, f32[12928]{0:T(1024)S(1)} %collective-permute-done.1), kind=kLoop, calls=%fused_computation.227 | loop fusion | flops 256 | bytes 1536 | tf_op jit(solution)/shard_map/mul | solution.py:145
  33.6 1.4 %collective-permute-done.3 = f32[6400]{0:T(1024)S(1)} collective-permute-done((f32[6400]{0:T(1024)S(1)}, f32[6400]{0:T(1024)S(1)}, u32[]{:S(2)}, u32[]{:S(2)}) %collective-permute-start.3) | collective-permute-done | bytes 25632 | tf_op jit(solution)/shard_map/ppermute | solution.py:46
  35.2 0.6 %multiply_bitcast_fusion = f32[128,16]{0,1:T(8,128)} fusion(f32[128,1,1,16]{0,3,2,1:T(8,128)S(1)} %copy.42, f32[128,2,1,16]{0,3,2,1:T(8,128)S(1)} %bitcast_add_fusion.1, s32[]{:T(128)S(6)} %select_n.80), kind=kLoop, calls=%fused_computation.135 | loop fusion | flops 4096 | bytes 24580 | tf_op jit(solution)/shard_map/mul | solution.py:147
  35.8 0.5 %reshape.592 = f32[2,1,576,2,1]{3,2,0,4,1:T(8,128)S(1)} reshape(f32[2304]{0:T(1024)S(1)} %slice.107) | data formatting | bytes 18432 | tf_op jit(solution)/shard_map/reshape | solution.py:49
  36.3 0.2 copy.43
  36.5 1.1 %convolution_multiply_fusion = f32[576,2,48]{0,2,1:T(8,128)} fusion(f32[2,1,576,2,1]{2,0,3,4,1:T(2,128)S(1)} %copy.43, f32[2,1,576,2,1]{2,0,3,4,1:T(2,128)S(1)} %get-tuple-element.14, s32[]{:T(128)} %bitcast.10, s32[4]{0:T(128)S(1)} %iota_xor_fusion, s32[48]{0:T(128)S(1)} %iota_multiply_fusion.1), kind=kOutput, calls=%fused_computation.6 | convolution fusion | flops 2717760 | bytes 239828 | tf_op jit(solution)/shard_map/rej,aj->rea/dot_general | solution.py:138
  37.6 0.6 %fusion.99 = f32[16,128]{1,0:T(8,128)} fusion(f32[6400]{0:T(1024)S(1)} %collective-permute-done.3, f32[2,1,1,16,128]{4,3,0,2,1:T(8,128)S(1)} %bitcast_add_fusion.2, s32[]{:T(128)S(6)} %select_n.80), kind=kLoop, calls=%fused_computation.134 | loop fusion | flops 4096 | bytes 24580 | tf_op jit(solution)/shard_map/mul | solution.py:146
  (48 shorter events, 0.7 us)
Async XLA Ops:
  0.6 2.1 %copy-start = (bf16[2,2,5,1,256,128]{5,4,3,2,1,0:T(8,128)(2,1)S(1)}, bf16[2,2,5,1,256,128]{5,4,3,2,1,0:T(8,128)(2,1)}, u32[]{:S(2)}) copy-start(bf16[2,2,5,1,256,128]{5,4,3,2,1,0:T(8,128)(2,1)} %param.3) | copy-start | bytes 3932164
  4.9 3.3 %copy-start.1 = (s32[2,2]{1,0:T(2,128)S(1)}, s32[2,2]{1,0:T(2,128)}, u32[]{:S(2)}) copy-start(s32[2,2]{1,0:T(2,128)} %param.5) | copy-start | bytes 52
  15.0 1.5 %collective-permute-start = (f32[29312]{0:T(1024)S(1)}, f32[29312]{0:T(1024)S(1)}, u32[]{:S(2)}, u32[]{:S(2)}) collective-permute-start(f32[29312]{0:T(1024)S(1)} %pad_maximum_fusion), channel_id=1, source_target_pairs={{0,1},{1,0},{2,3},{3,2},{4,5},{5,4},{6,7},{7,6},{8,9},{9,8},{10,11... | collective-permute-start | bytes 351752 | tf_op jit(solution)/shard_map/ppermute | solution.py:46
  16.6 5.3 %collective-permute-start.1 = (f32[12928]{0:T(1024)S(1)}, f32[12928]{0:T(1024)S(1)}, u32[]{:S(2)}, u32[]{:S(2)}) collective-permute-start(f32[12928]{0:T(1024)S(1)} %pad_maximum_fusion.1), channel_id=1, source_target_pairs={{0,2},{2,0},{1,3},{3,1},{4,6},{6,4},{5,7},{7,5},{8,10},{10,8},{9,1... | collective-permute-start | bytes 155144 | tf_op jit(solution)/shard_map/ppermute | solution.py:46
  24.2 4.1 %collective-permute-start.2 = (f32[10496]{0:T(1024)S(1)}, f32[10496]{0:T(1024)S(1)}, u32[]{:S(2)}, u32[]{:S(2)}) collective-permute-start(f32[10496]{0:T(1024)S(1)} %pad_maximum_fusion.2), channel_id=1, source_target_pairs={{0,4},{4,0},{8,12},{12,8},{1,5},{5,1},{9,13},{13,9},{2,6},{6,2},{1... | collective-permute-start | bytes 125960 | tf_op jit(solution)/shard_map/ppermute | solution.py:46
  30.2 4.8 %collective-permute-start.3 = (f32[6400]{0:T(1024)S(1)}, f32[6400]{0:T(1024)S(1)}, u32[]{:S(2)}, u32[]{:S(2)}) collective-permute-start(f32[6400]{0:T(1024)S(1)} %pad_maximum_fusion.3), channel_id=1, source_target_pairs={{0,8},{4,12},{8,0},{12,4},{1,9},{5,13},{9,1},{13,5},{2,10},{6,14},... | collective-permute-start | bytes 76808 | tf_op jit(solution)/shard_map/ppermute | solution.py:46

commit v2 on v1

v2 whole, which is shorter than its diff:
```python
import math

import jax
import jax.numpy as jnp
from jax import lax
from jax.sharding import PartitionSpec as P

K = 128
S = 48
E = 2


def hash_index(index, stream, salt):
    mixed = index * -1640531535 + stream * -2048144777 + salt
    mixed = jnp.bitwise_xor(mixed, lax.shift_right_logical(mixed, jnp.int32(16)))
    mixed = mixed * 739982445
    mixed = jnp.bitwise_xor(mixed, lax.shift_right_logical(mixed, jnp.int32(13)))
    mixed = mixed * 695872825
    return jnp.bitwise_xor(mixed, lax.shift_right_logical(mixed, jnp.int32(16)))


def unit_value(index, stream, salt):
    upper = lax.shift_right_logical(hash_index(index, stream, salt), jnp.int32(9))
    return ((2 * upper + 1).astype(jnp.float32) * 2.0 ** (-24) - 1.0).astype(jnp.bfloat16)


def test_table(row_ids, col_ids, stride, stream, salt):
    return unit_value(row_ids[:, None] * stride + col_ids[None, :], stream, salt)


def digit_steps(n):
    d, out = 1, []
    while d < n:
        r = 4 if n // d >= 4 else 2
        out.append((d, r))
        d *= r
    return out


def split_digit(arr, dim, r, digit):
    shape = arr.shape
    split = arr.reshape(shape[:dim] + (shape[dim] // r, r) + shape[dim + 1 :])

    def at(s):
        return lax.dynamic_index_in_dim(split, jnp.bitwise_xor(digit, s), dim + 1, keepdims=False)

    return at


def send_to(axes, n, shift, pieces):
    dense = all(p.size % 128 == 0 for p in pieces)
    if dense:
        flat = jnp.concatenate([p.reshape(-1, 128) for p in pieces], axis=0)
    else:
        flat = jnp.concatenate([p.reshape(-1) for p in pieces])
    got = lax.ppermute(flat, axes, [(i, i ^ shift) for i in range(n)])
    out, at = [], 0
    for p in pieces:
        rows = p.size // 128 if dense else p.size
        out.append(got[at : at + rows].reshape(p.shape))
        at += rows
    return out


def linear_index(axes):
    idx = 0
    for a in axes:
        idx = idx * lax.axis_size(a) + lax.axis_index(a)
    return idx


def shards(flow_field, test_streams, snapshot_ids):
    highest = lax.Precision.HIGHEST
    f32 = jnp.float32
    bf16 = jnp.bfloat16
    batches, local_snaps, variables, cells_x, cells_y, cells_z = flow_field.shape
    n_gx = lax.axis_size("gx")
    n_gz = lax.axis_size("gz")
    n_vert = lax.axis_size("vert")
    total_x = cells_x * n_gx
    total_z = cells_z * n_gz
    total_q = variables * batches * local_snaps * n_vert
    factor_stream = test_streams[0]
    core_stream = test_streams[1]
    gx_me = lax.axis_index("gx")
    rank_ids = jnp.arange(K, dtype=jnp.int32)
    sketch_ids = jnp.arange(S, dtype=jnp.int32)
    x_ids = gx_me * cells_x + jnp.arange(cells_x, dtype=jnp.int32)
    y_ids = jnp.arange(cells_y, dtype=jnp.int32)
    z_ids = lax.axis_index("gz") * cells_z + jnp.arange(cells_z, dtype=jnp.int32)
    q_ids = (
        snapshot_ids[:, :, None] * variables + jnp.arange(variables, dtype=jnp.int32)[None, None, :]
    ).reshape(-1)
    ax = test_table(x_ids, rank_ids, K, factor_stream, 1).astype(f32)
    ay = test_table(y_ids, rank_ids, K, factor_stream, 2)
    az = test_table(z_ids, rank_ids, K, factor_stream, 3)
    aq = test_table(q_ids, rank_ids, K, factor_stream, 4).astype(f32)
    phy = test_table(sketch_ids, y_ids, cells_y, core_stream, 6).astype(f32)
    phz = test_table(sketch_ids, z_ids, total_z, core_stream, 7)
    phq = test_table(q_ids, jnp.arange(E, dtype=jnp.int32), E, core_stream, 8).astype(f32)

    n_q = batches * local_snaps * variables
    field = flow_field.reshape(n_q, cells_x, cells_y, cells_z)
    rows_z = field.reshape(-1, cells_z)

    qz = aq[:, None, :] * az.astype(f32)[None, :, :]
    qz_hi = qz.astype(bf16)
    qz_lo = (qz - qz_hi.astype(f32)).astype(bf16)
    both = jnp.einsum(
        "qxyz,qzk->xyk", field, jnp.concatenate([qz_hi, qz_lo], axis=-1), preferred_element_type=f32
    )
    by_q = both[..., :K] + both[..., K:]
    part_y = jnp.sum(by_q * ax[:, None, :], axis=0)
    part_x = jnp.sum(by_q * ay.astype(f32)[None, :, :], axis=1)
    along_y = jnp.einsum("qxyz,yk->qxzk", field, ay, preferred_element_type=f32)
    weights = aq[:, None, :] * ax[None, :, :]
    part_z = jnp.sum(along_y * weights[:, :, None, :], axis=(0, 1))
    first = jnp.dot(rows_z, phz.T, preferred_element_type=f32).reshape(n_q, cells_x, cells_y, S)
    by_e = jnp.einsum("qxyn,qe->xeyn", first, phq, precision=highest)
    part_core = jnp.einsum("my,xeyn->xemn", phy, by_e, precision=highest)

    rows_each = cells_y // (n_gx * n_gz * n_vert)
    cols_each = K // (n_gx * n_vert)
    core_rows = S * S // n_gx
    n_gzv = n_gz * n_vert
    sy = part_y.reshape(n_gx, n_gzv, rows_each, K)
    sz = part_z.T.reshape(n_gx, n_vert, cols_each, cells_z)
    sx = part_x
    core = (
        part_core.reshape(cells_x, E, n_gx, core_rows)
        .transpose(2, 0, 1, 3)
        .reshape(1, n_gx, cells_x * E * core_rows)
    )

    v_me = lax.axis_index("vert")
    for d, r in digit_steps(n_vert):
        digit = (v_me // d) % r
        at = split_digit(sz, 1, r, digit)
        total = at(0)
        for s in range(1, r):
            (got,) = send_to("vert", n_vert, s * d, [at(s)])
            total = total + got
        sz = total
    gzv_me = linear_index(("gz", "vert"))
    for d, r in digit_steps(n_gzv):
        digit = (gzv_me // d) % r
        at = split_digit(sy, 1, r, digit)
        sy_total, sx_total, core_total = at(0), sx, core
        for s in range(1, r):
            g_sy, g_sx, g_core = send_to(("gz", "vert"), n_gzv, s * d, [at(s), sx, core])
            sy_total, sx_total, core_total = sy_total + g_sy, sx_total + g_sx, core_total + g_core
        sy, sx, core = sy_total, sx_total, core_total
    for d, r in digit_steps(n_gx):
        digit = (gx_me // d) % r
        at_y = split_digit(sy, 0, r, digit)
        at_z = split_digit(sz, 0, r, digit)
        at_c = split_digit(core, 1, r, digit)
        sy_total, sz_total, core_parts = at_y(0), at_z(0), [at_c(0)]
        for s in range(1, r):
            g_sy, g_sz, g_core = send_to("gx", n_gx, s * d, [at_y(s), at_z(s), at_c(s)])
            sy_total, sz_total = sy_total + g_sy, sz_total + g_sz
            core_parts.append(g_core)
        sy, sz = sy_total, sz_total
        core = jnp.concatenate(core_parts, axis=0)

    src = jnp.bitwise_xor(gx_me, jnp.arange(n_gx, dtype=jnp.int32))
    x_src = (src[:, None] * cells_x + jnp.arange(cells_x, dtype=jnp.int32)[None, :]).reshape(-1)
    phx = test_table(sketch_ids, x_src, total_x, core_stream, 5).astype(f32).reshape(S, n_gx, cells_x)
    held = core.reshape(n_gx, cells_x, E, core_rows)
    core_out = jnp.einsum("jxer,ajx->rea", held, phx, precision=highest)

    scale_x = 3.0**1.5 / math.sqrt(cells_y * total_z * total_q)
    scale_y = 3.0**1.5 / math.sqrt(total_x * total_z * total_q)
    scale_z = 3.0**1.5 / math.sqrt(total_x * cells_y * total_q)
    scale_core = 9.0 / math.sqrt(total_x * cells_y * total_z * total_q)
    return (
        sx * scale_x,
        sy.reshape(rows_each, K) * scale_y,
        sz.reshape(cols_each, cells_z).T * scale_z,
        core_out * scale_core,
    )


def solution(mesh):
    in_specs = (P("groups", "vert", None, "gx", None, "gz"), P("groups"), P("groups", "vert"))
    out_specs = (
        P(("groups", "gx"), None),
        P(("groups", "gx", "gz", "vert"), None),
        P(("groups", "gz"), ("gx", "vert")),
        P(("groups", "gx"), None, None),
    )
    return jax.shard_map(shards, mesh=mesh, in_specs=in_specs, out_specs=out_specs, check_vma=False)
```

time: 38.5 us -> 24.9 us (0.65)
  local copies, waits for them, and re-layouts: 13.8 us -> 3.05 us
  other arithmetic: 4.23 us -> 2.04 us
  matrix products: 5.24 us -> 3.5 us
  waiting for transfers between devices: 4.43 us -> 5.79 us
    reshape x20 -> x7, local copies, waits for them, and re-layouts: 6.59 us -> 0.24 us  [the longest x1 0.09 us: shards(): part_core.reshape(cells_x, E, n_gx, core_rows).transpose(2, 0, 1, 3)]
    dot_general x1 -> x0, local copies, waits for them, and re-layouts: 3.25 us -> none  [shards(): jnp.dot(rows_z, az, preferred_element_type=f32)]
    reduce_sum x2 -> x0, other arithmetic: 2.12 us -> none  [the longest x1 1.94 us: shards(): by_q = jnp.sum(along_z * aq[:, None, None, :], axis=0)]
    dot_general x3, matrix products: 3.53 us -> 1.87 us  [the longest x1 1.09 us: shards(): core_out = jnp.einsum('jxer,ajx->rea', held, phx, precision=highest)]
    ppermute x4 -> x7, waiting for transfers between devices: 4.43 us -> 5.79 us  [send_to(): got = lax.ppermute(flat, axes, [(i, i ^ shift) for i in range(n)])]
    another operation x7 -> x2, local copies, waits for them, and re-layouts: 1.18 us -> 0.25 us  [the longest x1 0.55 us: exchange(): flat = jnp.concatenate([p.reshape(-1) for p in pieces])]
    mul x2 -> x1, other arithmetic: 1.23 us -> 0.61 us  [shards(): sz.reshape(cols_each, cells_z).T * scale_z]
    transpose x2, local copies, waits for them, and re-layouts: 0.67 us -> 0.09 us  [the longest x1 0.07 us: shards(): part_core = jnp.einsum('my,xeyn->xemn', phy, by_e, precision=highest)]
  transfers between devices with their start and end apart: 4 -> 7, of which waited for: 3 -> 4; matrix products, arithmetic and copies ran while one was open for 8% -> 6% of each run, Pallas kernels for 0% -> 0%
where the time goes in v2:
time: 24.9 us; the launch traced here: 24.7 us
  starting transfers between devices  8.1 us (33%)
  waiting for transfers between devices  5.79 us (23%)
  matrix products  3.5 us (14%)
  local copies, waits for them, and re-layouts  3.05 us (12%)
  between operations  2.23 us (9%)
  other arithmetic  2.04 us (8%)
    ppermute x7, starting transfers between devices, send_to(): got = lax.ppermute(flat, axes, [(i, i ^ shift) for i in range(n)])  8.1 us
    ppermute x7, waiting for transfers between devices, send_to(): got = lax.ppermute(flat, axes, [(i, i ^ shift) for i in range(n)])  5.79 us
    slice x1, local copies, waits for them, and re-layouts, shards(): factor_stream = test_streams[0]  1.35 us
    dot_general x1, matrix products, shards(): core_out = jnp.einsum('jxer,ajx->rea', held, phx, precision=highest)  1.09 us
    mul x1, other arithmetic, shards(): sz.reshape(cols_each, cells_z).T * scale_z  0.61 us
    dot_general x1, matrix products, shards(): jnp.dot(rows_z, phz.T, preferred_element_type=f32)  0.6 us
    dot_general x1, matrix products, shards(): by_e = jnp.einsum('qxyn,qe->xeyn', first, phq, precision=highest)  0.54 us
    unnamed x4, local copies, waits for them, and re-layouts  0.52 us
  transfers between devices with their start and end apart: 7, of which 4 were waited for; matrix products, arithmetic and copies ran while one was open for 6% of the time, Pallas kernels for 0%

profile of v2, /device:TPU:0, one launch (start us, length us, event | category | flops | bytes accessed | tf_op | source)
XLA Modules:
  0.0 24.7 jit_solution(17103712076625255542)
XLA Ops:
  0.6 0.0 copy-start
  0.7 1.3 %fusion.242 = (s32[1]{0:T(128)}, s32[1]{0:T(128)}) fusion(s32[2]{0:T(128)} %param.4), kind=kLoop, calls=%fused_computation.316 | loop fusion | bytes 16 | tf_op jit(solution)/shard_map/slice | solution.py:83
  2.7 0.0 copy-done
  2.7 0.6 %convolution_bitcast_fusion = f32[5120,48]{0,1:T(8,128)S(1)} fusion(bf16[5120,128]{1,0:T(8,128)(2,1)S(1)} %bitcast.95, s32[]{:T(128)} %bitcast.10, s32[128]{0:T(128)S(1)} %get-tuple-element.32, s32[48]{0:T(128)S(1)} %iota_multiply_fusion.2), kind=kOutput, calls=%fused_computation | convolution fusion | flops 63031296 | bytes 2294468 | tf_op jit(solution)/shard_map/dot_general | solution.py:118
  3.3 0.0 copy-start.1
  3.3 0.2 reshape.623
  3.5 0.5 %copy-done.1 = s32[2,2]{1,0:T(2,128)S(1)} copy-done((s32[2,2]{1,0:T(2,128)S(1)}, s32[2,2]{1,0:T(2,128)}, u32[]{:S(2)}) %copy-start.1) | copy-done | bytes 40
  4.0 0.1 fusion.133
  4.1 0.1 mul.633
  4.2 0.5 %fusion.160 = f32[2,256,48]{1,0,2:T(2,128)S(1)} fusion(f32[20,256,48]{1,0,2:T(8,128)S(1)} %reshape.623, s32[]{:T(128)} %bitcast.10, s32[20]{0:T(128)S(1)} %mul.633), kind=kOutput, calls=%fused_computation.226 | convolution fusion | flops 5899000 | bytes 1081428 | tf_op jit(solution)/shard_map/qxyn,qe->xeyn/dot_general | solution.py:119
  4.7 0.3 %convolution_bitcast_fusion.2 = f32[1,2,48,48]{2,3,1,0:T(8,128)S(1)} fusion(f32[2,256,48]{1,0,2:T(2,128)S(1)} %fusion.160, s32[]{:T(128)} %bitcast.10, s32[48]{0:T(128)S(1)} %iota_multiply_fusion.2), kind=kOutput, calls=%fused_computation.14 | convolution fusion | flops 14389248 | bytes 116932 | tf_op jit(solution)/shard_map/my,xeyn->xemn/dot_general | solution.py:120
  5.0 0.1 copy.10
  5.0 0.1 reshape.624
  5.2 0.1 reshape_reshape.16
  5.9 0.1 fusion.62
  6.0 0.1 mul.577
  6.1 0.1 broadcast_multiply_fusion.1
  6.2 0.3 %multiply_convert_fusion = (bf16[20,128,128]{2,1,0:T(8,128)(2,1)S(1)}, bf16[20,128,128]{2,1,0:T(8,128)(2,1)S(1)}) fusion(f32[128,128]{1,0:T(8,128)S(1)} %fusion.62, f32[20,128]{1,0:T(8,128)S(1)} %get-tuple-element.29), kind=kLoop, calls=%fused_computation.2 | loop fusion | flops 1638400 | bytes 1386496 | tf_op jit(solution)/shard_map/convert_element_type | solution.py:107
  6.6 0.5 %fusion.7 = f32[1,256,256]{2,1,0:T(8,128)S(1)} fusion(bf16[20,256,128]{2,1,0:T(8,128)(2,1)S(1)} %bitcast.96, bf16[20,128,128]{2,1,0:T(8,128)(2,1)S(1)} %get-tuple-element.14, bf16[20,128,128]{2,1,0:T(8,128)(2,1)S(1)} %get-tuple-element.13), kind=kOutput, calls=%fused_computation.11 | convolution fusion | flops 338165760 | bytes 2883584 | tf_op jit(solution)/shard_map/qxyz,qzk->xyk/dot_general | solution.py:109
  7.1 0.2 broadcast_multiply_fusion
  7.3 2.4 %collective-permute-start.2 = (f32[101,128]{1,0:T(8,128)S(1)}, f32[101,128]{1,0:T(8,128)S(1)}, u32[]{:S(2)}, u32[]{:S(2)}) collective-permute-start(f32[101,128]{1,0:T(8,128)S(1)} %get-tuple-element.25), channel_id=1, source_target_pairs={{0,3},{1,2},{2,1},{3,0},{4,7},{5,6},{6,5},{7,4},{8,11},{9,10},{10,... | collective-permute-start | bytes 155144 | tf_op jit(solution)/shard_map/ppermute | solution.py:56
  9.8 0.6 %collective-permute-start.1 = (f32[101,128]{1,0:T(8,128)S(1)}, f32[101,128]{1,0:T(8,128)S(1)}, u32[]{:S(2)}, u32[]{:S(2)}) collective-permute-start(f32[101,128]{1,0:T(8,128)S(1)} %get-tuple-element.24), channel_id=1, source_target_pairs={{0,2},{1,3},{2,0},{3,1},{4,6},{5,7},{6,4},{7,5},{8,10},{9,11},{10,... | collective-permute-start | bytes 155144 | tf_op jit(solution)/shard_map/ppermute | solution.py:56
  10.4 0.0 collective-permute-start
  10.5 0.5 %fusion.6 = f32[128,128]{0,1:T(8,128)S(1)} fusion(bf16[20,256,128]{2,1,0:T(8,128)(2,1)S(1)} %bitcast.97, f32[20,128]{1,0:T(8,128)S(1)} %get-tuple-element.28, s32[]{:T(128)} %bitcast, s32[256]{0:T(256)S(1)} %iota_multiply_fusion), kind=kOutput, calls=%fused_computation.10 | convolution fusion | flops 169033728 | bytes 1387524 | tf_op jit(solution)/shard_map/qxyz,yk->qxzk/dot_general | solution.py:115
  11.0 0.5 %collective-permute-start.3 = (f32[64,128]{1,0:T(8,128)S(1)}, f32[64,128]{1,0:T(8,128)S(1)}, u32[]{:S(2)}, u32[]{:S(2)}) collective-permute-start(f32[64,128]{1,0:T(8,128)S(1)} %bitcast.110), channel_id=1, source_target_pairs={{0,1},{1,0},{2,3},{3,2},{4,5},{5,4},{6,7},{7,6},{8,9},{9,8},{10,11... | collective-permute-start | bytes 98312 | tf_op jit(solution)/shard_map/ppermute | solution.py:56
  11.5 0.1 reshape.634
  11.6 0.8 %collective-permute-done.3 = f32[64,128]{1,0:T(8,128)S(1)} collective-permute-done((f32[64,128]{1,0:T(8,128)S(1)}, f32[64,128]{1,0:T(8,128)S(1)}, u32[]{:S(2)}, u32[]{:S(2)}) %collective-permute-start.3) | collective-permute-done | bytes 32800 | tf_op jit(solution)/shard_map/ppermute | solution.py:56
  12.4 0.0 collective-permute-done.2
  12.4 1.8 %collective-permute-done.1 = f32[101,128]{1,0:T(8,128)S(1)} collective-permute-done((f32[101,128]{1,0:T(8,128)S(1)}, f32[101,128]{1,0:T(8,128)S(1)}, u32[]{:S(2)}, u32[]{:S(2)}) %collective-permute-start.1) | collective-permute-done | bytes 51744 | tf_op jit(solution)/shard_map/ppermute | solution.py:56
  14.2 0.0 collective-permute-done
  14.3 0.1 dynamic-slice_reduce_fusion
  14.4 3.7 %collective-permute-start.6 = (f32[41,128]{1,0:T(8,128)S(1)}, f32[41,128]{1,0:T(8,128)S(1)}, u32[]{:S(2)}, u32[]{:S(2)}) collective-permute-start(f32[41,128]{1,0:T(8,128)S(1)} %pad_maximum_fusion.8), channel_id=1, source_target_pairs={{0,12},{4,8},{8,4},{12,0},{1,13},{5,9},{9,5},{13,1},{2,14},{6,10},... | collective-permute-start | bytes 62984 | tf_op jit(solution)/shard_map/ppermute | solution.py:56
  18.1 0.0 collective-permute-start.5
  18.1 0.8 %collective-permute-start.4 = (f32[41,128]{1,0:T(8,128)S(1)}, f32[41,128]{1,0:T(8,128)S(1)}, u32[]{:S(2)}, u32[]{:S(2)}) collective-permute-start(f32[41,128]{1,0:T(8,128)S(1)} %pad_maximum_fusion.6), channel_id=1, source_target_pairs={{0,4},{4,0},{8,12},{12,8},{1,5},{5,1},{9,13},{13,9},{2,6},{6,2},{1... | collective-permute-start | bytes 62984 | tf_op jit(solution)/shard_map/ppermute | solution.py:56
  18.9 0.5 %fusion.172 = f32[1,128]{1,0:T(1,128)} fusion(f32[101,128]{1,0:T(8,128)S(1)} %collective-permute-done.2, f32[101,128]{1,0:T(8,128)S(1)} %collective-permute-done.1, f32[101,128]{1,0:T(8,128)S(1)} %collective-permute-done, f32[128]{0:T(128)S(1)} %get-tuple-element.9), kind=kLoop, calls=%fused_computation.238 | loop fusion | flops 512 | bytes 2560 | tf_op jit(solution)/shard_map/mul | solution.py:177
  19.4 0.1 concatenate.40
  19.5 0.6 %collective-permute-done.6 = f32[41,128]{1,0:T(8,128)S(1)} collective-permute-done((f32[41,128]{1,0:T(8,128)S(1)}, f32[41,128]{1,0:T(8,128)S(1)}, u32[]{:S(2)}, u32[]{:S(2)}) %collective-permute-start.6) | collective-permute-done | bytes 21024 | tf_op jit(solution)/shard_map/ppermute | solution.py:56
  20.1 0.1 concatenate.43
  20.2 2.6 %collective-permute-done.5 = f32[41,128]{1,0:T(8,128)S(1)} collective-permute-done((f32[41,128]{1,0:T(8,128)S(1)}, f32[41,128]{1,0:T(8,128)S(1)}, u32[]{:S(2)}, u32[]{:S(2)}) %collective-permute-start.5) | collective-permute-done | bytes 21024 | tf_op jit(solution)/shard_map/ppermute | solution.py:56
  22.8 0.1 concatenate.42
  22.9 0.0 collective-permute-done.4
  22.9 0.1 concatenate.41
  23.0 1.1 %fusion.10 = f32[576,2,48]{0,2,1:T(8,128)} fusion(f32[1,1,2,576]{3,0,2,1:T(1,128)S(1)} %concatenate.43, f32[1,1,2,576]{3,0,2,1:T(1,128)S(1)} %concatenate.42, f32[1,1,2,576]{3,0,2,1:T(1,128)S(1)} %concatenate.41, f32[1,1,2,576]{3,0,2,1:T(1,128)S(1)} %concatenate.40, s32[]{:T(128)} %bitcast.10, s32[4]{0:T(128)S(1)} %iota_xor_fusion, ...), kind=kOutput, calls=%fused_computation.13 | convolution fusion | flops 2726976 | bytes 239828 | tf_op jit(solution)/shard_map/jxer,ajx->rea/dot_general | solution.py:170
  24.1 0.6 %fusion.120 = (f32[128,16]{0,1:T(8,128)}, f32[16,128]{1,0:T(8,128)}) fusion(f32[41,128]{1,0:T(8,128)S(1)} %collective-permute-done.6, f32[41,128]{1,0:T(8,128)S(1)} %collective-permute-done.5, f32[41,128]{1,0:T(8,128)S(1)} %collective-permute-done.4, f32[4,1,16,128]{3,2,0,1:T(8,128)S(1)} %bitcast_add_fusion, s32[]{:T(128)S(6)} %select_n.67, ...), kind=kLoop, calls=%fused_computation.156 | loop fusion | flops 16384 | bytes 81924 | tf_op jit(solution)/shard_map/mul | solution.py:179
  (31 shorter events, 0.2 us)
Async XLA Ops:
  0.6 2.1 %copy-start = (bf16[2,2,5,1,256,128]{5,4,3,2,1,0:T(8,128)(2,1)S(1)}, bf16[2,2,5,1,256,128]{5,4,3,2,1,0:T(8,128)(2,1)}, u32[]{:S(2)}) copy-start(bf16[2,2,5,1,256,128]{5,4,3,2,1,0:T(8,128)(2,1)} %param.3) | copy-start | bytes 3932164
  3.3 0.7 %copy-start.1 = (s32[2,2]{1,0:T(2,128)S(1)}, s32[2,2]{1,0:T(2,128)}, u32[]{:S(2)}) copy-start(s32[2,2]{1,0:T(2,128)} %param.5) | copy-start | bytes 52
  7.3 5.1 %collective-permute-start.2 = (f32[101,128]{1,0:T(8,128)S(1)}, f32[101,128]{1,0:T(8,128)S(1)}, u32[]{:S(2)}, u32[]{:S(2)}) collective-permute-start(f32[101,128]{1,0:T(8,128)S(1)} %get-tuple-element.25), channel_id=1, source_target_pairs={{0,3},{1,2},{2,1},{3,0},{4,7},{5,6},{6,5},{7,4},{8,11},{9,10},{10,... | collective-permute-start | bytes 155144 | tf_op jit(solution)/shard_map/ppermute | solution.py:56
  9.8 4.4 %collective-permute-start.1 = (f32[101,128]{1,0:T(8,128)S(1)}, f32[101,128]{1,0:T(8,128)S(1)}, u32[]{:S(2)}, u32[]{:S(2)}) collective-permute-start(f32[101,128]{1,0:T(8,128)S(1)} %get-tuple-element.24), channel_id=1, source_target_pairs={{0,2},{1,3},{2,0},{3,1},{4,6},{5,7},{6,4},{7,5},{8,10},{9,11},{10,... | collective-permute-start | bytes 155144 | tf_op jit(solution)/shard_map/ppermute | solution.py:56
  10.4 3.8 %collective-permute-start = (f32[101,128]{1,0:T(8,128)S(1)}, f32[101,128]{1,0:T(8,128)S(1)}, u32[]{:S(2)}, u32[]{:S(2)}) collective-permute-start(f32[101,128]{1,0:T(8,128)S(1)} %get-tuple-element.23), channel_id=1, source_target_pairs={{0,1},{1,0},{2,3},{3,2},{4,5},{5,4},{6,7},{7,6},{8,9},{9,8},{10,11... | collective-permute-start | bytes 155144 | tf_op jit(solution)/shard_map/ppermute | solution.py:56
  11.0 1.4 %collective-permute-start.3 = (f32[64,128]{1,0:T(8,128)S(1)}, f32[64,128]{1,0:T(8,128)S(1)}, u32[]{:S(2)}, u32[]{:S(2)}) collective-permute-start(f32[64,128]{1,0:T(8,128)S(1)} %bitcast.110), channel_id=1, source_target_pairs={{0,1},{1,0},{2,3},{3,2},{4,5},{5,4},{6,7},{7,6},{8,9},{9,8},{10,11... | collective-permute-start | bytes 98312 | tf_op jit(solution)/shard_map/ppermute | solution.py:56
  14.4 5.7 %collective-permute-start.6 = (f32[41,128]{1,0:T(8,128)S(1)}, f32[41,128]{1,0:T(8,128)S(1)}, u32[]{:S(2)}, u32[]{:S(2)}) collective-permute-start(f32[41,128]{1,0:T(8,128)S(1)} %pad_maximum_fusion.8), channel_id=1, source_target_pairs={{0,12},{4,8},{8,4},{12,0},{1,13},{5,9},{9,5},{13,1},{2,14},{6,10},... | collective-permute-start | bytes 62984 | tf_op jit(solution)/shard_map/ppermute | solution.py:56
  18.1 4.7 %collective-permute-start.5 = (f32[41,128]{1,0:T(8,128)S(1)}, f32[41,128]{1,0:T(8,128)S(1)}, u32[]{:S(2)}, u32[]{:S(2)}) collective-permute-start(f32[41,128]{1,0:T(8,128)S(1)} %pad_maximum_fusion.7), channel_id=1, source_target_pairs={{0,8},{4,12},{8,0},{12,4},{1,9},{5,13},{9,1},{13,5},{2,10},{6,14},... | collective-permute-start | bytes 62984 | tf_op jit(solution)/shard_map/ppermute | solution.py:56
  18.1 4.8 %collective-permute-start.4 = (f32[41,128]{1,0:T(8,128)S(1)}, f32[41,128]{1,0:T(8,128)S(1)}, u32[]{:S(2)}, u32[]{:S(2)}) collective-permute-start(f32[41,128]{1,0:T(8,128)S(1)} %pad_maximum_fusion.6), channel_id=1, source_target_pairs={{0,4},{4,0},{8,12},{12,8},{1,5},{5,1},{9,13},{13,9},{2,6},{6,2},{1... | collective-permute-start | bytes 62984 | tf_op jit(solution)/shard_map/ppermute | solution.py:56

commit v3 on v2

--- a/solution.py
+++ b/solution.py
@@ -132,36 +132,67 @@
         .reshape(1, n_gx, cells_x * E * core_rows)
     )
 
-    v_me = lax.axis_index("vert")
-    for d, r in digit_steps(n_vert):
-        digit = (v_me // d) % r
-        at = split_digit(sz, 1, r, digit)
-        total = at(0)
-        for s in range(1, r):
-            (got,) = send_to("vert", n_vert, s * d, [at(s)])
-            total = total + got
-        sz = total
-    gzv_me = linear_index(("gz", "vert"))
-    for d, r in digit_steps(n_gzv):
-        digit = (gzv_me // d) % r
-        at = split_digit(sy, 1, r, digit)
-        sy_total, sx_total, core_total = at(0), sx, core
-        for s in range(1, r):
-            g_sy, g_sx, g_core = send_to(("gz", "vert"), n_gzv, s * d, [at(s), sx, core])
-            sy_total, sx_total, core_total = sy_total + g_sy, sx_total + g_sx, core_total + g_core
-        sy, sx, core = sy_total, sx_total, core_total
-    for d, r in digit_steps(n_gx):
-        digit = (gx_me // d) % r
-        at_y = split_digit(sy, 0, r, digit)
-        at_z = split_digit(sz, 0, r, digit)
-        at_c = split_digit(core, 1, r, digit)
-        sy_total, sz_total, core_parts = at_y(0), at_z(0), [at_c(0)]
-        for s in range(1, r):
-            g_sy, g_sz, g_core = send_to("gx", n_gx, s * d, [at_y(s), at_z(s), at_c(s)])
-            sy_total, sz_total = sy_total + g_sy, sz_total + g_sz
-            core_parts.append(g_core)
-        sy, sz = sy_total, sz_total
-        core = jnp.concatenate(core_parts, axis=0)
+    n_run = n_gx * n_gzv
+    if n_run <= 16:
+        me = linear_index(("gx", "gz", "vert"))
+        v_me = lax.axis_index("vert")
+        gz_me = lax.axis_index("gz")
+        sy_blocks = sy.reshape(n_run, rows_each, K)
+        sz_blocks = sz.reshape(n_gx * n_vert, cols_each, cells_z)
+        core_blocks = core.reshape(n_gx, -1)
+        own = lambda arr, i: lax.dynamic_index_in_dim(arr, i, 0, keepdims=False)
+        sy_total = own(sy_blocks, me)
+        sz_total = own(sz_blocks, gx_me * n_vert + v_me)
+        sx_total = sx
+        held = [own(core_blocks, gx_me)] + [None] * (n_gx - 1)
+        for s in range(1, n_run):
+            s_gx, s_gz, s_v = s // n_gzv, (s // n_vert) % n_gz, s % n_vert
+            to_gx = jnp.bitwise_xor(gx_me, s_gx)
+            pieces = [own(sy_blocks, jnp.bitwise_xor(me, s)), own(core_blocks, to_gx)]
+            if s_gz == 0:
+                pieces.append(own(sz_blocks, to_gx * n_vert + jnp.bitwise_xor(v_me, s_v)))
+            if s_gx == 0:
+                pieces.append(sx)
+            got = send_to(("gx", "gz", "vert"), n_run, s, pieces)
+            sy_total = sy_total + got[0]
+            held[s_gx] = got[1] if held[s_gx] is None else held[s_gx] + got[1]
+            if s_gz == 0:
+                sz_total = sz_total + got[2]
+            if s_gx == 0:
+                sx_total = sx_total + got[-1]
+        sy, sz, sx = sy_total, sz_total, sx_total
+        core = jnp.stack(held)
+    else:
+        v_me = lax.axis_index("vert")
+        for d, r in digit_steps(n_vert):
+            digit = (v_me // d) % r
+            at = split_digit(sz, 1, r, digit)
+            total = at(0)
+            for s in range(1, r):
+                (got,) = send_to("vert", n_vert, s * d, [at(s)])
+                total = total + got
+            sz = total
+        gzv_me = linear_index(("gz", "vert"))
+        for d, r in digit_steps(n_gzv):
+            digit = (gzv_me // d) % r
+            at = split_digit(sy, 1, r, digit)
+            sy_total, sx_total, core_total = at(0), sx, core
+            for s in range(1, r):
+                g_sy, g_sx, g_core = send_to(("gz", "vert"), n_gzv, s * d, [at(s), sx, core])
+                sy_total, sx_total, core_total = sy_total + g_sy, sx_total + g_sx, core_total + g_core
+            sy, sx, core = sy_total, sx_total, core_total
+        for d, r in digit_steps(n_gx):
+            digit = (gx_me // d) % r
+            at_y = split_digit(sy, 0, r, digit)
+            at_z = split_digit(sz, 0, r, digit)
+            at_c = split_digit(core, 1, r, digit)
+            sy_total, sz_total, core_parts = at_y(0), at_z(0), [at_c(0)]
+            for s in range(1, r):
+                g_sy, g_sz, g_core = send_to("gx", n_gx, s * d, [at_y(s), at_z(s), at_c(s)])
+                sy_total, sz_total = sy_total + g_sy, sz_total + g_sz
+                core_parts.append(g_core)
+            sy, sz = sy_total, sz_total
+            core = jnp.concatenate(core_parts, axis=0)
 
     src = jnp.bitwise_xor(gx_me, jnp.arange(n_gx, dtype=jnp.int32))
     x_src = (src[:, None] * cells_x + jnp.arange(cells_x, dtype=jnp.int32)[None, :]).reshape(-1)

time: 24.9 us -> 39.8 us (1.60)
  starting transfers between devices: 8.1 us -> 21.9 us
  other arithmetic: 2.04 us -> 3.42 us
  matrix products: 3.5 us -> 4.17 us
  local copies, waits for them, and re-layouts: 3.05 us -> 2.4 us
  waiting for transfers between devices: 5.79 us -> 5.39 us
    ppermute x7 -> x15, starting transfers between devices: 8.1 us -> 21.9 us  [send_to(): got = lax.ppermute(flat, axes, [(i, i ^ shift) for i in range(n)])]
    mul x1, other arithmetic: 0.01 us -> 0.68 us  [shards(): snapshot_ids[:, :, None] * variables]
    dot_general x1, matrix products: 0.27 us -> 0.93 us  [shards(): part_core = jnp.einsum('my,xeyn->xemn', phy, by_e, precision=highest)]
    mul x0 -> x1, other arithmetic: none -> 0.62 us  [shards(): sy.reshape(rows_each, K) * scale_y]
    unnamed x4 -> x7, local copies, waits for them, and re-layouts: 0.52 us -> 0.02 us
    ppermute x7 -> x15, waiting for transfers between devices: 5.79 us -> 5.39 us  [send_to(): got = lax.ppermute(flat, axes, [(i, i ^ shift) for i in range(n)])]
    slice x10 -> x1, local copies, waits for them, and re-layouts: 1.38 us -> 1.34 us  [shards(): core_stream = test_streams[1]]
  transfers between devices with their start and end apart: 7 -> 15, of which waited for: 4 -> 4; matrix products, arithmetic and copies ran while one was open for 6% -> 3% of each run, Pallas kernels for 0% -> 0%
where the time goes in v3:
time: 39.8 us; the launch traced here: 39.6 us
  starting transfers between devices  21.9 us (55%)
  waiting for transfers between devices  5.39 us (14%)
  matrix products  4.17 us (10%)
  other arithmetic  3.42 us (9%)
  local copies, waits for them, and re-layouts  2.4 us (6%)
  between operations  2.34 us (6%)
    ppermute x15, starting transfers between devices, send_to(): got = lax.ppermute(flat, axes, [(i, i ^ shift) for i in range(n)])  21.9 us
    ppermute x15, waiting for transfers between devices, send_to(): got = lax.ppermute(flat, axes, [(i, i ^ shift) for i in range(n)])  5.39 us
    slice x1, local copies, waits for them, and re-layouts, shards(): core_stream = test_streams[1]  1.34 us
    dot_general x1, matrix products, shards(): core_out = jnp.einsum('jxer,ajx->rea', held, phx, precision=highest)  1.09 us
    dot_general x1, matrix products, shards(): part_core = jnp.einsum('my,xeyn->xemn', phy, by_e, precision=highest)  0.93 us
  transfers between devices with their start and end apart: 15, of which 4 were waited for; matrix products, arithmetic and copies ran while one was open for 3% of the time, Pallas kernels for 0%

profile of v3, /device:TPU:0, one launch (start us, length us, event | category | flops | bytes accessed | tf_op | source)
XLA Modules:
  0.0 39.6 jit_solution(10735802404785809429)
XLA Ops:
  0.6 0.0 copy-start
  0.7 0.0 copy-start.1
  0.8 1.3 %fusion.251 = (s32[1]{0:T(128)}, s32[1]{0:T(128)}) fusion(s32[2]{0:T(128)} %param.4), kind=kLoop, calls=%fused_computation.373 | loop fusion | bytes 16 | tf_op jit(solution)/shard_map/slice | solution.py:84
  2.8 0.1 fusion.62
  2.9 0.7 %broadcast_multiply_fusion.2 = s32[2,2]{1,0:T(2,128)S(1)} fusion(s32[2,2]{1,0:T(2,128)} %param.5), kind=kLoop, calls=%fused_computation.315 | loop fusion | flops 4 | bytes 32 | tf_op jit(solution)/shard_map/mul | solution.py:92
  3.6 0.1 fusion.141
  3.7 0.1 mul.594
  4.4 0.6 %convolution_bitcast_fusion = f32[5120,48]{0,1:T(8,128)S(1)} fusion(bf16[5120,128]{1,0:T(8,128)(2,1)S(1)} %bitcast.133, s32[]{:T(128)} %bitcast.10, s32[128]{0:T(128)S(1)} %get-tuple-element.54, s32[48]{0:T(128)S(1)} %iota_multiply_fusion.2), kind=kOutput, calls=%fused_computation | convolution fusion | flops 63031296 | bytes 2294468 | tf_op jit(solution)/shard_map/dot_general | solution.py:118
  5.0 0.2 reshape.570
  5.2 0.1 mul.651
  5.3 0.5 %fusion.169 = f32[2,256,48]{1,0,2:T(2,128)S(1)} fusion(f32[20,256,48]{1,0,2:T(8,128)S(1)} %reshape.570, s32[]{:T(128)} %bitcast.10, s32[20]{0:T(128)S(1)} %mul.651), kind=kOutput, calls=%fused_computation.283 | convolution fusion | flops 5899000 | bytes 1081428 | tf_op jit(solution)/shard_map/qxyn,qe->xeyn/dot_general | solution.py:119
  5.8 0.9 %convolution_bitcast_fusion.2 = f32[1,2,48,48]{2,3,1,0:T(8,128)S(1)} fusion(f32[2,256,48]{1,0,2:T(2,128)S(1)} %fusion.169, s32[]{:T(128)} %bitcast.10, s32[48]{0:T(128)} %copy-done.1), kind=kOutput, calls=%fused_computation.14 | convolution fusion | flops 14389248 | bytes 116932 | tf_op jit(solution)/shard_map/my,xeyn->xemn/dot_general | solution.py:120
  6.7 0.1 copy.9
  6.8 0.1 reshape.571
  6.9 0.1 reshape_reshape.14
  7.0 0.1 broadcast_multiply_fusion.1
  7.1 0.3 multiply_convert_fusion
  7.5 0.5 %fusion.7 = f32[1,256,256]{2,1,0:T(8,128)S(1)} fusion(bf16[20,256,128]{2,1,0:T(8,128)(2,1)S(1)} %bitcast.131, bf16[20,128,128]{2,1,0:T(8,128)(2,1)S(1)} %get-tuple-element.26, bf16[20,128,128]{2,1,0:T(8,128)(2,1)S(1)} %get-tuple-element.25), kind=kOutput, calls=%fused_computation.11 | convolution fusion | flops 338165760 | bytes 2883584 | tf_op jit(solution)/shard_map/qxyz,qzk->xyk/dot_general | solution.py:109
  8.0 0.2 broadcast_multiply_fusion
  8.3 0.1 dynamic-slice_bitcast_fusion.17
  8.4 2.4 %collective-permute-start.2 = (f32[26,128]{1,0:T(8,128)S(1)}, f32[26,128]{1,0:T(8,128)S(1)}, u32[]{:S(2)}, u32[]{:S(2)}) collective-permute-start(f32[26,128]{1,0:T(8,128)S(1)} %get-tuple-element.35), channel_id=1, source_target_pairs={{0,3},{1,2},{2,1},{3,0},{4,7},{5,6},{6,5},{7,4},{8,11},{9,10},{10,... | collective-permute-start | bytes 39944 | tf_op jit(solution)/shard_map/ppermute | solution.py:56
  10.8 0.6 %collective-permute-start.1 = (f32[26,128]{1,0:T(8,128)S(1)}, f32[26,128]{1,0:T(8,128)S(1)}, u32[]{:S(2)}, u32[]{:S(2)}) collective-permute-start(f32[26,128]{1,0:T(8,128)S(1)} %get-tuple-element.34), channel_id=1, source_target_pairs={{0,2},{1,3},{2,0},{3,1},{4,6},{5,7},{6,4},{7,5},{8,10},{9,11},{10,... | collective-permute-start | bytes 39944 | tf_op jit(solution)/shard_map/ppermute | solution.py:56
  11.4 0.5 %fusion.6 = f32[128,128]{0,1:T(8,128)S(1)} fusion(bf16[20,256,128]{2,1,0:T(8,128)(2,1)S(1)} %bitcast.132, f32[20,128]{1,0:T(8,128)S(1)} %get-tuple-element.50, s32[]{:T(128)} %bitcast, s32[256]{0:T(256)S(1)} %iota_multiply_fusion), kind=kOutput, calls=%fused_computation.10 | convolution fusion | flops 169033728 | bytes 1387524 | tf_op jit(solution)/shard_map/qxyz,yk->qxzk/dot_general | solution.py:115
  12.0 0.1 collective-permute-start
  12.2 0.1 collective-permute-done.2
  12.3 2.3 %collective-permute-done.1 = f32[26,128]{1,0:T(8,128)S(1)} collective-permute-done((f32[26,128]{1,0:T(8,128)S(1)}, f32[26,128]{1,0:T(8,128)S(1)}, u32[]{:S(2)}, u32[]{:S(2)}) %collective-permute-start.1) | collective-permute-done | bytes 13344 | tf_op jit(solution)/shard_map/ppermute | solution.py:56
  14.6 0.1 fusion.130
  14.6 3.2 %collective-permute-start.14 = (f32[25,128]{1,0:T(8,128)S(1)}, f32[25,128]{1,0:T(8,128)S(1)}, u32[]{:S(2)}, u32[]{:S(2)}) collective-permute-start(f32[25,128]{1,0:T(8,128)S(1)} %get-tuple-element.47), channel_id=1, source_target_pairs={{0,15},{1,14},{2,13},{3,12},{4,11},{5,10},{6,9},{7,8},{8,7},{9,6},... | collective-permute-start | bytes 38408 | tf_op jit(solution)/shard_map/ppermute | solution.py:56
  17.9 0.7 %collective-permute-start.13 = (f32[25,128]{1,0:T(8,128)S(1)}, f32[25,128]{1,0:T(8,128)S(1)}, u32[]{:S(2)}, u32[]{:S(2)}) collective-permute-start(f32[25,128]{1,0:T(8,128)S(1)} %get-tuple-element.46), channel_id=1, source_target_pairs={{0,14},{1,15},{2,12},{3,13},{4,10},{5,11},{6,8},{7,9},{8,6},{9,7},... | collective-permute-start | bytes 38408 | tf_op jit(solution)/shard_map/ppermute | solution.py:56
  18.6 3.9 %collective-permute-start.12 = (f32[41,128]{1,0:T(8,128)S(1)}, f32[41,128]{1,0:T(8,128)S(1)}, u32[]{:S(2)}, u32[]{:S(2)}) collective-permute-start(f32[41,128]{1,0:T(8,128)S(1)} %get-tuple-element.45), channel_id=1, source_target_pairs={{0,13},{1,12},{2,15},{3,14},{4,9},{5,8},{6,11},{7,10},{8,5},{9,4},... | collective-permute-start | bytes 62984 | tf_op jit(solution)/shard_map/ppermute | solution.py:56
  22.5 0.2 collective-permute-start.11
  22.7 0.0 collective-permute-start.10
  22.7 0.5 %fusion.181 = f32[1,128]{1,0:T(1,128)} fusion(f32[26,128]{1,0:T(8,128)S(1)} %collective-permute-done.2, f32[26,128]{1,0:T(8,128)S(1)} %collective-permute-done.1, f32[42,128]{1,0:T(8,128)S(1)} %collective-permute-done, f32[128]{0:T(128)S(1)} %get-tuple-element.9), kind=kLoop, calls=%fused_computation.295 | loop fusion | flops 512 | bytes 2560 | tf_op jit(solution)/shard_map/mul | solution.py:208
  23.3 0.1 stack.4
  23.4 3.4 %collective-permute-start.9 = (f32[25,128]{1,0:T(8,128)S(1)}, f32[25,128]{1,0:T(8,128)S(1)}, u32[]{:S(2)}, u32[]{:S(2)}) collective-permute-start(f32[25,128]{1,0:T(8,128)S(1)} %get-tuple-element.42), channel_id=1, source_target_pairs={{0,10},{1,11},{2,8},{3,9},{4,14},{5,15},{6,12},{7,13},{8,2},{9,3},... | collective-permute-start | bytes 38408 | tf_op jit(solution)/shard_map/ppermute | solution.py:56
  26.8 2.8 %collective-permute-start.7 = (f32[41,128]{1,0:T(8,128)S(1)}, f32[41,128]{1,0:T(8,128)S(1)}, u32[]{:S(2)}, u32[]{:S(2)}) collective-permute-start(f32[41,128]{1,0:T(8,128)S(1)} %get-tuple-element.40), channel_id=1, source_target_pairs={{0,8},{1,9},{2,10},{3,11},{4,12},{5,13},{6,14},{7,15},{8,0},{9,1},... | collective-permute-start | bytes 62984 | tf_op jit(solution)/shard_map/ppermute | solution.py:56
  29.6 1.3 %collective-permute-start.6 = (f32[25,128]{1,0:T(8,128)S(1)}, f32[25,128]{1,0:T(8,128)S(1)}, u32[]{:S(2)}, u32[]{:S(2)}) collective-permute-start(f32[25,128]{1,0:T(8,128)S(1)} %get-tuple-element.39), channel_id=1, source_target_pairs={{0,7},{1,6},{2,5},{3,4},{4,3},{5,2},{6,1},{7,0},{8,15},{9,14},{10,... | collective-permute-start | bytes 38408 | tf_op jit(solution)/shard_map/ppermute | solution.py:56
  30.8 1.3 %collective-permute-start.5 = (f32[25,128]{1,0:T(8,128)S(1)}, f32[25,128]{1,0:T(8,128)S(1)}, u32[]{:S(2)}, u32[]{:S(2)}) collective-permute-start(f32[25,128]{1,0:T(8,128)S(1)} %get-tuple-element.38), channel_id=1, source_target_pairs={{0,6},{1,7},{2,4},{3,5},{4,2},{5,3},{6,0},{7,1},{8,14},{9,15},{10,... | collective-permute-start | bytes 38408 | tf_op jit(solution)/shard_map/ppermute | solution.py:56
  32.1 1.2 %collective-permute-start.4 = (f32[41,128]{1,0:T(8,128)S(1)}, f32[41,128]{1,0:T(8,128)S(1)}, u32[]{:S(2)}, u32[]{:S(2)}) collective-permute-start(f32[41,128]{1,0:T(8,128)S(1)} %get-tuple-element.37), channel_id=1, source_target_pairs={{0,5},{1,4},{2,7},{3,6},{4,1},{5,0},{6,3},{7,2},{8,13},{9,12},{10,... | collective-permute-start | bytes 62984 | tf_op jit(solution)/shard_map/ppermute | solution.py:56
  33.3 0.7 %collective-permute-start.3 = (f32[41,128]{1,0:T(8,128)S(1)}, f32[41,128]{1,0:T(8,128)S(1)}, u32[]{:S(2)}, u32[]{:S(2)}) collective-permute-start(f32[41,128]{1,0:T(8,128)S(1)} %get-tuple-element.36), channel_id=1, source_target_pairs={{0,4},{1,5},{2,6},{3,7},{4,0},{5,1},{6,2},{7,3},{8,12},{9,13},{10,... | collective-permute-start | bytes 62984 | tf_op jit(solution)/shard_map/ppermute | solution.py:56
  34.0 0.1 add.932
  34.1 0.1 add.928
  34.2 1.4 %collective-permute-done.5 = f32[25,128]{1,0:T(8,128)S(1)} collective-permute-done((f32[25,128]{1,0:T(8,128)S(1)}, f32[25,128]{1,0:T(8,128)S(1)}, u32[]{:S(2)}, u32[]{:S(2)}) %collective-permute-start.5) | collective-permute-done | bytes 12832 | tf_op jit(solution)/shard_map/ppermute | solution.py:56
  35.6 1.5 %collective-permute-done.3 = f32[41,128]{1,0:T(8,128)S(1)} collective-permute-done((f32[41,128]{1,0:T(8,128)S(1)}, f32[41,128]{1,0:T(8,128)S(1)}, u32[]{:S(2)}, u32[]{:S(2)}) %collective-permute-start.3) | collective-permute-done | bytes 21024 | tf_op jit(solution)/shard_map/ppermute | solution.py:56
  37.2 0.1 add.924
  37.3 1.1 %fusion.10 = f32[576,2,48]{0,2,1:T(8,128)} fusion(f32[1,1,2,576]{3,0,2,1:T(1,128)S(1)} %add.932, f32[1,1,2,576]{3,0,2,1:T(1,128)S(1)} %add.928, f32[1,1,2,576]{3,0,2,1:T(1,128)S(1)} %add.924, f32[1,1,2,576]{3,0,2,1:T(1,128)S(1)} %stack.4, s32[]{:T(128)} %bitcast.10, s32[4]{0:T(128)S(1)} %iota_xor_fusion, s32[48]{0:T(128)S(1)} %iota_multiply_fusion.1), kind=kOutput, calls=%fused_computation.13 | convolution fusion | flops 2726976 | bytes 239828 | tf_op jit(solution)/shard_map/jxer,ajx->rea/dot_general | solution.py:201
  38.4 0.6 %fusion.125 = f32[16,128]{1,0:T(8,128)} fusion(f32[25,128]{1,0:T(8,128)S(1)} %collective-permute-done.14, f32[25,128]{1,0:T(8,128)S(1)} %collective-permute-done.13, f32[41,128]{1,0:T(8,128)S(1)} %collective-permute-done.12, f32[41,128]{1,0:T(8,128)S(1)} %collective-permute-done.11, f32[25,128]{1,0:T(8,128)S(1)} %collective-permute-done.10, ...), kind=kLoop, calls=%fused_computation.185 | loop fusion | flops 32768 | bytes 139268 | tf_op jit(solution)/shard_map/mul | solution.py:209
  39.0 0.6 %fusion.124 = f32[128,16]{0,1:T(8,128)} fusion(f32[41,128]{1,0:T(8,128)S(1)} %collective-permute-done.12, f32[41,128]{1,0:T(8,128)S(1)} %collective-permute-done.11, f32[41,128]{1,0:T(8,128)S(1)} %collective-permute-done.8, f32[41,128]{1,0:T(8,128)S(1)} %collective-permute-done.7, f32[41,128]{1,0:T(8,128)S(1)} %collective-permute-done.4, ...), kind=kLoop, calls=%fused_computation.177 | loop fusion | flops 16384 | bytes 73732 | tf_op jit(solution)/shard_map/mul | solution.py:210
  (37 shorter events, 0.2 us)
Async XLA Ops:
  0.6 3.8 %copy-start = (bf16[2,2,5,1,256,128]{5,4,3,2,1,0:T(8,128)(2,1)S(1)}, bf16[2,2,5,1,256,128]{5,4,3,2,1,0:T(8,128)(2,1)}, u32[]{:S(2)}) copy-start(bf16[2,2,5,1,256,128]{5,4,3,2,1,0:T(8,128)(2,1)} %param.3) | copy-start | bytes 3932164
  0.7 3.7 %copy-start.1 = (s32[48]{0:T(128)}, s32[48]{0:T(128)S(1)}, u32[]{:S(2)}) copy-start(s32[48]{0:T(128)S(1)} %iota_multiply_fusion.2) | copy-start | bytes 580
  8.4 3.9 %collective-permute-start.2 = (f32[26,128]{1,0:T(8,128)S(1)}, f32[26,128]{1,0:T(8,128)S(1)}, u32[]{:S(2)}, u32[]{:S(2)}) collective-permute-start(f32[26,128]{1,0:T(8,128)S(1)} %get-tuple-element.35), channel_id=1, source_target_pairs={{0,3},{1,2},{2,1},{3,0},{4,7},{5,6},{6,5},{7,4},{8,11},{9,10},{10,... | collective-permute-start | bytes 39944 | tf_op jit(solution)/shard_map/ppermute | solution.py:56
  10.8 3.7 %collective-permute-start.1 = (f32[26,128]{1,0:T(8,128)S(1)}, f32[26,128]{1,0:T(8,128)S(1)}, u32[]{:S(2)}, u32[]{:S(2)}) collective-permute-start(f32[26,128]{1,0:T(8,128)S(1)} %get-tuple-element.34), channel_id=1, source_target_pairs={{0,2},{1,3},{2,0},{3,1},{4,6},{5,7},{6,4},{7,5},{8,10},{9,11},{10,... | collective-permute-start | bytes 39944 | tf_op jit(solution)/shard_map/ppermute | solution.py:56
  12.0 2.5 %collective-permute-start = (f32[42,128]{1,0:T(8,128)S(1)}, f32[42,128]{1,0:T(8,128)S(1)}, u32[]{:S(2)}, u32[]{:S(2)}) collective-permute-start(f32[42,128]{1,0:T(8,128)S(1)} %pad_maximum_fusion.6), channel_id=1, source_target_pairs={{0,1},{1,0},{2,3},{3,2},{4,5},{5,4},{6,7},{7,6},{8,9},{9,8},{10,11... | collective-permute-start | bytes 64520 | tf_op jit(solution)/shard_map/ppermute | solution.py:56
  14.6 8.7 %collective-permute-start.14 = (f32[25,128]{1,0:T(8,128)S(1)}, f32[25,128]{1,0:T(8,128)S(1)}, u32[]{:S(2)}, u32[]{:S(2)}) collective-permute-start(f32[25,128]{1,0:T(8,128)S(1)} %get-tuple-element.47), channel_id=1, source_target_pairs={{0,15},{1,14},{2,13},{3,12},{4,11},{5,10},{6,9},{7,8},{8,7},{9,6},... | collective-permute-start | bytes 38408 | tf_op jit(solution)/shard_map/ppermute | solution.py:56
  17.9 8.9 %collective-permute-start.13 = (f32[25,128]{1,0:T(8,128)S(1)}, f32[25,128]{1,0:T(8,128)S(1)}, u32[]{:S(2)}, u32[]{:S(2)}) collective-permute-start(f32[25,128]{1,0:T(8,128)S(1)} %get-tuple-element.46), channel_id=1, source_target_pairs={{0,14},{1,15},{2,12},{3,13},{4,10},{5,11},{6,8},{7,9},{8,6},{9,7},... | collective-permute-start | bytes 38408 | tf_op jit(solution)/shard_map/ppermute | solution.py:56
  18.6 8.2 %collective-permute-start.12 = (f32[41,128]{1,0:T(8,128)S(1)}, f32[41,128]{1,0:T(8,128)S(1)}, u32[]{:S(2)}, u32[]{:S(2)}) collective-permute-start(f32[41,128]{1,0:T(8,128)S(1)} %get-tuple-element.45), channel_id=1, source_target_pairs={{0,13},{1,12},{2,15},{3,14},{4,9},{5,8},{6,11},{7,10},{8,5},{9,4},... | collective-permute-start | bytes 62984 | tf_op jit(solution)/shard_map/ppermute | solution.py:56
  22.5 7.1 %collective-permute-start.11 = (f32[41,128]{1,0:T(8,128)S(1)}, f32[41,128]{1,0:T(8,128)S(1)}, u32[]{:S(2)}, u32[]{:S(2)}) collective-permute-start(f32[41,128]{1,0:T(8,128)S(1)} %get-tuple-element.44), channel_id=1, source_target_pairs={{0,12},{1,13},{2,14},{3,15},{4,8},{5,9},{6,10},{7,11},{8,4},{9,5},... | collective-permute-start | bytes 62984 | tf_op jit(solution)/shard_map/ppermute | solution.py:56
  22.7 8.1 %collective-permute-start.10 = (f32[25,128]{1,0:T(8,128)S(1)}, f32[25,128]{1,0:T(8,128)S(1)}, u32[]{:S(2)}, u32[]{:S(2)}) collective-permute-start(f32[25,128]{1,0:T(8,128)S(1)} %get-tuple-element.43), channel_id=1, source_target_pairs={{0,11},{1,10},{2,9},{3,8},{4,15},{5,14},{6,13},{7,12},{8,3},{9,2},... | collective-permute-start | bytes 38408 | tf_op jit(solution)/shard_map/ppermute | solution.py:56
  23.4 8.8 %collective-permute-start.9 = (f32[25,128]{1,0:T(8,128)S(1)}, f32[25,128]{1,0:T(8,128)S(1)}, u32[]{:S(2)}, u32[]{:S(2)}) collective-permute-start(f32[25,128]{1,0:T(8,128)S(1)} %get-tuple-element.42), channel_id=1, source_target_pairs={{0,10},{1,11},{2,8},{3,9},{4,14},{5,15},{6,12},{7,13},{8,2},{9,3},... | collective-permute-start | bytes 38408 | tf_op jit(solution)/shard_map/ppermute | solution.py:56
  26.7 6.6 %collective-permute-start.8 = (f32[41,128]{1,0:T(8,128)S(1)}, f32[41,128]{1,0:T(8,128)S(1)}, u32[]{:S(2)}, u32[]{:S(2)}) collective-permute-start(f32[41,128]{1,0:T(8,128)S(1)} %get-tuple-element.41), channel_id=1, source_target_pairs={{0,9},{1,8},{2,11},{3,10},{4,13},{5,12},{6,15},{7,14},{8,1},{9,0},... | collective-permute-start | bytes 62984 | tf_op jit(solution)/shard_map/ppermute | solution.py:56
  26.8 7.3 %collective-permute-start.7 = (f32[41,128]{1,0:T(8,128)S(1)}, f32[41,128]{1,0:T(8,128)S(1)}, u32[]{:S(2)}, u32[]{:S(2)}) collective-permute-start(f32[41,128]{1,0:T(8,128)S(1)} %get-tuple-element.40), channel_id=1, source_target_pairs={{0,8},{1,9},{2,10},{3,11},{4,12},{5,13},{6,14},{7,15},{8,0},{9,1},... | collective-permute-start | bytes 62984 | tf_op jit(solution)/shard_map/ppermute | solution.py:56
  29.6 4.6 %collective-permute-start.6 = (f32[25,128]{1,0:T(8,128)S(1)}, f32[25,128]{1,0:T(8,128)S(1)}, u32[]{:S(2)}, u32[]{:S(2)}) collective-permute-start(f32[25,128]{1,0:T(8,128)S(1)} %get-tuple-element.39), channel_id=1, source_target_pairs={{0,7},{1,6},{2,5},{3,4},{4,3},{5,2},{6,1},{7,0},{8,15},{9,14},{10,... | collective-permute-start | bytes 38408 | tf_op jit(solution)/shard_map/ppermute | solution.py:56
  30.8 4.8 %collective-permute-start.5 = (f32[25,128]{1,0:T(8,128)S(1)}, f32[25,128]{1,0:T(8,128)S(1)}, u32[]{:S(2)}, u32[]{:S(2)}) collective-permute-start(f32[25,128]{1,0:T(8,128)S(1)} %get-tuple-element.38), channel_id=1, source_target_pairs={{0,6},{1,7},{2,4},{3,5},{4,2},{5,3},{6,0},{7,1},{8,14},{9,15},{10,... | collective-permute-start | bytes 38408 | tf_op jit(solution)/shard_map/ppermute | solution.py:56
  32.1 3.5 %collective-permute-start.4 = (f32[41,128]{1,0:T(8,128)S(1)}, f32[41,128]{1,0:T(8,128)S(1)}, u32[]{:S(2)}, u32[]{:S(2)}) collective-permute-start(f32[41,128]{1,0:T(8,128)S(1)} %get-tuple-element.37), channel_id=1, source_target_pairs={{0,5},{1,4},{2,7},{3,6},{4,1},{5,0},{6,3},{7,2},{8,13},{9,12},{10,... | collective-permute-start | bytes 62984 | tf_op jit(solution)/shard_map/ppermute | solution.py:56
  33.3 3.8 %collective-permute-start.3 = (f32[41,128]{1,0:T(8,128)S(1)}, f32[41,128]{1,0:T(8,128)S(1)}, u32[]{:S(2)}, u32[]{:S(2)}) collective-permute-start(f32[41,128]{1,0:T(8,128)S(1)} %get-tuple-element.36), channel_id=1, source_target_pairs={{0,4},{1,5},{2,6},{3,7},{4,0},{5,1},{6,2},{7,3},{8,12},{9,13},{10,... | collective-permute-start | bytes 62984 | tf_op jit(solution)/shard_map/ppermute | solution.py:56

commit v4 on v2

--- a/solution.py
+++ b/solution.py
@@ -133,7 +133,8 @@
     )
 
     v_me = lax.axis_index("vert")
-    for d, r in digit_steps(n_vert):
+    merge_sz = n_vert == 2
+    for d, r in ([] if merge_sz else digit_steps(n_vert)):
         digit = (v_me // d) % r
         at = split_digit(sz, 1, r, digit)
         total = at(0)
@@ -146,10 +147,19 @@
         digit = (gzv_me // d) % r
         at = split_digit(sy, 1, r, digit)
         sy_total, sx_total, core_total = at(0), sx, core
+        with_sz = merge_sz and d == 1
+        if with_sz:
+            at_z = split_digit(sz, 1, 2, v_me)
+            sz_total = at_z(0)
         for s in range(1, r):
-            g_sy, g_sx, g_core = send_to(("gz", "vert"), n_gzv, s * d, [at(s), sx, core])
-            sy_total, sx_total, core_total = sy_total + g_sy, sx_total + g_sx, core_total + g_core
+            pieces = [at(s), sx, core] + ([at_z(1)] if with_sz and s == 1 else [])
+            got = send_to(("gz", "vert"), n_gzv, s * d, pieces)
+            sy_total, sx_total, core_total = sy_total + got[0], sx_total + got[1], core_total + got[2]
+            if with_sz and s == 1:
+                sz_total = sz_total + got[3]
         sy, sx, core = sy_total, sx_total, core_total
+        if with_sz:
+            sz = sz_total
     for d, r in digit_steps(n_gx):
         digit = (gx_me // d) % r
         at_y = split_digit(sy, 0, r, digit)

time: 24.9 us -> 24.9 us (level)
  starting transfers between devices: 8.1 us -> 7.62 us
  waiting for transfers between devices: 5.79 us -> 6.27 us
    ppermute x7 -> x6, waiting for transfers between devices: 5.79 us -> 6.27 us  [send_to(): got = lax.ppermute(flat, axes, [(i, i ^ shift) for i in range(n)])]
    ppermute x7 -> x6, starting transfers between devices: 8.1 us -> 7.62 us  [send_to(): got = lax.ppermute(flat, axes, [(i, i ^ shift) for i in range(n)])]
  transfers between devices with their start and end apart: 7 -> 6, of which waited for: 4 -> 4; matrix products, arithmetic and copies ran while one was open for 6% -> 6% of each run, Pallas kernels for 0% -> 0%
where the time goes in v4:
time: 24.9 us; the launch traced here: 24.7 us
  starting transfers between devices  7.62 us (31%)
  waiting for transfers between devices  6.27 us (25%)
  matrix products  3.5 us (14%)
  local copies, waits for them, and re-layouts  3.07 us (12%)
  between operations  2.23 us (9%)
  other arithmetic  2.05 us (8%)
    ppermute x6, starting transfers between devices, send_to(): got = lax.ppermute(flat, axes, [(i, i ^ shift) for i in range(n)])  7.62 us
    ppermute x6, waiting for transfers between devices, send_to(): got = lax.ppermute(flat, axes, [(i, i ^ shift) for i in range(n)])  6.27 us
    slice x1, local copies, waits for them, and re-layouts, shards(): factor_stream = test_streams[0]  1.35 us
    dot_general x1, matrix products, shards(): core_out = jnp.einsum('jxer,ajx->rea', held, phx, precision=highest)  1.09 us
    mul x1, other arithmetic, shards(): sz.reshape(cols_each, cells_z).T * scale_z  0.61 us
    dot_general x1, matrix products, shards(): jnp.dot(rows_z, phz.T, preferred_element_type=f32)  0.6 us
    dot_general x1, matrix products, shards(): by_e = jnp.einsum('qxyn,qe->xeyn', first, phq, precision=highest)  0.54 us
    unnamed x4, local copies, waits for them, and re-layouts  0.52 us
  transfers between devices with their start and end apart: 6, of which 4 were waited for; matrix products, arithmetic and copies ran while one was open for 6% of the time, Pallas kernels for 0%

profile of v4, /device:TPU:0, one launch (start us, length us, event | category | flops | bytes accessed | tf_op | source)
XLA Modules:
  0.0 24.7 jit_solution(7337469161201643693)
XLA Ops:
  0.6 0.0 copy-start
  0.7 1.3 %fusion.243 = (s32[1]{0:T(128)}, s32[1]{0:T(128)}) fusion(s32[2]{0:T(128)} %param.4), kind=kLoop, calls=%fused_computation.316 | loop fusion | bytes 16 | tf_op jit(solution)/shard_map/slice | solution.py:83
  2.7 0.0 copy-done
  2.7 0.6 %convolution_bitcast_fusion = f32[5120,48]{0,1:T(8,128)S(1)} fusion(bf16[5120,128]{1,0:T(8,128)(2,1)S(1)} %bitcast.95, s32[]{:T(128)} %bitcast.10, s32[128]{0:T(128)S(1)} %get-tuple-element.33, s32[48]{0:T(128)S(1)} %iota_multiply_fusion.2), kind=kOutput, calls=%fused_computation | convolution fusion | flops 63031296 | bytes 2294468 | tf_op jit(solution)/shard_map/dot_general | solution.py:118
  3.3 0.0 copy-start.1
  3.3 0.2 reshape.623
  3.5 0.5 %copy-done.1 = s32[2,2]{1,0:T(2,128)S(1)} copy-done((s32[2,2]{1,0:T(2,128)S(1)}, s32[2,2]{1,0:T(2,128)}, u32[]{:S(2)}) %copy-start.1) | copy-done | bytes 40
  4.0 0.1 fusion.133
  4.1 0.1 mul.633
  4.2 0.5 %fusion.160 = f32[2,256,48]{1,0,2:T(2,128)S(1)} fusion(f32[20,256,48]{1,0,2:T(8,128)S(1)} %reshape.623, s32[]{:T(128)} %bitcast.10, s32[20]{0:T(128)S(1)} %mul.633), kind=kOutput, calls=%fused_computation.225 | convolution fusion | flops 5899000 | bytes 1081428 | tf_op jit(solution)/shard_map/qxyn,qe->xeyn/dot_general | solution.py:119
  4.7 0.3 %convolution_bitcast_fusion.2 = f32[1,2,48,48]{2,3,1,0:T(8,128)S(1)} fusion(f32[2,256,48]{1,0,2:T(2,128)S(1)} %fusion.160, s32[]{:T(128)} %bitcast.10, s32[48]{0:T(128)S(1)} %iota_multiply_fusion.2), kind=kOutput, calls=%fused_computation.14 | convolution fusion | flops 14389248 | bytes 116932 | tf_op jit(solution)/shard_map/my,xeyn->xemn/dot_general | solution.py:120
  5.0 0.1 copy.10
  5.0 0.1 reshape.624
  5.2 0.1 reshape_reshape.16
  5.9 0.1 fusion.62
  6.0 0.1 mul.577
  6.1 0.1 broadcast_multiply_fusion.1
  6.2 0.3 %multiply_convert_fusion = (bf16[20,128,128]{2,1,0:T(8,128)(2,1)S(1)}, bf16[20,128,128]{2,1,0:T(8,128)(2,1)S(1)}) fusion(f32[128,128]{1,0:T(8,128)S(1)} %fusion.62, f32[20,128]{1,0:T(8,128)S(1)} %get-tuple-element.30), kind=kLoop, calls=%fused_computation.2 | loop fusion | flops 1638400 | bytes 1386496 | tf_op jit(solution)/shard_map/convert_element_type | solution.py:107
  6.6 0.5 %fusion.7 = f32[1,256,256]{2,1,0:T(8,128)S(1)} fusion(bf16[20,256,128]{2,1,0:T(8,128)(2,1)S(1)} %bitcast.96, bf16[20,128,128]{2,1,0:T(8,128)(2,1)S(1)} %get-tuple-element.16, bf16[20,128,128]{2,1,0:T(8,128)(2,1)S(1)} %get-tuple-element.15), kind=kOutput, calls=%fused_computation.11 | convolution fusion | flops 338165760 | bytes 2883584 | tf_op jit(solution)/shard_map/qxyz,qzk->xyk/dot_general | solution.py:109
  7.1 0.2 broadcast_multiply_fusion
  7.3 2.4 %collective-permute-start.2 = (f32[101,128]{1,0:T(8,128)S(1)}, f32[101,128]{1,0:T(8,128)S(1)}, u32[]{:S(2)}, u32[]{:S(2)}) collective-permute-start(f32[101,128]{1,0:T(8,128)S(1)} %get-tuple-element.26), channel_id=1, source_target_pairs={{0,3},{1,2},{2,1},{3,0},{4,7},{5,6},{6,5},{7,4},{8,11},{9,10},{10,... | collective-permute-start | bytes 155144 | tf_op jit(solution)/shard_map/ppermute | solution.py:56
  9.8 0.6 %collective-permute-start.1 = (f32[101,128]{1,0:T(8,128)S(1)}, f32[101,128]{1,0:T(8,128)S(1)}, u32[]{:S(2)}, u32[]{:S(2)}) collective-permute-start(f32[101,128]{1,0:T(8,128)S(1)} %get-tuple-element.25), channel_id=1, source_target_pairs={{0,2},{1,3},{2,0},{3,1},{4,6},{5,7},{6,4},{7,5},{8,10},{9,11},{10,... | collective-permute-start | bytes 155144 | tf_op jit(solution)/shard_map/ppermute | solution.py:56
  10.4 0.5 %fusion.6 = f32[128,128]{0,1:T(8,128)S(1)} fusion(bf16[20,256,128]{2,1,0:T(8,128)(2,1)S(1)} %bitcast.97, f32[20,128]{1,0:T(8,128)S(1)} %get-tuple-element.29, s32[]{:T(128)} %bitcast, s32[256]{0:T(256)S(1)} %iota_multiply_fusion), kind=kOutput, calls=%fused_computation.10 | convolution fusion | flops 169033728 | bytes 1387524 | tf_op jit(solution)/shard_map/qxyz,yk->qxzk/dot_general | solution.py:115
  11.0 0.1 collective-permute-start
  11.1 0.1 reshape.634
  11.1 0.8 %collective-permute-done.2 = f32[101,128]{1,0:T(8,128)S(1)} collective-permute-done((f32[101,128]{1,0:T(8,128)S(1)}, f32[101,128]{1,0:T(8,128)S(1)}, u32[]{:S(2)}, u32[]{:S(2)}) %collective-permute-start.2) | collective-permute-done | bytes 51744 | tf_op jit(solution)/shard_map/ppermute | solution.py:56
  12.0 2.2 %collective-permute-done.1 = f32[101,128]{1,0:T(8,128)S(1)} collective-permute-done((f32[101,128]{1,0:T(8,128)S(1)}, f32[101,128]{1,0:T(8,128)S(1)}, u32[]{:S(2)}, u32[]{:S(2)}) %collective-permute-start.1) | collective-permute-done | bytes 51744 | tf_op jit(solution)/shard_map/ppermute | solution.py:56
  14.2 0.0 collective-permute-done
  14.4 0.1 dynamic-slice_reduce_fusion
  14.5 3.7 %collective-permute-start.5 = (f32[41,128]{1,0:T(8,128)S(1)}, f32[41,128]{1,0:T(8,128)S(1)}, u32[]{:S(2)}, u32[]{:S(2)}) collective-permute-start(f32[41,128]{1,0:T(8,128)S(1)} %pad_maximum_fusion.7), channel_id=1, source_target_pairs={{0,12},{4,8},{8,4},{12,0},{1,13},{5,9},{9,5},{13,1},{2,14},{6,10},... | collective-permute-start | bytes 62984 | tf_op jit(solution)/shard_map/ppermute | solution.py:56
  18.1 0.0 collective-permute-start.4
  18.2 0.8 %collective-permute-start.3 = (f32[41,128]{1,0:T(8,128)S(1)}, f32[41,128]{1,0:T(8,128)S(1)}, u32[]{:S(2)}, u32[]{:S(2)}) collective-permute-start(f32[41,128]{1,0:T(8,128)S(1)} %pad_maximum_fusion.5), channel_id=1, source_target_pairs={{0,4},{4,0},{8,12},{12,8},{1,5},{5,1},{9,13},{13,9},{2,6},{6,2},{1... | collective-permute-start | bytes 62984 | tf_op jit(solution)/shard_map/ppermute | solution.py:56
  18.9 0.5 %fusion.172 = f32[1,128]{1,0:T(1,128)} fusion(f32[101,128]{1,0:T(8,128)S(1)} %collective-permute-done.2, f32[101,128]{1,0:T(8,128)S(1)} %collective-permute-done.1, f32[165,128]{1,0:T(8,128)S(1)} %collective-permute-done, f32[128]{0:T(128)S(1)} %get-tuple-element.9), kind=kLoop, calls=%fused_computation.237 | loop fusion | flops 512 | bytes 2560 | tf_op jit(solution)/shard_map/mul | solution.py:187
  19.5 0.1 concatenate.40
  19.5 0.6 %collective-permute-done.5 = f32[41,128]{1,0:T(8,128)S(1)} collective-permute-done((f32[41,128]{1,0:T(8,128)S(1)}, f32[41,128]{1,0:T(8,128)S(1)}, u32[]{:S(2)}, u32[]{:S(2)}) %collective-permute-start.5) | collective-permute-done | bytes 21024 | tf_op jit(solution)/shard_map/ppermute | solution.py:56
  20.2 0.1 concatenate.43
  20.2 2.6 %collective-permute-done.4 = f32[41,128]{1,0:T(8,128)S(1)} collective-permute-done((f32[41,128]{1,0:T(8,128)S(1)}, f32[41,128]{1,0:T(8,128)S(1)}, u32[]{:S(2)}, u32[]{:S(2)}) %collective-permute-start.4) | collective-permute-done | bytes 21024 | tf_op jit(solution)/shard_map/ppermute | solution.py:56
  22.9 0.1 concatenate.42
  23.0 0.0 collective-permute-done.3
  23.0 0.1 concatenate.41
  23.0 1.1 %fusion.10 = f32[576,2,48]{0,2,1:T(8,128)} fusion(f32[1,1,2,576]{3,0,2,1:T(1,128)S(1)} %concatenate.43, f32[1,1,2,576]{3,0,2,1:T(1,128)S(1)} %concatenate.42, f32[1,1,2,576]{3,0,2,1:T(1,128)S(1)} %concatenate.41, f32[1,1,2,576]{3,0,2,1:T(1,128)S(1)} %concatenate.40, s32[]{:T(128)} %bitcast.10, s32[4]{0:T(128)S(1)} %iota_xor_fusion, ...), kind=kOutput, calls=%fused_computation.13 | convolution fusion | flops 2726976 | bytes 239828 | tf_op jit(solution)/shard_map/jxer,ajx->rea/dot_general | solution.py:180
  24.1 0.6 %fusion.120 = (f32[128,16]{0,1:T(8,128)}, f32[16,128]{1,0:T(8,128)}) fusion(f32[41,128]{1,0:T(8,128)S(1)} %collective-permute-done.5, f32[41,128]{1,0:T(8,128)S(1)} %collective-permute-done.4, f32[41,128]{1,0:T(8,128)S(1)} %collective-permute-done.3, f32[4,1,16,128]{3,2,0,1:T(8,128)S(1)} %bitcast_add_fusion, s32[]{:T(128)S(6)} %select_n.63, ...), kind=kLoop, calls=%fused_computation.155 | loop fusion | flops 16384 | bytes 81924 | tf_op jit(solution)/shard_map/mul | solution.py:189
  (32 shorter events, 0.3 us)
Async XLA Ops:
  0.6 2.1 %copy-start = (bf16[2,2,5,1,256,128]{5,4,3,2,1,0:T(8,128)(2,1)S(1)}, bf16[2,2,5,1,256,128]{5,4,3,2,1,0:T(8,128)(2,1)}, u32[]{:S(2)}) copy-start(bf16[2,2,5,1,256,128]{5,4,3,2,1,0:T(8,128)(2,1)} %param.3) | copy-start | bytes 3932164
  3.3 0.7 %copy-start.1 = (s32[2,2]{1,0:T(2,128)S(1)}, s32[2,2]{1,0:T(2,128)}, u32[]{:S(2)}) copy-start(s32[2,2]{1,0:T(2,128)} %param.5) | copy-start | bytes 52
  7.3 4.7 %collective-permute-start.2 = (f32[101,128]{1,0:T(8,128)S(1)}, f32[101,128]{1,0:T(8,128)S(1)}, u32[]{:S(2)}, u32[]{:S(2)}) collective-permute-start(f32[101,128]{1,0:T(8,128)S(1)} %get-tuple-element.26), channel_id=1, source_target_pairs={{0,3},{1,2},{2,1},{3,0},{4,7},{5,6},{6,5},{7,4},{8,11},{9,10},{10,... | collective-permute-start | bytes 155144 | tf_op jit(solution)/shard_map/ppermute | solution.py:56
  9.8 4.4 %collective-permute-start.1 = (f32[101,128]{1,0:T(8,128)S(1)}, f32[101,128]{1,0:T(8,128)S(1)}, u32[]{:S(2)}, u32[]{:S(2)}) collective-permute-start(f32[101,128]{1,0:T(8,128)S(1)} %get-tuple-element.25), channel_id=1, source_target_pairs={{0,2},{1,3},{2,0},{3,1},{4,6},{5,7},{6,4},{7,5},{8,10},{9,11},{10,... | collective-permute-start | bytes 155144 | tf_op jit(solution)/shard_map/ppermute | solution.py:56
  11.0 3.3 %collective-permute-start = (f32[165,128]{1,0:T(8,128)S(1)}, f32[165,128]{1,0:T(8,128)S(1)}, u32[]{:S(2)}, u32[]{:S(2)}) collective-permute-start(f32[165,128]{1,0:T(8,128)S(1)} %pad_maximum_fusion), channel_id=1, source_target_pairs={{0,1},{1,0},{2,3},{3,2},{4,5},{5,4},{6,7},{7,6},{8,9},{9,8},{10,11... | collective-permute-start | bytes 253448 | tf_op jit(solution)/shard_map/ppermute | solution.py:56
  14.5 5.7 %collective-permute-start.5 = (f32[41,128]{1,0:T(8,128)S(1)}, f32[41,128]{1,0:T(8,128)S(1)}, u32[]{:S(2)}, u32[]{:S(2)}) collective-permute-start(f32[41,128]{1,0:T(8,128)S(1)} %pad_maximum_fusion.7), channel_id=1, source_target_pairs={{0,12},{4,8},{8,4},{12,0},{1,13},{5,9},{9,5},{13,1},{2,14},{6,10},... | collective-permute-start | bytes 62984 | tf_op jit(solution)/shard_map/ppermute | solution.py:56
  18.1 4.7 %collective-permute-start.4 = (f32[41,128]{1,0:T(8,128)S(1)}, f32[41,128]{1,0:T(8,128)S(1)}, u32[]{:S(2)}, u32[]{:S(2)}) collective-permute-start(f32[41,128]{1,0:T(8,128)S(1)} %pad_maximum_fusion.6), channel_id=1, source_target_pairs={{0,8},{4,12},{8,0},{12,4},{1,9},{5,13},{9,1},{13,5},{2,10},{6,14},... | collective-permute-start | bytes 62984 | tf_op jit(solution)/shard_map/ppermute | solution.py:56
  18.2 4.8 %collective-permute-start.3 = (f32[41,128]{1,0:T(8,128)S(1)}, f32[41,128]{1,0:T(8,128)S(1)}, u32[]{:S(2)}, u32[]{:S(2)}) collective-permute-start(f32[41,128]{1,0:T(8,128)S(1)} %pad_maximum_fusion.5), channel_id=1, source_target_pairs={{0,4},{4,0},{8,12},{12,8},{1,5},{5,1},{9,13},{13,9},{2,6},{6,2},{1... | collective-permute-start | bytes 62984 | tf_op jit(solution)/shard_map/ppermute | solution.py:56

commit v5 on v4

--- a/solution.py
+++ b/solution.py
@@ -28,10 +28,10 @@
     return unit_value(row_ids[:, None] * stride + col_ids[None, :], stream, salt)
 
 
-def digit_steps(n):
+def digit_steps(n, widest=4):
     d, out = 1, []
     while d < n:
-        r = 4 if n // d >= 4 else 2
+        r = widest if n // d >= widest else 2
         out.append((d, r))
         d *= r
     return out
@@ -143,7 +143,7 @@
             total = total + got
         sz = total
     gzv_me = linear_index(("gz", "vert"))
-    for d, r in digit_steps(n_gzv):
+    for d, r in digit_steps(n_gzv, 2):
         digit = (gzv_me // d) % r
         at = split_digit(sy, 1, r, digit)
         sy_total, sx_total, core_total = at(0), sx, core

time: 24.9 us -> 25.8 us (1.036)
  other arithmetic: 2.05 us -> 2.74 us
  starting transfers between devices: 7.62 us -> 8.23 us
  local copies, waits for them, and re-layouts: 3.07 us -> 2.54 us
    mul x1, other arithmetic: 0.01 us -> 0.68 us  [shards(): snapshot_ids[:, :, None] * variables]
    ppermute x6 -> x5, starting transfers between devices: 7.62 us -> 8.23 us  [send_to(): got = lax.ppermute(flat, axes, [(i, i ^ shift) for i in range(n)])]
    unnamed x4 -> x2, local copies, waits for them, and re-layouts: 0.52 us -> 0.01 us
    ppermute x6 -> x5, waiting for transfers between devices: 6.27 us -> 6.36 us  [send_to(): got = lax.ppermute(flat, axes, [(i, i ^ shift) for i in range(n)])]
  transfers between devices with their start and end apart: 6 -> 5, of which waited for: 4 -> 4; matrix products, arithmetic and copies ran while one was open for 6% -> 4% of each run, Pallas kernels for 0% -> 0%
where the time goes in v5:
time: 25.8 us; the launch traced here: 25.6 us
  starting transfers between devices  8.23 us (32%)
  waiting for transfers between devices  6.36 us (25%)
  matrix products  3.51 us (14%)
  other arithmetic  2.74 us (11%)
  local copies, waits for them, and re-layouts  2.54 us (10%)
  between operations  2.2 us (9%)
    ppermute x5, starting transfers between devices, send_to(): got = lax.ppermute(flat, axes, [(i, i ^ shift) for i in range(n)])  8.23 us
    ppermute x5, waiting for transfers between devices, send_to(): got = lax.ppermute(flat, axes, [(i, i ^ shift) for i in range(n)])  6.36 us
    slice x1, local copies, waits for them, and re-layouts, shards(): core_stream = test_streams[1]  1.35 us
    dot_general x1, matrix products, shards(): core_out = jnp.einsum('jxer,ajx->rea', held, phx, precision=highest)  1.09 us
    mul x1, other arithmetic, shards(): snapshot_ids[:, :, None] * variables  0.68 us
    mul x1, other arithmetic, shards(): sz.reshape(cols_each, cells_z).T * scale_z  0.61 us
    dot_general x1, matrix products, shards(): jnp.dot(rows_z, phz.T, preferred_element_type=f32)  0.6 us
    dot_general x1, matrix products, shards(): by_e = jnp.einsum('qxyn,qe->xeyn', first, phq, precision=highest)  0.54 us
  transfers between devices with their start and end apart: 5, of which 4 were waited for; matrix products, arithmetic and copies ran while one was open for 4% of the time, Pallas kernels for 0%

profile of v5, /device:TPU:0, one launch (start us, length us, event | category | flops | bytes accessed | tf_op | source)
XLA Modules:
  0.0 25.6 jit_solution(4718999882848667534)
XLA Ops:
  0.6 0.0 copy-start
  0.7 1.3 %fusion.241 = (s32[1]{0:T(128)}, s32[1]{0:T(128)}) fusion(s32[2]{0:T(128)} %param.4), kind=kLoop, calls=%fused_computation.311 | loop fusion | bytes 16 | tf_op jit(solution)/shard_map/slice | solution.py:84
  2.0 0.7 %broadcast_multiply_fusion.2 = s32[2,2]{1,0:T(2,128)S(1)} fusion(s32[2,2]{1,0:T(2,128)} %param.5), kind=kLoop, calls=%fused_computation.251 | loop fusion | flops 4 | bytes 32 | tf_op jit(solution)/shard_map/mul | solution.py:92
  2.7 0.1 fusion.130
  2.8 0.1 mul.577
  4.2 0.0 copy-done
  4.2 0.6 %convolution_bitcast_fusion = f32[5120,48]{0,1:T(8,128)S(1)} fusion(bf16[5120,128]{1,0:T(8,128)(2,1)S(1)} %bitcast.95, s32[]{:T(128)} %bitcast.10, s32[128]{0:T(128)S(1)} %get-tuple-element.28, s32[48]{0:T(128)S(1)} %iota_multiply_fusion.2), kind=kOutput, calls=%fused_computation | convolution fusion | flops 63031296 | bytes 2294468 | tf_op jit(solution)/shard_map/dot_general | solution.py:118
  4.8 0.2 reshape.570
  5.0 0.1 mul.633
  5.1 0.5 %fusion.158 = f32[2,256,48]{1,0,2:T(2,128)S(1)} fusion(f32[20,256,48]{1,0,2:T(8,128)S(1)} %reshape.570, s32[]{:T(128)} %bitcast.10, s32[20]{0:T(128)S(1)} %mul.633), kind=kOutput, calls=%fused_computation.220 | convolution fusion | flops 5899000 | bytes 1081428 | tf_op jit(solution)/shard_map/qxyn,qe->xeyn/dot_general | solution.py:119
  5.6 0.3 %convolution_bitcast_fusion.2 = f32[1,2,48,48]{2,3,1,0:T(8,128)S(1)} fusion(f32[2,256,48]{1,0,2:T(2,128)S(1)} %fusion.158, s32[]{:T(128)} %bitcast.10, s32[48]{0:T(128)S(1)} %iota_multiply_fusion.2), kind=kOutput, calls=%fused_computation.14 | convolution fusion | flops 14389248 | bytes 116932 | tf_op jit(solution)/shard_map/my,xeyn->xemn/dot_general | solution.py:120
  5.9 0.1 copy.13
  6.0 0.1 reshape.571
  6.1 0.1 reshape_reshape.14
  6.2 0.1 fusion.62
  6.3 0.1 fusion.120
  6.4 0.3 %multiply_convert_fusion = (bf16[20,128,128]{2,1,0:T(8,128)(2,1)S(1)}, bf16[20,128,128]{2,1,0:T(8,128)(2,1)S(1)}) fusion(f32[128,128]{1,0:T(8,128)S(1)} %fusion.62, f32[20,128]{1,0:T(8,128)S(1)} %get-tuple-element.24), kind=kLoop, calls=%fused_computation.2 | loop fusion | flops 1638400 | bytes 1386496 | tf_op jit(solution)/shard_map/convert_element_type | solution.py:107
  6.8 0.5 %fusion.6 = f32[128,128]{0,1:T(8,128)S(1)} fusion(bf16[20,256,128]{2,1,0:T(8,128)(2,1)S(1)} %bitcast.94, f32[20,128]{1,0:T(8,128)S(1)} %get-tuple-element.25, s32[]{:T(128)} %bitcast, s32[256]{0:T(256)S(1)} %iota_multiply_fusion), kind=kOutput, calls=%fused_computation.10 | convolution fusion | flops 169033728 | bytes 1387524 | tf_op jit(solution)/shard_map/qxyz,yk->qxzk/dot_general | solution.py:115
  7.3 0.5 %fusion.7 = f32[1,256,256]{2,1,0:T(8,128)S(1)} fusion(bf16[20,256,128]{2,1,0:T(8,128)(2,1)S(1)} %bitcast.93, bf16[20,128,128]{2,1,0:T(8,128)(2,1)S(1)} %get-tuple-element.13, bf16[20,128,128]{2,1,0:T(8,128)(2,1)S(1)} %get-tuple-element.12), kind=kOutput, calls=%fused_computation.11 | convolution fusion | flops 338165760 | bytes 2883584 | tf_op jit(solution)/shard_map/qxyz,qzk->xyk/dot_general | solution.py:109
  7.8 0.2 broadcast_multiply_fusion
  8.0 0.5 %collective-permute-start = (f32[229,128]{1,0:T(8,128)S(1)}, f32[229,128]{1,0:T(8,128)S(1)}, u32[]{:S(2)}, u32[]{:S(2)}) collective-permute-start(f32[229,128]{1,0:T(8,128)S(1)} %pad_maximum_fusion), channel_id=1, source_target_pairs={{0,1},{1,0},{2,3},{3,2},{4,5},{5,4},{6,7},{7,6},{8,9},{9,8},{10,11... | collective-permute-start | bytes 351752 | tf_op jit(solution)/shard_map/ppermute | solution.py:56
  8.5 0.1 reshape.579
  8.6 0.9 %collective-permute-done = f32[229,128]{1,0:T(8,128)S(1)} collective-permute-done((f32[229,128]{1,0:T(8,128)S(1)}, f32[229,128]{1,0:T(8,128)S(1)}, u32[]{:S(2)}, u32[]{:S(2)}) %collective-permute-start) | collective-permute-done | bytes 117280 | tf_op jit(solution)/shard_map/ppermute | solution.py:56
  9.6 2.9 %collective-permute-start.1 = (f32[101,128]{1,0:T(8,128)S(1)}, f32[101,128]{1,0:T(8,128)S(1)}, u32[]{:S(2)}, u32[]{:S(2)}) collective-permute-start(f32[101,128]{1,0:T(8,128)S(1)} %pad_maximum_fusion.1), channel_id=1, source_target_pairs={{0,2},{1,3},{2,0},{3,1},{4,6},{5,7},{6,4},{7,5},{8,10},{9,11},{10,... | collective-permute-start | bytes 155144 | tf_op jit(solution)/shard_map/ppermute | solution.py:56
  12.5 2.1 %collective-permute-done.1 = f32[101,128]{1,0:T(8,128)S(1)} collective-permute-done((f32[101,128]{1,0:T(8,128)S(1)}, f32[101,128]{1,0:T(8,128)S(1)}, u32[]{:S(2)}, u32[]{:S(2)}) %collective-permute-start.1) | collective-permute-done | bytes 51744 | tf_op jit(solution)/shard_map/ppermute | solution.py:56
  14.7 0.1 dynamic-slice_reduce_fusion
  14.8 4.2 %collective-permute-start.4 = (f32[41,128]{1,0:T(8,128)S(1)}, f32[41,128]{1,0:T(8,128)S(1)}, u32[]{:S(2)}, u32[]{:S(2)}) collective-permute-start(f32[41,128]{1,0:T(8,128)S(1)} %pad_maximum_fusion.4), channel_id=1, source_target_pairs={{0,12},{4,8},{8,4},{12,0},{1,13},{5,9},{9,5},{13,1},{2,14},{6,10},... | collective-permute-start | bytes 62984 | tf_op jit(solution)/shard_map/ppermute | solution.py:56
  19.0 0.0 collective-permute-start.3
  19.0 0.6 %collective-permute-start.2 = (f32[41,128]{1,0:T(8,128)S(1)}, f32[41,128]{1,0:T(8,128)S(1)}, u32[]{:S(2)}, u32[]{:S(2)}) collective-permute-start(f32[41,128]{1,0:T(8,128)S(1)} %pad_maximum_fusion.2), channel_id=1, source_target_pairs={{0,4},{4,0},{8,12},{12,8},{1,5},{5,1},{9,13},{13,9},{2,6},{6,2},{1... | collective-permute-start | bytes 62984 | tf_op jit(solution)/shard_map/ppermute | solution.py:56
  19.6 0.5 %fusion.170 = f32[1,128]{1,0:T(1,128)} fusion(f32[1,128]{1,0:T(1,128)S(1)} %slice_add_fusion.8, f32[101,128]{1,0:T(8,128)S(1)} %collective-permute-done.1), kind=kLoop, calls=%fused_computation.232 | loop fusion | flops 256 | bytes 1536 | tf_op jit(solution)/shard_map/mul | solution.py:187
  20.2 0.1 concatenate.36
  20.2 0.7 %collective-permute-done.4 = f32[41,128]{1,0:T(8,128)S(1)} collective-permute-done((f32[41,128]{1,0:T(8,128)S(1)}, f32[41,128]{1,0:T(8,128)S(1)}, u32[]{:S(2)}, u32[]{:S(2)}) %collective-permute-start.4) | collective-permute-done | bytes 21024 | tf_op jit(solution)/shard_map/ppermute | solution.py:56
  20.9 0.1 concatenate.39
  21.0 2.7 %collective-permute-done.3 = f32[41,128]{1,0:T(8,128)S(1)} collective-permute-done((f32[41,128]{1,0:T(8,128)S(1)}, f32[41,128]{1,0:T(8,128)S(1)}, u32[]{:S(2)}, u32[]{:S(2)}) %collective-permute-start.3) | collective-permute-done | bytes 21024 | tf_op jit(solution)/shard_map/ppermute | solution.py:56
  23.7 0.1 concatenate.38
  23.8 0.0 collective-permute-done.2
  23.8 0.1 concatenate.37
  23.9 1.1 %fusion.10 = f32[576,2,48]{0,2,1:T(8,128)} fusion(f32[1,1,2,576]{3,0,2,1:T(1,128)S(1)} %concatenate.39, f32[1,1,2,576]{3,0,2,1:T(1,128)S(1)} %concatenate.38, f32[1,1,2,576]{3,0,2,1:T(1,128)S(1)} %concatenate.37, f32[1,1,2,576]{3,0,2,1:T(1,128)S(1)} %concatenate.36, s32[]{:T(128)} %bitcast.10, s32[4]{0:T(128)S(1)} %iota_xor_fusion, ...), kind=kOutput, calls=%fused_computation.13 | convolution fusion | flops 2726976 | bytes 239828 | tf_op jit(solution)/shard_map/jxer,ajx->rea/dot_general | solution.py:180
  25.0 0.6 %fusion.118 = (f32[128,16]{0,1:T(8,128)}, f32[16,128]{1,0:T(8,128)}) fusion(f32[41,128]{1,0:T(8,128)S(1)} %collective-permute-done.4, f32[41,128]{1,0:T(8,128)S(1)} %collective-permute-done.3, f32[41,128]{1,0:T(8,128)S(1)} %collective-permute-done.2, f32[4,1,16,128]{3,2,0,1:T(8,128)S(1)} %bitcast_add_fusion.1, s32[]{:T(128)S(6)} %select_n.72, ...), kind=kLoop, calls=%fused_computation.151 | loop fusion | flops 16384 | bytes 81924 | tf_op jit(solution)/shard_map/mul | solution.py:189
  (32 shorter events, 0.3 us)
Async XLA Ops:
  0.6 3.6 %copy-start = (bf16[2,2,5,1,256,128]{5,4,3,2,1,0:T(8,128)(2,1)S(1)}, bf16[2,2,5,1,256,128]{5,4,3,2,1,0:T(8,128)(2,1)}, u32[]{:S(2)}) copy-start(bf16[2,2,5,1,256,128]{5,4,3,2,1,0:T(8,128)(2,1)} %param.3) | copy-start | bytes 3932164
  8.0 1.5 %collective-permute-start = (f32[229,128]{1,0:T(8,128)S(1)}, f32[229,128]{1,0:T(8,128)S(1)}, u32[]{:S(2)}, u32[]{:S(2)}) collective-permute-start(f32[229,128]{1,0:T(8,128)S(1)} %pad_maximum_fusion), channel_id=1, source_target_pairs={{0,1},{1,0},{2,3},{3,2},{4,5},{5,4},{6,7},{7,6},{8,9},{9,8},{10,11... | collective-permute-start | bytes 351752 | tf_op jit(solution)/shard_map/ppermute | solution.py:56
  9.6 5.1 %collective-permute-start.1 = (f32[101,128]{1,0:T(8,128)S(1)}, f32[101,128]{1,0:T(8,128)S(1)}, u32[]{:S(2)}, u32[]{:S(2)}) collective-permute-start(f32[101,128]{1,0:T(8,128)S(1)} %pad_maximum_fusion.1), channel_id=1, source_target_pairs={{0,2},{1,3},{2,0},{3,1},{4,6},{5,7},{6,4},{7,5},{8,10},{9,11},{10,... | collective-permute-start | bytes 155144 | tf_op jit(solution)/shard_map/ppermute | solution.py:56
  14.8 6.1 %collective-permute-start.4 = (f32[41,128]{1,0:T(8,128)S(1)}, f32[41,128]{1,0:T(8,128)S(1)}, u32[]{:S(2)}, u32[]{:S(2)}) collective-permute-start(f32[41,128]{1,0:T(8,128)S(1)} %pad_maximum_fusion.4), channel_id=1, source_target_pairs={{0,12},{4,8},{8,4},{12,0},{1,13},{5,9},{9,5},{13,1},{2,14},{6,10},... | collective-permute-start | bytes 62984 | tf_op jit(solution)/shard_map/ppermute | solution.py:56
  19.0 4.7 %collective-permute-start.3 = (f32[41,128]{1,0:T(8,128)S(1)}, f32[41,128]{1,0:T(8,128)S(1)}, u32[]{:S(2)}, u32[]{:S(2)}) collective-permute-start(f32[41,128]{1,0:T(8,128)S(1)} %pad_maximum_fusion.3), channel_id=1, source_target_pairs={{0,8},{4,12},{8,0},{12,4},{1,9},{5,13},{9,1},{13,5},{2,10},{6,14},... | collective-permute-start | bytes 62984 | tf_op jit(solution)/shard_map/ppermute | solution.py:56
  19.0 4.8 %collective-permute-start.2 = (f32[41,128]{1,0:T(8,128)S(1)}, f32[41,128]{1,0:T(8,128)S(1)}, u32[]{:S(2)}, u32[]{:S(2)}) collective-permute-start(f32[41,128]{1,0:T(8,128)S(1)} %pad_maximum_fusion.2), channel_id=1, source_target_pairs={{0,4},{4,0},{8,12},{12,8},{1,5},{5,1},{9,13},{13,9},{2,6},{6,2},{1... | collective-permute-start | bytes 62984 | tf_op jit(solution)/shard_map/ppermute | solution.py:56

commit v6 on v4

--- a/solution.py
+++ b/solution.py
@@ -98,6 +98,10 @@
     phy = test_table(sketch_ids, y_ids, cells_y, core_stream, 6).astype(f32)
     phz = test_table(sketch_ids, z_ids, total_z, core_stream, 7)
     phq = test_table(q_ids, jnp.arange(E, dtype=jnp.int32), E, core_stream, 8).astype(f32)
+    src = jnp.bitwise_xor(gx_me, jnp.arange(n_gx, dtype=jnp.int32))
+    x_src = (src[:, None] * cells_x + jnp.arange(cells_x, dtype=jnp.int32)[None, :]).reshape(-1)
+    phx = test_table(sketch_ids, x_src, total_x, core_stream, 5).astype(f32).reshape(S, n_gx, cells_x)
+    ax, ay, az, aq, phy, phz, phq, phx = lax.optimization_barrier((ax, ay, az, aq, phy, phz, phq, phx))
 
     n_q = batches * local_snaps * variables
     field = flow_field.reshape(n_q, cells_x, cells_y, cells_z)
@@ -173,9 +177,6 @@
         sy, sz = sy_total, sz_total
         core = jnp.concatenate(core_parts, axis=0)
 
-    src = jnp.bitwise_xor(gx_me, jnp.arange(n_gx, dtype=jnp.int32))
-    x_src = (src[:, None] * cells_x + jnp.arange(cells_x, dtype=jnp.int32)[None, :]).reshape(-1)
-    phx = test_table(sketch_ids, x_src, total_x, core_stream, 5).astype(f32).reshape(S, n_gx, cells_x)
     held = core.reshape(n_gx, cells_x, E, core_rows)
     core_out = jnp.einsum("jxer,ajx->rea", held, phx, precision=highest)
 

time: 24.9 us -> 29.7 us (1.19)
  other arithmetic: 2.05 us -> 5.39 us
  waiting for transfers between devices: 6.27 us -> 7.27 us
  matrix products: 3.5 us -> 4.3 us
  local copies, waits for them, and re-layouts: 3.07 us -> 2.57 us
    convert_element_type x0 -> x7, other arithmetic: none -> 2.46 us  [the longest x3 0.97 us: unit_value(): ((2 * upper + 1).astype(jnp.float32) * 2.0 ** (-24) - 1.0).astype(jnp.bfl...]
    ppermute x6, waiting for transfers between devices: 6.27 us -> 7.27 us  [send_to(): got = lax.ppermute(flat, axes, [(i, i ^ shift) for i in range(n)])]
    dot_general x1, matrix products: 0.54 us -> 1.42 us  [shards(): by_e = jnp.einsum('qxyn,qe->xeyn', first, phq, precision=highest)]
    mul x1, other arithmetic: 0.01 us -> 0.68 us  [shards(): snapshot_ids[:, :, None] * variables]
    convert_element_type x1, other arithmetic: 0.02 us -> 0.54 us  [shards(): ax = test_table(x_ids, rank_ids, K, factor_stream, 1).astype(f32)]
    unnamed x4 -> x8, local copies, waits for them, and re-layouts: 0.52 us -> 0.03 us
  transfers between devices with their start and end apart: 6 -> 6, of which waited for: 4 -> 4; matrix products, arithmetic and copies ran while one was open for 6% -> 3% of each run, Pallas kernels for 0% -> 0%
where the time goes in v6:
time: 29.7 us; the launch traced here: 29.5 us
  starting transfers between devices  7.65 us (26%)
  waiting for transfers between devices  7.27 us (24%)
  other arithmetic  5.39 us (18%)
  matrix products  4.3 us (14%)
  local copies, waits for them, and re-layouts  2.57 us (9%)
  between operations  2.32 us (8%)
    ppermute x6, starting transfers between devices, send_to(): got = lax.ppermute(flat, axes, [(i, i ^ shift) for i in range(n)])  7.65 us
    ppermute x6, waiting for transfers between devices, send_to(): got = lax.ppermute(flat, axes, [(i, i ^ shift) for i in range(n)])  7.27 us
    dot_general x1, matrix products, shards(): by_e = jnp.einsum('qxyn,qe->xeyn', first, phq, precision=highest)  1.42 us
    slice x1, local copies, waits for them, and re-layouts, shards(): core_stream = test_streams[1]  1.34 us
    dot_general x1, matrix products, shards(): core_out = jnp.einsum('jxer,ajx->rea', held, phx, precision=highest)  1.1 us
    convert_element_type x3, other arithmetic, unit_value(): ((2 * upper + 1).astype(jnp.float32) * 2.0 ** (-24) - 1.0).astype(jnp.bfl...  0.97 us
    convert_element_type x1, other arithmetic, shards(): phy = test_table(sketch_ids, y_ids, cells_y, core_stream, 6).astype(f32)  0.73 us
    mul x1, other arithmetic, shards(): snapshot_ids[:, :, None] * variables  0.68 us
  transfers between devices with their start and end apart: 6, of which 4 were waited for; matrix products, arithmetic and copies ran while one was open for 3% of the time, Pallas kernels for 0%

profile of v6, /device:TPU:0, one launch (start us, length us, event | category | flops | bytes accessed | tf_op | source)
XLA Modules:
  0.0 29.5 jit_solution(7973583839479910382)
XLA Ops:
  0.6 0.0 copy-start
  0.7 1.3 %fusion.111 = (s32[1]{0:T(128)}, s32[1]{0:T(128)}) fusion(s32[2]{0:T(128)} %param.4), kind=kLoop, calls=%fused_computation.186 | loop fusion | bytes 16 | tf_op jit(solution)/shard_map/slice | solution.py:84
  2.7 0.5 %fusion.106 = f32[1,128]{1,0:T(1,128)} fusion(s32[]{:T(128)} %bitcast, s32[]{:T(128)S(6)} %mul.482), kind=kLoop, calls=%fused_computation.172 | loop fusion | flops 2560 | bytes 520 | tf_op jit(solution)/shard_map/convert_element_type | solution.py:94
  3.3 0.2 fusion.20
  3.4 0.7 %fusion.31 = bf16[128,128]{1,0:T(8,128)(2,1)} fusion(s32[]{:T(128)} %bitcast, s32[128]{0:T(128)S(1)} %get-tuple-element.48), kind=kLoop, calls=%fused_computation.52 | loop fusion | flops 311296 | bytes 33284 | tf_op jit(solution)/shard_map/convert_element_type | solution.py:24
  4.2 0.7 %broadcast_multiply_fusion.2 = s32[2,2]{1,0:T(2,128)S(1)} fusion(s32[2,2]{1,0:T(2,128)} %param.5), kind=kLoop, calls=%fused_computation.180 | loop fusion | flops 4 | bytes 32 | tf_op jit(solution)/shard_map/mul | solution.py:92
  4.8 0.1 fusion.82
  4.9 0.1 mul.521
  5.0 0.1 fusion.72
  5.8 0.7 %fusion.44 = f32[48,256]{1,0:T(8,128)} fusion(s32[]{:T(128)} %bitcast.1, s32[48]{0:T(128)S(1)} %iota_multiply_fusion.2), kind=kLoop, calls=%fused_computation.70 | loop fusion | flops 245760 | bytes 49348 | tf_op jit(solution)/shard_map/convert_element_type | solution.py:98
  6.5 0.1 fusion.53
  6.6 0.1 mul.556
  6.7 0.6 %fusion.96 = f32[20,2]{0,1:T(2,128)} fusion(s32[]{:T(128)} %bitcast.1, s32[20]{0:T(128)S(1)} %mul.556), kind=kLoop, calls=%fused_computation.162 | loop fusion | flops 800 | bytes 244 | tf_op jit(solution)/shard_map/convert_element_type | solution.py:100
  7.3 0.1 fusion.84
  7.3 0.6 %convolution_bitcast_fusion = f32[5120,48]{0,1:T(8,128)S(1)} fusion(bf16[48,128]{1,0:T(8,128)(2,1)S(1)} %fusion.53, bf16[5120,128]{1,0:T(8,128)(2,1)S(1)} %bitcast.99), kind=kOutput, calls=%fused_computation | convolution fusion | flops 62914560 | bytes 2306048 | tf_op jit(solution)/shard_map/dot_general | solution.py:122
  7.9 0.2 reshape.549
  8.1 0.0 copy-start.1
  8.1 0.0 copy-start.3
  8.1 1.4 %fusion.93 = f32[2,256,48]{1,0,2:T(2,128)S(1)} fusion(f32[20,256,48]{1,0,2:T(8,128)S(1)} %reshape.549, f32[20,2]{0,1:T(2,128)} %fusion.96), kind=kOutput, calls=%fused_computation.155 | convolution fusion | flops 5898240 | bytes 1081504 | tf_op jit(solution)/shard_map/qxyn,qe->xeyn/dot_general | solution.py:123
  9.5 0.2 convolution_bitcast_fusion.2
  9.8 0.1 copy.12
  9.9 0.1 reshape.550
  10.0 0.1 reshape_reshape.16
  10.1 0.3 %multiply_convert_fusion = (bf16[20,128,128]{2,1,0:T(8,128)(2,1)S(1)}, bf16[20,128,128]{2,1,0:T(8,128)(2,1)S(1)}) fusion(f32[128,128]{1,0:T(8,128)S(1)} %convert_element_type.142, f32[20,128]{1,0:T(8,128)S(1)} %fusion.72), kind=kLoop, calls=%fused_computation.2 | loop fusion | flops 1638400 | bytes 1386496 | tf_op jit(solution)/shard_map/convert_element_type | solution.py:111
  10.4 0.5 %fusion.7 = f32[1,256,256]{2,1,0:T(8,128)S(1)} fusion(bf16[20,256,128]{2,1,0:T(8,128)(2,1)S(1)} %bitcast.100, bf16[20,128,128]{2,1,0:T(8,128)(2,1)S(1)} %get-tuple-element.32, bf16[20,128,128]{2,1,0:T(8,128)(2,1)S(1)} %get-tuple-element.31), kind=kOutput, calls=%fused_computation.11 | convolution fusion | flops 338165760 | bytes 2883584 | tf_op jit(solution)/shard_map/qxyz,qzk->xyk/dot_general | solution.py:113
  10.9 0.1 broadcast_multiply_fusion
  11.0 0.5 %fusion.6 = f32[128,128]{0,1:T(8,128)S(1)} fusion(bf16[20,256,128]{2,1,0:T(8,128)(2,1)S(1)} %bitcast.101, f32[20,128]{1,0:T(8,128)S(1)} %broadcast_multiply_fusion.1, bf16[256,128]{1,0:T(8,128)(2,1)S(1)} %fusion.20), kind=kOutput, calls=%fused_computation.10 | convolution fusion | flops 168411136 | bytes 1452032 | tf_op jit(solution)/shard_map/qxyz,yk->qxzk/dot_general | solution.py:119
  11.6 0.5 %collective-permute-start = (f32[165,128]{1,0:T(8,128)S(1)}, f32[165,128]{1,0:T(8,128)S(1)}, u32[]{:S(2)}, u32[]{:S(2)}) collective-permute-start(f32[165,128]{1,0:T(8,128)S(1)} %pad_maximum_fusion), channel_id=1, source_target_pairs={{0,1},{1,0},{2,3},{3,2},{4,5},{5,4},{6,7},{7,6},{8,9},{9,8},{10,11... | collective-permute-start | bytes 253448 | tf_op jit(solution)/shard_map/ppermute | solution.py:56
  12.1 2.7 %collective-permute-start.2 = (f32[101,128]{1,0:T(8,128)S(1)}, f32[101,128]{1,0:T(8,128)S(1)}, u32[]{:S(2)}, u32[]{:S(2)}) collective-permute-start(f32[101,128]{1,0:T(8,128)S(1)} %get-tuple-element.42), channel_id=1, source_target_pairs={{0,3},{1,2},{2,1},{3,0},{4,7},{5,6},{6,5},{7,4},{8,11},{9,10},{10,... | collective-permute-start | bytes 155144 | tf_op jit(solution)/shard_map/ppermute | solution.py:56
  14.8 0.0 collective-permute-start.1
  14.8 0.1 reshape.560
  14.9 2.1 %collective-permute-done.2 = f32[101,128]{1,0:T(8,128)S(1)} collective-permute-done((f32[101,128]{1,0:T(8,128)S(1)}, f32[101,128]{1,0:T(8,128)S(1)}, u32[]{:S(2)}, u32[]{:S(2)}) %collective-permute-start.2) | collective-permute-done | bytes 51744 | tf_op jit(solution)/shard_map/ppermute | solution.py:56
  17.0 1.9 %collective-permute-done.1 = f32[101,128]{1,0:T(8,128)S(1)} collective-permute-done((f32[101,128]{1,0:T(8,128)S(1)}, f32[101,128]{1,0:T(8,128)S(1)}, u32[]{:S(2)}, u32[]{:S(2)}) %collective-permute-start.1) | collective-permute-done | bytes 51744 | tf_op jit(solution)/shard_map/ppermute | solution.py:56
  19.0 0.0 collective-permute-done
  19.1 0.1 dynamic-slice_reduce_fusion
  19.2 3.7 %collective-permute-start.5 = (f32[41,128]{1,0:T(8,128)S(1)}, f32[41,128]{1,0:T(8,128)S(1)}, u32[]{:S(2)}, u32[]{:S(2)}) collective-permute-start(f32[41,128]{1,0:T(8,128)S(1)} %pad_maximum_fusion.7), channel_id=1, source_target_pairs={{0,12},{4,8},{8,4},{12,0},{1,13},{5,9},{9,5},{13,1},{2,14},{6,10},... | collective-permute-start | bytes 62984 | tf_op jit(solution)/shard_map/ppermute | solution.py:56
  22.9 0.0 collective-permute-start.4
  22.9 0.8 %collective-permute-start.3 = (f32[41,128]{1,0:T(8,128)S(1)}, f32[41,128]{1,0:T(8,128)S(1)}, u32[]{:S(2)}, u32[]{:S(2)}) collective-permute-start(f32[41,128]{1,0:T(8,128)S(1)} %pad_maximum_fusion.5), channel_id=1, source_target_pairs={{0,4},{4,0},{8,12},{12,8},{1,5},{5,1},{9,13},{13,9},{2,6},{6,2},{1... | collective-permute-start | bytes 62984 | tf_op jit(solution)/shard_map/ppermute | solution.py:56
  23.7 0.5 %fusion.107 = f32[1,128]{1,0:T(1,128)} fusion(f32[101,128]{1,0:T(8,128)S(1)} %collective-permute-done.2, f32[101,128]{1,0:T(8,128)S(1)} %collective-permute-done.1, f32[165,128]{1,0:T(8,128)S(1)} %collective-permute-done, f32[128]{0:T(128)S(1)} %get-tuple-element.25), kind=kLoop, calls=%fused_computation.174 | loop fusion | flops 512 | bytes 2560 | tf_op jit(solution)/shard_map/mul | solution.py:188
  24.2 0.1 concatenate.40
  24.3 0.6 %collective-permute-done.5 = f32[41,128]{1,0:T(8,128)S(1)} collective-permute-done((f32[41,128]{1,0:T(8,128)S(1)}, f32[41,128]{1,0:T(8,128)S(1)}, u32[]{:S(2)}, u32[]{:S(2)}) %collective-permute-start.5) | collective-permute-done | bytes 21024 | tf_op jit(solution)/shard_map/ppermute | solution.py:56
  24.9 0.1 concatenate.43
  25.0 2.6 %collective-permute-done.4 = f32[41,128]{1,0:T(8,128)S(1)} collective-permute-done((f32[41,128]{1,0:T(8,128)S(1)}, f32[41,128]{1,0:T(8,128)S(1)}, u32[]{:S(2)}, u32[]{:S(2)}) %collective-permute-start.4) | collective-permute-done | bytes 21024 | tf_op jit(solution)/shard_map/ppermute | solution.py:56
  27.6 0.1 concatenate.42
  27.7 0.0 collective-permute-done.3
  27.7 0.1 concatenate.41
  27.8 1.1 %fusion.10 = f32[576,2,48]{0,2,1:T(8,128)} fusion(f32[48,4,1]{0,1,2:T(4,128)S(1)} %fusion.84, f32[1,1,2,576]{3,0,2,1:T(1,128)S(1)} %concatenate.43, f32[1,1,2,576]{3,0,2,1:T(1,128)S(1)} %concatenate.42, f32[1,1,2,576]{3,0,2,1:T(1,128)S(1)} %concatenate.41, f32[1,1,2,576]{3,0,2,1:T(1,128)S(1)} %concatenate.40), kind=kOutput, calls=%fused_computation.13 | convolution fusion | flops 2723328 | bytes 240384 | tf_op jit(solution)/shard_map/jxer,ajx->rea/dot_general | solution.py:181
  28.9 0.6 %fusion.70 = (f32[128,16]{0,1:T(8,128)}, f32[16,128]{1,0:T(8,128)}) fusion(f32[41,128]{1,0:T(8,128)S(1)} %collective-permute-done.5, f32[41,128]{1,0:T(8,128)S(1)} %collective-permute-done.4, f32[41,128]{1,0:T(8,128)S(1)} %collective-permute-done.3, f32[4,1,16,128]{3,2,0,1:T(8,128)S(1)} %bitcast_add_fusion, s32[]{:T(128)S(6)} %select_n.63, ...), kind=kLoop, calls=%fused_computation.105 | loop fusion | flops 16384 | bytes 81924 | tf_op jit(solution)/shard_map/mul | solution.py:190
  (37 shorter events, 0.3 us)
Async XLA Ops:
  0.6 6.7 %copy-start = (bf16[2,2,5,1,256,128]{5,4,3,2,1,0:T(8,128)(2,1)S(1)}, bf16[2,2,5,1,256,128]{5,4,3,2,1,0:T(8,128)(2,1)}, u32[]{:S(2)}) copy-start(bf16[2,2,5,1,256,128]{5,4,3,2,1,0:T(8,128)(2,1)} %param.3) | copy-start | bytes 3932164
  8.1 1.5 %copy-start.1 = (f32[48,256]{1,0:T(8,128)S(1)}, f32[48,256]{1,0:T(8,128)}, u32[]{:S(2)}) copy-start(f32[48,256]{1,0:T(8,128)} %fusion.44) | copy-start | bytes 147460
  8.1 2.0 %copy-start.2 = (bf16[128,128]{1,0:T(8,128)(2,1)S(1)}, bf16[128,128]{1,0:T(8,128)(2,1)}, u32[]{:S(2)}) copy-start(bf16[128,128]{1,0:T(8,128)(2,1)} %fusion.31) | copy-start | bytes 98308
  8.1 2.3 %copy-start.3 = (f32[1,128]{1,0:T(1,128)S(1)}, f32[1,128]{1,0:T(1,128)}, u32[]{:S(2)}) copy-start(f32[1,128]{1,0:T(1,128)} %fusion.106) | copy-start | bytes 1540
  11.6 7.4 %collective-permute-start = (f32[165,128]{1,0:T(8,128)S(1)}, f32[165,128]{1,0:T(8,128)S(1)}, u32[]{:S(2)}, u32[]{:S(2)}) collective-permute-start(f32[165,128]{1,0:T(8,128)S(1)} %pad_maximum_fusion), channel_id=1, source_target_pairs={{0,1},{1,0},{2,3},{3,2},{4,5},{5,4},{6,7},{7,6},{8,9},{9,8},{10,11... | collective-permute-start | bytes 253448 | tf_op jit(solution)/shard_map/ppermute | solution.py:56
  12.1 4.9 %collective-permute-start.2 = (f32[101,128]{1,0:T(8,128)S(1)}, f32[101,128]{1,0:T(8,128)S(1)}, u32[]{:S(2)}, u32[]{:S(2)}) collective-permute-start(f32[101,128]{1,0:T(8,128)S(1)} %get-tuple-element.42), channel_id=1, source_target_pairs={{0,3},{1,2},{2,1},{3,0},{4,7},{5,6},{6,5},{7,4},{8,11},{9,10},{10,... | collective-permute-start | bytes 155144 | tf_op jit(solution)/shard_map/ppermute | solution.py:56
  14.8 4.1 %collective-permute-start.1 = (f32[101,128]{1,0:T(8,128)S(1)}, f32[101,128]{1,0:T(8,128)S(1)}, u32[]{:S(2)}, u32[]{:S(2)}) collective-permute-start(f32[101,128]{1,0:T(8,128)S(1)} %get-tuple-element.41), channel_id=1, source_target_pairs={{0,2},{1,3},{2,0},{3,1},{4,6},{5,7},{6,4},{7,5},{8,10},{9,11},{10,... | collective-permute-start | bytes 155144 | tf_op jit(solution)/shard_map/ppermute | solution.py:56
  19.2 5.7 %collective-permute-start.5 = (f32[41,128]{1,0:T(8,128)S(1)}, f32[41,128]{1,0:T(8,128)S(1)}, u32[]{:S(2)}, u32[]{:S(2)}) collective-permute-start(f32[41,128]{1,0:T(8,128)S(1)} %pad_maximum_fusion.7), channel_id=1, source_target_pairs={{0,12},{4,8},{8,4},{12,0},{1,13},{5,9},{9,5},{13,1},{2,14},{6,10},... | collective-permute-start | bytes 62984 | tf_op jit(solution)/shard_map/ppermute | solution.py:56
  22.9 4.7 %collective-permute-start.4 = (f32[41,128]{1,0:T(8,128)S(1)}, f32[41,128]{1,0:T(8,128)S(1)}, u32[]{:S(2)}, u32[]{:S(2)}) collective-permute-start(f32[41,128]{1,0:T(8,128)S(1)} %pad_maximum_fusion.6), channel_id=1, source_target_pairs={{0,8},{4,12},{8,0},{12,4},{1,9},{5,13},{9,1},{13,5},{2,10},{6,14},... | collective-permute-start | bytes 62984 | tf_op jit(solution)/shard_map/ppermute | solution.py:56
  22.9 4.8 %collective-permute-start.3 = (f32[41,128]{1,0:T(8,128)S(1)}, f32[41,128]{1,0:T(8,128)S(1)}, u32[]{:S(2)}, u32[]{:S(2)}) collective-permute-start(f32[41,128]{1,0:T(8,128)S(1)} %pad_maximum_fusion.5), channel_id=1, source_target_pairs={{0,4},{4,0},{8,12},{12,8},{1,5},{5,1},{9,13},{13,9},{2,6},{6,2},{1... | collective-permute-start | bytes 62984 | tf_op jit(solution)/shard_map/ppermute | solution.py:56

commit v7 on v4

--- a/solution.py
+++ b/solution.py
@@ -10,8 +10,7 @@
 E = 2
 
 
-def hash_index(index, stream, salt):
-    mixed = index * -1640531535 + stream * -2048144777 + salt
+def mix_bits(mixed):
     mixed = jnp.bitwise_xor(mixed, lax.shift_right_logical(mixed, jnp.int32(16)))
     mixed = mixed * 739982445
     mixed = jnp.bitwise_xor(mixed, lax.shift_right_logical(mixed, jnp.int32(13)))
@@ -19,13 +18,11 @@
     return jnp.bitwise_xor(mixed, lax.shift_right_logical(mixed, jnp.int32(16)))
 
 
-def unit_value(index, stream, salt):
-    upper = lax.shift_right_logical(hash_index(index, stream, salt), jnp.int32(9))
+def test_table(row_ids, col_ids, stride, stream, salt):
+    row_term = (row_ids * stride) * -1640531535
+    col_term = col_ids * -1640531535 + stream * -2048144777 + salt
+    upper = lax.shift_right_logical(mix_bits(row_term[:, None] + col_term[None, :]), jnp.int32(9))
     return ((2 * upper + 1).astype(jnp.float32) * 2.0 ** (-24) - 1.0).astype(jnp.bfloat16)
-
-
-def test_table(row_ids, col_ids, stride, stream, salt):
-    return unit_value(row_ids[:, None] * stride + col_ids[None, :], stream, salt)
 
 
 def digit_steps(n):

time: 24.9 us -> 25 us (level)
  no operation moved by 1% of the time
where the time goes in v7:
time: 25 us; the launch traced here: 24.8 us
  starting transfers between devices  7.63 us (31%)
  waiting for transfers between devices  6.26 us (25%)
  matrix products  3.49 us (14%)
  local copies, waits for them, and re-layouts  3.07 us (12%)
  between operations  2.26 us (9%)
  other arithmetic  2.06 us (8%)
    ppermute x6, starting transfers between devices, send_to(): got = lax.ppermute(flat, axes, [(i, i ^ shift) for i in range(n)])  7.63 us
    ppermute x6, waiting for transfers between devices, send_to(): got = lax.ppermute(flat, axes, [(i, i ^ shift) for i in range(n)])  6.26 us
    slice x1, local copies, waits for them, and re-layouts, shards(): factor_stream = test_streams[0]  1.35 us
    dot_general x1, matrix products, shards(): core_out = jnp.einsum('jxer,ajx->rea', held, phx, precision=highest)  1.09 us
    mul x1, other arithmetic, shards(): sz.reshape(cols_each, cells_z).T * scale_z  0.61 us
    dot_general x1, matrix products, shards(): jnp.dot(rows_z, phz.T, preferred_element_type=f32)  0.6 us
    dot_general x1, matrix products, shards(): by_e = jnp.einsum('qxyn,qe->xeyn', first, phq, precision=highest)  0.53 us
    unnamed x4, local copies, waits for them, and re-layouts  0.52 us
  transfers between devices with their start and end apart: 6, of which 4 were waited for; matrix products, arithmetic and copies ran while one was open for 6% of the time, Pallas kernels for 0%

profile of v7, /device:TPU:0, one launch (start us, length us, event | category | flops | bytes accessed | tf_op | source)
XLA Modules:
  0.0 24.8 jit_solution(6624305176304514029)
XLA Ops:
  0.6 0.0 copy-start
  0.7 1.4 %fusion.224 = (s32[1]{0:T(128)}, s32[1]{0:T(128)}) fusion(s32[2]{0:T(128)} %param.4), kind=kLoop, calls=%fused_computation.303 | loop fusion | bytes 16 | tf_op jit(solution)/shard_map/slice | solution.py:80
  3.4 0.0 copy-done
  3.4 0.6 %convolution_bitcast_fusion = f32[5120,48]{0,1:T(8,128)S(1)} fusion(bf16[5120,128]{1,0:T(8,128)(2,1)S(1)} %bitcast.95, s32[128]{0:T(128)S(1)} %get-tuple-element.33, s32[48]{0:T(128)S(1)} %iota_multiply_fusion.2), kind=kOutput, calls=%fused_computation | convolution fusion | flops 63012864 | bytes 2294464 | tf_op jit(solution)/shard_map/dot_general | solution.py:115
  4.0 0.0 copy-start.1
  4.0 0.2 reshape.657
  4.2 0.5 %copy-done.1 = s32[2,2]{1,0:T(2,128)S(1)} copy-done((s32[2,2]{1,0:T(2,128)S(1)}, s32[2,2]{1,0:T(2,128)}, u32[]{:S(2)}) %copy-start.1) | copy-done | bytes 40
  4.7 0.1 fusion.127
  4.8 0.1 mul.607
  4.9 0.5 %fusion.151 = f32[2,256,48]{1,0,2:T(2,128)S(1)} fusion(f32[20,256,48]{1,0,2:T(8,128)S(1)} %reshape.657, s32[20]{0:T(128)S(1)} %mul.607, s32[2]{0:T(128)S(1)} %add_add_fusion.4), kind=kOutput, calls=%fused_computation.217 | convolution fusion | flops 5898880 | bytes 1081432 | tf_op jit(solution)/shard_map/qxyn,qe->xeyn/dot_general | solution.py:116
  5.4 0.3 %convolution_bitcast_fusion.2 = f32[1,2,48,48]{2,3,1,0:T(8,128)S(1)} fusion(f32[2,256,48]{1,0,2:T(2,128)S(1)} %fusion.151, s32[256]{0:T(256)S(1)} %add_add_fusion.1, s32[48]{0:T(128)S(1)} %iota_multiply_fusion.2), kind=kOutput, calls=%fused_computation.14 | convolution fusion | flops 14352384 | bytes 117952 | tf_op jit(solution)/shard_map/my,xeyn->xemn/dot_general | solution.py:117
  5.7 0.1 copy.10
  5.8 0.1 reshape.658
  5.9 0.1 reshape_reshape.16
  6.0 0.1 mul.557
  6.1 0.1 fusion.61
  6.2 0.1 broadcast_multiply_fusion.1
  6.3 0.3 %multiply_convert_fusion = (bf16[20,128,128]{2,1,0:T(8,128)(2,1)S(1)}, bf16[20,128,128]{2,1,0:T(8,128)(2,1)S(1)}) fusion(f32[128,128]{1,0:T(8,128)S(1)} %fusion.61, f32[20,128]{1,0:T(8,128)S(1)} %get-tuple-element.28), kind=kLoop, calls=%fused_computation.2 | loop fusion | flops 1638400 | bytes 1386496 | tf_op jit(solution)/shard_map/convert_element_type | solution.py:104
  6.6 0.5 %fusion.7 = f32[1,256,256]{2,1,0:T(8,128)S(1)} fusion(bf16[20,256,128]{2,1,0:T(8,128)(2,1)S(1)} %bitcast.96, bf16[20,128,128]{2,1,0:T(8,128)(2,1)S(1)} %get-tuple-element.16, bf16[20,128,128]{2,1,0:T(8,128)(2,1)S(1)} %get-tuple-element.15), kind=kOutput, calls=%fused_computation.11 | convolution fusion | flops 338165760 | bytes 2883584 | tf_op jit(solution)/shard_map/qxyz,qzk->xyk/dot_general | solution.py:106
  7.1 0.2 broadcast_multiply_fusion
  7.3 2.4 %collective-permute-start.2 = (f32[101,128]{1,0:T(8,128)S(1)}, f32[101,128]{1,0:T(8,128)S(1)}, u32[]{:S(2)}, u32[]{:S(2)}) collective-permute-start(f32[101,128]{1,0:T(8,128)S(1)} %get-tuple-element.26), channel_id=1, source_target_pairs={{0,3},{1,2},{2,1},{3,0},{4,7},{5,6},{6,5},{7,4},{8,11},{9,10},{10,... | collective-permute-start | bytes 155144 | tf_op jit(solution)/shard_map/ppermute | solution.py:53
  9.8 0.6 %collective-permute-start.1 = (f32[101,128]{1,0:T(8,128)S(1)}, f32[101,128]{1,0:T(8,128)S(1)}, u32[]{:S(2)}, u32[]{:S(2)}) collective-permute-start(f32[101,128]{1,0:T(8,128)S(1)} %get-tuple-element.25), channel_id=1, source_target_pairs={{0,2},{1,3},{2,0},{3,1},{4,6},{5,7},{6,4},{7,5},{8,10},{9,11},{10,... | collective-permute-start | bytes 155144 | tf_op jit(solution)/shard_map/ppermute | solution.py:53
  10.4 0.5 %fusion.6 = f32[128,128]{0,1:T(8,128)S(1)} fusion(bf16[20,256,128]{2,1,0:T(8,128)(2,1)S(1)} %bitcast.97, f32[20,128]{1,0:T(8,128)S(1)} %get-tuple-element.27, s32[128]{0:T(128)S(1)} %get-tuple-element.35, s32[256]{0:T(256)S(1)} %iota_multiply_fusion), kind=kOutput, calls=%fused_computation.10 | convolution fusion | flops 168935424 | bytes 1388032 | tf_op jit(solution)/shard_map/qxyz,yk->qxzk/dot_general | solution.py:112
  11.0 0.1 collective-permute-start
  11.1 0.1 reshape.668
  11.2 0.8 %collective-permute-done.2 = f32[101,128]{1,0:T(8,128)S(1)} collective-permute-done((f32[101,128]{1,0:T(8,128)S(1)}, f32[101,128]{1,0:T(8,128)S(1)}, u32[]{:S(2)}, u32[]{:S(2)}) %collective-permute-start.2) | collective-permute-done | bytes 51744 | tf_op jit(solution)/shard_map/ppermute | solution.py:53
  12.0 2.2 %collective-permute-done.1 = f32[101,128]{1,0:T(8,128)S(1)} collective-permute-done((f32[101,128]{1,0:T(8,128)S(1)}, f32[101,128]{1,0:T(8,128)S(1)}, u32[]{:S(2)}, u32[]{:S(2)}) %collective-permute-start.1) | collective-permute-done | bytes 51744 | tf_op jit(solution)/shard_map/ppermute | solution.py:53
  14.2 0.0 collective-permute-done
  14.4 0.1 dynamic-slice_reduce_fusion
  14.5 3.7 %collective-permute-start.5 = (f32[41,128]{1,0:T(8,128)S(1)}, f32[41,128]{1,0:T(8,128)S(1)}, u32[]{:S(2)}, u32[]{:S(2)}) collective-permute-start(f32[41,128]{1,0:T(8,128)S(1)} %pad_maximum_fusion.7), channel_id=1, source_target_pairs={{0,12},{4,8},{8,4},{12,0},{1,13},{5,9},{9,5},{13,1},{2,14},{6,10},... | collective-permute-start | bytes 62984 | tf_op jit(solution)/shard_map/ppermute | solution.py:53
  18.2 0.0 collective-permute-start.4
  18.2 0.8 %collective-permute-start.3 = (f32[41,128]{1,0:T(8,128)S(1)}, f32[41,128]{1,0:T(8,128)S(1)}, u32[]{:S(2)}, u32[]{:S(2)}) collective-permute-start(f32[41,128]{1,0:T(8,128)S(1)} %pad_maximum_fusion.5), channel_id=1, source_target_pairs={{0,4},{4,0},{8,12},{12,8},{1,5},{5,1},{9,13},{13,9},{2,6},{6,2},{1... | collective-permute-start | bytes 62984 | tf_op jit(solution)/shard_map/ppermute | solution.py:53
  19.0 0.5 %fusion.163 = f32[1,128]{1,0:T(1,128)} fusion(f32[101,128]{1,0:T(8,128)S(1)} %collective-permute-done.2, f32[101,128]{1,0:T(8,128)S(1)} %collective-permute-done.1, f32[165,128]{1,0:T(8,128)S(1)} %collective-permute-done, f32[128]{0:T(128)S(1)} %get-tuple-element.9), kind=kLoop, calls=%fused_computation.229 | loop fusion | flops 512 | bytes 2560 | tf_op jit(solution)/shard_map/mul | solution.py:184
  19.5 0.1 concatenate.40
  19.6 0.6 %collective-permute-done.5 = f32[41,128]{1,0:T(8,128)S(1)} collective-permute-done((f32[41,128]{1,0:T(8,128)S(1)}, f32[41,128]{1,0:T(8,128)S(1)}, u32[]{:S(2)}, u32[]{:S(2)}) %collective-permute-start.5) | collective-permute-done | bytes 21024 | tf_op jit(solution)/shard_map/ppermute | solution.py:53
  20.2 0.1 concatenate.43
  20.3 2.6 %collective-permute-done.4 = f32[41,128]{1,0:T(8,128)S(1)} collective-permute-done((f32[41,128]{1,0:T(8,128)S(1)}, f32[41,128]{1,0:T(8,128)S(1)}, u32[]{:S(2)}, u32[]{:S(2)}) %collective-permute-start.4) | collective-permute-done | bytes 21024 | tf_op jit(solution)/shard_map/ppermute | solution.py:53
  22.9 0.1 concatenate.42
  23.0 0.0 collective-permute-done.3
  23.0 0.1 concatenate.41
  23.1 1.1 %fusion.10 = f32[576,2,48]{0,2,1:T(8,128)} fusion(f32[1,1,2,576]{3,0,2,1:T(1,128)S(1)} %concatenate.43, f32[1,1,2,576]{3,0,2,1:T(1,128)S(1)} %concatenate.42, f32[1,1,2,576]{3,0,2,1:T(1,128)S(1)} %concatenate.41, f32[1,1,2,576]{3,0,2,1:T(1,128)S(1)} %concatenate.40, s32[4]{0:T(128)S(1)} %add_add_fusion.2, s32[48]{0:T(128)S(1)} %iota_multiply_fusion.1), kind=kOutput, calls=%fused_computation.13 | convolution fusion | flops 2726400 | bytes 239824 | tf_op jit(solution)/shard_map/jxer,ajx->rea/dot_general | solution.py:177
  24.2 0.6 %fusion.114 = (f32[128,16]{0,1:T(8,128)}, f32[16,128]{1,0:T(8,128)}) fusion(f32[41,128]{1,0:T(8,128)S(1)} %collective-permute-done.5, f32[41,128]{1,0:T(8,128)S(1)} %collective-permute-done.4, f32[41,128]{1,0:T(8,128)S(1)} %collective-permute-done.3, f32[4,1,16,128]{3,2,0,1:T(8,128)S(1)} %bitcast_add_fusion, s32[]{:T(128)S(6)} %select_n.63, ...), kind=kLoop, calls=%fused_computation.149 | loop fusion | flops 16384 | bytes 81924 | tf_op jit(solution)/shard_map/mul | solution.py:186
  (36 shorter events, 0.3 us)
Async XLA Ops:
  0.6 2.8 %copy-start = (bf16[2,2,5,1,256,128]{5,4,3,2,1,0:T(8,128)(2,1)S(1)}, bf16[2,2,5,1,256,128]{5,4,3,2,1,0:T(8,128)(2,1)}, u32[]{:S(2)}) copy-start(bf16[2,2,5,1,256,128]{5,4,3,2,1,0:T(8,128)(2,1)} %param.3) | copy-start | bytes 3932164
  4.0 0.7 %copy-start.1 = (s32[2,2]{1,0:T(2,128)S(1)}, s32[2,2]{1,0:T(2,128)}, u32[]{:S(2)}) copy-start(s32[2,2]{1,0:T(2,128)} %param.5) | copy-start | bytes 52
  7.3 4.7 %collective-permute-start.2 = (f32[101,128]{1,0:T(8,128)S(1)}, f32[101,128]{1,0:T(8,128)S(1)}, u32[]{:S(2)}, u32[]{:S(2)}) collective-permute-start(f32[101,128]{1,0:T(8,128)S(1)} %get-tuple-element.26), channel_id=1, source_target_pairs={{0,3},{1,2},{2,1},{3,0},{4,7},{5,6},{6,5},{7,4},{8,11},{9,10},{10,... | collective-permute-start | bytes 155144 | tf_op jit(solution)/shard_map/ppermute | solution.py:53
  9.8 4.4 %collective-permute-start.1 = (f32[101,128]{1,0:T(8,128)S(1)}, f32[101,128]{1,0:T(8,128)S(1)}, u32[]{:S(2)}, u32[]{:S(2)}) collective-permute-start(f32[101,128]{1,0:T(8,128)S(1)} %get-tuple-element.25), channel_id=1, source_target_pairs={{0,2},{1,3},{2,0},{3,1},{4,6},{5,7},{6,4},{7,5},{8,10},{9,11},{10,... | collective-permute-start | bytes 155144 | tf_op jit(solution)/shard_map/ppermute | solution.py:53
  11.0 3.3 %collective-permute-start = (f32[165,128]{1,0:T(8,128)S(1)}, f32[165,128]{1,0:T(8,128)S(1)}, u32[]{:S(2)}, u32[]{:S(2)}) collective-permute-start(f32[165,128]{1,0:T(8,128)S(1)} %pad_maximum_fusion), channel_id=1, source_target_pairs={{0,1},{1,0},{2,3},{3,2},{4,5},{5,4},{6,7},{7,6},{8,9},{9,8},{10,11... | collective-permute-start | bytes 253448 | tf_op jit(solution)/shard_map/ppermute | solution.py:53
  14.5 5.7 %collective-permute-start.5 = (f32[41,128]{1,0:T(8,128)S(1)}, f32[41,128]{1,0:T(8,128)S(1)}, u32[]{:S(2)}, u32[]{:S(2)}) collective-permute-start(f32[41,128]{1,0:T(8,128)S(1)} %pad_maximum_fusion.7), channel_id=1, source_target_pairs={{0,12},{4,8},{8,4},{12,0},{1,13},{5,9},{9,5},{13,1},{2,14},{6,10},... | collective-permute-start | bytes 62984 | tf_op jit(solution)/shard_map/ppermute | solution.py:53
  18.2 4.7 %collective-permute-start.4 = (f32[41,128]{1,0:T(8,128)S(1)}, f32[41,128]{1,0:T(8,128)S(1)}, u32[]{:S(2)}, u32[]{:S(2)}) collective-permute-start(f32[41,128]{1,0:T(8,128)S(1)} %pad_maximum_fusion.6), channel_id=1, source_target_pairs={{0,8},{4,12},{8,0},{12,4},{1,9},{5,13},{9,1},{13,5},{2,10},{6,14},... | collective-permute-start | bytes 62984 | tf_op jit(solution)/shard_map/ppermute | solution.py:53
  18.2 4.8 %collective-permute-start.3 = (f32[41,128]{1,0:T(8,128)S(1)}, f32[41,128]{1,0:T(8,128)S(1)}, u32[]{:S(2)}, u32[]{:S(2)}) collective-permute-start(f32[41,128]{1,0:T(8,128)S(1)} %pad_maximum_fusion.5), channel_id=1, source_target_pairs={{0,4},{4,0},{8,12},{12,8},{1,5},{5,1},{9,13},{13,9},{2,6},{6,2},{1... | collective-permute-start | bytes 62984 | tf_op jit(solution)/shard_map/ppermute | solution.py:53

commit v8 on v7

--- a/solution.py
+++ b/solution.py
@@ -173,8 +173,9 @@
     src = jnp.bitwise_xor(gx_me, jnp.arange(n_gx, dtype=jnp.int32))
     x_src = (src[:, None] * cells_x + jnp.arange(cells_x, dtype=jnp.int32)[None, :]).reshape(-1)
     phx = test_table(sketch_ids, x_src, total_x, core_stream, 5).astype(f32).reshape(S, n_gx, cells_x)
-    held = core.reshape(n_gx, cells_x, E, core_rows)
-    core_out = jnp.einsum("jxer,ajx->rea", held, phx, precision=highest)
+    held = core.reshape(n_gx * cells_x, E, core_rows)
+    weights_x = phx.reshape(S, n_gx * cells_x)
+    core_out = jnp.sum(held[:, None, :, :] * weights_x.T[:, :, None, None], axis=0).transpose(2, 1, 0)
 
     scale_x = 3.0**1.5 / math.sqrt(cells_y * total_z * total_q)
     scale_y = 3.0**1.5 / math.sqrt(total_x * total_z * total_q)

time: 25 us -> 24.8 us (level)
  matrix products: 3.49 us -> 2.4 us
  other arithmetic: 2.06 us -> 3.01 us
    dot_general x1 -> x0, matrix products: 1.09 us -> none  [shards(): core_out = jnp.einsum('jxer,ajx->rea', held, phx, precision=highest)]
    mul x0 -> x2, other arithmetic: none -> 0.73 us  [the longest x1 0.72 us: shards(): core_out * scale_core]
where the time goes in v8:
time: 24.8 us; the launch traced here: 24.6 us
  starting transfers between devices  7.63 us (31%)
  waiting for transfers between devices  6.18 us (25%)
  local copies, waits for them, and re-layouts  3.07 us (12%)
  other arithmetic  3.01 us (12%)
  matrix products  2.4 us (10%)
  between operations  2.28 us (9%)
    ppermute x6, starting transfers between devices, send_to(): got = lax.ppermute(flat, axes, [(i, i ^ shift) for i in range(n)])  7.63 us
    ppermute x6, waiting for transfers between devices, send_to(): got = lax.ppermute(flat, axes, [(i, i ^ shift) for i in range(n)])  6.18 us
    slice x1, local copies, waits for them, and re-layouts, shards(): factor_stream = test_streams[0]  1.35 us
    mul x1, other arithmetic, shards(): core_out * scale_core  0.72 us
    mul x1, other arithmetic, shards(): sz.reshape(cols_each, cells_z).T * scale_z  0.61 us
    dot_general x1, matrix products, shards(): jnp.dot(rows_z, phz.T, preferred_element_type=f32)  0.6 us
    dot_general x1, matrix products, shards(): by_e = jnp.einsum('qxyn,qe->xeyn', first, phq, precision=highest)  0.53 us
    unnamed x4, local copies, waits for them, and re-layouts  0.52 us
  transfers between devices with their start and end apart: 6, of which 4 were waited for; matrix products, arithmetic and copies ran while one was open for 6% of the time, Pallas kernels for 0%

profile of v8, /device:TPU:0, one launch (start us, length us, event | category | flops | bytes accessed | tf_op | source)
XLA Modules:
  0.0 24.6 jit_solution(5111251089003774551)
XLA Ops:
  0.6 0.0 copy-start
  0.7 1.4 %fusion.195 = (s32[1]{0:T(128)}, s32[1]{0:T(128)}) fusion(s32[2]{0:T(128)} %param.4), kind=kLoop, calls=%fused_computation.276 | loop fusion | bytes 16 | tf_op jit(solution)/shard_map/slice | solution.py:80
  3.4 0.0 copy-done
  3.4 0.6 %convolution_bitcast_fusion = f32[5120,48]{0,1:T(8,128)S(1)} fusion(bf16[5120,128]{1,0:T(8,128)(2,1)S(1)} %bitcast.91, s32[128]{0:T(128)S(1)} %get-tuple-element.33, s32[48]{0:T(128)S(1)} %iota_multiply_fusion.2), kind=kOutput, calls=%fused_computation | convolution fusion | flops 63012864 | bytes 2294464 | tf_op jit(solution)/shard_map/dot_general | solution.py:115
  4.0 0.0 copy-start.1
  4.0 0.2 reshape.676
  4.2 0.5 %copy-done.1 = s32[2,2]{1,0:T(2,128)S(1)} copy-done((s32[2,2]{1,0:T(2,128)S(1)}, s32[2,2]{1,0:T(2,128)}, u32[]{:S(2)}) %copy-start.1) | copy-done | bytes 40
  4.7 0.1 fusion.120
  4.8 0.1 mul.630
  4.9 0.5 %fusion.132 = f32[2,256,48]{1,0,2:T(2,128)S(1)} fusion(f32[20,256,48]{1,0,2:T(8,128)S(1)} %reshape.676, s32[20]{0:T(128)S(1)} %mul.630, s32[2]{0:T(128)S(1)} %add_add_fusion.4), kind=kOutput, calls=%fused_computation.200 | convolution fusion | flops 5898880 | bytes 1081432 | tf_op jit(solution)/shard_map/qxyn,qe->xeyn/dot_general | solution.py:116
  5.4 0.3 %convolution_bitcast_fusion.2 = f32[1,2,48,48]{2,3,1,0:T(8,128)S(1)} fusion(f32[2,256,48]{1,0,2:T(2,128)S(1)} %fusion.132, s32[256]{0:T(256)S(1)} %add_add_fusion.1, s32[48]{0:T(128)S(1)} %iota_multiply_fusion.2), kind=kOutput, calls=%fused_computation.12 | convolution fusion | flops 14352384 | bytes 117952 | tf_op jit(solution)/shard_map/my,xeyn->xemn/dot_general | solution.py:117
  5.7 0.1 copy.14
  5.8 0.1 reshape.677
  5.9 0.1 reshape_reshape.16
  6.0 0.1 mul.580
  6.1 0.1 fusion.60
  6.2 0.1 broadcast_multiply_fusion.1
  6.3 0.3 %multiply_convert_fusion = (bf16[20,128,128]{2,1,0:T(8,128)(2,1)S(1)}, bf16[20,128,128]{2,1,0:T(8,128)(2,1)S(1)}) fusion(f32[128,128]{1,0:T(8,128)S(1)} %fusion.60, f32[20,128]{1,0:T(8,128)S(1)} %get-tuple-element.28), kind=kLoop, calls=%fused_computation.2 | loop fusion | flops 1638400 | bytes 1386496 | tf_op jit(solution)/shard_map/convert_element_type | solution.py:104
  6.6 0.5 %fusion.7 = f32[1,256,256]{2,1,0:T(8,128)S(1)} fusion(bf16[20,256,128]{2,1,0:T(8,128)(2,1)S(1)} %bitcast.92, bf16[20,128,128]{2,1,0:T(8,128)(2,1)S(1)} %get-tuple-element.16, bf16[20,128,128]{2,1,0:T(8,128)(2,1)S(1)} %get-tuple-element.15), kind=kOutput, calls=%fused_computation.11 | convolution fusion | flops 338165760 | bytes 2883584 | tf_op jit(solution)/shard_map/qxyz,qzk->xyk/dot_general | solution.py:106
  7.1 0.2 broadcast_multiply_fusion
  7.3 2.4 %collective-permute-start.2 = (f32[101,128]{1,0:T(8,128)S(1)}, f32[101,128]{1,0:T(8,128)S(1)}, u32[]{:S(2)}, u32[]{:S(2)}) collective-permute-start(f32[101,128]{1,0:T(8,128)S(1)} %get-tuple-element.26), channel_id=1, source_target_pairs={{0,3},{1,2},{2,1},{3,0},{4,7},{5,6},{6,5},{7,4},{8,11},{9,10},{10,... | collective-permute-start | bytes 155144 | tf_op jit(solution)/shard_map/ppermute | solution.py:53
  9.8 0.6 %collective-permute-start.1 = (f32[101,128]{1,0:T(8,128)S(1)}, f32[101,128]{1,0:T(8,128)S(1)}, u32[]{:S(2)}, u32[]{:S(2)}) collective-permute-start(f32[101,128]{1,0:T(8,128)S(1)} %get-tuple-element.25), channel_id=1, source_target_pairs={{0,2},{1,3},{2,0},{3,1},{4,6},{5,7},{6,4},{7,5},{8,10},{9,11},{10,... | collective-permute-start | bytes 155144 | tf_op jit(solution)/shard_map/ppermute | solution.py:53
  10.4 0.5 %fusion.6 = f32[128,128]{0,1:T(8,128)S(1)} fusion(bf16[20,256,128]{2,1,0:T(8,128)(2,1)S(1)} %bitcast.93, f32[20,128]{1,0:T(8,128)S(1)} %get-tuple-element.27, s32[128]{0:T(128)S(1)} %get-tuple-element.35, s32[256]{0:T(256)S(1)} %iota_multiply_fusion), kind=kOutput, calls=%fused_computation.10 | convolution fusion | flops 168935424 | bytes 1388032 | tf_op jit(solution)/shard_map/qxyz,yk->qxzk/dot_general | solution.py:112
  11.0 0.1 collective-permute-start
  11.1 0.1 fusion.121
  11.2 0.1 reshape.687
  11.3 0.7 %collective-permute-done.2 = f32[101,128]{1,0:T(8,128)S(1)} collective-permute-done((f32[101,128]{1,0:T(8,128)S(1)}, f32[101,128]{1,0:T(8,128)S(1)}, u32[]{:S(2)}, u32[]{:S(2)}) %collective-permute-start.2) | collective-permute-done | bytes 51744 | tf_op jit(solution)/shard_map/ppermute | solution.py:53
  12.0 2.2 %collective-permute-done.1 = f32[101,128]{1,0:T(8,128)S(1)} collective-permute-done((f32[101,128]{1,0:T(8,128)S(1)}, f32[101,128]{1,0:T(8,128)S(1)}, u32[]{:S(2)}, u32[]{:S(2)}) %collective-permute-start.1) | collective-permute-done | bytes 51744 | tf_op jit(solution)/shard_map/ppermute | solution.py:53
  14.2 0.0 collective-permute-done
  14.4 0.1 dynamic-slice_reduce_fusion
  14.5 3.7 %collective-permute-start.5 = (f32[41,128]{1,0:T(8,128)S(1)}, f32[41,128]{1,0:T(8,128)S(1)}, u32[]{:S(2)}, u32[]{:S(2)}) collective-permute-start(f32[41,128]{1,0:T(8,128)S(1)} %pad_maximum_fusion.7), channel_id=1, source_target_pairs={{0,12},{4,8},{8,4},{12,0},{1,13},{5,9},{9,5},{13,1},{2,14},{6,10},... | collective-permute-start | bytes 62984 | tf_op jit(solution)/shard_map/ppermute | solution.py:53
  18.2 0.0 collective-permute-start.4
  18.2 0.8 %collective-permute-start.3 = (f32[41,128]{1,0:T(8,128)S(1)}, f32[41,128]{1,0:T(8,128)S(1)}, u32[]{:S(2)}, u32[]{:S(2)}) collective-permute-start(f32[41,128]{1,0:T(8,128)S(1)} %pad_maximum_fusion.5), channel_id=1, source_target_pairs={{0,4},{4,0},{8,12},{12,8},{1,5},{5,1},{9,13},{13,9},{2,6},{6,2},{1... | collective-permute-start | bytes 62984 | tf_op jit(solution)/shard_map/ppermute | solution.py:53
  19.0 0.5 %fusion.144 = f32[1,128]{1,0:T(1,128)} fusion(f32[101,128]{1,0:T(8,128)S(1)} %collective-permute-done.2, f32[101,128]{1,0:T(8,128)S(1)} %collective-permute-done.1, f32[165,128]{1,0:T(8,128)S(1)} %collective-permute-done, f32[128]{0:T(128)S(1)} %get-tuple-element.9), kind=kLoop, calls=%fused_computation.212 | loop fusion | flops 512 | bytes 2560 | tf_op jit(solution)/shard_map/mul | solution.py:185
  19.5 0.1 concatenate.40
  19.6 0.6 %collective-permute-done.5 = f32[41,128]{1,0:T(8,128)S(1)} collective-permute-done((f32[41,128]{1,0:T(8,128)S(1)}, f32[41,128]{1,0:T(8,128)S(1)}, u32[]{:S(2)}, u32[]{:S(2)}) %collective-permute-start.5) | collective-permute-done | bytes 21024 | tf_op jit(solution)/shard_map/ppermute | solution.py:53
  20.2 0.1 concatenate.43
  20.3 2.6 %collective-permute-done.4 = f32[41,128]{1,0:T(8,128)S(1)} collective-permute-done((f32[41,128]{1,0:T(8,128)S(1)}, f32[41,128]{1,0:T(8,128)S(1)}, u32[]{:S(2)}, u32[]{:S(2)}) %collective-permute-start.4) | collective-permute-done | bytes 21024 | tf_op jit(solution)/shard_map/ppermute | solution.py:53
  22.9 0.1 concatenate.42
  23.0 0.0 collective-permute-done.3
  23.0 0.1 concatenate.41
  23.1 0.1 multiply_reduce_fusion
  23.2 0.7 %multiply_bitcast_fusion = f32[576,2,48]{0,2,1:T(8,128)} fusion(f32[48,2,576]{2,0,1:T(8,128)S(1)} %multiply_reduce_fusion), kind=kLoop, calls=%fused_computation.14 | loop fusion | flops 55296 | bytes 442368 | tf_op jit(solution)/shard_map/mul | solution.py:188
  24.0 0.6 %fusion.107 = (f32[128,16]{0,1:T(8,128)}, f32[16,128]{1,0:T(8,128)}) fusion(f32[41,128]{1,0:T(8,128)S(1)} %collective-permute-done.5, f32[41,128]{1,0:T(8,128)S(1)} %collective-permute-done.4, f32[41,128]{1,0:T(8,128)S(1)} %collective-permute-done.3, f32[4,1,16,128]{3,2,0,1:T(8,128)S(1)} %bitcast_add_fusion, s32[]{:T(128)S(6)} %select_n.63, ...), kind=kLoop, calls=%fused_computation.143 | loop fusion | flops 16384 | bytes 81924 | tf_op jit(solution)/shard_map/mul | solution.py:187
  (37 shorter events, 0.3 us)
Async XLA Ops:
  0.6 2.8 %copy-start = (bf16[2,2,5,1,256,128]{5,4,3,2,1,0:T(8,128)(2,1)S(1)}, bf16[2,2,5,1,256,128]{5,4,3,2,1,0:T(8,128)(2,1)}, u32[]{:S(2)}) copy-start(bf16[2,2,5,1,256,128]{5,4,3,2,1,0:T(8,128)(2,1)} %param.3) | copy-start | bytes 3932164
  4.0 0.7 %copy-start.1 = (s32[2,2]{1,0:T(2,128)S(1)}, s32[2,2]{1,0:T(2,128)}, u32[]{:S(2)}) copy-start(s32[2,2]{1,0:T(2,128)} %param.5) | copy-start | bytes 52
  7.3 4.7 %collective-permute-start.2 = (f32[101,128]{1,0:T(8,128)S(1)}, f32[101,128]{1,0:T(8,128)S(1)}, u32[]{:S(2)}, u32[]{:S(2)}) collective-permute-start(f32[101,128]{1,0:T(8,128)S(1)} %get-tuple-element.26), channel_id=1, source_target_pairs={{0,3},{1,2},{2,1},{3,0},{4,7},{5,6},{6,5},{7,4},{8,11},{9,10},{10,... | collective-permute-start | bytes 155144 | tf_op jit(solution)/shard_map/ppermute | solution.py:53
  9.8 4.4 %collective-permute-start.1 = (f32[101,128]{1,0:T(8,128)S(1)}, f32[101,128]{1,0:T(8,128)S(1)}, u32[]{:S(2)}, u32[]{:S(2)}) collective-permute-start(f32[101,128]{1,0:T(8,128)S(1)} %get-tuple-element.25), channel_id=1, source_target_pairs={{0,2},{1,3},{2,0},{3,1},{4,6},{5,7},{6,4},{7,5},{8,10},{9,11},{10,... | collective-permute-start | bytes 155144 | tf_op jit(solution)/shard_map/ppermute | solution.py:53
  11.0 3.3 %collective-permute-start = (f32[165,128]{1,0:T(8,128)S(1)}, f32[165,128]{1,0:T(8,128)S(1)}, u32[]{:S(2)}, u32[]{:S(2)}) collective-permute-start(f32[165,128]{1,0:T(8,128)S(1)} %pad_maximum_fusion), channel_id=1, source_target_pairs={{0,1},{1,0},{2,3},{3,2},{4,5},{5,4},{6,7},{7,6},{8,9},{9,8},{10,11... | collective-permute-start | bytes 253448 | tf_op jit(solution)/shard_map/ppermute | solution.py:53
  14.5 5.7 %collective-permute-start.5 = (f32[41,128]{1,0:T(8,128)S(1)}, f32[41,128]{1,0:T(8,128)S(1)}, u32[]{:S(2)}, u32[]{:S(2)}) collective-permute-start(f32[41,128]{1,0:T(8,128)S(1)} %pad_maximum_fusion.7), channel_id=1, source_target_pairs={{0,12},{4,8},{8,4},{12,0},{1,13},{5,9},{9,5},{13,1},{2,14},{6,10},... | collective-permute-start | bytes 62984 | tf_op jit(solution)/shard_map/ppermute | solution.py:53
  18.2 4.7 %collective-permute-start.4 = (f32[41,128]{1,0:T(8,128)S(1)}, f32[41,128]{1,0:T(8,128)S(1)}, u32[]{:S(2)}, u32[]{:S(2)}) collective-permute-start(f32[41,128]{1,0:T(8,128)S(1)} %pad_maximum_fusion.6), channel_id=1, source_target_pairs={{0,8},{4,12},{8,0},{12,4},{1,9},{5,13},{9,1},{13,5},{2,10},{6,14},... | collective-permute-start | bytes 62984 | tf_op jit(solution)/shard_map/ppermute | solution.py:53
  18.2 4.8 %collective-permute-start.3 = (f32[41,128]{1,0:T(8,128)S(1)}, f32[41,128]{1,0:T(8,128)S(1)}, u32[]{:S(2)}, u32[]{:S(2)}) collective-permute-start(f32[41,128]{1,0:T(8,128)S(1)} %pad_maximum_fusion.5), channel_id=1, source_target_pairs={{0,4},{4,0},{8,12},{12,8},{1,5},{5,1},{9,13},{13,9},{2,6},{6,2},{1... | collective-permute-start | bytes 62984 | tf_op jit(solution)/shard_map/ppermute | solution.py:53

commit v9 on v8

--- a/solution.py
+++ b/solution.py
@@ -139,6 +139,22 @@
             (got,) = send_to("vert", n_vert, s * d, [at(s)])
             total = total + got
         sz = total
+    for d, r in digit_steps(n_gx):
+        digit = (gx_me // d) % r
+        at_y = split_digit(sy, 0, r, digit)
+        at_z = split_digit(sz, 0, r, digit)
+        at_c = split_digit(core, 1, r, digit)
+        sy_total, sz_total, core_parts = at_y(0), at_z(0), [at_c(0)]
+        for s in range(1, r):
+            g_sy, g_sz, g_core = send_to("gx", n_gx, s * d, [at_y(s), at_z(s), at_c(s)])
+            sy_total, sz_total = sy_total + g_sy, sz_total + g_sz
+            core_parts.append(g_core)
+        sy, sz = sy_total, sz_total
+        core = jnp.concatenate(core_parts, axis=0)
+
+    src = jnp.bitwise_xor(gx_me, jnp.arange(n_gx, dtype=jnp.int32))
+    x_src = (src[:, None] * cells_x + jnp.arange(cells_x, dtype=jnp.int32)[None, :]).reshape(-1)
+    phx = test_table(sketch_ids, x_src, total_x, core_stream, 5).astype(f32).reshape(S, n_gx, cells_x)
     gzv_me = linear_index(("gz", "vert"))
     for d, r in digit_steps(n_gzv):
         digit = (gzv_me // d) % r
@@ -157,22 +173,6 @@
         sy, sx, core = sy_total, sx_total, core_total
         if with_sz:
             sz = sz_total
-    for d, r in digit_steps(n_gx):
-        digit = (gx_me // d) % r
-        at_y = split_digit(sy, 0, r, digit)
-        at_z = split_digit(sz, 0, r, digit)
-        at_c = split_digit(core, 1, r, digit)
-        sy_total, sz_total, core_parts = at_y(0), at_z(0), [at_c(0)]
-        for s in range(1, r):
-            g_sy, g_sz, g_core = send_to("gx", n_gx, s * d, [at_y(s), at_z(s), at_c(s)])
-            sy_total, sz_total = sy_total + g_sy, sz_total + g_sz
-            core_parts.append(g_core)
-        sy, sz = sy_total, sz_total
-        core = jnp.concatenate(core_parts, axis=0)
-
-    src = jnp.bitwise_xor(gx_me, jnp.arange(n_gx, dtype=jnp.int32))
-    x_src = (src[:, None] * cells_x + jnp.arange(cells_x, dtype=jnp.int32)[None, :]).reshape(-1)
-    phx = test_table(sketch_ids, x_src, total_x, core_stream, 5).astype(f32).reshape(S, n_gx, cells_x)
     held = core.reshape(n_gx * cells_x, E, core_rows)
     weights_x = phx.reshape(S, n_gx * cells_x)
     core_out = jnp.sum(held[:, None, :, :] * weights_x.T[:, :, None, None], axis=0).transpose(2, 1, 0)

time: 24.8 us -> 25 us (level)
    mul x3 -> x0, other arithmetic: 0.27 us -> none  [the longest x1 0.17 us: shards(): part_y = jnp.sum(by_q * ax[:, None, :], axis=0)]
  transfers between devices with their start and end apart: 6 -> 6, of which waited for: 4 -> 4; matrix products, arithmetic and copies ran while one was open for 6% -> 3% of each run, Pallas kernels for 0% -> 0%
where the time goes in v9:
time: 25 us; the launch traced here: 24.8 us
  starting transfers between devices  7.73 us (31%)
  waiting for transfers between devices  6.1 us (24%)
  local copies, waits for them, and re-layouts  3.25 us (13%)
  other arithmetic  3.03 us (12%)
  matrix products  2.41 us (10%)
  between operations  2.31 us (9%)
    ppermute x6, starting transfers between devices, send_to(): got = lax.ppermute(flat, axes, [(i, i ^ shift) for i in range(n)])  7.73 us
    ppermute x6, waiting for transfers between devices, send_to(): got = lax.ppermute(flat, axes, [(i, i ^ shift) for i in range(n)])  6.1 us
    slice x1, local copies, waits for them, and re-layouts, shards(): factor_stream = test_streams[0]  1.35 us
    mul x1, other arithmetic, shards(): core_out * scale_core  0.72 us
    mul x1, other arithmetic, shards(): sz.reshape(cols_each, cells_z).T * scale_z  0.61 us
    dot_general x1, matrix products, shards(): jnp.dot(rows_z, phz.T, preferred_element_type=f32)  0.6 us
    dot_general x1, matrix products, shards(): by_e = jnp.einsum('qxyn,qe->xeyn', first, phq, precision=highest)  0.53 us
    unnamed x4, local copies, waits for them, and re-layouts  0.52 us
  transfers between devices with their start and end apart: 6, of which 4 were waited for; matrix products, arithmetic and copies ran while one was open for 3% of the time, Pallas kernels for 0%

profile of v9, /device:TPU:0, one launch (start us, length us, event | category | flops | bytes accessed | tf_op | source)
XLA Modules:
  0.0 24.8 jit_solution(13908897947125788621)
XLA Ops:
  0.6 0.0 copy-start
  0.7 1.4 %fusion.200 = (s32[1]{0:T(128)}, s32[1]{0:T(128)}) fusion(s32[2]{0:T(128)} %param.4), kind=kLoop, calls=%fused_computation.279 | loop fusion | bytes 16 | tf_op jit(solution)/shard_map/slice | solution.py:80
  3.4 0.0 copy-done
  3.4 0.6 %convolution_bitcast_fusion = f32[5120,48]{0,1:T(8,128)S(1)} fusion(bf16[5120,128]{1,0:T(8,128)(2,1)S(1)} %bitcast.95, s32[128]{0:T(128)S(1)} %get-tuple-element.32, s32[48]{0:T(128)S(1)} %iota_multiply_fusion.2), kind=kOutput, calls=%fused_computation | convolution fusion | flops 63012864 | bytes 2294464 | tf_op jit(solution)/shard_map/dot_general | solution.py:115
  4.0 0.0 copy-start.1
  4.0 0.2 reshape.719
  4.2 0.5 %copy-done.1 = s32[2,2]{1,0:T(2,128)S(1)} copy-done((s32[2,2]{1,0:T(2,128)S(1)}, s32[2,2]{1,0:T(2,128)}, u32[]{:S(2)}) %copy-start.1) | copy-done | bytes 40
  4.7 0.1 fusion.126
  4.8 0.1 mul.639
  4.9 0.5 %fusion.138 = f32[2,256,48]{1,0,2:T(2,128)S(1)} fusion(f32[20,256,48]{1,0,2:T(8,128)S(1)} %reshape.719, s32[20]{0:T(128)S(1)} %mul.639, s32[2]{0:T(128)S(1)} %add_add_fusion.3), kind=kOutput, calls=%fused_computation.204 | convolution fusion | flops 5898880 | bytes 1081432 | tf_op jit(solution)/shard_map/qxyn,qe->xeyn/dot_general | solution.py:116
  5.4 0.3 %convolution_bitcast_fusion.2 = f32[1,2,48,48]{2,3,1,0:T(8,128)S(1)} fusion(f32[2,256,48]{1,0,2:T(2,128)S(1)} %fusion.138, s32[256]{0:T(256)S(1)} %add_add_fusion, s32[48]{0:T(128)S(1)} %iota_multiply_fusion.2), kind=kOutput, calls=%fused_computation.12 | convolution fusion | flops 14352384 | bytes 117952 | tf_op jit(solution)/shard_map/my,xeyn->xemn/dot_general | solution.py:117
  5.7 0.1 copy.12
  5.8 0.1 reshape.720
  5.9 0.1 reshape_reshape.15
  6.0 0.1 mul.578
  6.1 0.1 fusion.60
  6.2 0.1 fusion.113
  6.3 0.3 %multiply_convert_fusion = (bf16[20,128,128]{2,1,0:T(8,128)(2,1)S(1)}, bf16[20,128,128]{2,1,0:T(8,128)(2,1)S(1)}) fusion(f32[128,128]{1,0:T(8,128)S(1)} %fusion.60, f32[20,128]{1,0:T(8,128)S(1)} %get-tuple-element.26), kind=kLoop, calls=%fused_computation.2 | loop fusion | flops 1638400 | bytes 1386496 | tf_op jit(solution)/shard_map/convert_element_type | solution.py:104
  6.6 0.5 %fusion.7 = f32[1,256,256]{2,1,0:T(8,128)S(1)} fusion(bf16[20,256,128]{2,1,0:T(8,128)(2,1)S(1)} %bitcast.96, bf16[20,128,128]{2,1,0:T(8,128)(2,1)S(1)} %get-tuple-element.14, bf16[20,128,128]{2,1,0:T(8,128)(2,1)S(1)} %get-tuple-element.13), kind=kOutput, calls=%fused_computation.11 | convolution fusion | flops 338165760 | bytes 2883584 | tf_op jit(solution)/shard_map/qxyz,qzk->xyk/dot_general | solution.py:106
  7.1 0.5 %fusion.6 = f32[128,128]{0,1:T(8,128)S(1)} fusion(bf16[20,256,128]{2,1,0:T(8,128)(2,1)S(1)} %bitcast.97, f32[20,128]{1,0:T(8,128)S(1)} %get-tuple-element.27, s32[128]{0:T(128)S(1)} %get-tuple-element.34, s32[256]{0:T(256)S(1)} %iota_multiply_fusion), kind=kOutput, calls=%fused_computation.10 | convolution fusion | flops 168935424 | bytes 1388032 | tf_op jit(solution)/shard_map/qxyz,yk->qxzk/dot_general | solution.py:112
  7.7 0.2 multiply_reduce_fusion.1
  7.9 0.1 fusion.114
  8.0 5.1 %collective-permute-start.2 = (f32[105,128]{1,0:T(8,128)S(1)}, f32[105,128]{1,0:T(8,128)S(1)}, u32[]{:S(2)}, u32[]{:S(2)}) collective-permute-start(f32[105,128]{1,0:T(8,128)S(1)} %pad_maximum_fusion.2), channel_id=1, source_target_pairs={{0,12},{4,8},{8,4},{12,0},{1,13},{5,9},{9,5},{13,1},{2,14},{6,10},... | collective-permute-start | bytes 161288 | tf_op jit(solution)/shard_map/ppermute | solution.py:53
  13.1 0.0 collective-permute-start.1
  13.1 0.6 %collective-permute-start = (f32[105,128]{1,0:T(8,128)S(1)}, f32[105,128]{1,0:T(8,128)S(1)}, u32[]{:S(2)}, u32[]{:S(2)}) collective-permute-start(f32[105,128]{1,0:T(8,128)S(1)} %pad_maximum_fusion), channel_id=1, source_target_pairs={{0,4},{4,0},{8,12},{12,8},{1,5},{5,1},{9,13},{13,9},{2,6},{6,2},{1... | collective-permute-start | bytes 161288 | tf_op jit(solution)/shard_map/ppermute | solution.py:53
  13.8 1.7 %collective-permute-done.2 = f32[105,128]{1,0:T(8,128)S(1)} collective-permute-done((f32[105,128]{1,0:T(8,128)S(1)}, f32[105,128]{1,0:T(8,128)S(1)}, u32[]{:S(2)}, u32[]{:S(2)}) %collective-permute-start.2) | collective-permute-done | bytes 53792 | tf_op jit(solution)/shard_map/ppermute | solution.py:53
  15.5 2.7 %collective-permute-done.1 = f32[105,128]{1,0:T(8,128)S(1)} collective-permute-done((f32[105,128]{1,0:T(8,128)S(1)}, f32[105,128]{1,0:T(8,128)S(1)}, u32[]{:S(2)}, u32[]{:S(2)}) %collective-permute-start.1) | collective-permute-done | bytes 53792 | tf_op jit(solution)/shard_map/ppermute | solution.py:53
  18.2 0.0 collective-permute-done
  18.4 0.4 %collective-permute-start.5 = (f32[53,128]{1,0:T(8,128)S(1)}, f32[53,128]{1,0:T(8,128)S(1)}, u32[]{:S(2)}, u32[]{:S(2)}) collective-permute-start(f32[53,128]{1,0:T(8,128)S(1)} %get-tuple-element.24), channel_id=1, source_target_pairs={{0,3},{1,2},{2,1},{3,0},{4,7},{5,6},{6,5},{7,4},{8,11},{9,10},{10,... | collective-permute-start | bytes 81416 | tf_op jit(solution)/shard_map/ppermute | solution.py:53
  18.7 1.3 %collective-permute-start.4 = (f32[53,128]{1,0:T(8,128)S(1)}, f32[53,128]{1,0:T(8,128)S(1)}, u32[]{:S(2)}, u32[]{:S(2)}) collective-permute-start(f32[53,128]{1,0:T(8,128)S(1)} %get-tuple-element.23), channel_id=1, source_target_pairs={{0,2},{1,3},{2,0},{3,1},{4,6},{5,7},{6,4},{7,5},{8,10},{9,11},{10,... | collective-permute-start | bytes 81416 | tf_op jit(solution)/shard_map/ppermute | solution.py:53
  20.1 0.3 %collective-permute-start.3 = (f32[69,128]{1,0:T(8,128)S(1)}, f32[69,128]{1,0:T(8,128)S(1)}, u32[]{:S(2)}, u32[]{:S(2)}) collective-permute-start(f32[69,128]{1,0:T(8,128)S(1)} %pad_maximum_fusion.5), channel_id=1, source_target_pairs={{0,1},{1,0},{2,3},{3,2},{4,5},{5,4},{6,7},{7,6},{8,9},{9,8},{10,11... | collective-permute-start | bytes 105992 | tf_op jit(solution)/shard_map/ppermute | solution.py:53
  20.4 0.1 fusion.127
  20.5 0.1 concatenate.48
  20.6 0.1 concatenate.51
  20.7 0.1 concatenate.50
  20.7 0.1 concatenate.49
  20.8 1.1 %collective-permute-done.5 = f32[53,128]{1,0:T(8,128)S(1)} collective-permute-done((f32[53,128]{1,0:T(8,128)S(1)}, f32[53,128]{1,0:T(8,128)S(1)}, u32[]{:S(2)}, u32[]{:S(2)}) %collective-permute-start.5) | collective-permute-done | bytes 27168 | tf_op jit(solution)/shard_map/ppermute | solution.py:53
  21.9 0.1 reshape.744
  22.0 0.6 %collective-permute-done.4 = f32[53,128]{1,0:T(8,128)S(1)} collective-permute-done((f32[53,128]{1,0:T(8,128)S(1)}, f32[53,128]{1,0:T(8,128)S(1)}, u32[]{:S(2)}, u32[]{:S(2)}) %collective-permute-start.4) | collective-permute-done | bytes 27168 | tf_op jit(solution)/shard_map/ppermute | solution.py:53
  22.6 0.1 reshape.743
  22.7 0.0 collective-permute-done.3
  22.7 0.1 reshape.742
  22.8 0.1 multiply_reduce_fusion
  23.0 0.7 %multiply_bitcast_fusion = f32[576,2,48]{0,2,1:T(8,128)} fusion(f32[48,2,576]{2,0,1:T(8,128)S(1)} %multiply_reduce_fusion), kind=kLoop, calls=%fused_computation.14 | loop fusion | flops 55296 | bytes 442368 | tf_op jit(solution)/shard_map/mul | solution.py:188
  23.7 0.5 %fusion.150 = f32[1,128]{1,0:T(1,128)} fusion(f32[53,128]{1,0:T(8,128)S(1)} %collective-permute-done.5, f32[53,128]{1,0:T(8,128)S(1)} %collective-permute-done.4, f32[69,128]{1,0:T(8,128)S(1)} %collective-permute-done.3, f32[128]{0:T(128)S(1)} %get-tuple-element.8), kind=kLoop, calls=%fused_computation.216 | loop fusion | flops 512 | bytes 2560 | tf_op jit(solution)/shard_map/mul | solution.py:185
  24.2 0.6 %fusion.111 = (f32[128,16]{0,1:T(8,128)}, f32[16,128]{1,0:T(8,128)}) fusion(f32[69,128]{1,0:T(8,128)S(1)} %collective-permute-done.3, f32[1,2,16,128]{3,2,1,0:T(8,128)S(1)} %fusion.88, s32[]{:T(128)S(6)} %select_n.68, f32[53,128]{1,0:T(8,128)S(1)} %collective-permute-done.5, f32[53,128]{1,0:T(8,128)S(1)} %collective-permute-done.4, ...), kind=kLoop, calls=%fused_computation.147 | loop fusion | flops 12288 | bytes 65544 | tf_op jit(solution)/shard_map/mul | solution.py:187
  (41 shorter events, 0.3 us)
Async XLA Ops:
  0.6 2.8 %copy-start = (bf16[2,2,5,1,256,128]{5,4,3,2,1,0:T(8,128)(2,1)S(1)}, bf16[2,2,5,1,256,128]{5,4,3,2,1,0:T(8,128)(2,1)}, u32[]{:S(2)}) copy-start(bf16[2,2,5,1,256,128]{5,4,3,2,1,0:T(8,128)(2,1)} %param.3) | copy-start | bytes 3932164
  4.0 0.7 %copy-start.1 = (s32[2,2]{1,0:T(2,128)S(1)}, s32[2,2]{1,0:T(2,128)}, u32[]{:S(2)}) copy-start(s32[2,2]{1,0:T(2,128)} %param.5) | copy-start | bytes 52
  8.0 7.5 %collective-permute-start.2 = (f32[105,128]{1,0:T(8,128)S(1)}, f32[105,128]{1,0:T(8,128)S(1)}, u32[]{:S(2)}, u32[]{:S(2)}) collective-permute-start(f32[105,128]{1,0:T(8,128)S(1)} %pad_maximum_fusion.2), channel_id=1, source_target_pairs={{0,12},{4,8},{8,4},{12,0},{1,13},{5,9},{9,5},{13,1},{2,14},{6,10},... | collective-permute-start | bytes 161288 | tf_op jit(solution)/shard_map/ppermute | solution.py:53
  13.1 5.1 %collective-permute-start.1 = (f32[105,128]{1,0:T(8,128)S(1)}, f32[105,128]{1,0:T(8,128)S(1)}, u32[]{:S(2)}, u32[]{:S(2)}) collective-permute-start(f32[105,128]{1,0:T(8,128)S(1)} %pad_maximum_fusion.1), channel_id=1, source_target_pairs={{0,8},{4,12},{8,0},{12,4},{1,9},{5,13},{9,1},{13,5},{2,10},{6,14},... | collective-permute-start | bytes 161288 | tf_op jit(solution)/shard_map/ppermute | solution.py:53
  13.1 5.1 %collective-permute-start = (f32[105,128]{1,0:T(8,128)S(1)}, f32[105,128]{1,0:T(8,128)S(1)}, u32[]{:S(2)}, u32[]{:S(2)}) collective-permute-start(f32[105,128]{1,0:T(8,128)S(1)} %pad_maximum_fusion), channel_id=1, source_target_pairs={{0,4},{4,0},{8,12},{12,8},{1,5},{5,1},{9,13},{13,9},{2,6},{6,2},{1... | collective-permute-start | bytes 161288 | tf_op jit(solution)/shard_map/ppermute | solution.py:53
  18.4 3.6 %collective-permute-start.5 = (f32[53,128]{1,0:T(8,128)S(1)}, f32[53,128]{1,0:T(8,128)S(1)}, u32[]{:S(2)}, u32[]{:S(2)}) collective-permute-start(f32[53,128]{1,0:T(8,128)S(1)} %get-tuple-element.24), channel_id=1, source_target_pairs={{0,3},{1,2},{2,1},{3,0},{4,7},{5,6},{6,5},{7,4},{8,11},{9,10},{10,... | collective-permute-start | bytes 81416 | tf_op jit(solution)/shard_map/ppermute | solution.py:53
  18.7 3.9 %collective-permute-start.4 = (f32[53,128]{1,0:T(8,128)S(1)}, f32[53,128]{1,0:T(8,128)S(1)}, u32[]{:S(2)}, u32[]{:S(2)}) collective-permute-start(f32[53,128]{1,0:T(8,128)S(1)} %get-tuple-element.23), channel_id=1, source_target_pairs={{0,2},{1,3},{2,0},{3,1},{4,6},{5,7},{6,4},{7,5},{8,10},{9,11},{10,... | collective-permute-start | bytes 81416 | tf_op jit(solution)/shard_map/ppermute | solution.py:53
  20.1 2.6 %collective-permute-start.3 = (f32[69,128]{1,0:T(8,128)S(1)}, f32[69,128]{1,0:T(8,128)S(1)}, u32[]{:S(2)}, u32[]{:S(2)}) collective-permute-start(f32[69,128]{1,0:T(8,128)S(1)} %pad_maximum_fusion.5), channel_id=1, source_target_pairs={{0,1},{1,0},{2,3},{3,2},{4,5},{5,4},{6,7},{7,6},{8,9},{9,8},{10,11... | collective-permute-start | bytes 105992 | tf_op jit(solution)/shard_map/ppermute | solution.py:53

commit v10 on v8

--- a/solution.py
+++ b/solution.py
@@ -98,23 +98,25 @@
 
     n_q = batches * local_snaps * variables
     field = flow_field.reshape(n_q, cells_x, cells_y, cells_z)
-    rows_z = field.reshape(-1, cells_z)
 
     qz = aq[:, None, :] * az.astype(f32)[None, :, :]
-    qz_hi = qz.astype(bf16)
-    qz_lo = (qz - qz_hi.astype(f32)).astype(bf16)
+    qz_core = (phq[:, None, :, None] * phz.T.astype(f32)[None, :, None, :]).reshape(n_q, cells_z, E * S)
+    tab = jnp.concatenate([qz, qz_core], axis=-1)
+    tab_hi = tab.astype(bf16)
+    tab_lo = (tab - tab_hi.astype(f32)).astype(bf16)
+    width = K + E * S
     both = jnp.einsum(
-        "qxyz,qzk->xyk", field, jnp.concatenate([qz_hi, qz_lo], axis=-1), preferred_element_type=f32
-    )
-    by_q = both[..., :K] + both[..., K:]
+        "qxyz,qzk->xyk", field, jnp.concatenate([tab_hi, tab_lo], axis=-1), preferred_element_type=f32
+    )
+    summed = both[..., :width] + both[..., width:]
+    by_q = summed[..., :K]
+    by_e = summed[..., K:].reshape(cells_x, cells_y, E, S)
     part_y = jnp.sum(by_q * ax[:, None, :], axis=0)
     part_x = jnp.sum(by_q * ay.astype(f32)[None, :, :], axis=1)
     along_y = jnp.einsum("qxyz,yk->qxzk", field, ay, preferred_element_type=f32)
     weights = aq[:, None, :] * ax[None, :, :]
     part_z = jnp.sum(along_y * weights[:, :, None, :], axis=(0, 1))
-    first = jnp.dot(rows_z, phz.T, preferred_element_type=f32).reshape(n_q, cells_x, cells_y, S)
-    by_e = jnp.einsum("qxyn,qe->xeyn", first, phq, precision=highest)
-    part_core = jnp.einsum("my,xeyn->xemn", phy, by_e, precision=highest)
+    part_core = jnp.einsum("my,xyen->xemn", phy, by_e, precision=highest)
 
     rows_each = cells_y // (n_gx * n_gz * n_vert)
     cols_each = K // (n_gx * n_vert)

time: 24.8 us -> 27.5 us (1.11)
  other arithmetic: 3.01 us -> 5.67 us
  matrix products: 2.4 us -> 2.81 us
  local copies, waits for them, and re-layouts: 3.07 us -> 2.76 us
    convert_element_type x1 -> x4, other arithmetic: 0.34 us -> 1.52 us  [the longest x1 1.16 us: shards(): tab_hi = tab.astype(bf16)]
    mul x0 -> x2, other arithmetic: none -> 0.72 us  [the longest x1 0.4 us: shards(): qz = aq[:, None, :] * az.astype(f32)[None, :, :]]
    mul x1, other arithmetic: 0.01 us -> 0.68 us  [shards(): snapshot_ids[:, :, None] * variables]
    unnamed x4 -> x2, local copies, waits for them, and re-layouts: 0.52 us -> 0.01 us
    dot_general x4 -> x2, matrix products: 1.9 us -> 2.32 us  [the longest x1 2.05 us: shards(): jnp.einsum('qxyz,qzk->xyk', field, jnp.concatenate([tab_hi, tab_lo], axis...]
where the time goes in v10:
time: 27.5 us; the launch traced here: 27.3 us
  starting transfers between devices  7.63 us (28%)
  waiting for transfers between devices  6.18 us (22%)
  other arithmetic  5.67 us (21%)
  matrix products  2.81 us (10%)
  local copies, waits for them, and re-layouts  2.76 us (10%)
  between operations  2.28 us (8%)
    ppermute x6, starting transfers between devices, send_to(): got = lax.ppermute(flat, axes, [(i, i ^ shift) for i in range(n)])  7.63 us
    ppermute x6, waiting for transfers between devices, send_to(): got = lax.ppermute(flat, axes, [(i, i ^ shift) for i in range(n)])  6.18 us
    dot_general x1, matrix products, shards(): jnp.einsum('qxyz,qzk->xyk', field, jnp.concatenate([tab_hi, tab_lo], axis...  2.05 us
    slice x1, local copies, waits for them, and re-layouts, shards(): factor_stream = test_streams[0]  1.35 us
    convert_element_type x1, other arithmetic, shards(): tab_hi = tab.astype(bf16)  1.16 us
    mul x1, other arithmetic, shards(): core_out * scale_core  0.72 us
    mul x1, other arithmetic, shards(): snapshot_ids[:, :, None] * variables  0.68 us
    mul x1, other arithmetic, shards(): sz.reshape(cols_each, cells_z).T * scale_z  0.61 us
  transfers between devices with their start and end apart: 6, of which 4 were waited for; matrix products, arithmetic and copies ran while one was open for 6% of the time, Pallas kernels for 0%

profile of v10, /device:TPU:0, one launch (start us, length us, event | category | flops | bytes accessed | tf_op | source)
XLA Modules:
  0.0 27.3 jit_solution(13184689105321720487)
XLA Ops:
  0.6 0.0 copy-start
  0.7 1.4 %fusion.152 = (s32[1]{0:T(128)}, s32[1]{0:T(128)}) fusion(s32[2]{0:T(128)} %param.4), kind=kLoop, calls=%fused_computation.236 | loop fusion | bytes 16 | tf_op jit(solution)/shard_map/slice | solution.py:80
  3.4 0.7 %broadcast_multiply_fusion.3 = s32[2,2]{1,0:T(2,128)S(1)} fusion(s32[2,2]{1,0:T(2,128)} %param.5), kind=kLoop, calls=%fused_computation.212 | loop fusion | flops 4 | bytes 32 | tf_op jit(solution)/shard_map/mul | solution.py:89
  4.1 0.1 fusion.108
  4.1 0.1 mul.666
  4.2 0.1 fusion.119
  4.3 0.1 copy.21
  4.4 0.1 mul.678
  4.5 0.1 mul.679
  4.6 0.1 mul.638
  4.7 0.1 fusion.84
  4.8 0.3 %broadcast_multiply_fusion.1 = f32[20,128,96]{1,2,0:T(8,128)S(1)} fusion(f32[128,96]{0,1:T(8,128)S(1)} %bitcast.88, f32[20,96]{1,0:T(8,128)S(1)} %mul.679), kind=kLoop, calls=%fused_computation.14 | loop fusion | flops 245760 | bytes 1039872 | tf_op jit(solution)/shard_map/mul | solution.py:103
  5.1 0.1 fusion.59
  5.2 0.1 broadcast_multiply_fusion.2
  5.3 0.4 %broadcast_multiply_fusion = f32[20,128,128]{1,2,0:T(8,128)S(1)} fusion(f32[128,128]{0,1:T(8,128)S(1)} %fusion.59, f32[20,128]{1,0:T(8,128)S(1)} %get-tuple-element.26), kind=kLoop, calls=%fused_computation.13 | loop fusion | flops 327680 | bytes 1386496 | tf_op jit(solution)/shard_map/mul | solution.py:102
  5.7 0.2 subtract_convert_fusion
  5.9 1.2 %fusion.4 = bf16[20,128,224]{1,2,0:T(8,128)(2,1)} fusion(f32[20,128,96]{1,2,0:T(8,128)S(1)} %broadcast_multiply_fusion.1, f32[20,128,128]{1,2,0:T(8,128)S(1)} %broadcast_multiply_fusion), kind=kLoop, calls=%fused_computation.6 | loop fusion | flops 2293760 | bytes 3440640 | tf_op jit(solution)/shard_map/convert_element_type | solution.py:105
  7.1 2.0 %fusion.7 = f32[1,256,448]{1,2,0:T(8,128)S(1)} fusion(bf16[20,256,128]{2,1,0:T(8,128)(2,1)S(1)} %bitcast.84, bf16[20,128,224]{1,2,0:T(8,128)(2,1)S(1)} %subtract_convert_fusion, bf16[20,128,224]{1,2,0:T(8,128)(2,1)} %fusion.4), kind=kOutput, calls=%fused_computation.10 | convolution fusion | flops 591790080 | bytes 4063232 | tf_op jit(solution)/shard_map/qxyz,qzk->xyk/dot_general | solution.py:108
  9.2 0.3 convolution_bitcast_fusion.1
  9.5 0.1 copy.23
  9.5 0.1 reshape.761
  9.7 0.1 reshape_reshape.12
  9.7 0.2 slice_multiply_fusion
  10.0 0.1 copy.22
  10.1 2.4 %collective-permute-start.2 = (f32[101,128]{1,0:T(8,128)S(1)}, f32[101,128]{1,0:T(8,128)S(1)}, u32[]{:S(2)}, u32[]{:S(2)}) collective-permute-start(f32[101,128]{1,0:T(8,128)S(1)} %get-tuple-element.24), channel_id=1, source_target_pairs={{0,3},{1,2},{2,1},{3,0},{4,7},{5,6},{6,5},{7,4},{8,11},{9,10},{10,... | collective-permute-start | bytes 155144 | tf_op jit(solution)/shard_map/ppermute | solution.py:53
  12.6 0.6 %collective-permute-start.1 = (f32[101,128]{1,0:T(8,128)S(1)}, f32[101,128]{1,0:T(8,128)S(1)}, u32[]{:S(2)}, u32[]{:S(2)}) collective-permute-start(f32[101,128]{1,0:T(8,128)S(1)} %get-tuple-element.23), channel_id=1, source_target_pairs={{0,2},{1,3},{2,0},{3,1},{4,6},{5,7},{6,4},{7,5},{8,10},{9,11},{10,... | collective-permute-start | bytes 155144 | tf_op jit(solution)/shard_map/ppermute | solution.py:53
  13.2 0.5 %fusion.6 = f32[128,128]{0,1:T(8,128)S(1)} fusion(bf16[20,256,128]{2,1,0:T(8,128)(2,1)S(1)} %bitcast.85, f32[20,128]{1,0:T(8,128)S(1)} %get-tuple-element.25, s32[128]{0:T(128)S(1)} %get-tuple-element.33, s32[256]{0:T(256)S(1)} %iota_multiply_fusion), kind=kOutput, calls=%fused_computation.9 | convolution fusion | flops 168935424 | bytes 1388032 | tf_op jit(solution)/shard_map/qxyz,yk->qxzk/dot_general | solution.py:116
  13.7 0.1 collective-permute-start
  13.9 0.1 fusion.109
  14.0 0.1 reshape.771
  14.0 0.7 %collective-permute-done.2 = f32[101,128]{1,0:T(8,128)S(1)} collective-permute-done((f32[101,128]{1,0:T(8,128)S(1)}, f32[101,128]{1,0:T(8,128)S(1)}, u32[]{:S(2)}, u32[]{:S(2)}) %collective-permute-start.2) | collective-permute-done | bytes 51744 | tf_op jit(solution)/shard_map/ppermute | solution.py:53
  14.8 2.2 %collective-permute-done.1 = f32[101,128]{1,0:T(8,128)S(1)} collective-permute-done((f32[101,128]{1,0:T(8,128)S(1)}, f32[101,128]{1,0:T(8,128)S(1)}, u32[]{:S(2)}, u32[]{:S(2)}) %collective-permute-start.1) | collective-permute-done | bytes 51744 | tf_op jit(solution)/shard_map/ppermute | solution.py:53
  17.0 0.0 collective-permute-done
  17.2 0.1 dynamic-slice_reduce_fusion
  17.3 3.7 %collective-permute-start.5 = (f32[41,128]{1,0:T(8,128)S(1)}, f32[41,128]{1,0:T(8,128)S(1)}, u32[]{:S(2)}, u32[]{:S(2)}) collective-permute-start(f32[41,128]{1,0:T(8,128)S(1)} %pad_maximum_fusion.8), channel_id=1, source_target_pairs={{0,12},{4,8},{8,4},{12,0},{1,13},{5,9},{9,5},{13,1},{2,14},{6,10},... | collective-permute-start | bytes 62984 | tf_op jit(solution)/shard_map/ppermute | solution.py:53
  20.9 0.0 collective-permute-start.4
  21.0 0.8 %collective-permute-start.3 = (f32[41,128]{1,0:T(8,128)S(1)}, f32[41,128]{1,0:T(8,128)S(1)}, u32[]{:S(2)}, u32[]{:S(2)}) collective-permute-start(f32[41,128]{1,0:T(8,128)S(1)} %pad_maximum_fusion.6), channel_id=1, source_target_pairs={{0,4},{4,0},{8,12},{12,8},{1,5},{5,1},{9,13},{13,9},{2,6},{6,2},{1... | collective-permute-start | bytes 62984 | tf_op jit(solution)/shard_map/ppermute | solution.py:53
  21.7 0.5 %fusion.130 = f32[1,128]{1,0:T(1,128)} fusion(f32[101,128]{1,0:T(8,128)S(1)} %collective-permute-done.2, f32[101,128]{1,0:T(8,128)S(1)} %collective-permute-done.1, f32[165,128]{1,0:T(8,128)S(1)} %collective-permute-done, f32[128]{0:T(128)S(1)} %get-tuple-element.9), kind=kLoop, calls=%fused_computation.201 | loop fusion | flops 512 | bytes 2560 | tf_op jit(solution)/shard_map/mul | solution.py:187
  22.2 0.1 concatenate.44
  22.3 0.6 %collective-permute-done.5 = f32[41,128]{1,0:T(8,128)S(1)} collective-permute-done((f32[41,128]{1,0:T(8,128)S(1)}, f32[41,128]{1,0:T(8,128)S(1)}, u32[]{:S(2)}, u32[]{:S(2)}) %collective-permute-start.5) | collective-permute-done | bytes 21024 | tf_op jit(solution)/shard_map/ppermute | solution.py:53
  23.0 0.1 concatenate.47
  23.0 2.6 %collective-permute-done.4 = f32[41,128]{1,0:T(8,128)S(1)} collective-permute-done((f32[41,128]{1,0:T(8,128)S(1)}, f32[41,128]{1,0:T(8,128)S(1)}, u32[]{:S(2)}, u32[]{:S(2)}) %collective-permute-start.4) | collective-permute-done | bytes 21024 | tf_op jit(solution)/shard_map/ppermute | solution.py:53
  25.7 0.1 concatenate.46
  25.8 0.0 collective-permute-done.3
  25.8 0.1 concatenate.45
  25.9 0.1 multiply_reduce_fusion
  26.0 0.7 %multiply_bitcast_fusion = f32[576,2,48]{0,2,1:T(8,128)} fusion(f32[48,2,576]{2,0,1:T(8,128)S(1)} %multiply_reduce_fusion), kind=kLoop, calls=%fused_computation.15 | loop fusion | flops 55296 | bytes 442368 | tf_op jit(solution)/shard_map/mul | solution.py:190
  26.7 0.6 %fusion.95 = (f32[128,16]{0,1:T(8,128)}, f32[16,128]{1,0:T(8,128)}) fusion(f32[41,128]{1,0:T(8,128)S(1)} %collective-permute-done.5, f32[41,128]{1,0:T(8,128)S(1)} %collective-permute-done.4, f32[41,128]{1,0:T(8,128)S(1)} %collective-permute-done.3, f32[4,1,16,128]{3,2,0,1:T(8,128)S(1)} %bitcast_add_fusion, s32[]{:T(128)S(6)} %select_n.63, ...), kind=kLoop, calls=%fused_computation.133 | loop fusion | flops 16384 | bytes 81924 | tf_op jit(solution)/shard_map/mul | solution.py:189
  (40 shorter events, 0.4 us)
Async XLA Ops:
  0.6 6.5 %copy-start = (bf16[2,2,5,1,256,128]{5,4,3,2,1,0:T(8,128)(2,1)S(1)}, bf16[2,2,5,1,256,128]{5,4,3,2,1,0:T(8,128)(2,1)}, u32[]{:S(2)}) copy-start(bf16[2,2,5,1,256,128]{5,4,3,2,1,0:T(8,128)(2,1)} %param.3) | copy-start | bytes 3932164
  10.1 4.7 %collective-permute-start.2 = (f32[101,128]{1,0:T(8,128)S(1)}, f32[101,128]{1,0:T(8,128)S(1)}, u32[]{:S(2)}, u32[]{:S(2)}) collective-permute-start(f32[101,128]{1,0:T(8,128)S(1)} %get-tuple-element.24), channel_id=1, source_target_pairs={{0,3},{1,2},{2,1},{3,0},{4,7},{5,6},{6,5},{7,4},{8,11},{9,10},{10,... | collective-permute-start | bytes 155144 | tf_op jit(solution)/shard_map/ppermute | solution.py:53
  12.6 4.4 %collective-permute-start.1 = (f32[101,128]{1,0:T(8,128)S(1)}, f32[101,128]{1,0:T(8,128)S(1)}, u32[]{:S(2)}, u32[]{:S(2)}) collective-permute-start(f32[101,128]{1,0:T(8,128)S(1)} %get-tuple-element.23), channel_id=1, source_target_pairs={{0,2},{1,3},{2,0},{3,1},{4,6},{5,7},{6,4},{7,5},{8,10},{9,11},{10,... | collective-permute-start | bytes 155144 | tf_op jit(solution)/shard_map/ppermute | solution.py:53
  13.7 3.3 %collective-permute-start = (f32[165,128]{1,0:T(8,128)S(1)}, f32[165,128]{1,0:T(8,128)S(1)}, u32[]{:S(2)}, u32[]{:S(2)}) collective-permute-start(f32[165,128]{1,0:T(8,128)S(1)} %pad_maximum_fusion.1), channel_id=1, source_target_pairs={{0,1},{1,0},{2,3},{3,2},{4,5},{5,4},{6,7},{7,6},{8,9},{9,8},{10,11... | collective-permute-start | bytes 253448 | tf_op jit(solution)/shard_map/ppermute | solution.py:53
  17.3 5.7 %collective-permute-start.5 = (f32[41,128]{1,0:T(8,128)S(1)}, f32[41,128]{1,0:T(8,128)S(1)}, u32[]{:S(2)}, u32[]{:S(2)}) collective-permute-start(f32[41,128]{1,0:T(8,128)S(1)} %pad_maximum_fusion.8), channel_id=1, source_target_pairs={{0,12},{4,8},{8,4},{12,0},{1,13},{5,9},{9,5},{13,1},{2,14},{6,10},... | collective-permute-start | bytes 62984 | tf_op jit(solution)/shard_map/ppermute | solution.py:53
  20.9 4.7 %collective-permute-start.4 = (f32[41,128]{1,0:T(8,128)S(1)}, f32[41,128]{1,0:T(8,128)S(1)}, u32[]{:S(2)}, u32[]{:S(2)}) collective-permute-start(f32[41,128]{1,0:T(8,128)S(1)} %pad_maximum_fusion.7), channel_id=1, source_target_pairs={{0,8},{4,12},{8,0},{12,4},{1,9},{5,13},{9,1},{13,5},{2,10},{6,14},... | collective-permute-start | bytes 62984 | tf_op jit(solution)/shard_map/ppermute | solution.py:53
  21.0 4.8 %collective-permute-start.3 = (f32[41,128]{1,0:T(8,128)S(1)}, f32[41,128]{1,0:T(8,128)S(1)}, u32[]{:S(2)}, u32[]{:S(2)}) collective-permute-start(f32[41,128]{1,0:T(8,128)S(1)} %pad_maximum_fusion.6), channel_id=1, source_target_pairs={{0,4},{4,0},{8,12},{12,8},{1,5},{5,1},{9,13},{13,9},{2,6},{6,2},{1... | collective-permute-start | bytes 62984 | tf_op jit(solution)/shard_map/ppermute | solution.py:53

commit v11 on v8

--- a/solution.py
+++ b/solution.py
@@ -88,6 +88,8 @@
     q_ids = (
         snapshot_ids[:, :, None] * variables + jnp.arange(variables, dtype=jnp.int32)[None, None, :]
     ).reshape(-1)
+    n_q = batches * local_snaps * variables
+    field, q_ids = lax.optimization_barrier((flow_field.reshape(n_q, cells_x, cells_y, cells_z), q_ids))
     ax = test_table(x_ids, rank_ids, K, factor_stream, 1).astype(f32)
     ay = test_table(y_ids, rank_ids, K, factor_stream, 2)
     az = test_table(z_ids, rank_ids, K, factor_stream, 3)
@@ -96,8 +98,6 @@
     phz = test_table(sketch_ids, z_ids, total_z, core_stream, 7)
     phq = test_table(q_ids, jnp.arange(E, dtype=jnp.int32), E, core_stream, 8).astype(f32)
 
-    n_q = batches * local_snaps * variables
-    field = flow_field.reshape(n_q, cells_x, cells_y, cells_z)
     rows_z = field.reshape(-1, cells_z)
 
     qz = aq[:, None, :] * az.astype(f32)[None, :, :]

time: 24.8 us -> 27.3 us (1.10)
  waiting for transfers between devices: 6.18 us -> 8.08 us
  local copies, waits for them, and re-layouts: 3.07 us -> 2.38 us
  other arithmetic: 3.01 us -> 3.69 us
  matrix products: 2.4 us -> 3.04 us
    ppermute x6, waiting for transfers between devices: 6.18 us -> 8.08 us  [send_to(): got = lax.ppermute(flat, axes, [(i, i ^ shift) for i in range(n)])]
    mul x1, other arithmetic: 0.01 us -> 0.68 us  [shards(): snapshot_ids[:, :, None] * variables]
    unnamed x4 -> x2, local copies, waits for them, and re-layouts: 0.52 us -> 0.01 us
    dot_general x1, matrix products: 0.53 us -> 1.03 us  [shards(): by_e = jnp.einsum('qxyn,qe->xeyn', first, phq, precision=highest)]
  transfers between devices with their start and end apart: 6 -> 6, of which waited for: 4 -> 4; matrix products, arithmetic and copies ran while one was open for 6% -> 4% of each run, Pallas kernels for 0% -> 0%
where the time goes in v11:
time: 27.3 us; the launch traced here: 27.1 us
  waiting for transfers between devices  8.08 us (30%)
  starting transfers between devices  7.72 us (28%)
  other arithmetic  3.69 us (14%)
  matrix products  3.04 us (11%)
  local copies, waits for them, and re-layouts  2.38 us (9%)
  between operations  2.23 us (8%)
    ppermute x6, waiting for transfers between devices, send_to(): got = lax.ppermute(flat, axes, [(i, i ^ shift) for i in range(n)])  8.08 us
    ppermute x6, starting transfers between devices, send_to(): got = lax.ppermute(flat, axes, [(i, i ^ shift) for i in range(n)])  7.72 us
    slice x1, local copies, waits for them, and re-layouts, shards(): factor_stream = test_streams[0]  1.35 us
    dot_general x1, matrix products, shards(): by_e = jnp.einsum('qxyn,qe->xeyn', first, phq, precision=highest)  1.03 us
    mul x1, other arithmetic, shards(): core_out * scale_core  0.72 us
    mul x1, other arithmetic, shards(): snapshot_ids[:, :, None] * variables  0.68 us
    dot_general x1, matrix products, shards(): along_y = jnp.einsum('qxyz,yk->qxzk', field, ay, preferred_element_type=f32)  0.64 us
    mul x1, other arithmetic, shards(): sz.reshape(cols_each, cells_z).T * scale_z  0.61 us
  transfers between devices with their start and end apart: 6, of which 4 were waited for; matrix products, arithmetic and copies ran while one was open for 4% of the time, Pallas kernels for 0%

profile of v11, /device:TPU:0, one launch (start us, length us, event | category | flops | bytes accessed | tf_op | source)
XLA Modules:
  0.0 27.1 jit_solution(263411449817706076)
XLA Ops:
  0.6 0.0 copy-start
  0.7 1.4 %fusion.202 = (s32[1]{0:T(128)}, s32[1]{0:T(128)}) fusion(s32[2]{0:T(128)} %param.4), kind=kLoop, calls=%fused_computation.280 | loop fusion | bytes 16 | tf_op jit(solution)/shard_map/slice | solution.py:80
  3.4 0.7 %broadcast_multiply_fusion.2 = s32[2,2]{1,0:T(2,128)S(1)} fusion(s32[2,2]{1,0:T(2,128)} %param.5), kind=kLoop, calls=%fused_computation.235 | loop fusion | flops 4 | bytes 32 | tf_op jit(solution)/shard_map/mul | solution.py:89
  4.1 0.1 iota_add_fusion
  4.2 0.1 add.600
  4.3 0.0 copy-done
  4.3 0.1 fusion.69
  4.4 0.1 broadcast_multiply_fusion.1
  4.5 0.3 %multiply_convert_fusion = (bf16[20,128,128]{2,1,0:T(8,128)(2,1)S(1)}, bf16[20,128,128]{2,1,0:T(8,128)(2,1)S(1)}) fusion(f32[128,128]{1,0:T(8,128)S(1)} %fusion.69, f32[20,128]{1,0:T(8,128)S(1)} %get-tuple-element.32), kind=kLoop, calls=%fused_computation.1 | loop fusion | flops 1638400 | bytes 1386496 | tf_op jit(solution)/shard_map/convert_element_type | solution.py:104
  4.8 0.5 %fusion.14 = f32[1,256,256]{2,1,0:T(8,128)S(1)} fusion(bf16[20,128,128]{2,1,0:T(8,128)(2,1)S(1)} %get-tuple-element.20, bf16[20,128,128]{2,1,0:T(8,128)(2,1)S(1)} %get-tuple-element.19, bf16[20,1,256,128]{3,2,0,1:T(8,128)(2,1)S(1)} %bitcast.89), kind=kOutput, calls=%fused_computation.15 | convolution fusion | flops 338165760 | bytes 2883584 | tf_op jit(solution)/shard_map/qxyz,qzk->xyk/dot_general | solution.py:106
  5.4 0.2 broadcast_multiply_fusion
  5.5 0.6 %fusion.9 = f32[128,128]{1,0:T(8,128)S(1)} fusion(bf16[20,1,256,128]{3,2,0,1:T(8,128)(2,1)S(1)} %bitcast.91, f32[20,128]{1,0:T(8,128)S(1)} %get-tuple-element.31, s32[128]{0:T(128)S(1)} %get-tuple-element.39, s32[256]{0:T(256)S(1)} %iota_multiply_fusion), kind=kOutput, calls=%fused_computation.12 | convolution fusion | flops 168935424 | bytes 1388032 | tf_op jit(solution)/shard_map/qxyz,yk->qxzk/dot_general | solution.py:112
  6.2 0.1 copy.37
  6.3 0.6 %fusion.7 = f32[20,256,48]{1,2,0:T(8,128)S(1)} fusion(bf16[20,1,256,128]{3,2,0,1:T(8,128)(2,1)S(1)} %bitcast.90, s32[128]{0:T(128)S(1)} %get-tuple-element.37, s32[48]{0:T(128)S(1)} %iota_multiply_fusion.2), kind=kOutput, calls=%fused_computation.10 | convolution fusion | flops 63012864 | bytes 2294464 | tf_op jit(solution)/shard_map/dot_general | solution.py:115
  6.9 1.0 %fusion.12 = f32[2,256,48]{1,0,2:T(2,128)S(1)} fusion(f32[20,256,48]{1,2,0:T(8,128)S(1)} %fusion.7, s32[20]{0:T(128)S(1)} %get-tuple-element.34, s32[2]{0:T(128)S(1)} %add_add_fusion.4), kind=kOutput, calls=%fused_computation.13 | convolution fusion | flops 5898880 | bytes 1081432 | tf_op jit(solution)/shard_map/qxyn,qe->xeyn/dot_general | solution.py:116
  7.9 0.3 convolution_bitcast_fusion
  8.2 0.1 copy.35
  8.2 0.1 reshape.658
  8.4 0.1 reshape_reshape.12
  8.5 0.5 %collective-permute-start = (f32[165,128]{1,0:T(8,128)S(1)}, f32[165,128]{1,0:T(8,128)S(1)}, u32[]{:S(2)}, u32[]{:S(2)}) collective-permute-start(f32[165,128]{1,0:T(8,128)S(1)} %pad_maximum_fusion), channel_id=1, source_target_pairs={{0,1},{1,0},{2,3},{3,2},{4,5},{5,4},{6,7},{7,6},{8,9},{9,8},{10,11... | collective-permute-start | bytes 253448 | tf_op jit(solution)/shard_map/ppermute | solution.py:53
  9.0 2.6 %collective-permute-start.1 = (f32[101,128]{1,0:T(8,128)S(1)}, f32[101,128]{1,0:T(8,128)S(1)}, u32[]{:S(2)}, u32[]{:S(2)}) collective-permute-start(f32[101,128]{1,0:T(8,128)S(1)} %get-tuple-element.29), channel_id=1, source_target_pairs={{0,2},{1,3},{2,0},{3,1},{4,6},{5,7},{6,4},{7,5},{8,10},{9,11},{10,... | collective-permute-start | bytes 155144 | tf_op jit(solution)/shard_map/ppermute | solution.py:53
  11.6 0.2 collective-permute-start.2
  11.8 0.1 fusion.129
  11.9 0.1 reshape.668
  11.9 2.1 %collective-permute-done.1 = f32[101,128]{1,0:T(8,128)S(1)} collective-permute-done((f32[101,128]{1,0:T(8,128)S(1)}, f32[101,128]{1,0:T(8,128)S(1)}, u32[]{:S(2)}, u32[]{:S(2)}) %collective-permute-start.1) | collective-permute-done | bytes 51744 | tf_op jit(solution)/shard_map/ppermute | solution.py:53
  14.1 1.3 %collective-permute-done.2 = f32[101,128]{1,0:T(8,128)S(1)} collective-permute-done((f32[101,128]{1,0:T(8,128)S(1)}, f32[101,128]{1,0:T(8,128)S(1)}, u32[]{:S(2)}, u32[]{:S(2)}) %collective-permute-start.2) | collective-permute-done | bytes 51744 | tf_op jit(solution)/shard_map/ppermute | solution.py:53
  15.4 0.0 collective-permute-done
  15.6 0.1 dynamic-slice_reduce_fusion
  15.7 1.6 %collective-permute-start.3 = (f32[41,128]{1,0:T(8,128)S(1)}, f32[41,128]{1,0:T(8,128)S(1)}, u32[]{:S(2)}, u32[]{:S(2)}) collective-permute-start(f32[41,128]{1,0:T(8,128)S(1)} %pad_maximum_fusion.5), channel_id=1, source_target_pairs={{0,4},{4,0},{8,12},{12,8},{1,5},{5,1},{9,13},{13,9},{2,6},{6,2},{1... | collective-permute-start | bytes 62984 | tf_op jit(solution)/shard_map/ppermute | solution.py:53
  17.3 2.6 %collective-permute-start.4 = (f32[41,128]{1,0:T(8,128)S(1)}, f32[41,128]{1,0:T(8,128)S(1)}, u32[]{:S(2)}, u32[]{:S(2)}) collective-permute-start(f32[41,128]{1,0:T(8,128)S(1)} %pad_maximum_fusion.6), channel_id=1, source_target_pairs={{0,8},{4,12},{8,0},{12,4},{1,9},{5,13},{9,1},{13,5},{2,10},{6,14},... | collective-permute-start | bytes 62984 | tf_op jit(solution)/shard_map/ppermute | solution.py:53
  19.9 0.2 collective-permute-start.5
  20.2 0.5 %fusion.151 = f32[1,128]{1,0:T(1,128)} fusion(f32[101,128]{1,0:T(8,128)S(1)} %collective-permute-done.2, f32[101,128]{1,0:T(8,128)S(1)} %collective-permute-done.1, f32[165,128]{1,0:T(8,128)S(1)} %collective-permute-done, f32[128]{0:T(128)S(1)} %get-tuple-element.13), kind=kLoop, calls=%fused_computation.214 | loop fusion | flops 512 | bytes 2560 | tf_op jit(solution)/shard_map/mul | solution.py:185
  20.7 0.1 concatenate.40
  20.7 0.0 collective-permute-done.3
  20.8 0.1 concatenate.41
  20.8 1.6 %collective-permute-done.4 = f32[41,128]{1,0:T(8,128)S(1)} collective-permute-done((f32[41,128]{1,0:T(8,128)S(1)}, f32[41,128]{1,0:T(8,128)S(1)}, u32[]{:S(2)}, u32[]{:S(2)}) %collective-permute-start.4) | collective-permute-done | bytes 21024 | tf_op jit(solution)/shard_map/ppermute | solution.py:53
  22.4 0.1 concatenate.42
  22.5 3.1 %collective-permute-done.5 = f32[41,128]{1,0:T(8,128)S(1)} collective-permute-done((f32[41,128]{1,0:T(8,128)S(1)}, f32[41,128]{1,0:T(8,128)S(1)}, u32[]{:S(2)}, u32[]{:S(2)}) %collective-permute-start.5) | collective-permute-done | bytes 21024 | tf_op jit(solution)/shard_map/ppermute | solution.py:53
  25.6 0.1 concatenate.43
  25.7 0.1 multiply_reduce_fusion
  25.8 0.7 %multiply_bitcast_fusion = f32[576,2,48]{0,2,1:T(8,128)} fusion(f32[48,2,576]{2,0,1:T(8,128)S(1)} %multiply_reduce_fusion), kind=kLoop, calls=%fused_computation.18 | loop fusion | flops 55296 | bytes 442368 | tf_op jit(solution)/shard_map/mul | solution.py:188
  26.5 0.6 %fusion.117 = (f32[128,16]{0,1:T(8,128)}, f32[16,128]{1,0:T(8,128)}) fusion(f32[41,128]{1,0:T(8,128)S(1)} %collective-permute-done.5, f32[41,128]{1,0:T(8,128)S(1)} %collective-permute-done.4, f32[41,128]{1,0:T(8,128)S(1)} %collective-permute-done.3, f32[4,1,16,128]{3,2,0,1:T(8,128)S(1)} %bitcast_add_fusion, s32[]{:T(128)S(6)} %select_n.63, ...), kind=kLoop, calls=%fused_computation.148 | loop fusion | flops 16384 | bytes 81924 | tf_op jit(solution)/shard_map/mul | solution.py:187
  (37 shorter events, 0.3 us)
Async XLA Ops:
  0.6 3.6 %copy-start = (bf16[2,2,5,1,256,128]{5,4,3,2,1,0:T(8,128)(2,1)S(1)}, bf16[2,2,5,1,256,128]{5,4,3,2,1,0:T(8,128)(2,1)}, u32[]{:S(2)}) copy-start(bf16[2,2,5,1,256,128]{5,4,3,2,1,0:T(8,128)(2,1)} %param.3) | copy-start | bytes 3932164
  8.5 7.0 %collective-permute-start = (f32[165,128]{1,0:T(8,128)S(1)}, f32[165,128]{1,0:T(8,128)S(1)}, u32[]{:S(2)}, u32[]{:S(2)}) collective-permute-start(f32[165,128]{1,0:T(8,128)S(1)} %pad_maximum_fusion), channel_id=1, source_target_pairs={{0,1},{1,0},{2,3},{3,2},{4,5},{5,4},{6,7},{7,6},{8,9},{9,8},{10,11... | collective-permute-start | bytes 253448 | tf_op jit(solution)/shard_map/ppermute | solution.py:53
  9.0 5.1 %collective-permute-start.1 = (f32[101,128]{1,0:T(8,128)S(1)}, f32[101,128]{1,0:T(8,128)S(1)}, u32[]{:S(2)}, u32[]{:S(2)}) collective-permute-start(f32[101,128]{1,0:T(8,128)S(1)} %get-tuple-element.29), channel_id=1, source_target_pairs={{0,2},{1,3},{2,0},{3,1},{4,6},{5,7},{6,4},{7,5},{8,10},{9,11},{10,... | collective-permute-start | bytes 155144 | tf_op jit(solution)/shard_map/ppermute | solution.py:53
  11.6 3.8 %collective-permute-start.2 = (f32[101,128]{1,0:T(8,128)S(1)}, f32[101,128]{1,0:T(8,128)S(1)}, u32[]{:S(2)}, u32[]{:S(2)}) collective-permute-start(f32[101,128]{1,0:T(8,128)S(1)} %get-tuple-element.30), channel_id=1, source_target_pairs={{0,3},{1,2},{2,1},{3,0},{4,7},{5,6},{6,5},{7,4},{8,11},{9,10},{10,... | collective-permute-start | bytes 155144 | tf_op jit(solution)/shard_map/ppermute | solution.py:53
  15.7 5.1 %collective-permute-start.3 = (f32[41,128]{1,0:T(8,128)S(1)}, f32[41,128]{1,0:T(8,128)S(1)}, u32[]{:S(2)}, u32[]{:S(2)}) collective-permute-start(f32[41,128]{1,0:T(8,128)S(1)} %pad_maximum_fusion.5), channel_id=1, source_target_pairs={{0,4},{4,0},{8,12},{12,8},{1,5},{5,1},{9,13},{13,9},{2,6},{6,2},{1... | collective-permute-start | bytes 62984 | tf_op jit(solution)/shard_map/ppermute | solution.py:53
  17.3 5.1 %collective-permute-start.4 = (f32[41,128]{1,0:T(8,128)S(1)}, f32[41,128]{1,0:T(8,128)S(1)}, u32[]{:S(2)}, u32[]{:S(2)}) collective-permute-start(f32[41,128]{1,0:T(8,128)S(1)} %pad_maximum_fusion.6), channel_id=1, source_target_pairs={{0,8},{4,12},{8,0},{12,4},{1,9},{5,13},{9,1},{13,5},{2,10},{6,14},... | collective-permute-start | bytes 62984 | tf_op jit(solution)/shard_map/ppermute | solution.py:53
  19.9 5.6 %collective-permute-start.5 = (f32[41,128]{1,0:T(8,128)S(1)}, f32[41,128]{1,0:T(8,128)S(1)}, u32[]{:S(2)}, u32[]{:S(2)}) collective-permute-start(f32[41,128]{1,0:T(8,128)S(1)} %pad_maximum_fusion.7), channel_id=1, source_target_pairs={{0,12},{4,8},{8,4},{12,0},{1,13},{5,9},{9,5},{13,1},{2,14},{6,10},... | collective-permute-start | bytes 62984 | tf_op jit(solution)/shard_map/ppermute | solution.py:53

commit v12 on v8

--- a/solution.py
+++ b/solution.py
@@ -116,13 +116,17 @@
     by_e = jnp.einsum("qxyn,qe->xeyn", first, phq, precision=highest)
     part_core = jnp.einsum("my,xeyn->xemn", phy, by_e, precision=highest)
 
+    scale_x = 3.0**1.5 / math.sqrt(cells_y * total_z * total_q)
+    scale_y = 3.0**1.5 / math.sqrt(total_x * total_z * total_q)
+    scale_z = 3.0**1.5 / math.sqrt(total_x * cells_y * total_q)
+    scale_core = 9.0 / math.sqrt(total_x * cells_y * total_z * total_q)
     rows_each = cells_y // (n_gx * n_gz * n_vert)
     cols_each = K // (n_gx * n_vert)
     core_rows = S * S // n_gx
     n_gzv = n_gz * n_vert
-    sy = part_y.reshape(n_gx, n_gzv, rows_each, K)
-    sz = part_z.T.reshape(n_gx, n_vert, cols_each, cells_z)
-    sx = part_x
+    sy = (part_y * scale_y).reshape(n_gx, n_gzv, rows_each, K)
+    sz = (part_z * scale_z).T.reshape(n_gx, n_vert, cols_each, cells_z)
+    sx = part_x * scale_x
     core = (
         part_core.reshape(cells_x, E, n_gx, core_rows)
         .transpose(2, 0, 1, 3)
@@ -174,18 +178,14 @@
     x_src = (src[:, None] * cells_x + jnp.arange(cells_x, dtype=jnp.int32)[None, :]).reshape(-1)
     phx = test_table(sketch_ids, x_src, total_x, core_stream, 5).astype(f32).reshape(S, n_gx, cells_x)
     held = core.reshape(n_gx * cells_x, E, core_rows)
-    weights_x = phx.reshape(S, n_gx * cells_x)
+    weights_x = phx.reshape(S, n_gx * cells_x) * scale_core
     core_out = jnp.sum(held[:, None, :, :] * weights_x.T[:, :, None, None], axis=0).transpose(2, 1, 0)
 
-    scale_x = 3.0**1.5 / math.sqrt(cells_y * total_z * total_q)
-    scale_y = 3.0**1.5 / math.sqrt(total_x * total_z * total_q)
-    scale_z = 3.0**1.5 / math.sqrt(total_x * cells_y * total_q)
-    scale_core = 9.0 / math.sqrt(total_x * cells_y * total_z * total_q)
     return (
-        sx * scale_x,
-        sy.reshape(rows_each, K) * scale_y,
-        sz.reshape(cols_each, cells_z).T * scale_z,
-        core_out * scale_core,
+        sx,
+        sy.reshape(rows_each, K),
+        sz.reshape(cols_each, cells_z).T,
+        core_out,
     )
 
 

time: 24.8 us -> 24.7 us (level)
    mul x4, other arithmetic: 2.01 us -> 0.27 us  [the longest x1 0.17 us: shards(): sy = (part_y * scale_y).reshape(n_gx, n_gzv, rows_each, K)]
    reduce_sum x1, other arithmetic: 0.14 us -> 0.83 us  [shards(): jnp.sum(held[:, None, :, :] * weights_x.T[:, :, None, None], axis=0)]
    transpose x0 -> x1, other arithmetic: none -> 0.61 us  [shards(): sz.reshape(cols_each, cells_z)]
    add x0 -> x1, other arithmetic: none -> 0.52 us  [shards(): sx_total + got[1]]
where the time goes in v12:
time: 24.7 us; the launch traced here: 24.5 us
  starting transfers between devices  7.63 us (31%)
  waiting for transfers between devices  6.16 us (25%)
  local copies, waits for them, and re-layouts  3.07 us (12%)
  other arithmetic  3.01 us (12%)
  matrix products  2.4 us (10%)
  between operations  2.28 us (9%)
    ppermute x6, starting transfers between devices, send_to(): got = lax.ppermute(flat, axes, [(i, i ^ shift) for i in range(n)])  7.63 us
    ppermute x6, waiting for transfers between devices, send_to(): got = lax.ppermute(flat, axes, [(i, i ^ shift) for i in range(n)])  6.16 us
    slice x1, local copies, waits for them, and re-layouts, shards(): factor_stream = test_streams[0]  1.35 us
    reduce_sum x1, other arithmetic, shards(): jnp.sum(held[:, None, :, :] * weights_x.T[:, :, None, None], axis=0)  0.83 us
    transpose x1, other arithmetic, shards(): sz.reshape(cols_each, cells_z)  0.61 us
    dot_general x1, matrix products, shards(): jnp.dot(rows_z, phz.T, preferred_element_type=f32)  0.6 us
    dot_general x1, matrix products, shards(): by_e = jnp.einsum('qxyn,qe->xeyn', first, phq, precision=highest)  0.53 us
    unnamed x4, local copies, waits for them, and re-layouts  0.52 us
  transfers between devices with their start and end apart: 6, of which 4 were waited for; matrix products, arithmetic and copies ran while one was open for 6% of the time, Pallas kernels for 0%

profile of v12, /device:TPU:0, one launch (start us, length us, event | category | flops | bytes accessed | tf_op | source)
XLA Modules:
  0.0 24.5 jit_solution(5827611737618452239)
XLA Ops:
  0.6 0.0 copy-start
  0.7 1.4 %fusion.191 = (s32[1]{0:T(128)}, s32[1]{0:T(128)}) fusion(s32[2]{0:T(128)} %param.4), kind=kLoop, calls=%fused_computation.274 | loop fusion | bytes 16 | tf_op jit(solution)/shard_map/slice | solution.py:80
  3.4 0.0 copy-done
  3.4 0.6 %convolution_bitcast_fusion = f32[5120,48]{0,1:T(8,128)S(1)} fusion(bf16[5120,128]{1,0:T(8,128)(2,1)S(1)} %bitcast.92, s32[128]{0:T(128)S(1)} %get-tuple-element.33, s32[48]{0:T(128)S(1)} %iota_multiply_fusion.2), kind=kOutput, calls=%fused_computation | convolution fusion | flops 63012864 | bytes 2294464 | tf_op jit(solution)/shard_map/dot_general | solution.py:115
  4.0 0.0 copy-start.1
  4.0 0.2 reshape.698
  4.2 0.5 %copy-done.1 = s32[2,2]{1,0:T(2,128)S(1)} copy-done((s32[2,2]{1,0:T(2,128)S(1)}, s32[2,2]{1,0:T(2,128)}, u32[]{:S(2)}) %copy-start.1) | copy-done | bytes 40
  4.7 0.1 fusion.118
  4.8 0.1 mul.662
  4.9 0.5 %fusion.129 = f32[2,256,48]{1,0,2:T(2,128)S(1)} fusion(f32[20,256,48]{1,0,2:T(8,128)S(1)} %reshape.698, s32[20]{0:T(128)S(1)} %mul.662, s32[2]{0:T(128)S(1)} %add_add_fusion.4), kind=kOutput, calls=%fused_computation.198 | convolution fusion | flops 5898880 | bytes 1081432 | tf_op jit(solution)/shard_map/qxyn,qe->xeyn/dot_general | solution.py:116
  5.4 0.3 %convolution_bitcast_fusion.2 = f32[1,2,48,48]{2,3,1,0:T(8,128)S(1)} fusion(f32[2,256,48]{1,0,2:T(2,128)S(1)} %fusion.129, s32[256]{0:T(256)S(1)} %add_add_fusion.1, s32[48]{0:T(128)S(1)} %iota_multiply_fusion.2), kind=kOutput, calls=%fused_computation.12 | convolution fusion | flops 14352384 | bytes 117952 | tf_op jit(solution)/shard_map/my,xeyn->xemn/dot_general | solution.py:117
  5.7 0.1 copy.14
  5.8 0.1 reshape.699
  5.9 0.1 reshape_reshape.13
  6.0 0.1 mul.606
  6.1 0.1 fusion.60
  6.2 0.1 broadcast_multiply_fusion.1
  6.3 0.3 %multiply_convert_fusion = (bf16[20,128,128]{2,1,0:T(8,128)(2,1)S(1)}, bf16[20,128,128]{2,1,0:T(8,128)(2,1)S(1)}) fusion(f32[128,128]{1,0:T(8,128)S(1)} %fusion.60, f32[20,128]{1,0:T(8,128)S(1)} %get-tuple-element.28), kind=kLoop, calls=%fused_computation.2 | loop fusion | flops 1638400 | bytes 1386496 | tf_op jit(solution)/shard_map/convert_element_type | solution.py:104
  6.6 0.5 %fusion.7 = f32[1,256,256]{2,1,0:T(8,128)S(1)} fusion(bf16[20,256,128]{2,1,0:T(8,128)(2,1)S(1)} %bitcast.93, bf16[20,128,128]{2,1,0:T(8,128)(2,1)S(1)} %get-tuple-element.16, bf16[20,128,128]{2,1,0:T(8,128)(2,1)S(1)} %get-tuple-element.15), kind=kOutput, calls=%fused_computation.11 | convolution fusion | flops 338165760 | bytes 2883584 | tf_op jit(solution)/shard_map/qxyz,qzk->xyk/dot_general | solution.py:106
  7.1 0.2 multiply_multiply_fusion
  7.4 2.4 %collective-permute-start.2 = (f32[101,128]{1,0:T(8,128)S(1)}, f32[101,128]{1,0:T(8,128)S(1)}, u32[]{:S(2)}, u32[]{:S(2)}) collective-permute-start(f32[101,128]{1,0:T(8,128)S(1)} %get-tuple-element.26), channel_id=1, source_target_pairs={{0,3},{1,2},{2,1},{3,0},{4,7},{5,6},{6,5},{7,4},{8,11},{9,10},{10,... | collective-permute-start | bytes 155144 | tf_op jit(solution)/shard_map/ppermute | solution.py:53
  9.8 0.6 %collective-permute-start.1 = (f32[101,128]{1,0:T(8,128)S(1)}, f32[101,128]{1,0:T(8,128)S(1)}, u32[]{:S(2)}, u32[]{:S(2)}) collective-permute-start(f32[101,128]{1,0:T(8,128)S(1)} %get-tuple-element.25), channel_id=1, source_target_pairs={{0,2},{1,3},{2,0},{3,1},{4,6},{5,7},{6,4},{7,5},{8,10},{9,11},{10,... | collective-permute-start | bytes 155144 | tf_op jit(solution)/shard_map/ppermute | solution.py:53
  10.4 0.5 %fusion.6 = f32[128,128]{0,1:T(8,128)S(1)} fusion(bf16[20,256,128]{2,1,0:T(8,128)(2,1)S(1)} %bitcast.94, f32[20,128]{1,0:T(8,128)S(1)} %get-tuple-element.27, s32[128]{0:T(128)S(1)} %get-tuple-element.35, s32[256]{0:T(256)S(1)} %iota_multiply_fusion), kind=kOutput, calls=%fused_computation.10 | convolution fusion | flops 168935424 | bytes 1388032 | tf_op jit(solution)/shard_map/qxyz,yk->qxzk/dot_general | solution.py:112
  11.0 0.1 collective-permute-start
  11.1 0.1 convert_multiply_fusion
  11.2 0.1 reshape.709
  11.3 0.7 %collective-permute-done.2 = f32[101,128]{1,0:T(8,128)S(1)} collective-permute-done((f32[101,128]{1,0:T(8,128)S(1)}, f32[101,128]{1,0:T(8,128)S(1)}, u32[]{:S(2)}, u32[]{:S(2)}) %collective-permute-start.2) | collective-permute-done | bytes 51744 | tf_op jit(solution)/shard_map/ppermute | solution.py:53
  12.0 2.2 %collective-permute-done.1 = f32[101,128]{1,0:T(8,128)S(1)} collective-permute-done((f32[101,128]{1,0:T(8,128)S(1)}, f32[101,128]{1,0:T(8,128)S(1)}, u32[]{:S(2)}, u32[]{:S(2)}) %collective-permute-start.1) | collective-permute-done | bytes 51744 | tf_op jit(solution)/shard_map/ppermute | solution.py:53
  14.3 0.0 collective-permute-done
  14.4 0.1 dynamic-slice_reduce_fusion
  14.5 3.7 %collective-permute-start.5 = (f32[41,128]{1,0:T(8,128)S(1)}, f32[41,128]{1,0:T(8,128)S(1)}, u32[]{:S(2)}, u32[]{:S(2)}) collective-permute-start(f32[41,128]{1,0:T(8,128)S(1)} %pad_maximum_fusion.7), channel_id=1, source_target_pairs={{0,12},{4,8},{8,4},{12,0},{1,13},{5,9},{9,5},{13,1},{2,14},{6,10},... | collective-permute-start | bytes 62984 | tf_op jit(solution)/shard_map/ppermute | solution.py:53
  18.2 0.0 collective-permute-start.4
  18.2 0.8 %collective-permute-start.3 = (f32[41,128]{1,0:T(8,128)S(1)}, f32[41,128]{1,0:T(8,128)S(1)}, u32[]{:S(2)}, u32[]{:S(2)}) collective-permute-start(f32[41,128]{1,0:T(8,128)S(1)} %pad_maximum_fusion.5), channel_id=1, source_target_pairs={{0,4},{4,0},{8,12},{12,8},{1,5},{5,1},{9,13},{13,9},{2,6},{6,2},{1... | collective-permute-start | bytes 62984 | tf_op jit(solution)/shard_map/ppermute | solution.py:53
  19.0 0.5 %slice_add_fusion.7 = f32[1,128]{1,0:T(1,128)} fusion(f32[101,128]{1,0:T(8,128)S(1)} %collective-permute-done.2, f32[101,128]{1,0:T(8,128)S(1)} %collective-permute-done.1, f32[165,128]{1,0:T(8,128)S(1)} %collective-permute-done, f32[128]{0:T(128)S(1)} %get-tuple-element.9), kind=kLoop, calls=%fused_computation.209 | loop fusion | flops 512 | bytes 2560 | tf_op jit(solution)/shard_map/add | solution.py:158
  19.5 0.1 concatenate.40
  19.6 0.6 %collective-permute-done.5 = f32[41,128]{1,0:T(8,128)S(1)} collective-permute-done((f32[41,128]{1,0:T(8,128)S(1)}, f32[41,128]{1,0:T(8,128)S(1)}, u32[]{:S(2)}, u32[]{:S(2)}) %collective-permute-start.5) | collective-permute-done | bytes 21024 | tf_op jit(solution)/shard_map/ppermute | solution.py:53
  20.2 0.1 concatenate.43
  20.3 2.6 %collective-permute-done.4 = f32[41,128]{1,0:T(8,128)S(1)} collective-permute-done((f32[41,128]{1,0:T(8,128)S(1)}, f32[41,128]{1,0:T(8,128)S(1)}, u32[]{:S(2)}, u32[]{:S(2)}) %collective-permute-start.4) | collective-permute-done | bytes 21024 | tf_op jit(solution)/shard_map/ppermute | solution.py:53
  22.9 0.1 concatenate.42
  23.0 0.0 collective-permute-done.3
  23.0 0.1 concatenate.41
  23.1 0.8 %multiply_reduce_fusion = f32[48,2,576]{2,0,1:T(8,128)} fusion(f32[4,48]{1,0:T(4,128)S(1)} %convert_multiply_fusion, f32[4,2,576]{2,1,0:T(2,128)S(1)} %maximum_bitcast_fusion), kind=kLoop, calls=%fused_computation.13 | loop fusion | flops 387072 | bytes 240384 | tf_op jit(solution)/shard_map/reduce_sum | solution.py:182
  23.9 0.6 %fusion.106 = (f32[128,16]{0,1:T(8,128)}, f32[16,128]{1,0:T(8,128)}) fusion(f32[41,128]{1,0:T(8,128)S(1)} %collective-permute-done.5, f32[41,128]{1,0:T(8,128)S(1)} %collective-permute-done.4, f32[41,128]{1,0:T(8,128)S(1)} %collective-permute-done.3, f32[4,1,16,128]{3,2,0,1:T(8,128)S(1)} %bitcast_add_fusion, s32[]{:T(128)S(6)} %select_n.63, ...), kind=kLoop, calls=%fused_computation.142 | loop fusion | flops 12288 | bytes 81924 | tf_op jit(solution)/shard_map/transpose | solution.py:187
  (39 shorter events, 0.3 us)
Async XLA Ops:
  0.6 2.8 %copy-start = (bf16[2,2,5,1,256,128]{5,4,3,2,1,0:T(8,128)(2,1)S(1)}, bf16[2,2,5,1,256,128]{5,4,3,2,1,0:T(8,128)(2,1)}, u32[]{:S(2)}) copy-start(bf16[2,2,5,1,256,128]{5,4,3,2,1,0:T(8,128)(2,1)} %param.3) | copy-start | bytes 3932164
  4.0 0.7 %copy-start.1 = (s32[2,2]{1,0:T(2,128)S(1)}, s32[2,2]{1,0:T(2,128)}, u32[]{:S(2)}) copy-start(s32[2,2]{1,0:T(2,128)} %param.5) | copy-start | bytes 52
  7.4 4.7 %collective-permute-start.2 = (f32[101,128]{1,0:T(8,128)S(1)}, f32[101,128]{1,0:T(8,128)S(1)}, u32[]{:S(2)}, u32[]{:S(2)}) collective-permute-start(f32[101,128]{1,0:T(8,128)S(1)} %get-tuple-element.26), channel_id=1, source_target_pairs={{0,3},{1,2},{2,1},{3,0},{4,7},{5,6},{6,5},{7,4},{8,11},{9,10},{10,... | collective-permute-start | bytes 155144 | tf_op jit(solution)/shard_map/ppermute | solution.py:53
  9.8 4.4 %collective-permute-start.1 = (f32[101,128]{1,0:T(8,128)S(1)}, f32[101,128]{1,0:T(8,128)S(1)}, u32[]{:S(2)}, u32[]{:S(2)}) collective-permute-start(f32[101,128]{1,0:T(8,128)S(1)} %get-tuple-element.25), channel_id=1, source_target_pairs={{0,2},{1,3},{2,0},{3,1},{4,6},{5,7},{6,4},{7,5},{8,10},{9,11},{10,... | collective-permute-start | bytes 155144 | tf_op jit(solution)/shard_map/ppermute | solution.py:53
  11.0 3.2 %collective-permute-start = (f32[165,128]{1,0:T(8,128)S(1)}, f32[165,128]{1,0:T(8,128)S(1)}, u32[]{:S(2)}, u32[]{:S(2)}) collective-permute-start(f32[165,128]{1,0:T(8,128)S(1)} %pad_maximum_fusion), channel_id=1, source_target_pairs={{0,1},{1,0},{2,3},{3,2},{4,5},{5,4},{6,7},{7,6},{8,9},{9,8},{10,11... | collective-permute-start | bytes 253448 | tf_op jit(solution)/shard_map/ppermute | solution.py:53
  14.5 5.7 %collective-permute-start.5 = (f32[41,128]{1,0:T(8,128)S(1)}, f32[41,128]{1,0:T(8,128)S(1)}, u32[]{:S(2)}, u32[]{:S(2)}) collective-permute-start(f32[41,128]{1,0:T(8,128)S(1)} %pad_maximum_fusion.7), channel_id=1, source_target_pairs={{0,12},{4,8},{8,4},{12,0},{1,13},{5,9},{9,5},{13,1},{2,14},{6,10},... | collective-permute-start | bytes 62984 | tf_op jit(solution)/shard_map/ppermute | solution.py:53
  18.2 4.7 %collective-permute-start.4 = (f32[41,128]{1,0:T(8,128)S(1)}, f32[41,128]{1,0:T(8,128)S(1)}, u32[]{:S(2)}, u32[]{:S(2)}) collective-permute-start(f32[41,128]{1,0:T(8,128)S(1)} %pad_maximum_fusion.6), channel_id=1, source_target_pairs={{0,8},{4,12},{8,0},{12,4},{1,9},{5,13},{9,1},{13,5},{2,10},{6,14},... | collective-permute-start | bytes 62984 | tf_op jit(solution)/shard_map/ppermute | solution.py:53
  18.2 4.8 %collective-permute-start.3 = (f32[41,128]{1,0:T(8,128)S(1)}, f32[41,128]{1,0:T(8,128)S(1)}, u32[]{:S(2)}, u32[]{:S(2)}) collective-permute-start(f32[41,128]{1,0:T(8,128)S(1)} %pad_maximum_fusion.5), channel_id=1, source_target_pairs={{0,4},{4,0},{8,12},{12,8},{1,5},{5,1},{9,13},{13,9},{2,6},{6,2},{1... | collective-permute-start | bytes 62984 | tf_op jit(solution)/shard_map/ppermute | solution.py:53

commit v13 on v8

--- a/solution.py
+++ b/solution.py
@@ -113,8 +113,9 @@
     weights = aq[:, None, :] * ax[None, :, :]
     part_z = jnp.sum(along_y * weights[:, :, None, :], axis=(0, 1))
     first = jnp.dot(rows_z, phz.T, preferred_element_type=f32).reshape(n_q, cells_x, cells_y, S)
-    by_e = jnp.einsum("qxyn,qe->xeyn", first, phq, precision=highest)
-    part_core = jnp.einsum("my,xeyn->xemn", phy, by_e, precision=highest)
+    high = lax.Precision.HIGH
+    by_e = jnp.einsum("qxyn,qe->xeyn", first, phq, precision=high)
+    part_core = jnp.einsum("my,xeyn->xemn", phy, by_e, precision=high)
 
     rows_each = cells_y // (n_gx * n_gz * n_vert)
     cols_each = K // (n_gx * n_vert)

time: 24.8 us -> 24.6 us (level)
  no operation moved by 1% of the time
where the time goes in v13:
time: 24.6 us; the launch traced here: 24.4 us
  starting transfers between devices  7.63 us (31%)
  waiting for transfers between devices  6.17 us (25%)
  local copies, waits for them, and re-layouts  3.07 us (12%)
  other arithmetic  3.01 us (12%)
  between operations  2.28 us (9%)
  matrix products  2.23 us (9%)
    ppermute x6, starting transfers between devices, send_to(): got = lax.ppermute(flat, axes, [(i, i ^ shift) for i in range(n)])  7.63 us
    ppermute x6, waiting for transfers between devices, send_to(): got = lax.ppermute(flat, axes, [(i, i ^ shift) for i in range(n)])  6.17 us
    slice x1, local copies, waits for them, and re-layouts, shards(): factor_stream = test_streams[0]  1.35 us
    mul x1, other arithmetic, shards(): core_out * scale_core  0.72 us
    mul x1, other arithmetic, shards(): sz.reshape(cols_each, cells_z).T * scale_z  0.61 us
    dot_general x1, matrix products, shards(): jnp.dot(rows_z, phz.T, preferred_element_type=f32)  0.6 us
    unnamed x4, local copies, waits for them, and re-layouts  0.52 us
    mul x1, other arithmetic, shards(): sx * scale_x  0.52 us
  transfers between devices with their start and end apart: 6, of which 4 were waited for; matrix products, arithmetic and copies ran while one was open for 6% of the time, Pallas kernels for 0%

profile of v13, /device:TPU:0, one launch (start us, length us, event | category | flops | bytes accessed | tf_op | source)
XLA Modules:
  0.0 24.4 jit_solution(5863851614792812882)
XLA Ops:
  0.6 0.0 copy-start
  0.7 1.4 %fusion.195 = (s32[1]{0:T(128)}, s32[1]{0:T(128)}) fusion(s32[2]{0:T(128)} %param.4), kind=kLoop, calls=%fused_computation.276 | loop fusion | bytes 16 | tf_op jit(solution)/shard_map/slice | solution.py:80
  3.4 0.0 copy-done
  3.4 0.6 %convolution_bitcast_fusion = f32[5120,48]{0,1:T(8,128)S(1)} fusion(bf16[5120,128]{1,0:T(8,128)(2,1)S(1)} %bitcast.91, s32[128]{0:T(128)S(1)} %get-tuple-element.33, s32[48]{0:T(128)S(1)} %iota_multiply_fusion.2), kind=kOutput, calls=%fused_computation | convolution fusion | flops 63012864 | bytes 2294464 | tf_op jit(solution)/shard_map/dot_general | solution.py:115
  4.0 0.0 copy-start.1
  4.0 0.2 reshape.676
  4.2 0.5 %copy-done.1 = s32[2,2]{1,0:T(2,128)S(1)} copy-done((s32[2,2]{1,0:T(2,128)S(1)}, s32[2,2]{1,0:T(2,128)}, u32[]{:S(2)}) %copy-start.1) | copy-done | bytes 40
  4.7 0.1 fusion.120
  4.8 0.1 mul.630
  4.9 0.4 %fusion.132 = f32[2,256,48]{1,0,2:T(2,128)S(1)} fusion(f32[20,256,48]{1,0,2:T(8,128)S(1)} %reshape.676, s32[20]{0:T(128)S(1)} %mul.630, s32[2]{0:T(128)S(1)} %add_add_fusion.4), kind=kOutput, calls=%fused_computation.200 | convolution fusion | flops 2949760 | bytes 1081432 | tf_op jit(solution)/shard_map/qxyn,qe->xeyn/dot_general | solution.py:117
  5.3 0.2 %convolution_bitcast_fusion.2 = f32[1,2,48,48]{2,3,1,0:T(8,128)S(1)} fusion(f32[2,256,48]{1,0,2:T(2,128)S(1)} %fusion.132, s32[256]{0:T(256)S(1)} %add_add_fusion.1, s32[48]{0:T(128)S(1)} %iota_multiply_fusion.2), kind=kOutput, calls=%fused_computation.12 | convolution fusion | flops 7274496 | bytes 117952 | tf_op jit(solution)/shard_map/my,xeyn->xemn/dot_general | solution.py:118
  5.5 0.1 copy.14
  5.6 0.1 reshape.677
  5.7 0.1 reshape_reshape.16
  5.8 0.1 mul.580
  5.9 0.1 fusion.60
  6.0 0.1 broadcast_multiply_fusion.1
  6.1 0.3 %multiply_convert_fusion = (bf16[20,128,128]{2,1,0:T(8,128)(2,1)S(1)}, bf16[20,128,128]{2,1,0:T(8,128)(2,1)S(1)}) fusion(f32[128,128]{1,0:T(8,128)S(1)} %fusion.60, f32[20,128]{1,0:T(8,128)S(1)} %get-tuple-element.28), kind=kLoop, calls=%fused_computation.2 | loop fusion | flops 1638400 | bytes 1386496 | tf_op jit(solution)/shard_map/convert_element_type | solution.py:104
  6.5 0.5 %fusion.7 = f32[1,256,256]{2,1,0:T(8,128)S(1)} fusion(bf16[20,256,128]{2,1,0:T(8,128)(2,1)S(1)} %bitcast.92, bf16[20,128,128]{2,1,0:T(8,128)(2,1)S(1)} %get-tuple-element.16, bf16[20,128,128]{2,1,0:T(8,128)(2,1)S(1)} %get-tuple-element.15), kind=kOutput, calls=%fused_computation.11 | convolution fusion | flops 338165760 | bytes 2883584 | tf_op jit(solution)/shard_map/qxyz,qzk->xyk/dot_general | solution.py:106
  7.0 0.2 broadcast_multiply_fusion
  7.2 2.4 %collective-permute-start.2 = (f32[101,128]{1,0:T(8,128)S(1)}, f32[101,128]{1,0:T(8,128)S(1)}, u32[]{:S(2)}, u32[]{:S(2)}) collective-permute-start(f32[101,128]{1,0:T(8,128)S(1)} %get-tuple-element.26), channel_id=1, source_target_pairs={{0,3},{1,2},{2,1},{3,0},{4,7},{5,6},{6,5},{7,4},{8,11},{9,10},{10,... | collective-permute-start | bytes 155144 | tf_op jit(solution)/shard_map/ppermute | solution.py:53
  9.6 0.6 %collective-permute-start.1 = (f32[101,128]{1,0:T(8,128)S(1)}, f32[101,128]{1,0:T(8,128)S(1)}, u32[]{:S(2)}, u32[]{:S(2)}) collective-permute-start(f32[101,128]{1,0:T(8,128)S(1)} %get-tuple-element.25), channel_id=1, source_target_pairs={{0,2},{1,3},{2,0},{3,1},{4,6},{5,7},{6,4},{7,5},{8,10},{9,11},{10,... | collective-permute-start | bytes 155144 | tf_op jit(solution)/shard_map/ppermute | solution.py:53
  10.3 0.5 %fusion.6 = f32[128,128]{0,1:T(8,128)S(1)} fusion(bf16[20,256,128]{2,1,0:T(8,128)(2,1)S(1)} %bitcast.93, f32[20,128]{1,0:T(8,128)S(1)} %get-tuple-element.27, s32[128]{0:T(128)S(1)} %get-tuple-element.35, s32[256]{0:T(256)S(1)} %iota_multiply_fusion), kind=kOutput, calls=%fused_computation.10 | convolution fusion | flops 168935424 | bytes 1388032 | tf_op jit(solution)/shard_map/qxyz,yk->qxzk/dot_general | solution.py:112
  10.8 0.1 collective-permute-start
  10.9 0.1 fusion.121
  11.0 0.1 reshape.687
  11.1 0.7 %collective-permute-done.2 = f32[101,128]{1,0:T(8,128)S(1)} collective-permute-done((f32[101,128]{1,0:T(8,128)S(1)}, f32[101,128]{1,0:T(8,128)S(1)}, u32[]{:S(2)}, u32[]{:S(2)}) %collective-permute-start.2) | collective-permute-done | bytes 51744 | tf_op jit(solution)/shard_map/ppermute | solution.py:53
  11.9 2.2 %collective-permute-done.1 = f32[101,128]{1,0:T(8,128)S(1)} collective-permute-done((f32[101,128]{1,0:T(8,128)S(1)}, f32[101,128]{1,0:T(8,128)S(1)}, u32[]{:S(2)}, u32[]{:S(2)}) %collective-permute-start.1) | collective-permute-done | bytes 51744 | tf_op jit(solution)/shard_map/ppermute | solution.py:53
  14.1 0.0 collective-permute-done
  14.2 0.1 dynamic-slice_reduce_fusion
  14.3 3.7 %collective-permute-start.5 = (f32[41,128]{1,0:T(8,128)S(1)}, f32[41,128]{1,0:T(8,128)S(1)}, u32[]{:S(2)}, u32[]{:S(2)}) collective-permute-start(f32[41,128]{1,0:T(8,128)S(1)} %pad_maximum_fusion.7), channel_id=1, source_target_pairs={{0,12},{4,8},{8,4},{12,0},{1,13},{5,9},{9,5},{13,1},{2,14},{6,10},... | collective-permute-start | bytes 62984 | tf_op jit(solution)/shard_map/ppermute | solution.py:53
  18.0 0.0 collective-permute-start.4
  18.0 0.8 %collective-permute-start.3 = (f32[41,128]{1,0:T(8,128)S(1)}, f32[41,128]{1,0:T(8,128)S(1)}, u32[]{:S(2)}, u32[]{:S(2)}) collective-permute-start(f32[41,128]{1,0:T(8,128)S(1)} %pad_maximum_fusion.5), channel_id=1, source_target_pairs={{0,4},{4,0},{8,12},{12,8},{1,5},{5,1},{9,13},{13,9},{2,6},{6,2},{1... | collective-permute-start | bytes 62984 | tf_op jit(solution)/shard_map/ppermute | solution.py:53
  18.8 0.5 %fusion.144 = f32[1,128]{1,0:T(1,128)} fusion(f32[101,128]{1,0:T(8,128)S(1)} %collective-permute-done.2, f32[101,128]{1,0:T(8,128)S(1)} %collective-permute-done.1, f32[165,128]{1,0:T(8,128)S(1)} %collective-permute-done, f32[128]{0:T(128)S(1)} %get-tuple-element.9), kind=kLoop, calls=%fused_computation.212 | loop fusion | flops 512 | bytes 2560 | tf_op jit(solution)/shard_map/mul | solution.py:186
  19.3 0.1 concatenate.40
  19.4 0.6 %collective-permute-done.5 = f32[41,128]{1,0:T(8,128)S(1)} collective-permute-done((f32[41,128]{1,0:T(8,128)S(1)}, f32[41,128]{1,0:T(8,128)S(1)}, u32[]{:S(2)}, u32[]{:S(2)}) %collective-permute-start.5) | collective-permute-done | bytes 21024 | tf_op jit(solution)/shard_map/ppermute | solution.py:53
  20.0 0.1 concatenate.43
  20.1 2.6 %collective-permute-done.4 = f32[41,128]{1,0:T(8,128)S(1)} collective-permute-done((f32[41,128]{1,0:T(8,128)S(1)}, f32[41,128]{1,0:T(8,128)S(1)}, u32[]{:S(2)}, u32[]{:S(2)}) %collective-permute-start.4) | collective-permute-done | bytes 21024 | tf_op jit(solution)/shard_map/ppermute | solution.py:53
  22.7 0.1 concatenate.42
  22.8 0.0 collective-permute-done.3
  22.8 0.1 concatenate.41
  22.9 0.1 multiply_reduce_fusion
  23.1 0.7 %multiply_bitcast_fusion = f32[576,2,48]{0,2,1:T(8,128)} fusion(f32[48,2,576]{2,0,1:T(8,128)S(1)} %multiply_reduce_fusion), kind=kLoop, calls=%fused_computation.14 | loop fusion | flops 55296 | bytes 442368 | tf_op jit(solution)/shard_map/mul | solution.py:189
  23.8 0.6 %fusion.107 = (f32[128,16]{0,1:T(8,128)}, f32[16,128]{1,0:T(8,128)}) fusion(f32[41,128]{1,0:T(8,128)S(1)} %collective-permute-done.5, f32[41,128]{1,0:T(8,128)S(1)} %collective-permute-done.4, f32[41,128]{1,0:T(8,128)S(1)} %collective-permute-done.3, f32[4,1,16,128]{3,2,0,1:T(8,128)S(1)} %bitcast_add_fusion, s32[]{:T(128)S(6)} %select_n.63, ...), kind=kLoop, calls=%fused_computation.143 | loop fusion | flops 16384 | bytes 81924 | tf_op jit(solution)/shard_map/mul | solution.py:188
  (37 shorter events, 0.3 us)
Async XLA Ops:
  0.6 2.8 %copy-start = (bf16[2,2,5,1,256,128]{5,4,3,2,1,0:T(8,128)(2,1)S(1)}, bf16[2,2,5,1,256,128]{5,4,3,2,1,0:T(8,128)(2,1)}, u32[]{:S(2)}) copy-start(bf16[2,2,5,1,256,128]{5,4,3,2,1,0:T(8,128)(2,1)} %param.3) | copy-start | bytes 3932164
  4.0 0.7 %copy-start.1 = (s32[2,2]{1,0:T(2,128)S(1)}, s32[2,2]{1,0:T(2,128)}, u32[]{:S(2)}) copy-start(s32[2,2]{1,0:T(2,128)} %param.5) | copy-start | bytes 52
  7.2 4.7 %collective-permute-start.2 = (f32[101,128]{1,0:T(8,128)S(1)}, f32[101,128]{1,0:T(8,128)S(1)}, u32[]{:S(2)}, u32[]{:S(2)}) collective-permute-start(f32[101,128]{1,0:T(8,128)S(1)} %get-tuple-element.26), channel_id=1, source_target_pairs={{0,3},{1,2},{2,1},{3,0},{4,7},{5,6},{6,5},{7,4},{8,11},{9,10},{10,... | collective-permute-start | bytes 155144 | tf_op jit(solution)/shard_map/ppermute | solution.py:53
  9.6 4.4 %collective-permute-start.1 = (f32[101,128]{1,0:T(8,128)S(1)}, f32[101,128]{1,0:T(8,128)S(1)}, u32[]{:S(2)}, u32[]{:S(2)}) collective-permute-start(f32[101,128]{1,0:T(8,128)S(1)} %get-tuple-element.25), channel_id=1, source_target_pairs={{0,2},{1,3},{2,0},{3,1},{4,6},{5,7},{6,4},{7,5},{8,10},{9,11},{10,... | collective-permute-start | bytes 155144 | tf_op jit(solution)/shard_map/ppermute | solution.py:53
  10.8 3.3 %collective-permute-start = (f32[165,128]{1,0:T(8,128)S(1)}, f32[165,128]{1,0:T(8,128)S(1)}, u32[]{:S(2)}, u32[]{:S(2)}) collective-permute-start(f32[165,128]{1,0:T(8,128)S(1)} %pad_maximum_fusion), channel_id=1, source_target_pairs={{0,1},{1,0},{2,3},{3,2},{4,5},{5,4},{6,7},{7,6},{8,9},{9,8},{10,11... | collective-permute-start | bytes 253448 | tf_op jit(solution)/shard_map/ppermute | solution.py:53
  14.3 5.7 %collective-permute-start.5 = (f32[41,128]{1,0:T(8,128)S(1)}, f32[41,128]{1,0:T(8,128)S(1)}, u32[]{:S(2)}, u32[]{:S(2)}) collective-permute-start(f32[41,128]{1,0:T(8,128)S(1)} %pad_maximum_fusion.7), channel_id=1, source_target_pairs={{0,12},{4,8},{8,4},{12,0},{1,13},{5,9},{9,5},{13,1},{2,14},{6,10},... | collective-permute-start | bytes 62984 | tf_op jit(solution)/shard_map/ppermute | solution.py:53
  18.0 4.7 %collective-permute-start.4 = (f32[41,128]{1,0:T(8,128)S(1)}, f32[41,128]{1,0:T(8,128)S(1)}, u32[]{:S(2)}, u32[]{:S(2)}) collective-permute-start(f32[41,128]{1,0:T(8,128)S(1)} %pad_maximum_fusion.6), channel_id=1, source_target_pairs={{0,8},{4,12},{8,0},{12,4},{1,9},{5,13},{9,1},{13,5},{2,10},{6,14},... | collective-permute-start | bytes 62984 | tf_op jit(solution)/shard_map/ppermute | solution.py:53
  18.0 4.8 %collective-permute-start.3 = (f32[41,128]{1,0:T(8,128)S(1)}, f32[41,128]{1,0:T(8,128)S(1)}, u32[]{:S(2)}, u32[]{:S(2)}) collective-permute-start(f32[41,128]{1,0:T(8,128)S(1)} %pad_maximum_fusion.5), channel_id=1, source_target_pairs={{0,4},{4,0},{8,12},{12,8},{1,5},{5,1},{9,13},{13,9},{2,6},{6,2},{1... | collective-permute-start | bytes 62984 | tf_op jit(solution)/shard_map/ppermute | solution.py:53

commit v14 on v13

--- a/solution.py
+++ b/solution.py
@@ -18,11 +18,26 @@
     return jnp.bitwise_xor(mixed, lax.shift_right_logical(mixed, jnp.int32(16)))
 
 
-def test_table(row_ids, col_ids, stride, stream, salt):
-    row_term = (row_ids * stride) * -1640531535
-    col_term = col_ids * -1640531535 + stream * -2048144777 + salt
+def unit_from_terms(row_term, col_term):
     upper = lax.shift_right_logical(mix_bits(row_term[:, None] + col_term[None, :]), jnp.int32(9))
     return ((2 * upper + 1).astype(jnp.float32) * 2.0 ** (-24) - 1.0).astype(jnp.bfloat16)
+
+
+def row_terms(row_ids, stride):
+    return (row_ids * stride) * -1640531535
+
+
+def column_terms(test_streams, columns):
+    ids = jnp.concatenate([c for c, _, _ in columns])
+    which = jnp.concatenate([jnp.full(c.shape, w, jnp.int32) for c, w, _ in columns])
+    salts = jnp.concatenate([jnp.full(c.shape, s, jnp.int32) for c, _, s in columns])
+    streams = jnp.where(which == 1, test_streams[1], test_streams[0])
+    terms = ids * -1640531535 + streams * -2048144777 + salts
+    out, at = [], 0
+    for c, _, _ in columns:
+        out.append(terms[at : at + c.shape[0]])
+        at += c.shape[0]
+    return out
 
 
 def digit_steps(n):
@@ -77,8 +92,6 @@
     total_x = cells_x * n_gx
     total_z = cells_z * n_gz
     total_q = variables * batches * local_snaps * n_vert
-    factor_stream = test_streams[0]
-    core_stream = test_streams[1]
     gx_me = lax.axis_index("gx")
     rank_ids = jnp.arange(K, dtype=jnp.int32)
     sketch_ids = jnp.arange(S, dtype=jnp.int32)
@@ -88,13 +101,22 @@
     q_ids = (
         snapshot_ids[:, :, None] * variables + jnp.arange(variables, dtype=jnp.int32)[None, None, :]
     ).reshape(-1)
-    ax = test_table(x_ids, rank_ids, K, factor_stream, 1).astype(f32)
-    ay = test_table(y_ids, rank_ids, K, factor_stream, 2)
-    az = test_table(z_ids, rank_ids, K, factor_stream, 3)
-    aq = test_table(q_ids, rank_ids, K, factor_stream, 4).astype(f32)
-    phy = test_table(sketch_ids, y_ids, cells_y, core_stream, 6).astype(f32)
-    phz = test_table(sketch_ids, z_ids, total_z, core_stream, 7)
-    phq = test_table(q_ids, jnp.arange(E, dtype=jnp.int32), E, core_stream, 8).astype(f32)
+    src_gx = jnp.bitwise_xor(gx_me, jnp.arange(n_gx, dtype=jnp.int32))
+    x_src = (src_gx[:, None] * cells_x + jnp.arange(cells_x, dtype=jnp.int32)[None, :]).reshape(-1)
+    e_ids = jnp.arange(E, dtype=jnp.int32)
+    c_ax, c_ay, c_az, c_aq, c_phy, c_phz, c_phq, c_phx = column_terms(
+        test_streams,
+        [(rank_ids, 0, 1), (rank_ids, 0, 2), (rank_ids, 0, 3), (rank_ids, 0, 4),
+         (y_ids, 1, 6), (z_ids, 1, 7), (e_ids, 1, 8), (x_src, 1, 5)],
+    )
+    ax = unit_from_terms(row_terms(x_ids, K), c_ax).astype(f32)
+    ay = unit_from_terms(row_terms(y_ids, K), c_ay)
+    az = unit_from_terms(row_terms(z_ids, K), c_az)
+    aq = unit_from_terms(row_terms(q_ids, K), c_aq).astype(f32)
+    phy = unit_from_terms(row_terms(sketch_ids, cells_y), c_phy).astype(f32)
+    phz = unit_from_terms(row_terms(sketch_ids, total_z), c_phz)
+    phq = unit_from_terms(row_terms(q_ids, E), c_phq).astype(f32)
+    phx = unit_from_terms(row_terms(sketch_ids, total_x), c_phx).astype(f32).reshape(S, n_gx, cells_x)
 
     n_q = batches * local_snaps * variables
     field = flow_field.reshape(n_q, cells_x, cells_y, cells_z)
@@ -171,9 +193,6 @@
         sy, sz = sy_total, sz_total
         core = jnp.concatenate(core_parts, axis=0)
 
-    src = jnp.bitwise_xor(gx_me, jnp.arange(n_gx, dtype=jnp.int32))
-    x_src = (src[:, None] * cells_x + jnp.arange(cells_x, dtype=jnp.int32)[None, :]).reshape(-1)
-    phx = test_table(sketch_ids, x_src, total_x, core_stream, 5).astype(f32).reshape(S, n_gx, cells_x)
     held = core.reshape(n_gx * cells_x, E, core_rows)
     weights_x = phx.reshape(S, n_gx * cells_x)
     core_out = jnp.sum(held[:, None, :, :] * weights_x.T[:, :, None, None], axis=0).transpose(2, 1, 0)

time: 24.6 us -> 25.4 us (1.033)
  other arithmetic: 3.01 us -> 4.98 us
  between operations: 2.28 us -> 0.99 us
    add x6 -> x2, other arithmetic: 0.04 us -> 2 us  [the longest x1 1.99 us: column_terms(): terms = ids * -1640531535 + streams * -2048144777 + salts]
    slice x1 -> x5, local copies, waits for them, and re-layouts: 1.35 us -> 1.44 us  [the longest x1 1.35 us: column_terms(): streams = jnp.where(which == 1, test_streams[1], test_streams[0])]
where the time goes in v14:
time: 25.4 us; the launch traced here: 25.2 us
  starting transfers between devices  7.63 us (30%)
  waiting for transfers between devices  6.1 us (24%)
  other arithmetic  4.98 us (20%)
  local copies, waits for them, and re-layouts  3.23 us (13%)
  matrix products  2.24 us (9%)
  between operations  0.99 us (4%)
    ppermute x6, starting transfers between devices, send_to(): got = lax.ppermute(flat, axes, [(i, i ^ shift) for i in range(n)])  7.63 us
    ppermute x6, waiting for transfers between devices, send_to(): got = lax.ppermute(flat, axes, [(i, i ^ shift) for i in range(n)])  6.1 us
    add x1, other arithmetic, column_terms(): terms = ids * -1640531535 + streams * -2048144777 + salts  1.99 us
    slice x1, local copies, waits for them, and re-layouts, column_terms(): streams = jnp.where(which == 1, test_streams[1], test_streams[0])  1.35 us
    mul x1, other arithmetic, shards(): core_out * scale_core  0.72 us
    mul x1, other arithmetic, shards(): sz.reshape(cols_each, cells_z).T * scale_z  0.61 us
    dot_general x1, matrix products, shards(): jnp.dot(rows_z, phz.T, preferred_element_type=f32)  0.6 us
    unnamed x4, local copies, waits for them, and re-layouts  0.52 us
  transfers between devices with their start and end apart: 6, of which 4 were waited for; matrix products, arithmetic and copies ran while one was open for 6% of the time, Pallas kernels for 0%

profile of v14, /device:TPU:0, one launch (start us, length us, event | category | flops | bytes accessed | tf_op | source)
XLA Modules:
  0.0 25.2 jit_solution(8088413691204956388)
XLA Ops:
  0.6 0.0 copy-start
  0.7 1.3 %fusion.195 = (s32[1]{0:T(128)}, s32[1]{0:T(128)}) fusion(s32[2]{0:T(128)} %param.4), kind=kLoop, calls=%fused_computation.271 | loop fusion | bytes 16 | tf_op jit(solution)/shard_map/slice | solution.py:34
  2.1 0.1 concatenate.36
  2.1 2.0 %add_add_fusion.1 = s32[902]{0:T(1024)S(1)} fusion(s32[902]{0:T(1024)} %constant.92.clone.1, pred[902]{0:T(1024)(128)(4,1)} %constant.90.clone.1, s32[902]{0:T(1024)S(1)} %concatenate.36, s32[]{:T(128)} %bitcast.1, s32[]{:T(128)} %bitcast), kind=kLoop, calls=%fused_computation.166 | loop fusion | flops 4510 | bytes 11734 | tf_op jit(solution)/shard_map/add | solution.py:35
  4.2 0.0 copy-done
  4.2 0.6 %convolution_bitcast_fusion = f32[5120,48]{0,1:T(8,128)S(1)} fusion(bf16[5120,128]{1,0:T(8,128)(2,1)S(1)} %bitcast.91, s32[128]{0:T(128)S(1)} %get-tuple-element.28, s32[48]{0:T(128)S(1)} %iota_multiply_fusion.2), kind=kOutput, calls=%fused_computation | convolution fusion | flops 63012864 | bytes 2294464 | tf_op jit(solution)/shard_map/dot_general | solution.py:137
  4.8 0.0 copy-start.1
  4.8 0.2 reshape.615
  5.0 0.5 %copy-done.1 = s32[2,2]{1,0:T(2,128)S(1)} copy-done((s32[2,2]{1,0:T(2,128)S(1)}, s32[2,2]{1,0:T(2,128)}, u32[]{:S(2)}) %copy-start.1) | copy-done | bytes 40
  5.5 0.1 fusion.120
  5.6 0.1 mul.561
  5.7 0.4 %fusion.132 = f32[2,256,48]{1,0,2:T(2,128)S(1)} fusion(f32[20,256,48]{1,0,2:T(8,128)S(1)} %reshape.615, s32[20]{0:T(128)S(1)} %mul.561, s32[2]{0:T(128)S(1)} %slice.101), kind=kOutput, calls=%fused_computation.200 | convolution fusion | flops 2949760 | bytes 1081432 | tf_op jit(solution)/shard_map/qxyn,qe->xeyn/dot_general | solution.py:139
  6.0 0.2 convolution_bitcast_fusion.2
  6.3 0.1 copy.14
  6.4 0.1 reshape.616
  6.5 0.1 reshape_reshape.16
  6.6 0.1 mul.509
  6.7 0.1 fusion.60
  6.8 0.1 broadcast_multiply_fusion.1
  6.9 0.3 %multiply_convert_fusion = (bf16[20,128,128]{2,1,0:T(8,128)(2,1)S(1)}, bf16[20,128,128]{2,1,0:T(8,128)(2,1)S(1)}) fusion(f32[128,128]{1,0:T(8,128)S(1)} %fusion.60, f32[20,128]{1,0:T(8,128)S(1)} %get-tuple-element.32), kind=kLoop, calls=%fused_computation.2 | loop fusion | flops 1638400 | bytes 1386496 | tf_op jit(solution)/shard_map/convert_element_type | solution.py:126
  7.2 0.5 %fusion.7 = f32[1,256,256]{2,1,0:T(8,128)S(1)} fusion(bf16[20,256,128]{2,1,0:T(8,128)(2,1)S(1)} %bitcast.92, bf16[20,128,128]{2,1,0:T(8,128)(2,1)S(1)} %get-tuple-element.16, bf16[20,128,128]{2,1,0:T(8,128)(2,1)S(1)} %get-tuple-element.15), kind=kOutput, calls=%fused_computation.11 | convolution fusion | flops 338165760 | bytes 2883584 | tf_op jit(solution)/shard_map/qxyz,qzk->xyk/dot_general | solution.py:128
  7.8 0.2 broadcast_multiply_fusion
  8.0 2.4 %collective-permute-start.2 = (f32[101,128]{1,0:T(8,128)S(1)}, f32[101,128]{1,0:T(8,128)S(1)}, u32[]{:S(2)}, u32[]{:S(2)}) collective-permute-start(f32[101,128]{1,0:T(8,128)S(1)} %get-tuple-element.26), channel_id=1, source_target_pairs={{0,3},{1,2},{2,1},{3,0},{4,7},{5,6},{6,5},{7,4},{8,11},{9,10},{10,... | collective-permute-start | bytes 155144 | tf_op jit(solution)/shard_map/ppermute | solution.py:68
  10.4 0.6 %collective-permute-start.1 = (f32[101,128]{1,0:T(8,128)S(1)}, f32[101,128]{1,0:T(8,128)S(1)}, u32[]{:S(2)}, u32[]{:S(2)}) collective-permute-start(f32[101,128]{1,0:T(8,128)S(1)} %get-tuple-element.25), channel_id=1, source_target_pairs={{0,2},{1,3},{2,0},{3,1},{4,6},{5,7},{6,4},{7,5},{8,10},{9,11},{10,... | collective-permute-start | bytes 155144 | tf_op jit(solution)/shard_map/ppermute | solution.py:68
  11.0 0.5 %fusion.6 = f32[128,128]{0,1:T(8,128)S(1)} fusion(bf16[20,256,128]{2,1,0:T(8,128)(2,1)S(1)} %bitcast.93, f32[20,128]{1,0:T(8,128)S(1)} %get-tuple-element.31, s32[128]{0:T(128)S(1)} %get-tuple-element.29, s32[256]{0:T(256)S(1)} %iota_multiply_fusion), kind=kOutput, calls=%fused_computation.10 | convolution fusion | flops 168935424 | bytes 1388032 | tf_op jit(solution)/shard_map/qxyz,yk->qxzk/dot_general | solution.py:134
  11.6 0.1 collective-permute-start
  11.7 0.1 slice.123
  11.8 0.1 fusion.121
  11.9 0.1 reshape.626
  11.9 0.7 %collective-permute-done.2 = f32[101,128]{1,0:T(8,128)S(1)} collective-permute-done((f32[101,128]{1,0:T(8,128)S(1)}, f32[101,128]{1,0:T(8,128)S(1)}, u32[]{:S(2)}, u32[]{:S(2)}) %collective-permute-start.2) | collective-permute-done | bytes 51744 | tf_op jit(solution)/shard_map/ppermute | solution.py:68
  12.6 2.2 %collective-permute-done.1 = f32[101,128]{1,0:T(8,128)S(1)} collective-permute-done((f32[101,128]{1,0:T(8,128)S(1)}, f32[101,128]{1,0:T(8,128)S(1)}, u32[]{:S(2)}, u32[]{:S(2)}) %collective-permute-start.1) | collective-permute-done | bytes 51744 | tf_op jit(solution)/shard_map/ppermute | solution.py:68
  14.9 0.0 collective-permute-done
  15.0 0.1 dynamic-slice_reduce_fusion
  15.1 3.7 %collective-permute-start.5 = (f32[41,128]{1,0:T(8,128)S(1)}, f32[41,128]{1,0:T(8,128)S(1)}, u32[]{:S(2)}, u32[]{:S(2)}) collective-permute-start(f32[41,128]{1,0:T(8,128)S(1)} %pad_maximum_fusion.7), channel_id=1, source_target_pairs={{0,12},{4,8},{8,4},{12,0},{1,13},{5,9},{9,5},{13,1},{2,14},{6,10},... | collective-permute-start | bytes 62984 | tf_op jit(solution)/shard_map/ppermute | solution.py:68
  18.8 0.0 collective-permute-start.4
  18.8 0.8 %collective-permute-start.3 = (f32[41,128]{1,0:T(8,128)S(1)}, f32[41,128]{1,0:T(8,128)S(1)}, u32[]{:S(2)}, u32[]{:S(2)}) collective-permute-start(f32[41,128]{1,0:T(8,128)S(1)} %pad_maximum_fusion.5), channel_id=1, source_target_pairs={{0,4},{4,0},{8,12},{12,8},{1,5},{5,1},{9,13},{13,9},{2,6},{6,2},{1... | collective-permute-start | bytes 62984 | tf_op jit(solution)/shard_map/ppermute | solution.py:68
  19.6 0.5 %fusion.144 = f32[1,128]{1,0:T(1,128)} fusion(f32[101,128]{1,0:T(8,128)S(1)} %collective-permute-done.2, f32[101,128]{1,0:T(8,128)S(1)} %collective-permute-done.1, f32[165,128]{1,0:T(8,128)S(1)} %collective-permute-done, f32[128]{0:T(128)S(1)} %get-tuple-element.9), kind=kLoop, calls=%fused_computation.212 | loop fusion | flops 512 | bytes 2560 | tf_op jit(solution)/shard_map/mul | solution.py:205
  20.1 0.1 concatenate.44
  20.2 0.6 %collective-permute-done.5 = f32[41,128]{1,0:T(8,128)S(1)} collective-permute-done((f32[41,128]{1,0:T(8,128)S(1)}, f32[41,128]{1,0:T(8,128)S(1)}, u32[]{:S(2)}, u32[]{:S(2)}) %collective-permute-start.5) | collective-permute-done | bytes 21024 | tf_op jit(solution)/shard_map/ppermute | solution.py:68
  20.8 0.1 concatenate.47
  20.9 2.6 %collective-permute-done.4 = f32[41,128]{1,0:T(8,128)S(1)} collective-permute-done((f32[41,128]{1,0:T(8,128)S(1)}, f32[41,128]{1,0:T(8,128)S(1)}, u32[]{:S(2)}, u32[]{:S(2)}) %collective-permute-start.4) | collective-permute-done | bytes 21024 | tf_op jit(solution)/shard_map/ppermute | solution.py:68
  23.5 0.1 concatenate.46
  23.6 0.0 collective-permute-done.3
  23.6 0.1 concatenate.45
  23.7 0.1 multiply_reduce_fusion
  23.8 0.7 %multiply_bitcast_fusion = f32[576,2,48]{0,2,1:T(8,128)} fusion(f32[48,2,576]{2,0,1:T(8,128)S(1)} %multiply_reduce_fusion), kind=kLoop, calls=%fused_computation.14 | loop fusion | flops 55296 | bytes 442368 | tf_op jit(solution)/shard_map/mul | solution.py:208
  24.6 0.6 %fusion.107 = (f32[128,16]{0,1:T(8,128)}, f32[16,128]{1,0:T(8,128)}) fusion(f32[41,128]{1,0:T(8,128)S(1)} %collective-permute-done.5, f32[41,128]{1,0:T(8,128)S(1)} %collective-permute-done.4, f32[41,128]{1,0:T(8,128)S(1)} %collective-permute-done.3, f32[4,1,16,128]{3,2,0,1:T(8,128)S(1)} %bitcast_add_fusion, s32[]{:T(128)S(6)} %select_n.68, ...), kind=kLoop, calls=%fused_computation.143 | loop fusion | flops 16384 | bytes 81924 | tf_op jit(solution)/shard_map/mul | solution.py:207
  (39 shorter events, 0.3 us)
Async XLA Ops:
  0.6 3.6 %copy-start = (bf16[2,2,5,1,256,128]{5,4,3,2,1,0:T(8,128)(2,1)S(1)}, bf16[2,2,5,1,256,128]{5,4,3,2,1,0:T(8,128)(2,1)}, u32[]{:S(2)}) copy-start(bf16[2,2,5,1,256,128]{5,4,3,2,1,0:T(8,128)(2,1)} %param.3) | copy-start | bytes 3932164
  4.8 0.7 %copy-start.1 = (s32[2,2]{1,0:T(2,128)S(1)}, s32[2,2]{1,0:T(2,128)}, u32[]{:S(2)}) copy-start(s32[2,2]{1,0:T(2,128)} %param.5) | copy-start | bytes 52
  8.0 4.7 %collective-permute-start.2 = (f32[101,128]{1,0:T(8,128)S(1)}, f32[101,128]{1,0:T(8,128)S(1)}, u32[]{:S(2)}, u32[]{:S(2)}) collective-permute-start(f32[101,128]{1,0:T(8,128)S(1)} %get-tuple-element.26), channel_id=1, source_target_pairs={{0,3},{1,2},{2,1},{3,0},{4,7},{5,6},{6,5},{7,4},{8,11},{9,10},{10,... | collective-permute-start | bytes 155144 | tf_op jit(solution)/shard_map/ppermute | solution.py:68
  10.4 4.4 %collective-permute-start.1 = (f32[101,128]{1,0:T(8,128)S(1)}, f32[101,128]{1,0:T(8,128)S(1)}, u32[]{:S(2)}, u32[]{:S(2)}) collective-permute-start(f32[101,128]{1,0:T(8,128)S(1)} %get-tuple-element.25), channel_id=1, source_target_pairs={{0,2},{1,3},{2,0},{3,1},{4,6},{5,7},{6,4},{7,5},{8,10},{9,11},{10,... | collective-permute-start | bytes 155144 | tf_op jit(solution)/shard_map/ppermute | solution.py:68
  11.6 3.3 %collective-permute-start = (f32[165,128]{1,0:T(8,128)S(1)}, f32[165,128]{1,0:T(8,128)S(1)}, u32[]{:S(2)}, u32[]{:S(2)}) collective-permute-start(f32[165,128]{1,0:T(8,128)S(1)} %pad_maximum_fusion), channel_id=1, source_target_pairs={{0,1},{1,0},{2,3},{3,2},{4,5},{5,4},{6,7},{7,6},{8,9},{9,8},{10,11... | collective-permute-start | bytes 253448 | tf_op jit(solution)/shard_map/ppermute | solution.py:68
  15.1 5.7 %collective-permute-start.5 = (f32[41,128]{1,0:T(8,128)S(1)}, f32[41,128]{1,0:T(8,128)S(1)}, u32[]{:S(2)}, u32[]{:S(2)}) collective-permute-start(f32[41,128]{1,0:T(8,128)S(1)} %pad_maximum_fusion.7), channel_id=1, source_target_pairs={{0,12},{4,8},{8,4},{12,0},{1,13},{5,9},{9,5},{13,1},{2,14},{6,10},... | collective-permute-start | bytes 62984 | tf_op jit(solution)/shard_map/ppermute | solution.py:68
  18.8 4.7 %collective-permute-start.4 = (f32[41,128]{1,0:T(8,128)S(1)}, f32[41,128]{1,0:T(8,128)S(1)}, u32[]{:S(2)}, u32[]{:S(2)}) collective-permute-start(f32[41,128]{1,0:T(8,128)S(1)} %pad_maximum_fusion.6), channel_id=1, source_target_pairs={{0,8},{4,12},{8,0},{12,4},{1,9},{5,13},{9,1},{13,5},{2,10},{6,14},... | collective-permute-start | bytes 62984 | tf_op jit(solution)/shard_map/ppermute | solution.py:68
  18.8 4.8 %collective-permute-start.3 = (f32[41,128]{1,0:T(8,128)S(1)}, f32[41,128]{1,0:T(8,128)S(1)}, u32[]{:S(2)}, u32[]{:S(2)}) collective-permute-start(f32[41,128]{1,0:T(8,128)S(1)} %pad_maximum_fusion.5), channel_id=1, source_target_pairs={{0,4},{4,0},{8,12},{12,8},{1,5},{5,1},{9,13},{13,9},{2,6},{6,2},{1... | collective-permute-start | bytes 62984 | tf_op jit(solution)/shard_map/ppermute | solution.py:68

commit v15 on v13

--- a/solution.py
+++ b/solution.py
@@ -20,8 +20,9 @@
 
 def test_table(row_ids, col_ids, stride, stream, salt):
     row_term = (row_ids * stride) * -1640531535
-    col_term = col_ids * -1640531535 + stream * -2048144777 + salt
-    upper = lax.shift_right_logical(mix_bits(row_term[:, None] + col_term[None, :]), jnp.int32(9))
+    col_term = col_ids * -1640531535
+    mixed = row_term[:, None] + col_term[None, :] + (stream * -2048144777 + salt)
+    upper = lax.shift_right_logical(mix_bits(mixed), jnp.int32(9))
     return ((2 * upper + 1).astype(jnp.float32) * 2.0 ** (-24) - 1.0).astype(jnp.bfloat16)
 
 

time: 24.6 us -> 24.6 us (level)
  no operation moved by 1% of the time
where the time goes in v15:
time: 24.6 us; the launch traced here: 24.4 us
  starting transfers between devices  7.64 us (31%)
  waiting for transfers between devices  6.18 us (25%)
  local copies, waits for them, and re-layouts  3.05 us (12%)
  other arithmetic  3.01 us (12%)
  between operations  2.28 us (9%)
  matrix products  2.23 us (9%)
    ppermute x6, starting transfers between devices, send_to(): got = lax.ppermute(flat, axes, [(i, i ^ shift) for i in range(n)])  7.64 us
    ppermute x6, waiting for transfers between devices, send_to(): got = lax.ppermute(flat, axes, [(i, i ^ shift) for i in range(n)])  6.18 us
    slice x1, local copies, waits for them, and re-layouts, shards(): factor_stream = test_streams[0]  1.34 us
    mul x1, other arithmetic, shards(): core_out * scale_core  0.72 us
    mul x1, other arithmetic, shards(): sz.reshape(cols_each, cells_z).T * scale_z  0.61 us
    dot_general x1, matrix products, shards(): jnp.dot(rows_z, phz.T, preferred_element_type=f32)  0.6 us
    unnamed x4, local copies, waits for them, and re-layouts  0.52 us
    mul x1, other arithmetic, shards(): sx * scale_x  0.52 us
  transfers between devices with their start and end apart: 6, of which 4 were waited for; matrix products, arithmetic and copies ran while one was open for 6% of the time, Pallas kernels for 0%

profile of v15, /device:TPU:0, one launch (start us, length us, event | category | flops | bytes accessed | tf_op | source)
XLA Modules:
  0.0 24.4 jit_solution(8687630302185280213)
XLA Ops:
  0.6 0.0 copy-start
  0.7 1.3 %fusion.200 = (s32[1]{0:T(128)}, s32[1]{0:T(128)}) fusion(s32[2]{0:T(128)} %param.4), kind=kLoop, calls=%fused_computation.277 | loop fusion | bytes 16 | tf_op jit(solution)/shard_map/slice | solution.py:81
  2.7 0.0 copy-done
  2.7 0.6 %convolution_bitcast_fusion = f32[5120,48]{0,1:T(8,128)S(1)} fusion(bf16[5120,128]{1,0:T(8,128)(2,1)S(1)} %bitcast.97, s32[]{:T(128)} %bitcast.15, s32[128]{0:T(128)S(1)} %get-tuple-element.33, s32[48]{0:T(128)S(1)} %iota_multiply_fusion.3), kind=kOutput, calls=%fused_computation | convolution fusion | flops 63019008 | bytes 2294468 | tf_op jit(solution)/shard_map/dot_general | solution.py:116
  3.3 0.0 copy-start.1
  3.3 0.2 reshape.683
  3.5 0.5 %copy-done.1 = s32[2,2]{1,0:T(2,128)S(1)} copy-done((s32[2,2]{1,0:T(2,128)S(1)}, s32[2,2]{1,0:T(2,128)}, u32[]{:S(2)}) %copy-start.1) | copy-done | bytes 40
  4.0 0.1 fusion.123
  4.1 0.1 mul.630
  4.2 0.4 %fusion.135 = f32[2,256,48]{1,0,2:T(2,128)S(1)} fusion(f32[20,256,48]{1,0,2:T(8,128)S(1)} %reshape.683, s32[]{:T(128)} %bitcast.13, s32[20]{0:T(128)S(1)} %mul.630, s32[2]{0:T(128)S(1)} %iota_multiply_fusion.4), kind=kOutput, calls=%fused_computation.203 | convolution fusion | flops 2949800 | bytes 1081436 | tf_op jit(solution)/shard_map/qxyn,qe->xeyn/dot_general | solution.py:118
  4.6 0.3 %convolution_bitcast_fusion.2 = f32[1,2,48,48]{2,3,1,0:T(8,128)S(1)} fusion(f32[2,256,48]{1,0,2:T(2,128)S(1)} %fusion.135, s32[]{:T(128)} %bitcast.18, s32[256]{0:T(256)S(1)} %iota_multiply_fusion, s32[48]{0:T(128)S(1)} %iota_multiply_fusion.3), kind=kOutput, calls=%fused_computation.12 | convolution fusion | flops 7286784 | bytes 117956 | tf_op jit(solution)/shard_map/my,xeyn->xemn/dot_general | solution.py:119
  4.8 0.1 copy.14
  4.9 0.1 reshape.684
  5.0 0.1 reshape_reshape.16
  5.8 0.1 mul.580
  5.9 0.1 fusion.61
  6.0 0.1 broadcast_multiply_fusion.1
  6.1 0.3 %multiply_convert_fusion = (bf16[20,128,128]{2,1,0:T(8,128)(2,1)S(1)}, bf16[20,128,128]{2,1,0:T(8,128)(2,1)S(1)}) fusion(f32[128,128]{1,0:T(8,128)S(1)} %fusion.61, f32[20,128]{1,0:T(8,128)S(1)} %get-tuple-element.28), kind=kLoop, calls=%fused_computation.2 | loop fusion | flops 1638400 | bytes 1386496 | tf_op jit(solution)/shard_map/convert_element_type | solution.py:105
  6.5 0.5 %fusion.7 = f32[1,256,256]{2,1,0:T(8,128)S(1)} fusion(bf16[20,256,128]{2,1,0:T(8,128)(2,1)S(1)} %bitcast.98, bf16[20,128,128]{2,1,0:T(8,128)(2,1)S(1)} %get-tuple-element.16, bf16[20,128,128]{2,1,0:T(8,128)(2,1)S(1)} %get-tuple-element.15), kind=kOutput, calls=%fused_computation.11 | convolution fusion | flops 338165760 | bytes 2883584 | tf_op jit(solution)/shard_map/qxyz,qzk->xyk/dot_general | solution.py:107
  7.0 0.2 broadcast_multiply_fusion
  7.2 2.4 %collective-permute-start.2 = (f32[101,128]{1,0:T(8,128)S(1)}, f32[101,128]{1,0:T(8,128)S(1)}, u32[]{:S(2)}, u32[]{:S(2)}) collective-permute-start(f32[101,128]{1,0:T(8,128)S(1)} %get-tuple-element.26), channel_id=1, source_target_pairs={{0,3},{1,2},{2,1},{3,0},{4,7},{5,6},{6,5},{7,4},{8,11},{9,10},{10,... | collective-permute-start | bytes 155144 | tf_op jit(solution)/shard_map/ppermute | solution.py:54
  9.6 0.6 %collective-permute-start.1 = (f32[101,128]{1,0:T(8,128)S(1)}, f32[101,128]{1,0:T(8,128)S(1)}, u32[]{:S(2)}, u32[]{:S(2)}) collective-permute-start(f32[101,128]{1,0:T(8,128)S(1)} %get-tuple-element.25), channel_id=1, source_target_pairs={{0,2},{1,3},{2,0},{3,1},{4,6},{5,7},{6,4},{7,5},{8,10},{9,11},{10,... | collective-permute-start | bytes 155144 | tf_op jit(solution)/shard_map/ppermute | solution.py:54
  10.3 0.5 %fusion.6 = f32[128,128]{0,1:T(8,128)S(1)} fusion(bf16[20,256,128]{2,1,0:T(8,128)(2,1)S(1)} %bitcast.99, f32[20,128]{1,0:T(8,128)S(1)} %get-tuple-element.27, s32[]{:T(128)} %bitcast.8, s32[128]{0:T(128)S(1)} %iota_multiply_fusion.5, s32[256]{0:T(256)S(1)} %iota_multiply_fusion.1), kind=kOutput, calls=%fused_computation.10 | convolution fusion | flops 168968192 | bytes 1388036 | tf_op jit(solution)/shard_map/qxyz,yk->qxzk/dot_general | solution.py:113
  10.8 0.1 collective-permute-start
  10.9 0.1 fusion.124
  11.0 0.1 reshape.694
  11.1 0.7 %collective-permute-done.2 = f32[101,128]{1,0:T(8,128)S(1)} collective-permute-done((f32[101,128]{1,0:T(8,128)S(1)}, f32[101,128]{1,0:T(8,128)S(1)}, u32[]{:S(2)}, u32[]{:S(2)}) %collective-permute-start.2) | collective-permute-done | bytes 51744 | tf_op jit(solution)/shard_map/ppermute | solution.py:54
  11.9 2.2 %collective-permute-done.1 = f32[101,128]{1,0:T(8,128)S(1)} collective-permute-done((f32[101,128]{1,0:T(8,128)S(1)}, f32[101,128]{1,0:T(8,128)S(1)}, u32[]{:S(2)}, u32[]{:S(2)}) %collective-permute-start.1) | collective-permute-done | bytes 51744 | tf_op jit(solution)/shard_map/ppermute | solution.py:54
  14.1 0.0 collective-permute-done
  14.2 0.1 dynamic-slice_reduce_fusion
  14.3 3.7 %collective-permute-start.5 = (f32[41,128]{1,0:T(8,128)S(1)}, f32[41,128]{1,0:T(8,128)S(1)}, u32[]{:S(2)}, u32[]{:S(2)}) collective-permute-start(f32[41,128]{1,0:T(8,128)S(1)} %pad_maximum_fusion.7), channel_id=1, source_target_pairs={{0,12},{4,8},{8,4},{12,0},{1,13},{5,9},{9,5},{13,1},{2,14},{6,10},... | collective-permute-start | bytes 62984 | tf_op jit(solution)/shard_map/ppermute | solution.py:54
  18.0 0.0 collective-permute-start.4
  18.0 0.8 %collective-permute-start.3 = (f32[41,128]{1,0:T(8,128)S(1)}, f32[41,128]{1,0:T(8,128)S(1)}, u32[]{:S(2)}, u32[]{:S(2)}) collective-permute-start(f32[41,128]{1,0:T(8,128)S(1)} %pad_maximum_fusion.5), channel_id=1, source_target_pairs={{0,4},{4,0},{8,12},{12,8},{1,5},{5,1},{9,13},{13,9},{2,6},{6,2},{1... | collective-permute-start | bytes 62984 | tf_op jit(solution)/shard_map/ppermute | solution.py:54
  18.8 0.5 %fusion.147 = f32[1,128]{1,0:T(1,128)} fusion(f32[101,128]{1,0:T(8,128)S(1)} %collective-permute-done.2, f32[101,128]{1,0:T(8,128)S(1)} %collective-permute-done.1, f32[165,128]{1,0:T(8,128)S(1)} %collective-permute-done, f32[128]{0:T(128)S(1)} %get-tuple-element.9), kind=kLoop, calls=%fused_computation.215 | loop fusion | flops 512 | bytes 2560 | tf_op jit(solution)/shard_map/mul | solution.py:187
  19.3 0.1 concatenate.40
  19.4 0.6 %collective-permute-done.5 = f32[41,128]{1,0:T(8,128)S(1)} collective-permute-done((f32[41,128]{1,0:T(8,128)S(1)}, f32[41,128]{1,0:T(8,128)S(1)}, u32[]{:S(2)}, u32[]{:S(2)}) %collective-permute-start.5) | collective-permute-done | bytes 21024 | tf_op jit(solution)/shard_map/ppermute | solution.py:54
  20.0 0.1 concatenate.43
  20.1 2.6 %collective-permute-done.4 = f32[41,128]{1,0:T(8,128)S(1)} collective-permute-done((f32[41,128]{1,0:T(8,128)S(1)}, f32[41,128]{1,0:T(8,128)S(1)}, u32[]{:S(2)}, u32[]{:S(2)}) %collective-permute-start.4) | collective-permute-done | bytes 21024 | tf_op jit(solution)/shard_map/ppermute | solution.py:54
  22.7 0.1 concatenate.42
  22.8 0.0 collective-permute-done.3
  22.8 0.1 concatenate.41
  22.9 0.1 multiply_reduce_fusion
  23.1 0.7 %multiply_bitcast_fusion = f32[576,2,48]{0,2,1:T(8,128)} fusion(f32[48,2,576]{2,0,1:T(8,128)S(1)} %multiply_reduce_fusion), kind=kLoop, calls=%fused_computation.14 | loop fusion | flops 55296 | bytes 442368 | tf_op jit(solution)/shard_map/mul | solution.py:190
  23.8 0.6 %fusion.110 = (f32[128,16]{0,1:T(8,128)}, f32[16,128]{1,0:T(8,128)}) fusion(f32[41,128]{1,0:T(8,128)S(1)} %collective-permute-done.5, f32[41,128]{1,0:T(8,128)S(1)} %collective-permute-done.4, f32[41,128]{1,0:T(8,128)S(1)} %collective-permute-done.3, f32[4,1,16,128]{3,2,0,1:T(8,128)S(1)} %bitcast_add_fusion, s32[]{:T(128)S(6)} %select_n.63, ...), kind=kLoop, calls=%fused_computation.146 | loop fusion | flops 16384 | bytes 81924 | tf_op jit(solution)/shard_map/mul | solution.py:189
  (36 shorter events, 0.3 us)
Async XLA Ops:
  0.6 2.1 %copy-start = (bf16[2,2,5,1,256,128]{5,4,3,2,1,0:T(8,128)(2,1)S(1)}, bf16[2,2,5,1,256,128]{5,4,3,2,1,0:T(8,128)(2,1)}, u32[]{:S(2)}) copy-start(bf16[2,2,5,1,256,128]{5,4,3,2,1,0:T(8,128)(2,1)} %param.3) | copy-start | bytes 3932164
  3.3 0.7 %copy-start.1 = (s32[2,2]{1,0:T(2,128)S(1)}, s32[2,2]{1,0:T(2,128)}, u32[]{:S(2)}) copy-start(s32[2,2]{1,0:T(2,128)} %param.5) | copy-start | bytes 52
  7.2 4.7 %collective-permute-start.2 = (f32[101,128]{1,0:T(8,128)S(1)}, f32[101,128]{1,0:T(8,128)S(1)}, u32[]{:S(2)}, u32[]{:S(2)}) collective-permute-start(f32[101,128]{1,0:T(8,128)S(1)} %get-tuple-element.26), channel_id=1, source_target_pairs={{0,3},{1,2},{2,1},{3,0},{4,7},{5,6},{6,5},{7,4},{8,11},{9,10},{10,... | collective-permute-start | bytes 155144 | tf_op jit(solution)/shard_map/ppermute | solution.py:54
  9.6 4.4 %collective-permute-start.1 = (f32[101,128]{1,0:T(8,128)S(1)}, f32[101,128]{1,0:T(8,128)S(1)}, u32[]{:S(2)}, u32[]{:S(2)}) collective-permute-start(f32[101,128]{1,0:T(8,128)S(1)} %get-tuple-element.25), channel_id=1, source_target_pairs={{0,2},{1,3},{2,0},{3,1},{4,6},{5,7},{6,4},{7,5},{8,10},{9,11},{10,... | collective-permute-start | bytes 155144 | tf_op jit(solution)/shard_map/ppermute | solution.py:54
  10.8 3.3 %collective-permute-start = (f32[165,128]{1,0:T(8,128)S(1)}, f32[165,128]{1,0:T(8,128)S(1)}, u32[]{:S(2)}, u32[]{:S(2)}) collective-permute-start(f32[165,128]{1,0:T(8,128)S(1)} %pad_maximum_fusion), channel_id=1, source_target_pairs={{0,1},{1,0},{2,3},{3,2},{4,5},{5,4},{6,7},{7,6},{8,9},{9,8},{10,11... | collective-permute-start | bytes 253448 | tf_op jit(solution)/shard_map/ppermute | solution.py:54
  14.3 5.7 %collective-permute-start.5 = (f32[41,128]{1,0:T(8,128)S(1)}, f32[41,128]{1,0:T(8,128)S(1)}, u32[]{:S(2)}, u32[]{:S(2)}) collective-permute-start(f32[41,128]{1,0:T(8,128)S(1)} %pad_maximum_fusion.7), channel_id=1, source_target_pairs={{0,12},{4,8},{8,4},{12,0},{1,13},{5,9},{9,5},{13,1},{2,14},{6,10},... | collective-permute-start | bytes 62984 | tf_op jit(solution)/shard_map/ppermute | solution.py:54
  18.0 4.7 %collective-permute-start.4 = (f32[41,128]{1,0:T(8,128)S(1)}, f32[41,128]{1,0:T(8,128)S(1)}, u32[]{:S(2)}, u32[]{:S(2)}) collective-permute-start(f32[41,128]{1,0:T(8,128)S(1)} %pad_maximum_fusion.6), channel_id=1, source_target_pairs={{0,8},{4,12},{8,0},{12,4},{1,9},{5,13},{9,1},{13,5},{2,10},{6,14},... | collective-permute-start | bytes 62984 | tf_op jit(solution)/shard_map/ppermute | solution.py:54
  18.0 4.8 %collective-permute-start.3 = (f32[41,128]{1,0:T(8,128)S(1)}, f32[41,128]{1,0:T(8,128)S(1)}, u32[]{:S(2)}, u32[]{:S(2)}) collective-permute-start(f32[41,128]{1,0:T(8,128)S(1)} %pad_maximum_fusion.5), channel_id=1, source_target_pairs={{0,4},{4,0},{8,12},{12,8},{1,5},{5,1},{9,13},{13,9},{2,6},{6,2},{1... | collective-permute-start | bytes 62984 | tf_op jit(solution)/shard_map/ppermute | solution.py:54

commit v16 on v15

--- a/solution.py
+++ b/solution.py
@@ -89,6 +89,7 @@
     q_ids = (
         snapshot_ids[:, :, None] * variables + jnp.arange(variables, dtype=jnp.int32)[None, None, :]
     ).reshape(-1)
+    factor_stream, core_stream, q_ids = lax.optimization_barrier((factor_stream, core_stream, q_ids))
     ax = test_table(x_ids, rank_ids, K, factor_stream, 1).astype(f32)
     ay = test_table(y_ids, rank_ids, K, factor_stream, 2)
     az = test_table(z_ids, rank_ids, K, factor_stream, 3)

time: 24.6 us -> 24.7 us (level)
  other arithmetic: 3.01 us -> 3.69 us
  local copies, waits for them, and re-layouts: 3.05 us -> 2.47 us
    mul x1, other arithmetic: 0.01 us -> 0.68 us  [shards(): snapshot_ids[:, :, None] * variables]
    unnamed x4 -> x2, local copies, waits for them, and re-layouts: 0.52 us -> 0.01 us
where the time goes in v16:
time: 24.7 us; the launch traced here: 24.5 us
  starting transfers between devices  7.64 us (31%)
  waiting for transfers between devices  6.18 us (25%)
  other arithmetic  3.69 us (15%)
  local copies, waits for them, and re-layouts  2.47 us (10%)
  between operations  2.29 us (9%)
  matrix products  2.23 us (9%)
    ppermute x6, starting transfers between devices, send_to(): got = lax.ppermute(flat, axes, [(i, i ^ shift) for i in range(n)])  7.64 us
    ppermute x6, waiting for transfers between devices, send_to(): got = lax.ppermute(flat, axes, [(i, i ^ shift) for i in range(n)])  6.18 us
    slice x1, local copies, waits for them, and re-layouts, shards(): core_stream = test_streams[1]  1.35 us
    mul x1, other arithmetic, shards(): core_out * scale_core  0.72 us
    mul x1, other arithmetic, shards(): snapshot_ids[:, :, None] * variables  0.68 us
    mul x1, other arithmetic, shards(): sz.reshape(cols_each, cells_z).T * scale_z  0.61 us
    dot_general x1, matrix products, shards(): jnp.dot(rows_z, phz.T, preferred_element_type=f32)  0.6 us
    mul x1, other arithmetic, shards(): sx * scale_x  0.52 us
  transfers between devices with their start and end apart: 6, of which 4 were waited for; matrix products, arithmetic and copies ran while one was open for 6% of the time, Pallas kernels for 0%

profile of v16, /device:TPU:0, one launch (start us, length us, event | category | flops | bytes accessed | tf_op | source)
XLA Modules:
  0.0 24.5 jit_solution(7602841281924281935)
XLA Ops:
  0.6 0.0 copy-start
  0.7 1.3 %fusion.198 = (s32[1]{0:T(128)}, s32[1]{0:T(128)}) fusion(s32[2]{0:T(128)} %param.4), kind=kLoop, calls=%fused_computation.277 | loop fusion | bytes 16 | tf_op jit(solution)/shard_map/slice | solution.py:82
  2.1 0.7 %broadcast_multiply_fusion.2 = s32[2,2]{1,0:T(2,128)S(1)} fusion(s32[2,2]{1,0:T(2,128)} %param.5), kind=kLoop, calls=%fused_computation.235 | loop fusion | flops 4 | bytes 32 | tf_op jit(solution)/shard_map/mul | solution.py:90
  2.7 0.1 iota_add_fusion
  2.8 0.1 add.567
  4.2 0.0 copy-done
  4.3 0.6 %convolution_bitcast_fusion = f32[5120,48]{0,1:T(8,128)S(1)} fusion(bf16[5120,128]{1,0:T(8,128)(2,1)S(1)} %bitcast.91, s32[]{:T(128)S(6)} %add.616, s32[128]{0:T(128)S(1)} %get-tuple-element.39, s32[48]{0:T(128)S(1)} %iota_multiply_fusion.3), kind=kOutput, calls=%fused_computation | convolution fusion | flops 63019008 | bytes 2294468 | tf_op jit(solution)/shard_map/dot_general | solution.py:117
  4.9 0.2 reshape.641
  5.0 0.4 %fusion.133 = f32[2,256,48]{1,0,2:T(2,128)S(1)} fusion(f32[20,256,48]{1,0,2:T(8,128)S(1)} %reshape.641, s32[]{:T(128)S(6)} %add.608, s32[20]{0:T(128)S(1)} %get-tuple-element.36, s32[2]{0:T(128)S(1)} %iota_multiply_fusion.4), kind=kOutput, calls=%fused_computation.201 | convolution fusion | flops 2949800 | bytes 1081436 | tf_op jit(solution)/shard_map/qxyn,qe->xeyn/dot_general | solution.py:119
  5.4 0.3 %convolution_bitcast_fusion.2 = f32[1,2,48,48]{2,3,1,0:T(8,128)S(1)} fusion(f32[2,256,48]{1,0,2:T(2,128)S(1)} %fusion.133, s32[]{:T(128)S(6)} %add.624, s32[256]{0:T(256)S(1)} %iota_multiply_fusion, s32[48]{0:T(128)S(1)} %iota_multiply_fusion.3), kind=kOutput, calls=%fused_computation.12 | convolution fusion | flops 7286784 | bytes 117956 | tf_op jit(solution)/shard_map/my,xeyn->xemn/dot_general | solution.py:120
  5.7 0.1 copy.14
  5.8 0.1 reshape.642
  5.9 0.1 reshape_reshape.16
  6.0 0.1 fusion.61
  6.1 0.1 broadcast_multiply_fusion.1
  6.2 0.3 %multiply_convert_fusion = (bf16[20,128,128]{2,1,0:T(8,128)(2,1)S(1)}, bf16[20,128,128]{2,1,0:T(8,128)(2,1)S(1)}) fusion(f32[128,128]{1,0:T(8,128)S(1)} %fusion.61, f32[20,128]{1,0:T(8,128)S(1)} %get-tuple-element.34), kind=kLoop, calls=%fused_computation.2 | loop fusion | flops 1638400 | bytes 1386496 | tf_op jit(solution)/shard_map/convert_element_type | solution.py:106
  6.6 0.5 %fusion.7 = f32[1,256,256]{2,1,0:T(8,128)S(1)} fusion(bf16[20,256,128]{2,1,0:T(8,128)(2,1)S(1)} %bitcast.92, bf16[20,128,128]{2,1,0:T(8,128)(2,1)S(1)} %get-tuple-element.22, bf16[20,128,128]{2,1,0:T(8,128)(2,1)S(1)} %get-tuple-element.21), kind=kOutput, calls=%fused_computation.11 | convolution fusion | flops 338165760 | bytes 2883584 | tf_op jit(solution)/shard_map/qxyz,qzk->xyk/dot_general | solution.py:108
  7.1 0.2 broadcast_multiply_fusion
  7.3 2.4 %collective-permute-start.2 = (f32[101,128]{1,0:T(8,128)S(1)}, f32[101,128]{1,0:T(8,128)S(1)}, u32[]{:S(2)}, u32[]{:S(2)}) collective-permute-start(f32[101,128]{1,0:T(8,128)S(1)} %get-tuple-element.32), channel_id=1, source_target_pairs={{0,3},{1,2},{2,1},{3,0},{4,7},{5,6},{6,5},{7,4},{8,11},{9,10},{10,... | collective-permute-start | bytes 155144 | tf_op jit(solution)/shard_map/ppermute | solution.py:54
  9.7 0.6 %collective-permute-start.1 = (f32[101,128]{1,0:T(8,128)S(1)}, f32[101,128]{1,0:T(8,128)S(1)}, u32[]{:S(2)}, u32[]{:S(2)}) collective-permute-start(f32[101,128]{1,0:T(8,128)S(1)} %get-tuple-element.31), channel_id=1, source_target_pairs={{0,2},{1,3},{2,0},{3,1},{4,6},{5,7},{6,4},{7,5},{8,10},{9,11},{10,... | collective-permute-start | bytes 155144 | tf_op jit(solution)/shard_map/ppermute | solution.py:54
  10.4 0.5 %fusion.6 = f32[128,128]{0,1:T(8,128)S(1)} fusion(bf16[20,256,128]{2,1,0:T(8,128)(2,1)S(1)} %bitcast.93, f32[20,128]{1,0:T(8,128)S(1)} %get-tuple-element.33, s32[]{:T(128)S(6)} %add.590, s32[128]{0:T(128)S(1)} %iota_multiply_fusion.5, s32[256]{0:T(256)S(1)} %iota_multiply_fusion.1), kind=kOutput, calls=%fused_computation.10 | convolution fusion | flops 168968192 | bytes 1388036 | tf_op jit(solution)/shard_map/qxyz,yk->qxzk/dot_general | solution.py:114
  10.9 0.1 collective-permute-start
  11.0 0.1 fusion.122
  11.1 0.1 reshape.652
  11.2 0.7 %collective-permute-done.2 = f32[101,128]{1,0:T(8,128)S(1)} collective-permute-done((f32[101,128]{1,0:T(8,128)S(1)}, f32[101,128]{1,0:T(8,128)S(1)}, u32[]{:S(2)}, u32[]{:S(2)}) %collective-permute-start.2) | collective-permute-done | bytes 51744 | tf_op jit(solution)/shard_map/ppermute | solution.py:54
  12.0 2.2 %collective-permute-done.1 = f32[101,128]{1,0:T(8,128)S(1)} collective-permute-done((f32[101,128]{1,0:T(8,128)S(1)}, f32[101,128]{1,0:T(8,128)S(1)}, u32[]{:S(2)}, u32[]{:S(2)}) %collective-permute-start.1) | collective-permute-done | bytes 51744 | tf_op jit(solution)/shard_map/ppermute | solution.py:54
  14.2 0.0 collective-permute-done
  14.3 0.1 dynamic-slice_reduce_fusion
  14.4 3.7 %collective-permute-start.5 = (f32[41,128]{1,0:T(8,128)S(1)}, f32[41,128]{1,0:T(8,128)S(1)}, u32[]{:S(2)}, u32[]{:S(2)}) collective-permute-start(f32[41,128]{1,0:T(8,128)S(1)} %pad_maximum_fusion.7), channel_id=1, source_target_pairs={{0,12},{4,8},{8,4},{12,0},{1,13},{5,9},{9,5},{13,1},{2,14},{6,10},... | collective-permute-start | bytes 62984 | tf_op jit(solution)/shard_map/ppermute | solution.py:54
  18.1 0.0 collective-permute-start.4
  18.1 0.8 %collective-permute-start.3 = (f32[41,128]{1,0:T(8,128)S(1)}, f32[41,128]{1,0:T(8,128)S(1)}, u32[]{:S(2)}, u32[]{:S(2)}) collective-permute-start(f32[41,128]{1,0:T(8,128)S(1)} %pad_maximum_fusion.5), channel_id=1, source_target_pairs={{0,4},{4,0},{8,12},{12,8},{1,5},{5,1},{9,13},{13,9},{2,6},{6,2},{1... | collective-permute-start | bytes 62984 | tf_op jit(solution)/shard_map/ppermute | solution.py:54
  18.9 0.5 %fusion.145 = f32[1,128]{1,0:T(1,128)} fusion(f32[101,128]{1,0:T(8,128)S(1)} %collective-permute-done.2, f32[101,128]{1,0:T(8,128)S(1)} %collective-permute-done.1, f32[165,128]{1,0:T(8,128)S(1)} %collective-permute-done, f32[128]{0:T(128)S(1)} %get-tuple-element.15), kind=kLoop, calls=%fused_computation.213 | loop fusion | flops 512 | bytes 2560 | tf_op jit(solution)/shard_map/mul | solution.py:188
  19.4 0.1 concatenate.40
  19.5 0.6 %collective-permute-done.5 = f32[41,128]{1,0:T(8,128)S(1)} collective-permute-done((f32[41,128]{1,0:T(8,128)S(1)}, f32[41,128]{1,0:T(8,128)S(1)}, u32[]{:S(2)}, u32[]{:S(2)}) %collective-permute-start.5) | collective-permute-done | bytes 21024 | tf_op jit(solution)/shard_map/ppermute | solution.py:54
  20.1 0.1 concatenate.43
  20.2 2.6 %collective-permute-done.4 = f32[41,128]{1,0:T(8,128)S(1)} collective-permute-done((f32[41,128]{1,0:T(8,128)S(1)}, f32[41,128]{1,0:T(8,128)S(1)}, u32[]{:S(2)}, u32[]{:S(2)}) %collective-permute-start.4) | collective-permute-done | bytes 21024 | tf_op jit(solution)/shard_map/ppermute | solution.py:54
  22.8 0.1 concatenate.42
  22.9 0.0 collective-permute-done.3
  22.9 0.1 concatenate.41
  23.0 0.1 multiply_reduce_fusion
  23.2 0.7 %multiply_bitcast_fusion = f32[576,2,48]{0,2,1:T(8,128)} fusion(f32[48,2,576]{2,0,1:T(8,128)S(1)} %multiply_reduce_fusion), kind=kLoop, calls=%fused_computation.14 | loop fusion | flops 55296 | bytes 442368 | tf_op jit(solution)/shard_map/mul | solution.py:191
  23.9 0.6 %fusion.110 = (f32[128,16]{0,1:T(8,128)}, f32[16,128]{1,0:T(8,128)}) fusion(f32[41,128]{1,0:T(8,128)S(1)} %collective-permute-done.5, f32[41,128]{1,0:T(8,128)S(1)} %collective-permute-done.4, f32[41,128]{1,0:T(8,128)S(1)} %collective-permute-done.3, f32[4,1,16,128]{3,2,0,1:T(8,128)S(1)} %bitcast_add_fusion, s32[]{:T(128)S(6)} %select_n.63, ...), kind=kLoop, calls=%fused_computation.146 | loop fusion | flops 16384 | bytes 81924 | tf_op jit(solution)/shard_map/mul | solution.py:190
  (36 shorter events, 0.3 us)
Async XLA Ops:
  0.6 3.6 %copy-start = (bf16[2,2,5,1,256,128]{5,4,3,2,1,0:T(8,128)(2,1)S(1)}, bf16[2,2,5,1,256,128]{5,4,3,2,1,0:T(8,128)(2,1)}, u32[]{:S(2)}) copy-start(bf16[2,2,5,1,256,128]{5,4,3,2,1,0:T(8,128)(2,1)} %param.3) | copy-start | bytes 3932164
  7.3 4.7 %collective-permute-start.2 = (f32[101,128]{1,0:T(8,128)S(1)}, f32[101,128]{1,0:T(8,128)S(1)}, u32[]{:S(2)}, u32[]{:S(2)}) collective-permute-start(f32[101,128]{1,0:T(8,128)S(1)} %get-tuple-element.32), channel_id=1, source_target_pairs={{0,3},{1,2},{2,1},{3,0},{4,7},{5,6},{6,5},{7,4},{8,11},{9,10},{10,... | collective-permute-start | bytes 155144 | tf_op jit(solution)/shard_map/ppermute | solution.py:54
  9.7 4.4 %collective-permute-start.1 = (f32[101,128]{1,0:T(8,128)S(1)}, f32[101,128]{1,0:T(8,128)S(1)}, u32[]{:S(2)}, u32[]{:S(2)}) collective-permute-start(f32[101,128]{1,0:T(8,128)S(1)} %get-tuple-element.31), channel_id=1, source_target_pairs={{0,2},{1,3},{2,0},{3,1},{4,6},{5,7},{6,4},{7,5},{8,10},{9,11},{10,... | collective-permute-start | bytes 155144 | tf_op jit(solution)/shard_map/ppermute | solution.py:54
  10.9 3.3 %collective-permute-start = (f32[165,128]{1,0:T(8,128)S(1)}, f32[165,128]{1,0:T(8,128)S(1)}, u32[]{:S(2)}, u32[]{:S(2)}) collective-permute-start(f32[165,128]{1,0:T(8,128)S(1)} %pad_maximum_fusion), channel_id=1, source_target_pairs={{0,1},{1,0},{2,3},{3,2},{4,5},{5,4},{6,7},{7,6},{8,9},{9,8},{10,11... | collective-permute-start | bytes 253448 | tf_op jit(solution)/shard_map/ppermute | solution.py:54
  14.4 5.7 %collective-permute-start.5 = (f32[41,128]{1,0:T(8,128)S(1)}, f32[41,128]{1,0:T(8,128)S(1)}, u32[]{:S(2)}, u32[]{:S(2)}) collective-permute-start(f32[41,128]{1,0:T(8,128)S(1)} %pad_maximum_fusion.7), channel_id=1, source_target_pairs={{0,12},{4,8},{8,4},{12,0},{1,13},{5,9},{9,5},{13,1},{2,14},{6,10},... | collective-permute-start | bytes 62984 | tf_op jit(solution)/shard_map/ppermute | solution.py:54
  18.1 4.7 %collective-permute-start.4 = (f32[41,128]{1,0:T(8,128)S(1)}, f32[41,128]{1,0:T(8,128)S(1)}, u32[]{:S(2)}, u32[]{:S(2)}) collective-permute-start(f32[41,128]{1,0:T(8,128)S(1)} %pad_maximum_fusion.6), channel_id=1, source_target_pairs={{0,8},{4,12},{8,0},{12,4},{1,9},{5,13},{9,1},{13,5},{2,10},{6,14},... | collective-permute-start | bytes 62984 | tf_op jit(solution)/shard_map/ppermute | solution.py:54
  18.1 4.8 %collective-permute-start.3 = (f32[41,128]{1,0:T(8,128)S(1)}, f32[41,128]{1,0:T(8,128)S(1)}, u32[]{:S(2)}, u32[]{:S(2)}) collective-permute-start(f32[41,128]{1,0:T(8,128)S(1)} %pad_maximum_fusion.5), channel_id=1, source_target_pairs={{0,4},{4,0},{8,12},{12,8},{1,5},{5,1},{9,13},{13,9},{2,6},{6,2},{1... | collective-permute-start | bytes 62984 | tf_op jit(solution)/shard_map/ppermute | solution.py:54

commit v17 on v15

--- a/solution.py
+++ b/solution.py
@@ -86,9 +86,13 @@
     x_ids = gx_me * cells_x + jnp.arange(cells_x, dtype=jnp.int32)
     y_ids = jnp.arange(cells_y, dtype=jnp.int32)
     z_ids = lax.axis_index("gz") * cells_z + jnp.arange(cells_z, dtype=jnp.int32)
-    q_ids = (
-        snapshot_ids[:, :, None] * variables + jnp.arange(variables, dtype=jnp.int32)[None, None, :]
-    ).reshape(-1)
+    flat_q = jnp.arange(batches * local_snaps * variables, dtype=jnp.int32)
+    slot = (
+        jnp.arange(batches, dtype=jnp.int32)[:, None] * local_snaps
+        + jnp.arange(local_snaps, dtype=jnp.int32)[None, :]
+    )
+    picks = jnp.where((flat_q // variables)[:, None, None] == slot[None], snapshot_ids[None], 0)
+    q_ids = jnp.sum(picks, axis=(1, 2)) * variables + flat_q % variables
     ax = test_table(x_ids, rank_ids, K, factor_stream, 1).astype(f32)
     ay = test_table(y_ids, rank_ids, K, factor_stream, 2)
     az = test_table(z_ids, rank_ids, K, factor_stream, 3)

time: 24.6 us -> 24.5 us (level)
  no operation moved by 1% of the time
where the time goes in v17:
time: 24.5 us; the launch traced here: 24.3 us
  starting transfers between devices  7.64 us (31%)
  waiting for transfers between devices  6.17 us (25%)
  other arithmetic  3.13 us (13%)
  local copies, waits for them, and re-layouts  2.81 us (11%)
  between operations  2.29 us (9%)
  matrix products  2.23 us (9%)
    ppermute x6, starting transfers between devices, send_to(): got = lax.ppermute(flat, axes, [(i, i ^ shift) for i in range(n)])  7.64 us
    ppermute x6, waiting for transfers between devices, send_to(): got = lax.ppermute(flat, axes, [(i, i ^ shift) for i in range(n)])  6.17 us
    slice x1, local copies, waits for them, and re-layouts, shards(): factor_stream = test_streams[0]  1.34 us
    mul x1, other arithmetic, shards(): core_out * scale_core  0.72 us
    mul x1, other arithmetic, shards(): sz.reshape(cols_each, cells_z).T * scale_z  0.61 us
    dot_general x1, matrix products, shards(): jnp.dot(rows_z, phz.T, preferred_element_type=f32)  0.6 us
    mul x1, other arithmetic, shards(): sx * scale_x  0.52 us
    dot_general x1, matrix products, shards(): jnp.einsum('qxyz,qzk->xyk', field, jnp.concatenate([qz_hi, qz_lo], axis=-...  0.5 us
  transfers between devices with their start and end apart: 6, of which 4 were waited for; matrix products, arithmetic and copies ran while one was open for 6% of the time, Pallas kernels for 0%

profile of v17, /device:TPU:0, one launch (start us, length us, event | category | flops | bytes accessed | tf_op | source)
XLA Modules:
  0.0 24.3 jit_solution(6288393411801871509)
XLA Ops:
  0.6 0.0 copy-start
  0.8 1.3 %fusion.201 = (s32[1]{0:T(128)}, s32[1]{0:T(128)}) fusion(s32[2]{0:T(128)} %param.4), kind=kLoop, calls=%fused_computation.285 | loop fusion | bytes 16 | tf_op jit(solution)/shard_map/slice | solution.py:81
  2.7 0.0 copy-done
  2.8 0.6 %convolution_bitcast_fusion = f32[5120,48]{0,1:T(8,128)S(1)} fusion(bf16[5120,128]{1,0:T(8,128)(2,1)S(1)} %bitcast.97, s32[]{:T(128)} %bitcast.15, s32[128]{0:T(128)S(1)} %get-tuple-element.33, s32[48]{0:T(128)S(1)} %iota_multiply_fusion.3), kind=kOutput, calls=%fused_computation | convolution fusion | flops 63019008 | bytes 2294468 | tf_op jit(solution)/shard_map/dot_general | solution.py:120
  3.4 0.0 copy-start.1
  3.4 0.2 reshape.713
  3.5 0.1 iota_add_fusion
  3.6 0.4 %copy-done.1 = s32[2,2]{1,0:T(2,128)S(1)} copy-done((s32[2,2]{1,0:T(2,128)S(1)}, s32[2,2]{1,0:T(2,128)}, u32[]{:S(2)}) %copy-start.1) | copy-done | bytes 40
  4.0 0.1 fusion.121
  4.2 0.4 %fusion.135 = f32[2,256,48]{1,0,2:T(2,128)S(1)} fusion(f32[20,256,48]{1,0,2:T(8,128)S(1)} %reshape.713, s32[]{:T(128)} %bitcast.13, s32[20]{0:T(128)S(1)} %broadcast_multiply_fusion.2, s32[2]{0:T(128)S(1)} %iota_multiply_fusion.4), kind=kOutput, calls=%fused_computation.209 | convolution fusion | flops 2949800 | bytes 1081436 | tf_op jit(solution)/shard_map/qxyn,qe->xeyn/dot_general | solution.py:122
  4.5 0.3 %convolution_bitcast_fusion.2 = f32[1,2,48,48]{2,3,1,0:T(8,128)S(1)} fusion(f32[2,256,48]{1,0,2:T(2,128)S(1)} %fusion.135, s32[]{:T(128)} %bitcast.18, s32[256]{0:T(256)S(1)} %iota_multiply_fusion, s32[48]{0:T(128)S(1)} %iota_multiply_fusion.3), kind=kOutput, calls=%fused_computation.12 | convolution fusion | flops 7286784 | bytes 117956 | tf_op jit(solution)/shard_map/my,xeyn->xemn/dot_general | solution.py:123
  4.8 0.1 copy.14
  4.9 0.1 reshape.714
  5.0 0.1 reshape_reshape.16
  5.8 0.1 fusion.61
  5.9 0.1 broadcast_multiply_fusion.1
  6.0 0.3 %multiply_convert_fusion = (bf16[20,128,128]{2,1,0:T(8,128)(2,1)S(1)}, bf16[20,128,128]{2,1,0:T(8,128)(2,1)S(1)}) fusion(f32[128,128]{1,0:T(8,128)S(1)} %fusion.61, f32[20,128]{1,0:T(8,128)S(1)} %get-tuple-element.30), kind=kLoop, calls=%fused_computation.2 | loop fusion | flops 1638400 | bytes 1386496 | tf_op jit(solution)/shard_map/convert_element_type | solution.py:109
  6.3 0.5 %fusion.7 = f32[1,256,256]{2,1,0:T(8,128)S(1)} fusion(bf16[20,256,128]{2,1,0:T(8,128)(2,1)S(1)} %bitcast.98, bf16[20,128,128]{2,1,0:T(8,128)(2,1)S(1)} %get-tuple-element.18, bf16[20,128,128]{2,1,0:T(8,128)(2,1)S(1)} %get-tuple-element.17), kind=kOutput, calls=%fused_computation.11 | convolution fusion | flops 338165760 | bytes 2883584 | tf_op jit(solution)/shard_map/qxyz,qzk->xyk/dot_general | solution.py:111
  6.8 0.2 broadcast_multiply_fusion
  7.1 2.4 %collective-permute-start.2 = (f32[101,128]{1,0:T(8,128)S(1)}, f32[101,128]{1,0:T(8,128)S(1)}, u32[]{:S(2)}, u32[]{:S(2)}) collective-permute-start(f32[101,128]{1,0:T(8,128)S(1)} %get-tuple-element.28), channel_id=1, source_target_pairs={{0,3},{1,2},{2,1},{3,0},{4,7},{5,6},{6,5},{7,4},{8,11},{9,10},{10,... | collective-permute-start | bytes 155144 | tf_op jit(solution)/shard_map/ppermute | solution.py:54
  9.5 0.6 %collective-permute-start.1 = (f32[101,128]{1,0:T(8,128)S(1)}, f32[101,128]{1,0:T(8,128)S(1)}, u32[]{:S(2)}, u32[]{:S(2)}) collective-permute-start(f32[101,128]{1,0:T(8,128)S(1)} %get-tuple-element.27), channel_id=1, source_target_pairs={{0,2},{1,3},{2,0},{3,1},{4,6},{5,7},{6,4},{7,5},{8,10},{9,11},{10,... | collective-permute-start | bytes 155144 | tf_op jit(solution)/shard_map/ppermute | solution.py:54
  10.1 0.5 %fusion.6 = f32[128,128]{0,1:T(8,128)S(1)} fusion(bf16[20,256,128]{2,1,0:T(8,128)(2,1)S(1)} %bitcast.99, f32[20,128]{1,0:T(8,128)S(1)} %get-tuple-element.29, s32[]{:T(128)} %bitcast.8, s32[128]{0:T(128)S(1)} %iota_multiply_fusion.5, s32[256]{0:T(256)S(1)} %iota_multiply_fusion.1), kind=kOutput, calls=%fused_computation.10 | convolution fusion | flops 168968192 | bytes 1388036 | tf_op jit(solution)/shard_map/qxyz,yk->qxzk/dot_general | solution.py:117
  10.7 0.1 collective-permute-start
  10.8 0.1 fusion.123
  10.9 0.1 reshape.724
  11.0 0.7 %collective-permute-done.2 = f32[101,128]{1,0:T(8,128)S(1)} collective-permute-done((f32[101,128]{1,0:T(8,128)S(1)}, f32[101,128]{1,0:T(8,128)S(1)}, u32[]{:S(2)}, u32[]{:S(2)}) %collective-permute-start.2) | collective-permute-done | bytes 51744 | tf_op jit(solution)/shard_map/ppermute | solution.py:54
  11.7 2.2 %collective-permute-done.1 = f32[101,128]{1,0:T(8,128)S(1)} collective-permute-done((f32[101,128]{1,0:T(8,128)S(1)}, f32[101,128]{1,0:T(8,128)S(1)}, u32[]{:S(2)}, u32[]{:S(2)}) %collective-permute-start.1) | collective-permute-done | bytes 51744 | tf_op jit(solution)/shard_map/ppermute | solution.py:54
  14.0 0.0 collective-permute-done
  14.1 0.1 dynamic-slice_reduce_fusion
  14.2 3.7 %collective-permute-start.5 = (f32[41,128]{1,0:T(8,128)S(1)}, f32[41,128]{1,0:T(8,128)S(1)}, u32[]{:S(2)}, u32[]{:S(2)}) collective-permute-start(f32[41,128]{1,0:T(8,128)S(1)} %pad_maximum_fusion.7), channel_id=1, source_target_pairs={{0,12},{4,8},{8,4},{12,0},{1,13},{5,9},{9,5},{13,1},{2,14},{6,10},... | collective-permute-start | bytes 62984 | tf_op jit(solution)/shard_map/ppermute | solution.py:54
  17.9 0.0 collective-permute-start.4
  17.9 0.8 %collective-permute-start.3 = (f32[41,128]{1,0:T(8,128)S(1)}, f32[41,128]{1,0:T(8,128)S(1)}, u32[]{:S(2)}, u32[]{:S(2)}) collective-permute-start(f32[41,128]{1,0:T(8,128)S(1)} %pad_maximum_fusion.5), channel_id=1, source_target_pairs={{0,4},{4,0},{8,12},{12,8},{1,5},{5,1},{9,13},{13,9},{2,6},{6,2},{1... | collective-permute-start | bytes 62984 | tf_op jit(solution)/shard_map/ppermute | solution.py:54
  18.7 0.5 %fusion.147 = f32[1,128]{1,0:T(1,128)} fusion(f32[101,128]{1,0:T(8,128)S(1)} %collective-permute-done.2, f32[101,128]{1,0:T(8,128)S(1)} %collective-permute-done.1, f32[165,128]{1,0:T(8,128)S(1)} %collective-permute-done, f32[128]{0:T(128)S(1)} %get-tuple-element.11), kind=kLoop, calls=%fused_computation.221 | loop fusion | flops 512 | bytes 2560 | tf_op jit(solution)/shard_map/mul | solution.py:191
  19.2 0.1 concatenate.40
  19.3 0.6 %collective-permute-done.5 = f32[41,128]{1,0:T(8,128)S(1)} collective-permute-done((f32[41,128]{1,0:T(8,128)S(1)}, f32[41,128]{1,0:T(8,128)S(1)}, u32[]{:S(2)}, u32[]{:S(2)}) %collective-permute-start.5) | collective-permute-done | bytes 21024 | tf_op jit(solution)/shard_map/ppermute | solution.py:54
  19.9 0.1 concatenate.43
  20.0 2.6 %collective-permute-done.4 = f32[41,128]{1,0:T(8,128)S(1)} collective-permute-done((f32[41,128]{1,0:T(8,128)S(1)}, f32[41,128]{1,0:T(8,128)S(1)}, u32[]{:S(2)}, u32[]{:S(2)}) %collective-permute-start.4) | collective-permute-done | bytes 21024 | tf_op jit(solution)/shard_map/ppermute | solution.py:54
  22.6 0.1 concatenate.42
  22.7 0.0 collective-permute-done.3
  22.7 0.1 concatenate.41
  22.8 0.1 multiply_reduce_fusion
  22.9 0.7 %multiply_bitcast_fusion = f32[576,2,48]{0,2,1:T(8,128)} fusion(f32[48,2,576]{2,0,1:T(8,128)S(1)} %multiply_reduce_fusion), kind=kLoop, calls=%fused_computation.14 | loop fusion | flops 55296 | bytes 442368 | tf_op jit(solution)/shard_map/mul | solution.py:194
  23.7 0.6 %fusion.110 = (f32[128,16]{0,1:T(8,128)}, f32[16,128]{1,0:T(8,128)}) fusion(f32[41,128]{1,0:T(8,128)S(1)} %collective-permute-done.5, f32[41,128]{1,0:T(8,128)S(1)} %collective-permute-done.4, f32[41,128]{1,0:T(8,128)S(1)} %collective-permute-done.3, f32[4,1,16,128]{3,2,0,1:T(8,128)S(1)} %bitcast_add_fusion, s32[]{:T(128)S(6)} %select_n.92, ...), kind=kLoop, calls=%fused_computation.146 | loop fusion | flops 16384 | bytes 81924 | tf_op jit(solution)/shard_map/mul | solution.py:193
  (39 shorter events, 0.3 us)
Async XLA Ops:
  0.6 2.1 %copy-start = (bf16[2,2,5,1,256,128]{5,4,3,2,1,0:T(8,128)(2,1)S(1)}, bf16[2,2,5,1,256,128]{5,4,3,2,1,0:T(8,128)(2,1)}, u32[]{:S(2)}) copy-start(bf16[2,2,5,1,256,128]{5,4,3,2,1,0:T(8,128)(2,1)} %param.3) | copy-start | bytes 3932164
  3.4 0.7 %copy-start.1 = (s32[2,2]{1,0:T(2,128)S(1)}, s32[2,2]{1,0:T(2,128)}, u32[]{:S(2)}) copy-start(s32[2,2]{1,0:T(2,128)} %param.5) | copy-start | bytes 52
  7.1 4.7 %collective-permute-start.2 = (f32[101,128]{1,0:T(8,128)S(1)}, f32[101,128]{1,0:T(8,128)S(1)}, u32[]{:S(2)}, u32[]{:S(2)}) collective-permute-start(f32[101,128]{1,0:T(8,128)S(1)} %get-tuple-element.28), channel_id=1, source_target_pairs={{0,3},{1,2},{2,1},{3,0},{4,7},{5,6},{6,5},{7,4},{8,11},{9,10},{10,... | collective-permute-start | bytes 155144 | tf_op jit(solution)/shard_map/ppermute | solution.py:54
  9.5 4.4 %collective-permute-start.1 = (f32[101,128]{1,0:T(8,128)S(1)}, f32[101,128]{1,0:T(8,128)S(1)}, u32[]{:S(2)}, u32[]{:S(2)}) collective-permute-start(f32[101,128]{1,0:T(8,128)S(1)} %get-tuple-element.27), channel_id=1, source_target_pairs={{0,2},{1,3},{2,0},{3,1},{4,6},{5,7},{6,4},{7,5},{8,10},{9,11},{10,... | collective-permute-start | bytes 155144 | tf_op jit(solution)/shard_map/ppermute | solution.py:54
  10.7 3.3 %collective-permute-start = (f32[165,128]{1,0:T(8,128)S(1)}, f32[165,128]{1,0:T(8,128)S(1)}, u32[]{:S(2)}, u32[]{:S(2)}) collective-permute-start(f32[165,128]{1,0:T(8,128)S(1)} %pad_maximum_fusion), channel_id=1, source_target_pairs={{0,1},{1,0},{2,3},{3,2},{4,5},{5,4},{6,7},{7,6},{8,9},{9,8},{10,11... | collective-permute-start | bytes 253448 | tf_op jit(solution)/shard_map/ppermute | solution.py:54
  14.2 5.7 %collective-permute-start.5 = (f32[41,128]{1,0:T(8,128)S(1)}, f32[41,128]{1,0:T(8,128)S(1)}, u32[]{:S(2)}, u32[]{:S(2)}) collective-permute-start(f32[41,128]{1,0:T(8,128)S(1)} %pad_maximum_fusion.7), channel_id=1, source_target_pairs={{0,12},{4,8},{8,4},{12,0},{1,13},{5,9},{9,5},{13,1},{2,14},{6,10},... | collective-permute-start | bytes 62984 | tf_op jit(solution)/shard_map/ppermute | solution.py:54
  17.9 4.7 %collective-permute-start.4 = (f32[41,128]{1,0:T(8,128)S(1)}, f32[41,128]{1,0:T(8,128)S(1)}, u32[]{:S(2)}, u32[]{:S(2)}) collective-permute-start(f32[41,128]{1,0:T(8,128)S(1)} %pad_maximum_fusion.6), channel_id=1, source_target_pairs={{0,8},{4,12},{8,0},{12,4},{1,9},{5,13},{9,1},{13,5},{2,10},{6,14},... | collective-permute-start | bytes 62984 | tf_op jit(solution)/shard_map/ppermute | solution.py:54
  17.9 4.8 %collective-permute-start.3 = (f32[41,128]{1,0:T(8,128)S(1)}, f32[41,128]{1,0:T(8,128)S(1)}, u32[]{:S(2)}, u32[]{:S(2)}) collective-permute-start(f32[41,128]{1,0:T(8,128)S(1)} %pad_maximum_fusion.5), channel_id=1, source_target_pairs={{0,4},{4,0},{8,12},{12,8},{1,5},{5,1},{9,13},{13,9},{2,6},{6,2},{1... | collective-permute-start | bytes 62984 | tf_op jit(solution)/shard_map/ppermute | solution.py:54

commit v18 on v17

--- a/solution.py
+++ b/solution.py
@@ -93,13 +93,28 @@
     )
     picks = jnp.where((flat_q // variables)[:, None, None] == slot[None], snapshot_ids[None], 0)
     q_ids = jnp.sum(picks, axis=(1, 2)) * variables + flat_q % variables
-    ax = test_table(x_ids, rank_ids, K, factor_stream, 1).astype(f32)
-    ay = test_table(y_ids, rank_ids, K, factor_stream, 2)
-    az = test_table(z_ids, rank_ids, K, factor_stream, 3)
-    aq = test_table(q_ids, rank_ids, K, factor_stream, 4).astype(f32)
-    phy = test_table(sketch_ids, y_ids, cells_y, core_stream, 6).astype(f32)
-    phz = test_table(sketch_ids, z_ids, total_z, core_stream, 7)
-    phq = test_table(q_ids, jnp.arange(E, dtype=jnp.int32), E, core_stream, 8).astype(f32)
+    src_gx = jnp.bitwise_xor(gx_me, jnp.arange(n_gx, dtype=jnp.int32))
+    x_src = (src_gx[:, None] * cells_x + jnp.arange(cells_x, dtype=jnp.int32)[None, :]).reshape(-1)
+    cols = [rank_ids, rank_ids, rank_ids, rank_ids, y_ids, z_ids, jnp.arange(E, dtype=jnp.int32), x_src]
+    width = max(c.shape[0] for c in cols)
+    ids = jnp.stack([jnp.pad(c, (0, width - c.shape[0])) for c in cols])
+    salts = jnp.array([1, 2, 3, 4, 6, 7, 8, 5], jnp.int32)[:, None]
+    streams = jnp.where(jnp.arange(8, dtype=jnp.int32)[:, None] < 4, test_streams[0], test_streams[1])
+    terms = ids * -1640531535 + streams * -2048144777 + salts
+
+    def table(row_ids, stride, r):
+        row_term = (row_ids * stride) * -1640531535
+        upper = lax.shift_right_logical(mix_bits(row_term[:, None] + terms[r, None, : cols[r].shape[0]]), jnp.int32(9))
+        return ((2 * upper + 1).astype(f32) * 2.0 ** (-24) - 1.0).astype(bf16)
+
+    ax = table(x_ids, K, 0).astype(f32)
+    ay = table(y_ids, K, 1)
+    az = table(z_ids, K, 2)
+    aq = table(q_ids, K, 3).astype(f32)
+    phy = table(sketch_ids, cells_y, 4).astype(f32)
+    phz = table(sketch_ids, total_z, 5)
+    phq = table(q_ids, E, 6).astype(f32)
+    phx = table(sketch_ids, total_x, 7).astype(f32).reshape(S, n_gx, cells_x)
 
     n_q = batches * local_snaps * variables
     field = flow_field.reshape(n_q, cells_x, cells_y, cells_z)
@@ -176,9 +191,6 @@
         sy, sz = sy_total, sz_total
         core = jnp.concatenate(core_parts, axis=0)
 
-    src = jnp.bitwise_xor(gx_me, jnp.arange(n_gx, dtype=jnp.int32))
-    x_src = (src[:, None] * cells_x + jnp.arange(cells_x, dtype=jnp.int32)[None, :]).reshape(-1)
-    phx = test_table(sketch_ids, x_src, total_x, core_stream, 5).astype(f32).reshape(S, n_gx, cells_x)
     held = core.reshape(n_gx * cells_x, E, core_rows)
     weights_x = phx.reshape(S, n_gx * cells_x)
     core_out = jnp.sum(held[:, None, :, :] * weights_x.T[:, :, None, None], axis=0).transpose(2, 1, 0)

time: 24.5 us -> 26.1 us (1.065)
  other arithmetic: 3.13 us -> 5.12 us
  between operations: 2.29 us -> 1.02 us
  local copies, waits for them, and re-layouts: 2.81 us -> 3.7 us
    mul x10 -> x6, other arithmetic: 0.05 us -> 1.32 us  [the longest x1 1.29 us: shards(): terms = ids * -1640531535 + streams * -2048144777 + salts]
    another operation x1 -> x2, local copies, waits for them, and re-layouts: 0.16 us -> 1.02 us  [the longest x1 0.85 us: shards(): ids = jnp.stack([jnp.pad(c, (0, width - c.shape[0])) for c in cols])]
    add x0 -> x2, other arithmetic: none -> 0.73 us  [the longest x1 0.73 us: shards(): terms = ids * -1640531535 + streams * -2048144777 + salts]
    slice x1 -> x2, local copies, waits for them, and re-layouts: 1.34 us -> 1.34 us  [the longest x1 1.34 us: shards(): test_streams[0]]
where the time goes in v18:
time: 26.1 us; the launch traced here: 25.9 us
  starting transfers between devices  7.63 us (29%)
  waiting for transfers between devices  6.18 us (24%)
  other arithmetic  5.12 us (20%)
  local copies, waits for them, and re-layouts  3.7 us (14%)
  matrix products  2.23 us (9%)
  between operations  1.02 us (4%)
    ppermute x6, starting transfers between devices, send_to(): got = lax.ppermute(flat, axes, [(i, i ^ shift) for i in range(n)])  7.63 us
    ppermute x6, waiting for transfers between devices, send_to(): got = lax.ppermute(flat, axes, [(i, i ^ shift) for i in range(n)])  6.18 us
    slice x1, local copies, waits for them, and re-layouts, shards(): test_streams[0]  1.34 us
    mul x1, other arithmetic, shards(): terms = ids * -1640531535 + streams * -2048144777 + salts  1.29 us
    another operation x1, local copies, waits for them, and re-layouts, shards(): ids = jnp.stack([jnp.pad(c, (0, width - c.shape[0])) for c in cols])  0.85 us
    add x1, other arithmetic, shards(): terms = ids * -1640531535 + streams * -2048144777 + salts  0.73 us
    mul x1, other arithmetic, shards(): core_out * scale_core  0.72 us
    mul x1, other arithmetic, shards(): sz.reshape(cols_each, cells_z).T * scale_z  0.61 us
  transfers between devices with their start and end apart: 6, of which 4 were waited for; matrix products, arithmetic and copies ran while one was open for 6% of the time, Pallas kernels for 0%

profile of v18, /device:TPU:0, one launch (start us, length us, event | category | flops | bytes accessed | tf_op | source)
XLA Modules:
  0.0 25.9 jit_solution(2096631767925323125)
XLA Ops:
  0.6 0.0 copy-start
  0.7 1.3 %fusion.197 = (s32[1]{0:T(128)}, s32[1]{0:T(128)}) fusion(s32[2]{0:T(128)} %param.5), kind=kLoop, calls=%fused_computation.288 | loop fusion | bytes 16 | tf_op jit(solution)/shard_map/slice | solution.py:102
  2.1 1.3 %fusion.145 = s32[8]{0:T(128)S(1)} fusion(s32[]{:T(128)} %bitcast.3, s32[]{:T(128)} %bitcast.2), kind=kLoop, calls=%fused_computation.219 | loop fusion | flops 24 | bytes 40 | tf_op jit(solution)/shard_map/mul | solution.py:103
  3.4 0.9 %stack.8 = s32[8,256]{1,0:T(8,128)S(1)} concatenate(s32[1,256]{1,0:T(1,128)} %constant.104.clone.1, s32[1,256]{1,0:T(1,128)} %constant.104.clone.1, s32[1,256]{1,0:T(1,128)} %constant.104.clone.1, s32[1,256]{1,0:T(1,128)} %constant.104.clone.1, s32[1,256]{1,0:T(1,128)S(1)} %iota.62, s32[1,256]{1,0:T(1,128)S(1)} %bitcast.132, s32[1,256]{1,0:T(1,128)} %constant.109.clone.1, ...), dimensions={0} | concatenate | bytes 16384 | tf_op jit(solution)/shard_map/stack | solution.py:100
  4.2 0.7 %add_add_fusion.1 = s32[8,256]{1,0:T(8,128)S(1)} fusion(s32[8,256]{1,0:T(8,128)S(1)} %stack.8, s32[8]{0:T(128)} %constant.250.clone, s32[8]{0:T(128)S(1)} %fusion.145), kind=kLoop, calls=%fused_computation.156 | loop fusion | flops 6144 | bytes 16448 | tf_op jit(solution)/shard_map/add | solution.py:103
  5.0 0.0 copy-done
  5.0 0.6 %convolution_bitcast_fusion = f32[5120,48]{0,1:T(8,128)S(1)} fusion(bf16[5120,128]{1,0:T(8,128)(2,1)S(1)} %bitcast.111, s32[128]{0:T(128)S(1)} %get-tuple-element.30, s32[48]{0:T(128)S(1)} %iota_multiply_fusion.2), kind=kOutput, calls=%fused_computation | convolution fusion | flops 63012864 | bytes 2294464 | tf_op jit(solution)/shard_map/dot_general | solution.py:135
  5.6 0.0 copy-start.1
  5.7 0.2 reshape.645
  5.8 0.1 iota_add_fusion
  5.9 0.4 %copy-done.1 = s32[2,2]{1,0:T(2,128)S(1)} copy-done((s32[2,2]{1,0:T(2,128)S(1)}, s32[2,2]{1,0:T(2,128)}, u32[]{:S(2)}) %copy-start.1) | copy-done | bytes 40
  6.3 0.1 fusion.118
  6.4 0.4 %fusion.132 = f32[2,256,48]{1,0,2:T(2,128)S(1)} fusion(f32[20,256,48]{1,0,2:T(8,128)S(1)} %reshape.645, s32[20]{0:T(128)S(1)} %broadcast_multiply_fusion.2, s32[2]{0:T(128)S(1)} %slice_bitcast_fusion.2), kind=kOutput, calls=%fused_computation.207 | convolution fusion | flops 2949760 | bytes 1081432 | tf_op jit(solution)/shard_map/qxyn,qe->xeyn/dot_general | solution.py:137
  6.8 0.2 convolution_bitcast_fusion.2
  7.1 0.1 copy.15
  7.2 0.1 reshape.646
  7.3 0.1 reshape_reshape.16
  7.4 0.1 fusion.60
  7.5 0.1 broadcast_multiply_fusion.1
  7.6 0.3 %multiply_convert_fusion = (bf16[20,128,128]{2,1,0:T(8,128)(2,1)S(1)}, bf16[20,128,128]{2,1,0:T(8,128)(2,1)S(1)}) fusion(f32[128,128]{1,0:T(8,128)S(1)} %fusion.60, f32[20,128]{1,0:T(8,128)S(1)} %get-tuple-element.34), kind=kLoop, calls=%fused_computation.2 | loop fusion | flops 1638400 | bytes 1386496 | tf_op jit(solution)/shard_map/convert_element_type | solution.py:124
  7.9 0.5 %fusion.7 = f32[1,256,256]{2,1,0:T(8,128)S(1)} fusion(bf16[20,256,128]{2,1,0:T(8,128)(2,1)S(1)} %bitcast.112, bf16[20,128,128]{2,1,0:T(8,128)(2,1)S(1)} %get-tuple-element.18, bf16[20,128,128]{2,1,0:T(8,128)(2,1)S(1)} %get-tuple-element.17), kind=kOutput, calls=%fused_computation.11 | convolution fusion | flops 338165760 | bytes 2883584 | tf_op jit(solution)/shard_map/qxyz,qzk->xyk/dot_general | solution.py:126
  8.5 0.2 broadcast_multiply_fusion
  8.7 2.4 %collective-permute-start.2 = (f32[101,128]{1,0:T(8,128)S(1)}, f32[101,128]{1,0:T(8,128)S(1)}, u32[]{:S(2)}, u32[]{:S(2)}) collective-permute-start(f32[101,128]{1,0:T(8,128)S(1)} %get-tuple-element.28), channel_id=1, source_target_pairs={{0,3},{1,2},{2,1},{3,0},{4,7},{5,6},{6,5},{7,4},{8,11},{9,10},{10,... | collective-permute-start | bytes 155144 | tf_op jit(solution)/shard_map/ppermute | solution.py:54
  11.1 0.6 %collective-permute-start.1 = (f32[101,128]{1,0:T(8,128)S(1)}, f32[101,128]{1,0:T(8,128)S(1)}, u32[]{:S(2)}, u32[]{:S(2)}) collective-permute-start(f32[101,128]{1,0:T(8,128)S(1)} %get-tuple-element.27), channel_id=1, source_target_pairs={{0,2},{1,3},{2,0},{3,1},{4,6},{5,7},{6,4},{7,5},{8,10},{9,11},{10,... | collective-permute-start | bytes 155144 | tf_op jit(solution)/shard_map/ppermute | solution.py:54
  11.7 0.5 %fusion.6 = f32[128,128]{0,1:T(8,128)S(1)} fusion(bf16[20,256,128]{2,1,0:T(8,128)(2,1)S(1)} %bitcast.113, f32[20,128]{1,0:T(8,128)S(1)} %get-tuple-element.33, s32[128]{0:T(128)S(1)} %get-tuple-element.31, s32[256]{0:T(256)S(1)} %iota_multiply_fusion), kind=kOutput, calls=%fused_computation.10 | convolution fusion | flops 168935424 | bytes 1388032 | tf_op jit(solution)/shard_map/qxyz,yk->qxzk/dot_general | solution.py:132
  12.3 0.1 collective-permute-start
  12.4 0.1 fusion.120
  12.5 0.1 reshape.656
  12.6 0.7 %collective-permute-done.2 = f32[101,128]{1,0:T(8,128)S(1)} collective-permute-done((f32[101,128]{1,0:T(8,128)S(1)}, f32[101,128]{1,0:T(8,128)S(1)}, u32[]{:S(2)}, u32[]{:S(2)}) %collective-permute-start.2) | collective-permute-done | bytes 51744 | tf_op jit(solution)/shard_map/ppermute | solution.py:54
  13.3 2.2 %collective-permute-done.1 = f32[101,128]{1,0:T(8,128)S(1)} collective-permute-done((f32[101,128]{1,0:T(8,128)S(1)}, f32[101,128]{1,0:T(8,128)S(1)}, u32[]{:S(2)}, u32[]{:S(2)}) %collective-permute-start.1) | collective-permute-done | bytes 51744 | tf_op jit(solution)/shard_map/ppermute | solution.py:54
  15.6 0.0 collective-permute-done
  15.7 0.1 dynamic-slice_reduce_fusion
  15.8 3.7 %collective-permute-start.5 = (f32[41,128]{1,0:T(8,128)S(1)}, f32[41,128]{1,0:T(8,128)S(1)}, u32[]{:S(2)}, u32[]{:S(2)}) collective-permute-start(f32[41,128]{1,0:T(8,128)S(1)} %pad_maximum_fusion.7), channel_id=1, source_target_pairs={{0,12},{4,8},{8,4},{12,0},{1,13},{5,9},{9,5},{13,1},{2,14},{6,10},... | collective-permute-start | bytes 62984 | tf_op jit(solution)/shard_map/ppermute | solution.py:54
  19.5 0.0 collective-permute-start.4
  19.5 0.8 %collective-permute-start.3 = (f32[41,128]{1,0:T(8,128)S(1)}, f32[41,128]{1,0:T(8,128)S(1)}, u32[]{:S(2)}, u32[]{:S(2)}) collective-permute-start(f32[41,128]{1,0:T(8,128)S(1)} %pad_maximum_fusion.5), channel_id=1, source_target_pairs={{0,4},{4,0},{8,12},{12,8},{1,5},{5,1},{9,13},{13,9},{2,6},{6,2},{1... | collective-permute-start | bytes 62984 | tf_op jit(solution)/shard_map/ppermute | solution.py:54
  20.3 0.5 %fusion.146 = f32[1,128]{1,0:T(1,128)} fusion(f32[101,128]{1,0:T(8,128)S(1)} %collective-permute-done.2, f32[101,128]{1,0:T(8,128)S(1)} %collective-permute-done.1, f32[165,128]{1,0:T(8,128)S(1)} %collective-permute-done, f32[128]{0:T(128)S(1)} %get-tuple-element.11), kind=kLoop, calls=%fused_computation.222 | loop fusion | flops 512 | bytes 2560 | tf_op jit(solution)/shard_map/mul | solution.py:203
  20.8 0.1 concatenate.40
  20.9 0.6 %collective-permute-done.5 = f32[41,128]{1,0:T(8,128)S(1)} collective-permute-done((f32[41,128]{1,0:T(8,128)S(1)}, f32[41,128]{1,0:T(8,128)S(1)}, u32[]{:S(2)}, u32[]{:S(2)}) %collective-permute-start.5) | collective-permute-done | bytes 21024 | tf_op jit(solution)/shard_map/ppermute | solution.py:54
  21.5 0.1 concatenate.43
  21.6 2.6 %collective-permute-done.4 = f32[41,128]{1,0:T(8,128)S(1)} collective-permute-done((f32[41,128]{1,0:T(8,128)S(1)}, f32[41,128]{1,0:T(8,128)S(1)}, u32[]{:S(2)}, u32[]{:S(2)}) %collective-permute-start.4) | collective-permute-done | bytes 21024 | tf_op jit(solution)/shard_map/ppermute | solution.py:54
  24.2 0.1 concatenate.42
  24.3 0.0 collective-permute-done.3
  24.3 0.1 concatenate.41
  24.4 0.1 multiply_reduce_fusion
  24.5 0.7 %multiply_bitcast_fusion = f32[576,2,48]{0,2,1:T(8,128)} fusion(f32[48,2,576]{2,0,1:T(8,128)S(1)} %multiply_reduce_fusion), kind=kLoop, calls=%fused_computation.14 | loop fusion | flops 55296 | bytes 442368 | tf_op jit(solution)/shard_map/mul | solution.py:206
  25.3 0.6 %fusion.107 = (f32[128,16]{0,1:T(8,128)}, f32[16,128]{1,0:T(8,128)}) fusion(f32[41,128]{1,0:T(8,128)S(1)} %collective-permute-done.5, f32[41,128]{1,0:T(8,128)S(1)} %collective-permute-done.4, f32[41,128]{1,0:T(8,128)S(1)} %collective-permute-done.3, f32[4,1,16,128]{3,2,0,1:T(8,128)S(1)} %bitcast_add_fusion, s32[]{:T(128)S(6)} %select_n.102, ...), kind=kLoop, calls=%fused_computation.143 | loop fusion | flops 16384 | bytes 81924 | tf_op jit(solution)/shard_map/mul | solution.py:205
  (43 shorter events, 0.3 us)
Async XLA Ops:
  0.6 4.4 %copy-start = (bf16[2,2,5,1,256,128]{5,4,3,2,1,0:T(8,128)(2,1)S(1)}, bf16[2,2,5,1,256,128]{5,4,3,2,1,0:T(8,128)(2,1)}, u32[]{:S(2)}) copy-start(bf16[2,2,5,1,256,128]{5,4,3,2,1,0:T(8,128)(2,1)} %param.4) | copy-start | bytes 3932164
  5.6 0.7 %copy-start.1 = (s32[2,2]{1,0:T(2,128)S(1)}, s32[2,2]{1,0:T(2,128)}, u32[]{:S(2)}) copy-start(s32[2,2]{1,0:T(2,128)} %param.6) | copy-start | bytes 52
  8.7 4.7 %collective-permute-start.2 = (f32[101,128]{1,0:T(8,128)S(1)}, f32[101,128]{1,0:T(8,128)S(1)}, u32[]{:S(2)}, u32[]{:S(2)}) collective-permute-start(f32[101,128]{1,0:T(8,128)S(1)} %get-tuple-element.28), channel_id=1, source_target_pairs={{0,3},{1,2},{2,1},{3,0},{4,7},{5,6},{6,5},{7,4},{8,11},{9,10},{10,... | collective-permute-start | bytes 155144 | tf_op jit(solution)/shard_map/ppermute | solution.py:54
  11.1 4.4 %collective-permute-start.1 = (f32[101,128]{1,0:T(8,128)S(1)}, f32[101,128]{1,0:T(8,128)S(1)}, u32[]{:S(2)}, u32[]{:S(2)}) collective-permute-start(f32[101,128]{1,0:T(8,128)S(1)} %get-tuple-element.27), channel_id=1, source_target_pairs={{0,2},{1,3},{2,0},{3,1},{4,6},{5,7},{6,4},{7,5},{8,10},{9,11},{10,... | collective-permute-start | bytes 155144 | tf_op jit(solution)/shard_map/ppermute | solution.py:54
  12.3 3.3 %collective-permute-start = (f32[165,128]{1,0:T(8,128)S(1)}, f32[165,128]{1,0:T(8,128)S(1)}, u32[]{:S(2)}, u32[]{:S(2)}) collective-permute-start(f32[165,128]{1,0:T(8,128)S(1)} %pad_maximum_fusion), channel_id=1, source_target_pairs={{0,1},{1,0},{2,3},{3,2},{4,5},{5,4},{6,7},{7,6},{8,9},{9,8},{10,11... | collective-permute-start | bytes 253448 | tf_op jit(solution)/shard_map/ppermute | solution.py:54
  15.8 5.7 %collective-permute-start.5 = (f32[41,128]{1,0:T(8,128)S(1)}, f32[41,128]{1,0:T(8,128)S(1)}, u32[]{:S(2)}, u32[]{:S(2)}) collective-permute-start(f32[41,128]{1,0:T(8,128)S(1)} %pad_maximum_fusion.7), channel_id=1, source_target_pairs={{0,12},{4,8},{8,4},{12,0},{1,13},{5,9},{9,5},{13,1},{2,14},{6,10},... | collective-permute-start | bytes 62984 | tf_op jit(solution)/shard_map/ppermute | solution.py:54
  19.5 4.7 %collective-permute-start.4 = (f32[41,128]{1,0:T(8,128)S(1)}, f32[41,128]{1,0:T(8,128)S(1)}, u32[]{:S(2)}, u32[]{:S(2)}) collective-permute-start(f32[41,128]{1,0:T(8,128)S(1)} %pad_maximum_fusion.6), channel_id=1, source_target_pairs={{0,8},{4,12},{8,0},{12,4},{1,9},{5,13},{9,1},{13,5},{2,10},{6,14},... | collective-permute-start | bytes 62984 | tf_op jit(solution)/shard_map/ppermute | solution.py:54
  19.5 4.8 %collective-permute-start.3 = (f32[41,128]{1,0:T(8,128)S(1)}, f32[41,128]{1,0:T(8,128)S(1)}, u32[]{:S(2)}, u32[]{:S(2)}) collective-permute-start(f32[41,128]{1,0:T(8,128)S(1)} %pad_maximum_fusion.5), channel_id=1, source_target_pairs={{0,4},{4,0},{8,12},{12,8},{1,5},{5,1},{9,13},{13,9},{2,6},{6,2},{1... | collective-permute-start | bytes 62984 | tf_op jit(solution)/shard_map/ppermute | solution.py:54

commit v19 on v17

--- a/solution.py
+++ b/solution.py
@@ -163,6 +163,10 @@
         sy, sx, core = sy_total, sx_total, core_total
         if with_sz:
             sz = sz_total
+    src = jnp.bitwise_xor(gx_me, jnp.arange(n_gx, dtype=jnp.int32))
+    x_src = (src[:, None] * cells_x + jnp.arange(cells_x, dtype=jnp.int32)[None, :]).reshape(-1)
+    phx = test_table(sketch_ids, x_src, total_x, core_stream, 5).astype(f32).reshape(S, n_gx, cells_x)
+    core, phx = lax.optimization_barrier((core, phx))
     for d, r in digit_steps(n_gx):
         digit = (gx_me // d) % r
         at_y = split_digit(sy, 0, r, digit)
@@ -176,9 +180,6 @@
         sy, sz = sy_total, sz_total
         core = jnp.concatenate(core_parts, axis=0)
 
-    src = jnp.bitwise_xor(gx_me, jnp.arange(n_gx, dtype=jnp.int32))
-    x_src = (src[:, None] * cells_x + jnp.arange(cells_x, dtype=jnp.int32)[None, :]).reshape(-1)
-    phx = test_table(sketch_ids, x_src, total_x, core_stream, 5).astype(f32).reshape(S, n_gx, cells_x)
     held = core.reshape(n_gx * cells_x, E, core_rows)
     weights_x = phx.reshape(S, n_gx * cells_x)
     core_out = jnp.sum(held[:, None, :, :] * weights_x.T[:, :, None, None], axis=0).transpose(2, 1, 0)

time: 24.5 us -> 24.5 us (level)
  no operation moved by 1% of the time
where the time goes in v19:
time: 24.5 us; the launch traced here: 24.3 us
  starting transfers between devices  7.64 us (31%)
  waiting for transfers between devices  6.17 us (25%)
  other arithmetic  3.13 us (13%)
  local copies, waits for them, and re-layouts  2.81 us (11%)
  between operations  2.29 us (9%)
  matrix products  2.23 us (9%)
    ppermute x6, starting transfers between devices, send_to(): got = lax.ppermute(flat, axes, [(i, i ^ shift) for i in range(n)])  7.64 us
    ppermute x6, waiting for transfers between devices, send_to(): got = lax.ppermute(flat, axes, [(i, i ^ shift) for i in range(n)])  6.17 us
    slice x1, local copies, waits for them, and re-layouts, shards(): factor_stream = test_streams[0]  1.34 us
    mul x1, other arithmetic, shards(): core_out * scale_core  0.72 us
    mul x1, other arithmetic, shards(): sz.reshape(cols_each, cells_z).T * scale_z  0.61 us
    dot_general x1, matrix products, shards(): jnp.dot(rows_z, phz.T, preferred_element_type=f32)  0.6 us
    mul x1, other arithmetic, shards(): sx * scale_x  0.52 us
    dot_general x1, matrix products, shards(): jnp.einsum('qxyz,qzk->xyk', field, jnp.concatenate([qz_hi, qz_lo], axis=-...  0.5 us
  transfers between devices with their start and end apart: 6, of which 4 were waited for; matrix products, arithmetic and copies ran while one was open for 6% of the time, Pallas kernels for 0%

profile of v19, /device:TPU:0, one launch (start us, length us, event | category | flops | bytes accessed | tf_op | source)
XLA Modules:
  0.0 24.3 jit_solution(13885593374490823583)
XLA Ops:
  0.6 0.0 copy-start
  0.8 1.3 %fusion.201 = (s32[1]{0:T(128)}, s32[1]{0:T(128)}) fusion(s32[2]{0:T(128)} %param.4), kind=kLoop, calls=%fused_computation.285 | loop fusion | bytes 16 | tf_op jit(solution)/shard_map/slice | solution.py:81
  2.7 0.0 copy-done
  2.8 0.6 %convolution_bitcast_fusion = f32[5120,48]{0,1:T(8,128)S(1)} fusion(bf16[5120,128]{1,0:T(8,128)(2,1)S(1)} %bitcast.100, s32[]{:T(128)} %bitcast.15, s32[128]{0:T(128)S(1)} %get-tuple-element.37, s32[48]{0:T(128)S(1)} %iota_multiply_fusion.3), kind=kOutput, calls=%fused_computation | convolution fusion | flops 63019008 | bytes 2294468 | tf_op jit(solution)/shard_map/dot_general | solution.py:120
  3.4 0.0 copy-start.1
  3.4 0.2 reshape.769
  3.5 0.1 iota_add_fusion
  3.6 0.4 %copy-done.1 = s32[2,2]{1,0:T(2,128)S(1)} copy-done((s32[2,2]{1,0:T(2,128)S(1)}, s32[2,2]{1,0:T(2,128)}, u32[]{:S(2)}) %copy-start.1) | copy-done | bytes 40
  4.0 0.1 fusion.121
  4.2 0.4 %fusion.135 = f32[2,256,48]{1,0,2:T(2,128)S(1)} fusion(f32[20,256,48]{1,0,2:T(8,128)S(1)} %reshape.769, s32[]{:T(128)} %bitcast.13, s32[20]{0:T(128)S(1)} %broadcast_multiply_fusion.2, s32[2]{0:T(128)S(1)} %iota_multiply_fusion.4), kind=kOutput, calls=%fused_computation.209 | convolution fusion | flops 2949800 | bytes 1081436 | tf_op jit(solution)/shard_map/qxyn,qe->xeyn/dot_general | solution.py:122
  4.5 0.3 %convolution_bitcast_fusion.2 = f32[1,2,48,48]{2,3,1,0:T(8,128)S(1)} fusion(f32[2,256,48]{1,0,2:T(2,128)S(1)} %fusion.135, s32[]{:T(128)} %bitcast.18, s32[256]{0:T(256)S(1)} %iota_multiply_fusion, s32[48]{0:T(128)S(1)} %iota_multiply_fusion.3), kind=kOutput, calls=%fused_computation.12 | convolution fusion | flops 7286784 | bytes 117956 | tf_op jit(solution)/shard_map/my,xeyn->xemn/dot_general | solution.py:123
  4.8 0.1 copy.15
  4.9 0.1 reshape.770
  5.0 0.1 reshape_reshape.16
  5.8 0.1 fusion.61
  5.9 0.1 broadcast_multiply_fusion.1
  6.0 0.3 %multiply_convert_fusion = (bf16[20,128,128]{2,1,0:T(8,128)(2,1)S(1)}, bf16[20,128,128]{2,1,0:T(8,128)(2,1)S(1)}) fusion(f32[128,128]{1,0:T(8,128)S(1)} %fusion.61, f32[20,128]{1,0:T(8,128)S(1)} %get-tuple-element.34), kind=kLoop, calls=%fused_computation.2 | loop fusion | flops 1638400 | bytes 1386496 | tf_op jit(solution)/shard_map/convert_element_type | solution.py:109
  6.3 0.5 %fusion.7 = f32[1,256,256]{2,1,0:T(8,128)S(1)} fusion(bf16[20,256,128]{2,1,0:T(8,128)(2,1)S(1)} %bitcast.101, bf16[20,128,128]{2,1,0:T(8,128)(2,1)S(1)} %get-tuple-element.22, bf16[20,128,128]{2,1,0:T(8,128)(2,1)S(1)} %get-tuple-element.21), kind=kOutput, calls=%fused_computation.11 | convolution fusion | flops 338165760 | bytes 2883584 | tf_op jit(solution)/shard_map/qxyz,qzk->xyk/dot_general | solution.py:111
  6.8 0.2 broadcast_multiply_fusion
  7.1 2.4 %collective-permute-start.2 = (f32[101,128]{1,0:T(8,128)S(1)}, f32[101,128]{1,0:T(8,128)S(1)}, u32[]{:S(2)}, u32[]{:S(2)}) collective-permute-start(f32[101,128]{1,0:T(8,128)S(1)} %get-tuple-element.32), channel_id=1, source_target_pairs={{0,3},{1,2},{2,1},{3,0},{4,7},{5,6},{6,5},{7,4},{8,11},{9,10},{10,... | collective-permute-start | bytes 155144 | tf_op jit(solution)/shard_map/ppermute | solution.py:54
  9.5 0.6 %collective-permute-start.1 = (f32[101,128]{1,0:T(8,128)S(1)}, f32[101,128]{1,0:T(8,128)S(1)}, u32[]{:S(2)}, u32[]{:S(2)}) collective-permute-start(f32[101,128]{1,0:T(8,128)S(1)} %get-tuple-element.31), channel_id=1, source_target_pairs={{0,2},{1,3},{2,0},{3,1},{4,6},{5,7},{6,4},{7,5},{8,10},{9,11},{10,... | collective-permute-start | bytes 155144 | tf_op jit(solution)/shard_map/ppermute | solution.py:54
  10.1 0.5 %fusion.6 = f32[128,128]{0,1:T(8,128)S(1)} fusion(bf16[20,256,128]{2,1,0:T(8,128)(2,1)S(1)} %bitcast.102, f32[20,128]{1,0:T(8,128)S(1)} %get-tuple-element.33, s32[]{:T(128)} %bitcast.8, s32[128]{0:T(128)S(1)} %iota_multiply_fusion.5, s32[256]{0:T(256)S(1)} %iota_multiply_fusion.1), kind=kOutput, calls=%fused_computation.10 | convolution fusion | flops 168968192 | bytes 1388036 | tf_op jit(solution)/shard_map/qxyz,yk->qxzk/dot_general | solution.py:117
  10.7 0.1 collective-permute-start
  10.8 0.1 fusion.123
  10.9 0.1 reshape.780
  11.0 0.7 %collective-permute-done.2 = f32[101,128]{1,0:T(8,128)S(1)} collective-permute-done((f32[101,128]{1,0:T(8,128)S(1)}, f32[101,128]{1,0:T(8,128)S(1)}, u32[]{:S(2)}, u32[]{:S(2)}) %collective-permute-start.2) | collective-permute-done | bytes 51744 | tf_op jit(solution)/shard_map/ppermute | solution.py:54
  11.7 2.2 %collective-permute-done.1 = f32[101,128]{1,0:T(8,128)S(1)} collective-permute-done((f32[101,128]{1,0:T(8,128)S(1)}, f32[101,128]{1,0:T(8,128)S(1)}, u32[]{:S(2)}, u32[]{:S(2)}) %collective-permute-start.1) | collective-permute-done | bytes 51744 | tf_op jit(solution)/shard_map/ppermute | solution.py:54
  14.0 0.0 collective-permute-done
  14.1 0.1 dynamic-slice_reduce_fusion
  14.2 3.7 %collective-permute-start.5 = (f32[41,128]{1,0:T(8,128)S(1)}, f32[41,128]{1,0:T(8,128)S(1)}, u32[]{:S(2)}, u32[]{:S(2)}) collective-permute-start(f32[41,128]{1,0:T(8,128)S(1)} %pad_maximum_fusion.7), channel_id=1, source_target_pairs={{0,12},{4,8},{8,4},{12,0},{1,13},{5,9},{9,5},{13,1},{2,14},{6,10},... | collective-permute-start | bytes 62984 | tf_op jit(solution)/shard_map/ppermute | solution.py:54
  17.9 0.0 collective-permute-start.4
  17.9 0.8 %collective-permute-start.3 = (f32[41,128]{1,0:T(8,128)S(1)}, f32[41,128]{1,0:T(8,128)S(1)}, u32[]{:S(2)}, u32[]{:S(2)}) collective-permute-start(f32[41,128]{1,0:T(8,128)S(1)} %pad_maximum_fusion.5), channel_id=1, source_target_pairs={{0,4},{4,0},{8,12},{12,8},{1,5},{5,1},{9,13},{13,9},{2,6},{6,2},{1... | collective-permute-start | bytes 62984 | tf_op jit(solution)/shard_map/ppermute | solution.py:54
  18.7 0.5 %fusion.147 = f32[1,128]{1,0:T(1,128)} fusion(f32[101,128]{1,0:T(8,128)S(1)} %collective-permute-done.2, f32[101,128]{1,0:T(8,128)S(1)} %collective-permute-done.1, f32[165,128]{1,0:T(8,128)S(1)} %collective-permute-done, f32[128]{0:T(128)S(1)} %get-tuple-element.15), kind=kLoop, calls=%fused_computation.221 | loop fusion | flops 512 | bytes 2560 | tf_op jit(solution)/shard_map/mul | solution.py:192
  19.2 0.1 concatenate.40
  19.3 0.6 %collective-permute-done.5 = f32[41,128]{1,0:T(8,128)S(1)} collective-permute-done((f32[41,128]{1,0:T(8,128)S(1)}, f32[41,128]{1,0:T(8,128)S(1)}, u32[]{:S(2)}, u32[]{:S(2)}) %collective-permute-start.5) | collective-permute-done | bytes 21024 | tf_op jit(solution)/shard_map/ppermute | solution.py:54
  19.9 0.1 concatenate.43
  20.0 2.6 %collective-permute-done.4 = f32[41,128]{1,0:T(8,128)S(1)} collective-permute-done((f32[41,128]{1,0:T(8,128)S(1)}, f32[41,128]{1,0:T(8,128)S(1)}, u32[]{:S(2)}, u32[]{:S(2)}) %collective-permute-start.4) | collective-permute-done | bytes 21024 | tf_op jit(solution)/shard_map/ppermute | solution.py:54
  22.6 0.1 concatenate.42
  22.7 0.0 collective-permute-done.3
  22.7 0.1 concatenate.41
  22.8 0.1 multiply_reduce_fusion
  22.9 0.7 %multiply_bitcast_fusion = f32[576,2,48]{0,2,1:T(8,128)} fusion(f32[48,2,576]{2,0,1:T(8,128)S(1)} %multiply_reduce_fusion), kind=kLoop, calls=%fused_computation.14 | loop fusion | flops 55296 | bytes 442368 | tf_op jit(solution)/shard_map/mul | solution.py:195
  23.7 0.6 %fusion.110 = (f32[128,16]{0,1:T(8,128)}, f32[16,128]{1,0:T(8,128)}) fusion(f32[41,128]{1,0:T(8,128)S(1)} %collective-permute-done.5, f32[41,128]{1,0:T(8,128)S(1)} %collective-permute-done.4, f32[41,128]{1,0:T(8,128)S(1)} %collective-permute-done.3, f32[4,1,16,128]{3,2,0,1:T(8,128)S(1)} %bitcast_add_fusion, s32[]{:T(128)S(6)} %select_n.92, ...), kind=kLoop, calls=%fused_computation.146 | loop fusion | flops 16384 | bytes 81924 | tf_op jit(solution)/shard_map/mul | solution.py:194
  (39 shorter events, 0.3 us)
Async XLA Ops:
  0.6 2.1 %copy-start = (bf16[2,2,5,1,256,128]{5,4,3,2,1,0:T(8,128)(2,1)S(1)}, bf16[2,2,5,1,256,128]{5,4,3,2,1,0:T(8,128)(2,1)}, u32[]{:S(2)}) copy-start(bf16[2,2,5,1,256,128]{5,4,3,2,1,0:T(8,128)(2,1)} %param.3) | copy-start | bytes 3932164
  3.4 0.7 %copy-start.1 = (s32[2,2]{1,0:T(2,128)S(1)}, s32[2,2]{1,0:T(2,128)}, u32[]{:S(2)}) copy-start(s32[2,2]{1,0:T(2,128)} %param.5) | copy-start | bytes 52
  7.1 4.7 %collective-permute-start.2 = (f32[101,128]{1,0:T(8,128)S(1)}, f32[101,128]{1,0:T(8,128)S(1)}, u32[]{:S(2)}, u32[]{:S(2)}) collective-permute-start(f32[101,128]{1,0:T(8,128)S(1)} %get-tuple-element.32), channel_id=1, source_target_pairs={{0,3},{1,2},{2,1},{3,0},{4,7},{5,6},{6,5},{7,4},{8,11},{9,10},{10,... | collective-permute-start | bytes 155144 | tf_op jit(solution)/shard_map/ppermute | solution.py:54
  9.5 4.4 %collective-permute-start.1 = (f32[101,128]{1,0:T(8,128)S(1)}, f32[101,128]{1,0:T(8,128)S(1)}, u32[]{:S(2)}, u32[]{:S(2)}) collective-permute-start(f32[101,128]{1,0:T(8,128)S(1)} %get-tuple-element.31), channel_id=1, source_target_pairs={{0,2},{1,3},{2,0},{3,1},{4,6},{5,7},{6,4},{7,5},{8,10},{9,11},{10,... | collective-permute-start | bytes 155144 | tf_op jit(solution)/shard_map/ppermute | solution.py:54
  10.7 3.3 %collective-permute-start = (f32[165,128]{1,0:T(8,128)S(1)}, f32[165,128]{1,0:T(8,128)S(1)}, u32[]{:S(2)}, u32[]{:S(2)}) collective-permute-start(f32[165,128]{1,0:T(8,128)S(1)} %pad_maximum_fusion), channel_id=1, source_target_pairs={{0,1},{1,0},{2,3},{3,2},{4,5},{5,4},{6,7},{7,6},{8,9},{9,8},{10,11... | collective-permute-start | bytes 253448 | tf_op jit(solution)/shard_map/ppermute | solution.py:54
  14.2 5.7 %collective-permute-start.5 = (f32[41,128]{1,0:T(8,128)S(1)}, f32[41,128]{1,0:T(8,128)S(1)}, u32[]{:S(2)}, u32[]{:S(2)}) collective-permute-start(f32[41,128]{1,0:T(8,128)S(1)} %pad_maximum_fusion.7), channel_id=1, source_target_pairs={{0,12},{4,8},{8,4},{12,0},{1,13},{5,9},{9,5},{13,1},{2,14},{6,10},... | collective-permute-start | bytes 62984 | tf_op jit(solution)/shard_map/ppermute | solution.py:54
  17.9 4.7 %collective-permute-start.4 = (f32[41,128]{1,0:T(8,128)S(1)}, f32[41,128]{1,0:T(8,128)S(1)}, u32[]{:S(2)}, u32[]{:S(2)}) collective-permute-start(f32[41,128]{1,0:T(8,128)S(1)} %pad_maximum_fusion.6), channel_id=1, source_target_pairs={{0,8},{4,12},{8,0},{12,4},{1,9},{5,13},{9,1},{13,5},{2,10},{6,14},... | collective-permute-start | bytes 62984 | tf_op jit(solution)/shard_map/ppermute | solution.py:54
  17.9 4.8 %collective-permute-start.3 = (f32[41,128]{1,0:T(8,128)S(1)}, f32[41,128]{1,0:T(8,128)S(1)}, u32[]{:S(2)}, u32[]{:S(2)}) collective-permute-start(f32[41,128]{1,0:T(8,128)S(1)} %pad_maximum_fusion.5), channel_id=1, source_target_pairs={{0,4},{4,0},{8,12},{12,8},{1,5},{5,1},{9,13},{13,9},{2,6},{6,2},{1... | collective-permute-start | bytes 62984 | tf_op jit(solution)/shard_map/ppermute | solution.py:54

commit v20 on v19

--- a/solution.py
+++ b/solution.py
@@ -100,6 +100,7 @@
     phy = test_table(sketch_ids, y_ids, cells_y, core_stream, 6).astype(f32)
     phz = test_table(sketch_ids, z_ids, total_z, core_stream, 7)
     phq = test_table(q_ids, jnp.arange(E, dtype=jnp.int32), E, core_stream, 8).astype(f32)
+    phz, az = lax.optimization_barrier((phz, az))
 
     n_q = batches * local_snaps * variables
     field = flow_field.reshape(n_q, cells_x, cells_y, cells_z)

time: 24.5 us -> 24.5 us (level)
  no operation moved by 1% of the time
where the time goes in v20:
time: 24.5 us; the launch traced here: 24.3 us
  starting transfers between devices  7.63 us (31%)
  waiting for transfers between devices  6.18 us (25%)
  other arithmetic  3.23 us (13%)
  local copies, waits for them, and re-layouts  2.8 us (11%)
  between operations  2.3 us (9%)
  matrix products  2.2 us (9%)
    ppermute x6, starting transfers between devices, send_to(): got = lax.ppermute(flat, axes, [(i, i ^ shift) for i in range(n)])  7.63 us
    ppermute x6, waiting for transfers between devices, send_to(): got = lax.ppermute(flat, axes, [(i, i ^ shift) for i in range(n)])  6.18 us
    slice x1, local copies, waits for them, and re-layouts, shards(): factor_stream = test_streams[0]  1.34 us
    mul x1, other arithmetic, shards(): core_out * scale_core  0.72 us
    mul x1, other arithmetic, shards(): sz.reshape(cols_each, cells_z).T * scale_z  0.61 us
    dot_general x1, matrix products, shards(): jnp.dot(rows_z, phz.T, preferred_element_type=f32)  0.56 us
    mul x1, other arithmetic, shards(): sx * scale_x  0.52 us
    dot_general x1, matrix products, shards(): jnp.einsum('qxyz,qzk->xyk', field, jnp.concatenate([qz_hi, qz_lo], axis=-...  0.5 us
  transfers between devices with their start and end apart: 6, of which 4 were waited for; matrix products, arithmetic and copies ran while one was open for 6% of the time, Pallas kernels for 0%

profile of v20, /device:TPU:0, one launch (start us, length us, event | category | flops | bytes accessed | tf_op | source)
XLA Modules:
  0.0 24.3 jit_solution(2557420845395167774)
XLA Ops:
  0.6 0.0 copy-start
  0.8 1.3 %fusion.178 = (s32[1]{0:T(128)}, s32[1]{0:T(128)}) fusion(s32[2]{0:T(128)} %param.4), kind=kLoop, calls=%fused_computation.263 | loop fusion | bytes 16 | tf_op jit(solution)/shard_map/slice | solution.py:81
  3.4 0.1 fusion.85
  3.5 0.1 fusion.51
  3.6 0.0 copy-done
  3.6 0.6 %convolution_bitcast_fusion = f32[5120,48]{0,1:T(8,128)S(1)} fusion(bf16[48,128]{1,0:T(8,128)(2,1)S(1)} %fusion.85, bf16[5120,128]{1,0:T(8,128)(2,1)S(1)} %bitcast.101), kind=kOutput, calls=%fused_computation | convolution fusion | flops 62914560 | bytes 2306048 | tf_op jit(solution)/shard_map/dot_general | solution.py:121
  4.2 0.0 copy-start.1
  4.2 0.2 reshape.726
  4.4 0.1 iota_add_fusion
  4.4 0.4 %copy-done.1 = s32[2,2]{1,0:T(2,128)S(1)} copy-done((s32[2,2]{1,0:T(2,128)S(1)}, s32[2,2]{1,0:T(2,128)}, u32[]{:S(2)}) %copy-start.1) | copy-done | bytes 40
  4.9 0.1 fusion.107
  5.0 0.4 %fusion.121 = f32[2,256,48]{1,0,2:T(2,128)S(1)} fusion(f32[20,256,48]{1,0,2:T(8,128)S(1)} %reshape.726, s32[]{:T(128)} %bitcast.14, s32[20]{0:T(128)S(1)} %broadcast_multiply_fusion.2, s32[2]{0:T(128)S(1)} %iota_multiply_fusion.3), kind=kOutput, calls=%fused_computation.196 | convolution fusion | flops 2949800 | bytes 1081436 | tf_op jit(solution)/shard_map/qxyn,qe->xeyn/dot_general | solution.py:123
  5.4 0.3 %convolution_bitcast_fusion.2 = f32[1,2,48,48]{2,3,1,0:T(8,128)S(1)} fusion(f32[2,256,48]{1,0,2:T(2,128)S(1)} %fusion.121, s32[]{:T(128)} %bitcast.18, s32[256]{0:T(256)S(1)} %iota_multiply_fusion, s32[48]{0:T(128)S(1)} %iota_multiply_fusion.4), kind=kOutput, calls=%fused_computation.12 | convolution fusion | flops 7286784 | bytes 117956 | tf_op jit(solution)/shard_map/my,xeyn->xemn/dot_general | solution.py:124
  5.6 0.1 copy.15
  5.7 0.1 reshape.727
  5.8 0.1 reshape_reshape.16
  5.9 0.1 broadcast_multiply_fusion.1
  6.0 0.3 %multiply_convert_fusion = (bf16[20,128,128]{2,1,0:T(8,128)(2,1)S(1)}, bf16[20,128,128]{2,1,0:T(8,128)(2,1)S(1)}) fusion(f32[128,128]{1,0:T(8,128)S(1)} %convert_element_type.172, f32[20,128]{1,0:T(8,128)S(1)} %get-tuple-element.38), kind=kLoop, calls=%fused_computation.2 | loop fusion | flops 1638400 | bytes 1386496 | tf_op jit(solution)/shard_map/convert_element_type | solution.py:110
  6.4 0.5 %fusion.7 = f32[1,256,256]{2,1,0:T(8,128)S(1)} fusion(bf16[20,256,128]{2,1,0:T(8,128)(2,1)S(1)} %bitcast.102, bf16[20,128,128]{2,1,0:T(8,128)(2,1)S(1)} %get-tuple-element.26, bf16[20,128,128]{2,1,0:T(8,128)(2,1)S(1)} %get-tuple-element.25), kind=kOutput, calls=%fused_computation.11 | convolution fusion | flops 338165760 | bytes 2883584 | tf_op jit(solution)/shard_map/qxyz,qzk->xyk/dot_general | solution.py:112
  6.9 0.2 broadcast_multiply_fusion
  7.1 2.4 %collective-permute-start.2 = (f32[101,128]{1,0:T(8,128)S(1)}, f32[101,128]{1,0:T(8,128)S(1)}, u32[]{:S(2)}, u32[]{:S(2)}) collective-permute-start(f32[101,128]{1,0:T(8,128)S(1)} %get-tuple-element.36), channel_id=1, source_target_pairs={{0,3},{1,2},{2,1},{3,0},{4,7},{5,6},{6,5},{7,4},{8,11},{9,10},{10,... | collective-permute-start | bytes 155144 | tf_op jit(solution)/shard_map/ppermute | solution.py:54
  9.6 0.6 %collective-permute-start.1 = (f32[101,128]{1,0:T(8,128)S(1)}, f32[101,128]{1,0:T(8,128)S(1)}, u32[]{:S(2)}, u32[]{:S(2)}) collective-permute-start(f32[101,128]{1,0:T(8,128)S(1)} %get-tuple-element.35), channel_id=1, source_target_pairs={{0,2},{1,3},{2,0},{3,1},{4,6},{5,7},{6,4},{7,5},{8,10},{9,11},{10,... | collective-permute-start | bytes 155144 | tf_op jit(solution)/shard_map/ppermute | solution.py:54
  10.2 0.5 %fusion.6 = f32[128,128]{0,1:T(8,128)S(1)} fusion(bf16[20,256,128]{2,1,0:T(8,128)(2,1)S(1)} %bitcast.103, f32[20,128]{1,0:T(8,128)S(1)} %get-tuple-element.37, s32[]{:T(128)} %bitcast.9, s32[128]{0:T(128)S(1)} %iota_multiply_fusion.5, s32[256]{0:T(256)S(1)} %iota_multiply_fusion.1), kind=kOutput, calls=%fused_computation.10 | convolution fusion | flops 168968192 | bytes 1388036 | tf_op jit(solution)/shard_map/qxyz,yk->qxzk/dot_general | solution.py:118
  10.8 0.1 collective-permute-start
  10.9 0.1 fusion.109
  11.0 0.1 reshape.737
  11.0 0.7 %collective-permute-done.2 = f32[101,128]{1,0:T(8,128)S(1)} collective-permute-done((f32[101,128]{1,0:T(8,128)S(1)}, f32[101,128]{1,0:T(8,128)S(1)}, u32[]{:S(2)}, u32[]{:S(2)}) %collective-permute-start.2) | collective-permute-done | bytes 51744 | tf_op jit(solution)/shard_map/ppermute | solution.py:54
  11.8 2.2 %collective-permute-done.1 = f32[101,128]{1,0:T(8,128)S(1)} collective-permute-done((f32[101,128]{1,0:T(8,128)S(1)}, f32[101,128]{1,0:T(8,128)S(1)}, u32[]{:S(2)}, u32[]{:S(2)}) %collective-permute-start.1) | collective-permute-done | bytes 51744 | tf_op jit(solution)/shard_map/ppermute | solution.py:54
  14.0 0.0 collective-permute-done
  14.2 0.1 dynamic-slice_reduce_fusion
  14.3 3.7 %collective-permute-start.5 = (f32[41,128]{1,0:T(8,128)S(1)}, f32[41,128]{1,0:T(8,128)S(1)}, u32[]{:S(2)}, u32[]{:S(2)}) collective-permute-start(f32[41,128]{1,0:T(8,128)S(1)} %pad_maximum_fusion.7), channel_id=1, source_target_pairs={{0,12},{4,8},{8,4},{12,0},{1,13},{5,9},{9,5},{13,1},{2,14},{6,10},... | collective-permute-start | bytes 62984 | tf_op jit(solution)/shard_map/ppermute | solution.py:54
  17.9 0.0 collective-permute-start.4
  18.0 0.8 %collective-permute-start.3 = (f32[41,128]{1,0:T(8,128)S(1)}, f32[41,128]{1,0:T(8,128)S(1)}, u32[]{:S(2)}, u32[]{:S(2)}) collective-permute-start(f32[41,128]{1,0:T(8,128)S(1)} %pad_maximum_fusion.5), channel_id=1, source_target_pairs={{0,4},{4,0},{8,12},{12,8},{1,5},{5,1},{9,13},{13,9},{2,6},{6,2},{1... | collective-permute-start | bytes 62984 | tf_op jit(solution)/shard_map/ppermute | solution.py:54
  18.7 0.5 %fusion.133 = f32[1,128]{1,0:T(1,128)} fusion(f32[101,128]{1,0:T(8,128)S(1)} %collective-permute-done.2, f32[101,128]{1,0:T(8,128)S(1)} %collective-permute-done.1, f32[165,128]{1,0:T(8,128)S(1)} %collective-permute-done, f32[128]{0:T(128)S(1)} %get-tuple-element.19), kind=kLoop, calls=%fused_computation.208 | loop fusion | flops 512 | bytes 2560 | tf_op jit(solution)/shard_map/mul | solution.py:193
  19.3 0.1 concatenate.40
  19.3 0.6 %collective-permute-done.5 = f32[41,128]{1,0:T(8,128)S(1)} collective-permute-done((f32[41,128]{1,0:T(8,128)S(1)}, f32[41,128]{1,0:T(8,128)S(1)}, u32[]{:S(2)}, u32[]{:S(2)}) %collective-permute-start.5) | collective-permute-done | bytes 21024 | tf_op jit(solution)/shard_map/ppermute | solution.py:54
  20.0 0.1 concatenate.43
  20.0 2.6 %collective-permute-done.4 = f32[41,128]{1,0:T(8,128)S(1)} collective-permute-done((f32[41,128]{1,0:T(8,128)S(1)}, f32[41,128]{1,0:T(8,128)S(1)}, u32[]{:S(2)}, u32[]{:S(2)}) %collective-permute-start.4) | collective-permute-done | bytes 21024 | tf_op jit(solution)/shard_map/ppermute | solution.py:54
  22.7 0.1 concatenate.42
  22.8 0.0 collective-permute-done.3
  22.8 0.1 concatenate.41
  22.9 0.1 multiply_reduce_fusion
  23.0 0.7 %multiply_bitcast_fusion = f32[576,2,48]{0,2,1:T(8,128)} fusion(f32[48,2,576]{2,0,1:T(8,128)S(1)} %multiply_reduce_fusion), kind=kLoop, calls=%fused_computation.14 | loop fusion | flops 55296 | bytes 442368 | tf_op jit(solution)/shard_map/mul | solution.py:196
  23.7 0.6 %fusion.96 = (f32[128,16]{0,1:T(8,128)}, f32[16,128]{1,0:T(8,128)}) fusion(f32[41,128]{1,0:T(8,128)S(1)} %collective-permute-done.5, f32[41,128]{1,0:T(8,128)S(1)} %collective-permute-done.4, f32[41,128]{1,0:T(8,128)S(1)} %collective-permute-done.3, f32[4,1,16,128]{3,2,0,1:T(8,128)S(1)} %bitcast_add_fusion, s32[]{:T(128)S(6)} %select_n.92, ...), kind=kLoop, calls=%fused_computation.133 | loop fusion | flops 16384 | bytes 81924 | tf_op jit(solution)/shard_map/mul | solution.py:195
  (40 shorter events, 0.3 us)
Async XLA Ops:
  0.6 3.0 %copy-start = (bf16[2,2,5,1,256,128]{5,4,3,2,1,0:T(8,128)(2,1)S(1)}, bf16[2,2,5,1,256,128]{5,4,3,2,1,0:T(8,128)(2,1)}, u32[]{:S(2)}) copy-start(bf16[2,2,5,1,256,128]{5,4,3,2,1,0:T(8,128)(2,1)} %param.3) | copy-start | bytes 3932164
  4.2 0.7 %copy-start.1 = (s32[2,2]{1,0:T(2,128)S(1)}, s32[2,2]{1,0:T(2,128)}, u32[]{:S(2)}) copy-start(s32[2,2]{1,0:T(2,128)} %param.5) | copy-start | bytes 52
  7.1 4.7 %collective-permute-start.2 = (f32[101,128]{1,0:T(8,128)S(1)}, f32[101,128]{1,0:T(8,128)S(1)}, u32[]{:S(2)}, u32[]{:S(2)}) collective-permute-start(f32[101,128]{1,0:T(8,128)S(1)} %get-tuple-element.36), channel_id=1, source_target_pairs={{0,3},{1,2},{2,1},{3,0},{4,7},{5,6},{6,5},{7,4},{8,11},{9,10},{10,... | collective-permute-start | bytes 155144 | tf_op jit(solution)/shard_map/ppermute | solution.py:54
  9.6 4.4 %collective-permute-start.1 = (f32[101,128]{1,0:T(8,128)S(1)}, f32[101,128]{1,0:T(8,128)S(1)}, u32[]{:S(2)}, u32[]{:S(2)}) collective-permute-start(f32[101,128]{1,0:T(8,128)S(1)} %get-tuple-element.35), channel_id=1, source_target_pairs={{0,2},{1,3},{2,0},{3,1},{4,6},{5,7},{6,4},{7,5},{8,10},{9,11},{10,... | collective-permute-start | bytes 155144 | tf_op jit(solution)/shard_map/ppermute | solution.py:54
  10.8 3.3 %collective-permute-start = (f32[165,128]{1,0:T(8,128)S(1)}, f32[165,128]{1,0:T(8,128)S(1)}, u32[]{:S(2)}, u32[]{:S(2)}) collective-permute-start(f32[165,128]{1,0:T(8,128)S(1)} %pad_maximum_fusion), channel_id=1, source_target_pairs={{0,1},{1,0},{2,3},{3,2},{4,5},{5,4},{6,7},{7,6},{8,9},{9,8},{10,11... | collective-permute-start | bytes 253448 | tf_op jit(solution)/shard_map/ppermute | solution.py:54
  14.3 5.7 %collective-permute-start.5 = (f32[41,128]{1,0:T(8,128)S(1)}, f32[41,128]{1,0:T(8,128)S(1)}, u32[]{:S(2)}, u32[]{:S(2)}) collective-permute-start(f32[41,128]{1,0:T(8,128)S(1)} %pad_maximum_fusion.7), channel_id=1, source_target_pairs={{0,12},{4,8},{8,4},{12,0},{1,13},{5,9},{9,5},{13,1},{2,14},{6,10},... | collective-permute-start | bytes 62984 | tf_op jit(solution)/shard_map/ppermute | solution.py:54
  17.9 4.7 %collective-permute-start.4 = (f32[41,128]{1,0:T(8,128)S(1)}, f32[41,128]{1,0:T(8,128)S(1)}, u32[]{:S(2)}, u32[]{:S(2)}) collective-permute-start(f32[41,128]{1,0:T(8,128)S(1)} %pad_maximum_fusion.6), channel_id=1, source_target_pairs={{0,8},{4,12},{8,0},{12,4},{1,9},{5,13},{9,1},{13,5},{2,10},{6,14},... | collective-permute-start | bytes 62984 | tf_op jit(solution)/shard_map/ppermute | solution.py:54
  18.0 4.8 %collective-permute-start.3 = (f32[41,128]{1,0:T(8,128)S(1)}, f32[41,128]{1,0:T(8,128)S(1)}, u32[]{:S(2)}, u32[]{:S(2)}) collective-permute-start(f32[41,128]{1,0:T(8,128)S(1)} %pad_maximum_fusion.5), channel_id=1, source_target_pairs={{0,4},{4,0},{8,12},{12,8},{1,5},{5,1},{9,13},{13,9},{2,6},{6,2},{1... | collective-permute-start | bytes 62984 | tf_op jit(solution)/shard_map/ppermute | solution.py:54

commit v21 on v19

--- a/solution.py
+++ b/solution.py
@@ -78,8 +78,9 @@
     total_x = cells_x * n_gx
     total_z = cells_z * n_gz
     total_q = variables * batches * local_snaps * n_vert
-    factor_stream = test_streams[0]
-    core_stream = test_streams[1]
+    which_stream = jnp.arange(test_streams.shape[0], dtype=jnp.int32)
+    factor_stream = jnp.sum(jnp.where(which_stream == 0, test_streams, 0))
+    core_stream = jnp.sum(jnp.where(which_stream == 1, test_streams, 0))
     gx_me = lax.axis_index("gx")
     rank_ids = jnp.arange(K, dtype=jnp.int32)
     sketch_ids = jnp.arange(S, dtype=jnp.int32)

time: 24.5 us -> 24.5 us (level)
  other arithmetic: 3.13 us -> 4.51 us
  local copies, waits for them, and re-layouts: 2.81 us -> 1.47 us
    reduce_sum x0 -> x1, other arithmetic: none -> 1.38 us  [shards(): factor_stream = jnp.sum(jnp.where(which_stream == 0, test_streams, 0))]
    slice x1 -> x0, local copies, waits for them, and re-layouts: 1.34 us -> none  [shards(): factor_stream = test_streams[0]]
where the time goes in v21:
time: 24.5 us; the launch traced here: 24.3 us
  starting transfers between devices  7.65 us (31%)
  waiting for transfers between devices  6.17 us (25%)
  other arithmetic  4.51 us (18%)
  between operations  2.29 us (9%)
  matrix products  2.23 us (9%)
  local copies, waits for them, and re-layouts  1.47 us (6%)
    ppermute x6, starting transfers between devices, send_to(): got = lax.ppermute(flat, axes, [(i, i ^ shift) for i in range(n)])  7.65 us
    ppermute x6, waiting for transfers between devices, send_to(): got = lax.ppermute(flat, axes, [(i, i ^ shift) for i in range(n)])  6.17 us
    reduce_sum x1, other arithmetic, shards(): factor_stream = jnp.sum(jnp.where(which_stream == 0, test_streams, 0))  1.38 us
    mul x1, other arithmetic, shards(): core_out * scale_core  0.72 us
    mul x1, other arithmetic, shards(): sz.reshape(cols_each, cells_z).T * scale_z  0.61 us
    dot_general x1, matrix products, shards(): jnp.dot(rows_z, phz.T, preferred_element_type=f32)  0.6 us
    mul x1, other arithmetic, shards(): sx * scale_x  0.52 us
    dot_general x1, matrix products, shards(): jnp.einsum('qxyz,qzk->xyk', field, jnp.concatenate([qz_hi, qz_lo], axis=-...  0.5 us
  transfers between devices with their start and end apart: 6, of which 4 were waited for; matrix products, arithmetic and copies ran while one was open for 6% of the time, Pallas kernels for 0%

profile of v21, /device:TPU:0, one launch (start us, length us, event | category | flops | bytes accessed | tf_op | source)
XLA Modules:
  0.0 24.3 jit_solution(3140272917934429257)
XLA Ops:
  0.6 0.0 copy-start
  0.7 1.4 %fusion.147 = (s32[]{:T(128)}, s32[]{:T(128)}) fusion(s32[2]{0:T(128)} %param.4), kind=kLoop, calls=%fused_computation.222 | loop fusion | flops 10 | bytes 16 | tf_op jit(solution)/shard_map/reduce_sum | solution.py:82
  3.5 0.0 copy-done
  3.5 0.6 %convolution_bitcast_fusion = f32[5120,48]{0,1:T(8,128)S(1)} fusion(bf16[5120,128]{1,0:T(8,128)(2,1)S(1)} %bitcast.92, s32[]{:T(128)S(6)} %add.653, s32[128]{0:T(128)S(1)} %get-tuple-element.37, s32[48]{0:T(128)S(1)} %iota_multiply_fusion.3), kind=kOutput, calls=%fused_computation | convolution fusion | flops 63019008 | bytes 2294468 | tf_op jit(solution)/shard_map/dot_general | solution.py:121
  4.1 0.0 copy-start.1
  4.1 0.2 reshape.749
  4.2 0.1 iota_add_fusion
  4.3 0.4 %copy-done.1 = s32[2,2]{1,0:T(2,128)S(1)} copy-done((s32[2,2]{1,0:T(2,128)S(1)}, s32[2,2]{1,0:T(2,128)}, u32[]{:S(2)}) %copy-start.1) | copy-done | bytes 40
  4.8 0.1 fusion.121
  4.9 0.4 %fusion.135 = f32[2,256,48]{1,0,2:T(2,128)S(1)} fusion(f32[20,256,48]{1,0,2:T(8,128)S(1)} %reshape.749, s32[]{:T(128)S(6)} %add.645, s32[20]{0:T(128)S(1)} %broadcast_multiply_fusion.2, s32[2]{0:T(128)S(1)} %iota_multiply_fusion.4), kind=kOutput, calls=%fused_computation.211 | convolution fusion | flops 2949800 | bytes 1081436 | tf_op jit(solution)/shard_map/qxyn,qe->xeyn/dot_general | solution.py:123
  5.3 0.3 %convolution_bitcast_fusion.2 = f32[1,2,48,48]{2,3,1,0:T(8,128)S(1)} fusion(f32[2,256,48]{1,0,2:T(2,128)S(1)} %fusion.135, s32[]{:T(128)S(6)} %add.661, s32[256]{0:T(256)S(1)} %iota_multiply_fusion, s32[48]{0:T(128)S(1)} %iota_multiply_fusion.3), kind=kOutput, calls=%fused_computation.12 | convolution fusion | flops 7286784 | bytes 117956 | tf_op jit(solution)/shard_map/my,xeyn->xemn/dot_general | solution.py:124
  5.5 0.1 copy.15
  5.6 0.1 reshape.750
  5.7 0.1 reshape_reshape.16
  5.8 0.1 fusion.61
  5.9 0.1 broadcast_multiply_fusion.1
  6.0 0.3 %multiply_convert_fusion = (bf16[20,128,128]{2,1,0:T(8,128)(2,1)S(1)}, bf16[20,128,128]{2,1,0:T(8,128)(2,1)S(1)}) fusion(f32[128,128]{1,0:T(8,128)S(1)} %fusion.61, f32[20,128]{1,0:T(8,128)S(1)} %get-tuple-element.36), kind=kLoop, calls=%fused_computation.2 | loop fusion | flops 1638400 | bytes 1386496 | tf_op jit(solution)/shard_map/convert_element_type | solution.py:110
  6.4 0.5 %fusion.7 = f32[1,256,256]{2,1,0:T(8,128)S(1)} fusion(bf16[20,256,128]{2,1,0:T(8,128)(2,1)S(1)} %bitcast.93, bf16[20,128,128]{2,1,0:T(8,128)(2,1)S(1)} %get-tuple-element.24, bf16[20,128,128]{2,1,0:T(8,128)(2,1)S(1)} %get-tuple-element.23), kind=kOutput, calls=%fused_computation.11 | convolution fusion | flops 338165760 | bytes 2883584 | tf_op jit(solution)/shard_map/qxyz,qzk->xyk/dot_general | solution.py:112
  6.9 0.2 broadcast_multiply_fusion
  7.1 2.4 %collective-permute-start.2 = (f32[101,128]{1,0:T(8,128)S(1)}, f32[101,128]{1,0:T(8,128)S(1)}, u32[]{:S(2)}, u32[]{:S(2)}) collective-permute-start(f32[101,128]{1,0:T(8,128)S(1)} %get-tuple-element.34), channel_id=1, source_target_pairs={{0,3},{1,2},{2,1},{3,0},{4,7},{5,6},{6,5},{7,4},{8,11},{9,10},{10,... | collective-permute-start | bytes 155144 | tf_op jit(solution)/shard_map/ppermute | solution.py:54
  9.5 0.6 %collective-permute-start.1 = (f32[101,128]{1,0:T(8,128)S(1)}, f32[101,128]{1,0:T(8,128)S(1)}, u32[]{:S(2)}, u32[]{:S(2)}) collective-permute-start(f32[101,128]{1,0:T(8,128)S(1)} %get-tuple-element.33), channel_id=1, source_target_pairs={{0,2},{1,3},{2,0},{3,1},{4,6},{5,7},{6,4},{7,5},{8,10},{9,11},{10,... | collective-permute-start | bytes 155144 | tf_op jit(solution)/shard_map/ppermute | solution.py:54
  10.2 0.5 %fusion.6 = f32[128,128]{0,1:T(8,128)S(1)} fusion(bf16[20,256,128]{2,1,0:T(8,128)(2,1)S(1)} %bitcast.94, f32[20,128]{1,0:T(8,128)S(1)} %get-tuple-element.35, s32[]{:T(128)S(6)} %add.627, s32[128]{0:T(128)S(1)} %iota_multiply_fusion.5, s32[256]{0:T(256)S(1)} %iota_multiply_fusion.1), kind=kOutput, calls=%fused_computation.10 | convolution fusion | flops 168968192 | bytes 1388036 | tf_op jit(solution)/shard_map/qxyz,yk->qxzk/dot_general | solution.py:118
  10.7 0.1 collective-permute-start
  10.9 0.1 fusion.123
  10.9 0.1 reshape.760
  11.0 0.7 %collective-permute-done.2 = f32[101,128]{1,0:T(8,128)S(1)} collective-permute-done((f32[101,128]{1,0:T(8,128)S(1)}, f32[101,128]{1,0:T(8,128)S(1)}, u32[]{:S(2)}, u32[]{:S(2)}) %collective-permute-start.2) | collective-permute-done | bytes 51744 | tf_op jit(solution)/shard_map/ppermute | solution.py:54
  11.8 2.2 %collective-permute-done.1 = f32[101,128]{1,0:T(8,128)S(1)} collective-permute-done((f32[101,128]{1,0:T(8,128)S(1)}, f32[101,128]{1,0:T(8,128)S(1)}, u32[]{:S(2)}, u32[]{:S(2)}) %collective-permute-start.1) | collective-permute-done | bytes 51744 | tf_op jit(solution)/shard_map/ppermute | solution.py:54
  14.0 0.0 collective-permute-done
  14.2 0.1 dynamic-slice_reduce_fusion
  14.3 3.7 %collective-permute-start.5 = (f32[41,128]{1,0:T(8,128)S(1)}, f32[41,128]{1,0:T(8,128)S(1)}, u32[]{:S(2)}, u32[]{:S(2)}) collective-permute-start(f32[41,128]{1,0:T(8,128)S(1)} %pad_maximum_fusion.7), channel_id=1, source_target_pairs={{0,12},{4,8},{8,4},{12,0},{1,13},{5,9},{9,5},{13,1},{2,14},{6,10},... | collective-permute-start | bytes 62984 | tf_op jit(solution)/shard_map/ppermute | solution.py:54
  17.9 0.0 collective-permute-start.4
  17.9 0.8 %collective-permute-start.3 = (f32[41,128]{1,0:T(8,128)S(1)}, f32[41,128]{1,0:T(8,128)S(1)}, u32[]{:S(2)}, u32[]{:S(2)}) collective-permute-start(f32[41,128]{1,0:T(8,128)S(1)} %pad_maximum_fusion.5), channel_id=1, source_target_pairs={{0,4},{4,0},{8,12},{12,8},{1,5},{5,1},{9,13},{13,9},{2,6},{6,2},{1... | collective-permute-start | bytes 62984 | tf_op jit(solution)/shard_map/ppermute | solution.py:54
  18.7 0.5 %fusion.149 = f32[1,128]{1,0:T(1,128)} fusion(f32[101,128]{1,0:T(8,128)S(1)} %collective-permute-done.2, f32[101,128]{1,0:T(8,128)S(1)} %collective-permute-done.1, f32[165,128]{1,0:T(8,128)S(1)} %collective-permute-done, f32[128]{0:T(128)S(1)} %get-tuple-element.17), kind=kLoop, calls=%fused_computation.225 | loop fusion | flops 512 | bytes 2560 | tf_op jit(solution)/shard_map/mul | solution.py:193
  19.2 0.1 concatenate.40
  19.3 0.6 %collective-permute-done.5 = f32[41,128]{1,0:T(8,128)S(1)} collective-permute-done((f32[41,128]{1,0:T(8,128)S(1)}, f32[41,128]{1,0:T(8,128)S(1)}, u32[]{:S(2)}, u32[]{:S(2)}) %collective-permute-start.5) | collective-permute-done | bytes 21024 | tf_op jit(solution)/shard_map/ppermute | solution.py:54
  19.9 0.1 concatenate.43
  20.0 2.6 %collective-permute-done.4 = f32[41,128]{1,0:T(8,128)S(1)} collective-permute-done((f32[41,128]{1,0:T(8,128)S(1)}, f32[41,128]{1,0:T(8,128)S(1)}, u32[]{:S(2)}, u32[]{:S(2)}) %collective-permute-start.4) | collective-permute-done | bytes 21024 | tf_op jit(solution)/shard_map/ppermute | solution.py:54
  22.6 0.1 concatenate.42
  22.7 0.0 collective-permute-done.3
  22.7 0.1 concatenate.41
  22.8 0.1 multiply_reduce_fusion
  23.0 0.7 %multiply_bitcast_fusion = f32[576,2,48]{0,2,1:T(8,128)} fusion(f32[48,2,576]{2,0,1:T(8,128)S(1)} %multiply_reduce_fusion), kind=kLoop, calls=%fused_computation.14 | loop fusion | flops 55296 | bytes 442368 | tf_op jit(solution)/shard_map/mul | solution.py:196
  23.7 0.6 %fusion.110 = (f32[128,16]{0,1:T(8,128)}, f32[16,128]{1,0:T(8,128)}) fusion(f32[41,128]{1,0:T(8,128)S(1)} %collective-permute-done.5, f32[41,128]{1,0:T(8,128)S(1)} %collective-permute-done.4, f32[41,128]{1,0:T(8,128)S(1)} %collective-permute-done.3, f32[4,1,16,128]{3,2,0,1:T(8,128)S(1)} %bitcast_add_fusion, s32[]{:T(128)S(6)} %select_n.101, ...), kind=kLoop, calls=%fused_computation.146 | loop fusion | flops 16384 | bytes 81924 | tf_op jit(solution)/shard_map/mul | solution.py:195
  (39 shorter events, 0.3 us)
Async XLA Ops:
  0.6 2.8 %copy-start = (bf16[2,2,5,1,256,128]{5,4,3,2,1,0:T(8,128)(2,1)S(1)}, bf16[2,2,5,1,256,128]{5,4,3,2,1,0:T(8,128)(2,1)}, u32[]{:S(2)}) copy-start(bf16[2,2,5,1,256,128]{5,4,3,2,1,0:T(8,128)(2,1)} %param.3) | copy-start | bytes 3932164
  4.1 0.7 %copy-start.1 = (s32[2,2]{1,0:T(2,128)S(1)}, s32[2,2]{1,0:T(2,128)}, u32[]{:S(2)}) copy-start(s32[2,2]{1,0:T(2,128)} %param.5) | copy-start | bytes 52
  7.1 4.7 %collective-permute-start.2 = (f32[101,128]{1,0:T(8,128)S(1)}, f32[101,128]{1,0:T(8,128)S(1)}, u32[]{:S(2)}, u32[]{:S(2)}) collective-permute-start(f32[101,128]{1,0:T(8,128)S(1)} %get-tuple-element.34), channel_id=1, source_target_pairs={{0,3},{1,2},{2,1},{3,0},{4,7},{5,6},{6,5},{7,4},{8,11},{9,10},{10,... | collective-permute-start | bytes 155144 | tf_op jit(solution)/shard_map/ppermute | solution.py:54
  9.5 4.4 %collective-permute-start.1 = (f32[101,128]{1,0:T(8,128)S(1)}, f32[101,128]{1,0:T(8,128)S(1)}, u32[]{:S(2)}, u32[]{:S(2)}) collective-permute-start(f32[101,128]{1,0:T(8,128)S(1)} %get-tuple-element.33), channel_id=1, source_target_pairs={{0,2},{1,3},{2,0},{3,1},{4,6},{5,7},{6,4},{7,5},{8,10},{9,11},{10,... | collective-permute-start | bytes 155144 | tf_op jit(solution)/shard_map/ppermute | solution.py:54
  10.7 3.3 %collective-permute-start = (f32[165,128]{1,0:T(8,128)S(1)}, f32[165,128]{1,0:T(8,128)S(1)}, u32[]{:S(2)}, u32[]{:S(2)}) collective-permute-start(f32[165,128]{1,0:T(8,128)S(1)} %pad_maximum_fusion), channel_id=1, source_target_pairs={{0,1},{1,0},{2,3},{3,2},{4,5},{5,4},{6,7},{7,6},{8,9},{9,8},{10,11... | collective-permute-start | bytes 253448 | tf_op jit(solution)/shard_map/ppermute | solution.py:54
  14.3 5.7 %collective-permute-start.5 = (f32[41,128]{1,0:T(8,128)S(1)}, f32[41,128]{1,0:T(8,128)S(1)}, u32[]{:S(2)}, u32[]{:S(2)}) collective-permute-start(f32[41,128]{1,0:T(8,128)S(1)} %pad_maximum_fusion.7), channel_id=1, source_target_pairs={{0,12},{4,8},{8,4},{12,0},{1,13},{5,9},{9,5},{13,1},{2,14},{6,10},... | collective-permute-start | bytes 62984 | tf_op jit(solution)/shard_map/ppermute | solution.py:54
  17.9 4.7 %collective-permute-start.4 = (f32[41,128]{1,0:T(8,128)S(1)}, f32[41,128]{1,0:T(8,128)S(1)}, u32[]{:S(2)}, u32[]{:S(2)}) collective-permute-start(f32[41,128]{1,0:T(8,128)S(1)} %pad_maximum_fusion.6), channel_id=1, source_target_pairs={{0,8},{4,12},{8,0},{12,4},{1,9},{5,13},{9,1},{13,5},{2,10},{6,14},... | collective-permute-start | bytes 62984 | tf_op jit(solution)/shard_map/ppermute | solution.py:54
  17.9 4.8 %collective-permute-start.3 = (f32[41,128]{1,0:T(8,128)S(1)}, f32[41,128]{1,0:T(8,128)S(1)}, u32[]{:S(2)}, u32[]{:S(2)}) collective-permute-start(f32[41,128]{1,0:T(8,128)S(1)} %pad_maximum_fusion.5), channel_id=1, source_target_pairs={{0,4},{4,0},{8,12},{12,8},{1,5},{5,1},{9,13},{13,9},{2,6},{6,2},{1... | collective-permute-start | bytes 62984 | tf_op jit(solution)/shard_map/ppermute | solution.py:54

commit v22 on v19

--- a/solution.py
+++ b/solution.py
@@ -154,7 +154,7 @@
         if with_sz:
             at_z = split_digit(sz, 1, 2, v_me)
             sz_total = at_z(0)
-        for s in range(1, r):
+        for s in range(r - 1, 0, -1):
             pieces = [at(s), sx, core] + ([at_z(1)] if with_sz and s == 1 else [])
             got = send_to(("gz", "vert"), n_gzv, s * d, pieces)
             sy_total, sx_total, core_total = sy_total + got[0], sx_total + got[1], core_total + got[2]
@@ -172,11 +172,11 @@
         at_y = split_digit(sy, 0, r, digit)
         at_z = split_digit(sz, 0, r, digit)
         at_c = split_digit(core, 1, r, digit)
-        sy_total, sz_total, core_parts = at_y(0), at_z(0), [at_c(0)]
-        for s in range(1, r):
+        sy_total, sz_total, core_parts = at_y(0), at_z(0), [at_c(0)] + [None] * (r - 1)
+        for s in range(r - 1, 0, -1):
             g_sy, g_sz, g_core = send_to("gx", n_gx, s * d, [at_y(s), at_z(s), at_c(s)])
             sy_total, sz_total = sy_total + g_sy, sz_total + g_sz
-            core_parts.append(g_core)
+            core_parts[s] = g_core
         sy, sz = sy_total, sz_total
         core = jnp.concatenate(core_parts, axis=0)
 

time: 24.5 us -> 26.9 us (1.098)
  waiting for transfers between devices: 6.17 us -> 8.26 us
  other arithmetic: 3.13 us -> 3.8 us
  local copies, waits for them, and re-layouts: 2.81 us -> 2.37 us
    ppermute x6, waiting for transfers between devices: 6.17 us -> 8.26 us  [send_to(): got = lax.ppermute(flat, axes, [(i, i ^ shift) for i in range(n)])]
    reduce_sum x1, other arithmetic: 0.09 us -> 0.77 us  [shards(): q_ids = jnp.sum(picks, axis=(1, 2)) * variables + flat_q % variables]
    unnamed x4 -> x2, local copies, waits for them, and re-layouts: 0.45 us -> 0.01 us
  transfers between devices with their start and end apart: 6 -> 6, of which waited for: 4 -> 3; matrix products, arithmetic and copies ran while one was open for 6% -> 4% of each run, Pallas kernels for 0% -> 0%
where the time goes in v22:
time: 26.9 us; the launch traced here: 26.7 us
  waiting for transfers between devices  8.26 us (31%)
  starting transfers between devices  7.72 us (29%)
  other arithmetic  3.8 us (14%)
  local copies, waits for them, and re-layouts  2.37 us (9%)
  between operations  2.29 us (9%)
  matrix products  2.25 us (8%)
    ppermute x6, waiting for transfers between devices, send_to(): got = lax.ppermute(flat, axes, [(i, i ^ shift) for i in range(n)])  8.26 us
    ppermute x6, starting transfers between devices, send_to(): got = lax.ppermute(flat, axes, [(i, i ^ shift) for i in range(n)])  7.72 us
    slice x1, local copies, waits for them, and re-layouts, shards(): core_stream = test_streams[1]  1.34 us
    reduce_sum x1, other arithmetic, shards(): q_ids = jnp.sum(picks, axis=(1, 2)) * variables + flat_q % variables  0.77 us
    mul x1, other arithmetic, shards(): core_out * scale_core  0.72 us
    mul x1, other arithmetic, shards(): sz.reshape(cols_each, cells_z).T * scale_z  0.61 us
    dot_general x1, matrix products, shards(): jnp.dot(rows_z, phz.T, preferred_element_type=f32)  0.6 us
  transfers between devices with their start and end apart: 6, of which 3 were waited for; matrix products, arithmetic and copies ran while one was open for 4% of the time, Pallas kernels for 0%

profile of v22, /device:TPU:0, one launch (start us, length us, event | category | flops | bytes accessed | tf_op | source)
XLA Modules:
  0.0 26.7 jit_solution(3538390482315418486)
XLA Ops:
  0.6 0.0 copy-start
  0.8 1.3 %fusion.201 = (s32[1]{0:T(128)}, s32[1]{0:T(128)}) fusion(s32[2]{0:T(128)} %param.4), kind=kLoop, calls=%fused_computation.285 | loop fusion | bytes 16 | tf_op jit(solution)/shard_map/slice | solution.py:82
  2.1 0.1 iota_add_fusion
  2.2 0.8 %fusion.121 = s32[20]{0:T(128)S(1)} fusion(s32[2,2]{1,0:T(2,128)} %param.5, s32[2,2]{1,0:T(2,128)S(1)} %iota_add_fusion, s32[20]{0:T(128)S(1)} %and_select_fusion.1), kind=kLoop, calls=%fused_computation.181 | loop fusion | flops 220 | bytes 192 | tf_op jit(solution)/shard_map/reduce_sum | solution.py:95
  4.3 0.0 copy-done
  4.3 0.6 %convolution_bitcast_fusion = f32[5120,48]{0,1:T(8,128)S(1)} fusion(bf16[5120,128]{1,0:T(8,128)(2,1)S(1)} %bitcast.102, s32[]{:T(128)} %bitcast.15, s32[128]{0:T(128)S(1)} %get-tuple-element.37, s32[48]{0:T(128)S(1)} %iota_multiply_fusion.3), kind=kOutput, calls=%fused_computation | convolution fusion | flops 63019008 | bytes 2294468 | tf_op jit(solution)/shard_map/dot_general | solution.py:120
  4.9 0.2 reshape.769
  5.1 0.4 %fusion.135 = f32[2,256,48]{1,0,2:T(2,128)S(1)} fusion(f32[20,256,48]{1,0,2:T(8,128)S(1)} %reshape.769, s32[]{:T(128)} %bitcast.13, s32[20]{0:T(128)S(1)} %get-tuple-element.12, s32[2]{0:T(128)S(1)} %iota_multiply_fusion.4), kind=kOutput, calls=%fused_computation.209 | convolution fusion | flops 2949800 | bytes 1081436 | tf_op jit(solution)/shard_map/qxyn,qe->xeyn/dot_general | solution.py:122
  5.5 0.3 convolution_bitcast_fusion.2
  5.7 0.1 copy.15
  5.8 0.1 reshape.770
  5.9 0.1 reshape_reshape.16
  6.0 0.1 fusion.61
  6.1 0.1 fusion.112
  6.2 0.3 %multiply_convert_fusion = (bf16[20,128,128]{2,1,0:T(8,128)(2,1)S(1)}, bf16[20,128,128]{2,1,0:T(8,128)(2,1)S(1)}) fusion(f32[128,128]{1,0:T(8,128)S(1)} %fusion.61, f32[20,128]{1,0:T(8,128)S(1)} %get-tuple-element.33), kind=kLoop, calls=%fused_computation.2 | loop fusion | flops 1638400 | bytes 1386496 | tf_op jit(solution)/shard_map/convert_element_type | solution.py:109
  6.6 0.5 %fusion.7 = f32[1,256,256]{2,1,0:T(8,128)S(1)} fusion(bf16[20,256,128]{2,1,0:T(8,128)(2,1)S(1)} %bitcast.100, bf16[20,128,128]{2,1,0:T(8,128)(2,1)S(1)} %get-tuple-element.22, bf16[20,128,128]{2,1,0:T(8,128)(2,1)S(1)} %get-tuple-element.21), kind=kOutput, calls=%fused_computation.11 | convolution fusion | flops 338165760 | bytes 2883584 | tf_op jit(solution)/shard_map/qxyz,qzk->xyk/dot_general | solution.py:111
  7.1 0.5 %fusion.6 = f32[128,128]{0,1:T(8,128)S(1)} fusion(bf16[20,256,128]{2,1,0:T(8,128)(2,1)S(1)} %bitcast.101, f32[20,128]{1,0:T(8,128)S(1)} %get-tuple-element.34, s32[]{:T(128)} %bitcast.8, s32[128]{0:T(128)S(1)} %iota_multiply_fusion.5, s32[256]{0:T(256)S(1)} %iota_multiply_fusion.1), kind=kOutput, calls=%fused_computation.10 | convolution fusion | flops 168968192 | bytes 1388036 | tf_op jit(solution)/shard_map/qxyz,yk->qxzk/dot_general | solution.py:117
  7.6 0.2 broadcast_multiply_fusion
  7.8 0.5 %collective-permute-start.2 = (f32[165,128]{1,0:T(8,128)S(1)}, f32[165,128]{1,0:T(8,128)S(1)}, u32[]{:S(2)}, u32[]{:S(2)}) collective-permute-start(f32[165,128]{1,0:T(8,128)S(1)} %pad_maximum_fusion), channel_id=1, source_target_pairs={{0,1},{1,0},{2,3},{3,2},{4,5},{5,4},{6,7},{7,6},{8,9},{9,8},{10,11... | collective-permute-start | bytes 253448 | tf_op jit(solution)/shard_map/ppermute | solution.py:54
  8.4 2.6 %collective-permute-start.1 = (f32[101,128]{1,0:T(8,128)S(1)}, f32[101,128]{1,0:T(8,128)S(1)}, u32[]{:S(2)}, u32[]{:S(2)}) collective-permute-start(f32[101,128]{1,0:T(8,128)S(1)} %get-tuple-element.32), channel_id=1, source_target_pairs={{0,2},{1,3},{2,0},{3,1},{4,6},{5,7},{6,4},{7,5},{8,10},{9,11},{10,... | collective-permute-start | bytes 155144 | tf_op jit(solution)/shard_map/ppermute | solution.py:54
  11.0 0.2 collective-permute-start
  11.1 0.1 fusion.123
  11.2 0.1 reshape.780
  11.3 2.1 %collective-permute-done.1 = f32[101,128]{1,0:T(8,128)S(1)} collective-permute-done((f32[101,128]{1,0:T(8,128)S(1)}, f32[101,128]{1,0:T(8,128)S(1)}, u32[]{:S(2)}, u32[]{:S(2)}) %collective-permute-start.1) | collective-permute-done | bytes 51744 | tf_op jit(solution)/shard_map/ppermute | solution.py:54
  13.5 1.3 %collective-permute-done = f32[101,128]{1,0:T(8,128)S(1)} collective-permute-done((f32[101,128]{1,0:T(8,128)S(1)}, f32[101,128]{1,0:T(8,128)S(1)}, u32[]{:S(2)}, u32[]{:S(2)}) %collective-permute-start) | collective-permute-done | bytes 51744 | tf_op jit(solution)/shard_map/ppermute | solution.py:54
  14.8 0.0 collective-permute-done.2
  15.0 0.1 dynamic-slice_reduce_fusion
  15.1 1.7 %collective-permute-start.5 = (f32[41,128]{1,0:T(8,128)S(1)}, f32[41,128]{1,0:T(8,128)S(1)}, u32[]{:S(2)}, u32[]{:S(2)}) collective-permute-start(f32[41,128]{1,0:T(8,128)S(1)} %pad_maximum_fusion.7), channel_id=1, source_target_pairs={{0,4},{4,0},{8,12},{12,8},{1,5},{5,1},{9,13},{13,9},{2,6},{6,2},{1... | collective-permute-start | bytes 62984 | tf_op jit(solution)/shard_map/ppermute | solution.py:54
  16.7 2.6 %collective-permute-start.4 = (f32[41,128]{1,0:T(8,128)S(1)}, f32[41,128]{1,0:T(8,128)S(1)}, u32[]{:S(2)}, u32[]{:S(2)}) collective-permute-start(f32[41,128]{1,0:T(8,128)S(1)} %pad_maximum_fusion.6), channel_id=1, source_target_pairs={{0,8},{4,12},{8,0},{12,4},{1,9},{5,13},{9,1},{13,5},{2,10},{6,14},... | collective-permute-start | bytes 62984 | tf_op jit(solution)/shard_map/ppermute | solution.py:54
  19.3 0.2 collective-permute-start.3
  19.5 0.5 %fusion.147 = f32[1,128]{1,0:T(1,128)} fusion(f32[165,128]{1,0:T(8,128)S(1)} %collective-permute-done.2, f32[101,128]{1,0:T(8,128)S(1)} %collective-permute-done.1, f32[101,128]{1,0:T(8,128)S(1)} %collective-permute-done, f32[128]{0:T(128)S(1)} %get-tuple-element.15), kind=kLoop, calls=%fused_computation.221 | loop fusion | flops 512 | bytes 2560 | tf_op jit(solution)/shard_map/mul | solution.py:192
  20.0 0.1 concatenate.40
  20.1 4.8 %collective-permute-done.3 = f32[41,128]{1,0:T(8,128)S(1)} collective-permute-done((f32[41,128]{1,0:T(8,128)S(1)}, f32[41,128]{1,0:T(8,128)S(1)}, u32[]{:S(2)}, u32[]{:S(2)}) %collective-permute-start.3) | collective-permute-done | bytes 21024 | tf_op jit(solution)/shard_map/ppermute | solution.py:54
  24.9 0.1 concatenate.43
  25.0 0.0 collective-permute-done.4
  25.0 0.1 concatenate.42
  25.1 0.0 collective-permute-done.5
  25.1 0.1 concatenate.41
  25.2 0.1 multiply_reduce_fusion
  25.4 0.7 %multiply_bitcast_fusion = f32[576,2,48]{0,2,1:T(8,128)} fusion(f32[48,2,576]{2,0,1:T(8,128)S(1)} %multiply_reduce_fusion), kind=kLoop, calls=%fused_computation.14 | loop fusion | flops 55296 | bytes 442368 | tf_op jit(solution)/shard_map/mul | solution.py:195
  26.1 0.6 %fusion.110 = (f32[128,16]{0,1:T(8,128)}, f32[16,128]{1,0:T(8,128)}) fusion(f32[41,128]{1,0:T(8,128)S(1)} %collective-permute-done.5, f32[41,128]{1,0:T(8,128)S(1)} %collective-permute-done.4, f32[41,128]{1,0:T(8,128)S(1)} %collective-permute-done.3, f32[4,1,16,128]{3,2,0,1:T(8,128)S(1)} %bitcast_add_fusion, s32[]{:T(128)S(6)} %select_n.92, ...), kind=kLoop, calls=%fused_computation.146 | loop fusion | flops 16384 | bytes 81924 | tf_op jit(solution)/shard_map/mul | solution.py:194
  (39 shorter events, 0.3 us)
Async XLA Ops:
  0.6 3.7 %copy-start = (bf16[2,2,5,1,256,128]{5,4,3,2,1,0:T(8,128)(2,1)S(1)}, bf16[2,2,5,1,256,128]{5,4,3,2,1,0:T(8,128)(2,1)}, u32[]{:S(2)}) copy-start(bf16[2,2,5,1,256,128]{5,4,3,2,1,0:T(8,128)(2,1)} %param.3) | copy-start | bytes 3932164
  7.8 7.0 %collective-permute-start.2 = (f32[165,128]{1,0:T(8,128)S(1)}, f32[165,128]{1,0:T(8,128)S(1)}, u32[]{:S(2)}, u32[]{:S(2)}) collective-permute-start(f32[165,128]{1,0:T(8,128)S(1)} %pad_maximum_fusion), channel_id=1, source_target_pairs={{0,1},{1,0},{2,3},{3,2},{4,5},{5,4},{6,7},{7,6},{8,9},{9,8},{10,11... | collective-permute-start | bytes 253448 | tf_op jit(solution)/shard_map/ppermute | solution.py:54
  8.4 5.1 %collective-permute-start.1 = (f32[101,128]{1,0:T(8,128)S(1)}, f32[101,128]{1,0:T(8,128)S(1)}, u32[]{:S(2)}, u32[]{:S(2)}) collective-permute-start(f32[101,128]{1,0:T(8,128)S(1)} %get-tuple-element.32), channel_id=1, source_target_pairs={{0,2},{1,3},{2,0},{3,1},{4,6},{5,7},{6,4},{7,5},{8,10},{9,11},{10,... | collective-permute-start | bytes 155144 | tf_op jit(solution)/shard_map/ppermute | solution.py:54
  11.0 3.8 %collective-permute-start = (f32[101,128]{1,0:T(8,128)S(1)}, f32[101,128]{1,0:T(8,128)S(1)}, u32[]{:S(2)}, u32[]{:S(2)}) collective-permute-start(f32[101,128]{1,0:T(8,128)S(1)} %get-tuple-element.31), channel_id=1, source_target_pairs={{0,3},{1,2},{2,1},{3,0},{4,7},{5,6},{6,5},{7,4},{8,11},{9,10},{10,... | collective-permute-start | bytes 155144 | tf_op jit(solution)/shard_map/ppermute | solution.py:54
  15.1 10.1 %collective-permute-start.5 = (f32[41,128]{1,0:T(8,128)S(1)}, f32[41,128]{1,0:T(8,128)S(1)}, u32[]{:S(2)}, u32[]{:S(2)}) collective-permute-start(f32[41,128]{1,0:T(8,128)S(1)} %pad_maximum_fusion.7), channel_id=1, source_target_pairs={{0,4},{4,0},{8,12},{12,8},{1,5},{5,1},{9,13},{13,9},{2,6},{6,2},{1... | collective-permute-start | bytes 62984 | tf_op jit(solution)/shard_map/ppermute | solution.py:54
  16.7 8.3 %collective-permute-start.4 = (f32[41,128]{1,0:T(8,128)S(1)}, f32[41,128]{1,0:T(8,128)S(1)}, u32[]{:S(2)}, u32[]{:S(2)}) collective-permute-start(f32[41,128]{1,0:T(8,128)S(1)} %pad_maximum_fusion.6), channel_id=1, source_target_pairs={{0,8},{4,12},{8,0},{12,4},{1,9},{5,13},{9,1},{13,5},{2,10},{6,14},... | collective-permute-start | bytes 62984 | tf_op jit(solution)/shard_map/ppermute | solution.py:54
  19.3 5.6 %collective-permute-start.3 = (f32[41,128]{1,0:T(8,128)S(1)}, f32[41,128]{1,0:T(8,128)S(1)}, u32[]{:S(2)}, u32[]{:S(2)}) collective-permute-start(f32[41,128]{1,0:T(8,128)S(1)} %pad_maximum_fusion.5), channel_id=1, source_target_pairs={{0,12},{4,8},{8,4},{12,0},{1,13},{5,9},{9,5},{13,1},{2,14},{6,10},... | collective-permute-start | bytes 62984 | tf_op jit(solution)/shard_map/ppermute | solution.py:54

commit v23 on v22

--- a/solution.py
+++ b/solution.py
@@ -154,7 +154,7 @@
         if with_sz:
             at_z = split_digit(sz, 1, 2, v_me)
             sz_total = at_z(0)
-        for s in range(r - 1, 0, -1):
+        for s in range(1, r):
             pieces = [at(s), sx, core] + ([at_z(1)] if with_sz and s == 1 else [])
             got = send_to(("gz", "vert"), n_gzv, s * d, pieces)
             sy_total, sx_total, core_total = sy_total + got[0], sx_total + got[1], core_total + got[2]
@@ -173,7 +173,7 @@
         at_z = split_digit(sz, 0, r, digit)
         at_c = split_digit(core, 1, r, digit)
         sy_total, sz_total, core_parts = at_y(0), at_z(0), [at_c(0)] + [None] * (r - 1)
-        for s in range(r - 1, 0, -1):
+        for s in ([1, 3, 2] if r == 4 else list(range(1, r))):
             g_sy, g_sz, g_core = send_to("gx", n_gx, s * d, [at_y(s), at_z(s), at_c(s)])
             sy_total, sz_total = sy_total + g_sy, sz_total + g_sz
             core_parts[s] = g_core

time: 26.9 us -> 24.4 us (0.907)
  waiting for transfers between devices: 8.26 us -> 6.29 us
  other arithmetic: 3.8 us -> 3.13 us
  local copies, waits for them, and re-layouts: 2.37 us -> 2.81 us
    ppermute x6, waiting for transfers between devices: 8.26 us -> 6.29 us  [send_to(): got = lax.ppermute(flat, axes, [(i, i ^ shift) for i in range(n)])]
    reduce_sum x1, other arithmetic: 0.77 us -> 0.09 us  [shards(): q_ids = jnp.sum(picks, axis=(1, 2)) * variables + flat_q % variables]
    unnamed x2 -> x4, local copies, waits for them, and re-layouts: 0.01 us -> 0.45 us
  transfers between devices with their start and end apart: 6 -> 6, of which waited for: 3 -> 3; matrix products, arithmetic and copies ran while one was open for 4% -> 6% of each run, Pallas kernels for 0% -> 0%
where the time goes in v23:
time: 24.4 us; the launch traced here: 24.2 us
  starting transfers between devices  7.51 us (31%)
  waiting for transfers between devices  6.29 us (26%)
  other arithmetic  3.13 us (13%)
  local copies, waits for them, and re-layouts  2.81 us (12%)
  between operations  2.28 us (9%)
  matrix products  2.23 us (9%)
    ppermute x6, starting transfers between devices, send_to(): got = lax.ppermute(flat, axes, [(i, i ^ shift) for i in range(n)])  7.51 us
    ppermute x6, waiting for transfers between devices, send_to(): got = lax.ppermute(flat, axes, [(i, i ^ shift) for i in range(n)])  6.29 us
    slice x1, local copies, waits for them, and re-layouts, shards(): factor_stream = test_streams[0]  1.34 us
    mul x1, other arithmetic, shards(): core_out * scale_core  0.72 us
    mul x1, other arithmetic, shards(): sz.reshape(cols_each, cells_z).T * scale_z  0.61 us
    dot_general x1, matrix products, shards(): jnp.dot(rows_z, phz.T, preferred_element_type=f32)  0.6 us
    mul x1, other arithmetic, shards(): sx * scale_x  0.52 us
    dot_general x1, matrix products, shards(): jnp.einsum('qxyz,qzk->xyk', field, jnp.concatenate([qz_hi, qz_lo], axis=-...  0.5 us
  transfers between devices with their start and end apart: 6, of which 3 were waited for; matrix products, arithmetic and copies ran while one was open for 6% of the time, Pallas kernels for 0%

profile of v23, /device:TPU:0, one launch (start us, length us, event | category | flops | bytes accessed | tf_op | source)
XLA Modules:
  0.0 24.2 jit_solution(16641773538747891714)
XLA Ops:
  0.6 0.0 copy-start
  0.8 1.3 %fusion.201 = (s32[1]{0:T(128)}, s32[1]{0:T(128)}) fusion(s32[2]{0:T(128)} %param.4), kind=kLoop, calls=%fused_computation.285 | loop fusion | bytes 16 | tf_op jit(solution)/shard_map/slice | solution.py:81
  2.7 0.0 copy-done
  2.8 0.6 %convolution_bitcast_fusion = f32[5120,48]{0,1:T(8,128)S(1)} fusion(bf16[5120,128]{1,0:T(8,128)(2,1)S(1)} %bitcast.100, s32[]{:T(128)} %bitcast.15, s32[128]{0:T(128)S(1)} %get-tuple-element.37, s32[48]{0:T(128)S(1)} %iota_multiply_fusion.3), kind=kOutput, calls=%fused_computation | convolution fusion | flops 63019008 | bytes 2294468 | tf_op jit(solution)/shard_map/dot_general | solution.py:120
  3.4 0.0 copy-start.1
  3.4 0.2 reshape.769
  3.5 0.1 iota_add_fusion
  3.6 0.4 %copy-done.1 = s32[2,2]{1,0:T(2,128)S(1)} copy-done((s32[2,2]{1,0:T(2,128)S(1)}, s32[2,2]{1,0:T(2,128)}, u32[]{:S(2)}) %copy-start.1) | copy-done | bytes 40
  4.0 0.1 fusion.121
  4.2 0.4 %fusion.135 = f32[2,256,48]{1,0,2:T(2,128)S(1)} fusion(f32[20,256,48]{1,0,2:T(8,128)S(1)} %reshape.769, s32[]{:T(128)} %bitcast.13, s32[20]{0:T(128)S(1)} %broadcast_multiply_fusion.2, s32[2]{0:T(128)S(1)} %iota_multiply_fusion.4), kind=kOutput, calls=%fused_computation.209 | convolution fusion | flops 2949800 | bytes 1081436 | tf_op jit(solution)/shard_map/qxyn,qe->xeyn/dot_general | solution.py:122
  4.5 0.3 %convolution_bitcast_fusion.2 = f32[1,2,48,48]{2,3,1,0:T(8,128)S(1)} fusion(f32[2,256,48]{1,0,2:T(2,128)S(1)} %fusion.135, s32[]{:T(128)} %bitcast.18, s32[256]{0:T(256)S(1)} %iota_multiply_fusion, s32[48]{0:T(128)S(1)} %iota_multiply_fusion.3), kind=kOutput, calls=%fused_computation.12 | convolution fusion | flops 7286784 | bytes 117956 | tf_op jit(solution)/shard_map/my,xeyn->xemn/dot_general | solution.py:123
  4.8 0.1 copy.15
  4.9 0.1 reshape.770
  5.0 0.1 reshape_reshape.16
  5.8 0.1 fusion.61
  5.9 0.1 broadcast_multiply_fusion.1
  6.0 0.3 %multiply_convert_fusion = (bf16[20,128,128]{2,1,0:T(8,128)(2,1)S(1)}, bf16[20,128,128]{2,1,0:T(8,128)(2,1)S(1)}) fusion(f32[128,128]{1,0:T(8,128)S(1)} %fusion.61, f32[20,128]{1,0:T(8,128)S(1)} %get-tuple-element.34), kind=kLoop, calls=%fused_computation.2 | loop fusion | flops 1638400 | bytes 1386496 | tf_op jit(solution)/shard_map/convert_element_type | solution.py:109
  6.3 0.5 %fusion.7 = f32[1,256,256]{2,1,0:T(8,128)S(1)} fusion(bf16[20,256,128]{2,1,0:T(8,128)(2,1)S(1)} %bitcast.101, bf16[20,128,128]{2,1,0:T(8,128)(2,1)S(1)} %get-tuple-element.22, bf16[20,128,128]{2,1,0:T(8,128)(2,1)S(1)} %get-tuple-element.21), kind=kOutput, calls=%fused_computation.11 | convolution fusion | flops 338165760 | bytes 2883584 | tf_op jit(solution)/shard_map/qxyz,qzk->xyk/dot_general | solution.py:111
  6.8 0.2 broadcast_multiply_fusion
  7.1 2.4 %collective-permute-start.2 = (f32[101,128]{1,0:T(8,128)S(1)}, f32[101,128]{1,0:T(8,128)S(1)}, u32[]{:S(2)}, u32[]{:S(2)}) collective-permute-start(f32[101,128]{1,0:T(8,128)S(1)} %get-tuple-element.32), channel_id=1, source_target_pairs={{0,3},{1,2},{2,1},{3,0},{4,7},{5,6},{6,5},{7,4},{8,11},{9,10},{10,... | collective-permute-start | bytes 155144 | tf_op jit(solution)/shard_map/ppermute | solution.py:54
  9.5 0.6 %collective-permute-start.1 = (f32[101,128]{1,0:T(8,128)S(1)}, f32[101,128]{1,0:T(8,128)S(1)}, u32[]{:S(2)}, u32[]{:S(2)}) collective-permute-start(f32[101,128]{1,0:T(8,128)S(1)} %get-tuple-element.31), channel_id=1, source_target_pairs={{0,2},{1,3},{2,0},{3,1},{4,6},{5,7},{6,4},{7,5},{8,10},{9,11},{10,... | collective-permute-start | bytes 155144 | tf_op jit(solution)/shard_map/ppermute | solution.py:54
  10.1 0.5 %fusion.6 = f32[128,128]{0,1:T(8,128)S(1)} fusion(bf16[20,256,128]{2,1,0:T(8,128)(2,1)S(1)} %bitcast.102, f32[20,128]{1,0:T(8,128)S(1)} %get-tuple-element.33, s32[]{:T(128)} %bitcast.8, s32[128]{0:T(128)S(1)} %iota_multiply_fusion.5, s32[256]{0:T(256)S(1)} %iota_multiply_fusion.1), kind=kOutput, calls=%fused_computation.10 | convolution fusion | flops 168968192 | bytes 1388036 | tf_op jit(solution)/shard_map/qxyz,yk->qxzk/dot_general | solution.py:117
  10.7 0.1 collective-permute-start
  10.8 0.1 fusion.123
  10.9 0.1 reshape.780
  11.0 0.7 %collective-permute-done.2 = f32[101,128]{1,0:T(8,128)S(1)} collective-permute-done((f32[101,128]{1,0:T(8,128)S(1)}, f32[101,128]{1,0:T(8,128)S(1)}, u32[]{:S(2)}, u32[]{:S(2)}) %collective-permute-start.2) | collective-permute-done | bytes 51744 | tf_op jit(solution)/shard_map/ppermute | solution.py:54
  11.7 2.2 %collective-permute-done.1 = f32[101,128]{1,0:T(8,128)S(1)} collective-permute-done((f32[101,128]{1,0:T(8,128)S(1)}, f32[101,128]{1,0:T(8,128)S(1)}, u32[]{:S(2)}, u32[]{:S(2)}) %collective-permute-start.1) | collective-permute-done | bytes 51744 | tf_op jit(solution)/shard_map/ppermute | solution.py:54
  14.0 0.0 collective-permute-done
  14.1 0.1 dynamic-slice_reduce_fusion
  14.2 2.7 %collective-permute-start.5 = (f32[41,128]{1,0:T(8,128)S(1)}, f32[41,128]{1,0:T(8,128)S(1)}, u32[]{:S(2)}, u32[]{:S(2)}) collective-permute-start(f32[41,128]{1,0:T(8,128)S(1)} %pad_maximum_fusion.7), channel_id=1, source_target_pairs={{0,8},{4,12},{8,0},{12,4},{1,9},{5,13},{9,1},{13,5},{2,10},{6,14},... | collective-permute-start | bytes 62984 | tf_op jit(solution)/shard_map/ppermute | solution.py:54
  16.9 1.3 %collective-permute-start.4 = (f32[41,128]{1,0:T(8,128)S(1)}, f32[41,128]{1,0:T(8,128)S(1)}, u32[]{:S(2)}, u32[]{:S(2)}) collective-permute-start(f32[41,128]{1,0:T(8,128)S(1)} %pad_maximum_fusion.6), channel_id=1, source_target_pairs={{0,12},{4,8},{8,4},{12,0},{1,13},{5,9},{9,5},{13,1},{2,14},{6,10},... | collective-permute-start | bytes 62984 | tf_op jit(solution)/shard_map/ppermute | solution.py:54
  18.2 0.3 %collective-permute-start.3 = (f32[41,128]{1,0:T(8,128)S(1)}, f32[41,128]{1,0:T(8,128)S(1)}, u32[]{:S(2)}, u32[]{:S(2)}) collective-permute-start(f32[41,128]{1,0:T(8,128)S(1)} %pad_maximum_fusion.5), channel_id=1, source_target_pairs={{0,4},{4,0},{8,12},{12,8},{1,5},{5,1},{9,13},{13,9},{2,6},{6,2},{1... | collective-permute-start | bytes 62984 | tf_op jit(solution)/shard_map/ppermute | solution.py:54
  18.5 0.5 %fusion.147 = f32[1,128]{1,0:T(1,128)} fusion(f32[101,128]{1,0:T(8,128)S(1)} %collective-permute-done.2, f32[101,128]{1,0:T(8,128)S(1)} %collective-permute-done.1, f32[165,128]{1,0:T(8,128)S(1)} %collective-permute-done, f32[128]{0:T(128)S(1)} %get-tuple-element.15), kind=kLoop, calls=%fused_computation.221 | loop fusion | flops 512 | bytes 2560 | tf_op jit(solution)/shard_map/mul | solution.py:192
  19.0 0.1 concatenate.40
  19.1 3.4 %collective-permute-done.4 = f32[41,128]{1,0:T(8,128)S(1)} collective-permute-done((f32[41,128]{1,0:T(8,128)S(1)}, f32[41,128]{1,0:T(8,128)S(1)}, u32[]{:S(2)}, u32[]{:S(2)}) %collective-permute-start.4) | collective-permute-done | bytes 21024 | tf_op jit(solution)/shard_map/ppermute | solution.py:54
  22.5 0.1 concatenate.43
  22.6 0.0 collective-permute-done.5
  22.6 0.1 concatenate.42
  22.7 0.0 collective-permute-done.3
  22.7 0.1 concatenate.41
  22.8 0.1 multiply_reduce_fusion
  22.9 0.7 %multiply_bitcast_fusion = f32[576,2,48]{0,2,1:T(8,128)} fusion(f32[48,2,576]{2,0,1:T(8,128)S(1)} %multiply_reduce_fusion), kind=kLoop, calls=%fused_computation.14 | loop fusion | flops 55296 | bytes 442368 | tf_op jit(solution)/shard_map/mul | solution.py:195
  23.6 0.6 %fusion.110 = (f32[128,16]{0,1:T(8,128)}, f32[16,128]{1,0:T(8,128)}) fusion(f32[41,128]{1,0:T(8,128)S(1)} %collective-permute-done.5, f32[41,128]{1,0:T(8,128)S(1)} %collective-permute-done.4, f32[41,128]{1,0:T(8,128)S(1)} %collective-permute-done.3, f32[4,1,16,128]{3,2,0,1:T(8,128)S(1)} %bitcast_add_fusion, s32[]{:T(128)S(6)} %select_n.92, ...), kind=kLoop, calls=%fused_computation.146 | loop fusion | flops 16384 | bytes 81924 | tf_op jit(solution)/shard_map/mul | solution.py:194
  (39 shorter events, 0.3 us)
Async XLA Ops:
  0.6 2.1 %copy-start = (bf16[2,2,5,1,256,128]{5,4,3,2,1,0:T(8,128)(2,1)S(1)}, bf16[2,2,5,1,256,128]{5,4,3,2,1,0:T(8,128)(2,1)}, u32[]{:S(2)}) copy-start(bf16[2,2,5,1,256,128]{5,4,3,2,1,0:T(8,128)(2,1)} %param.3) | copy-start | bytes 3932164
  3.4 0.7 %copy-start.1 = (s32[2,2]{1,0:T(2,128)S(1)}, s32[2,2]{1,0:T(2,128)}, u32[]{:S(2)}) copy-start(s32[2,2]{1,0:T(2,128)} %param.5) | copy-start | bytes 52
  7.1 4.7 %collective-permute-start.2 = (f32[101,128]{1,0:T(8,128)S(1)}, f32[101,128]{1,0:T(8,128)S(1)}, u32[]{:S(2)}, u32[]{:S(2)}) collective-permute-start(f32[101,128]{1,0:T(8,128)S(1)} %get-tuple-element.32), channel_id=1, source_target_pairs={{0,3},{1,2},{2,1},{3,0},{4,7},{5,6},{6,5},{7,4},{8,11},{9,10},{10,... | collective-permute-start | bytes 155144 | tf_op jit(solution)/shard_map/ppermute | solution.py:54
  9.5 4.4 %collective-permute-start.1 = (f32[101,128]{1,0:T(8,128)S(1)}, f32[101,128]{1,0:T(8,128)S(1)}, u32[]{:S(2)}, u32[]{:S(2)}) collective-permute-start(f32[101,128]{1,0:T(8,128)S(1)} %get-tuple-element.31), channel_id=1, source_target_pairs={{0,2},{1,3},{2,0},{3,1},{4,6},{5,7},{6,4},{7,5},{8,10},{9,11},{10,... | collective-permute-start | bytes 155144 | tf_op jit(solution)/shard_map/ppermute | solution.py:54
  10.7 3.3 %collective-permute-start = (f32[165,128]{1,0:T(8,128)S(1)}, f32[165,128]{1,0:T(8,128)S(1)}, u32[]{:S(2)}, u32[]{:S(2)}) collective-permute-start(f32[165,128]{1,0:T(8,128)S(1)} %pad_maximum_fusion), channel_id=1, source_target_pairs={{0,1},{1,0},{2,3},{3,2},{4,5},{5,4},{6,7},{7,6},{8,9},{9,8},{10,11... | collective-permute-start | bytes 253448 | tf_op jit(solution)/shard_map/ppermute | solution.py:54
  14.2 8.4 %collective-permute-start.5 = (f32[41,128]{1,0:T(8,128)S(1)}, f32[41,128]{1,0:T(8,128)S(1)}, u32[]{:S(2)}, u32[]{:S(2)}) collective-permute-start(f32[41,128]{1,0:T(8,128)S(1)} %pad_maximum_fusion.7), channel_id=1, source_target_pairs={{0,8},{4,12},{8,0},{12,4},{1,9},{5,13},{9,1},{13,5},{2,10},{6,14},... | collective-permute-start | bytes 62984 | tf_op jit(solution)/shard_map/ppermute | solution.py:54
  16.9 5.6 %collective-permute-start.4 = (f32[41,128]{1,0:T(8,128)S(1)}, f32[41,128]{1,0:T(8,128)S(1)}, u32[]{:S(2)}, u32[]{:S(2)}) collective-permute-start(f32[41,128]{1,0:T(8,128)S(1)} %pad_maximum_fusion.6), channel_id=1, source_target_pairs={{0,12},{4,8},{8,4},{12,0},{1,13},{5,9},{9,5},{13,1},{2,14},{6,10},... | collective-permute-start | bytes 62984 | tf_op jit(solution)/shard_map/ppermute | solution.py:54
  18.2 4.4 %collective-permute-start.3 = (f32[41,128]{1,0:T(8,128)S(1)}, f32[41,128]{1,0:T(8,128)S(1)}, u32[]{:S(2)}, u32[]{:S(2)}) collective-permute-start(f32[41,128]{1,0:T(8,128)S(1)} %pad_maximum_fusion.5), channel_id=1, source_target_pairs={{0,4},{4,0},{8,12},{12,8},{1,5},{5,1},{9,13},{13,9},{2,6},{6,2},{1... | collective-permute-start | bytes 62984 | tf_op jit(solution)/shard_map/ppermute | solution.py:54

commit v24 on v19

--- a/solution.py
+++ b/solution.py
@@ -154,7 +154,7 @@
         if with_sz:
             at_z = split_digit(sz, 1, 2, v_me)
             sz_total = at_z(0)
-        for s in range(1, r):
+        for s in ([1, 3, 2] if r == 4 else list(range(1, r))):
             pieces = [at(s), sx, core] + ([at_z(1)] if with_sz and s == 1 else [])
             got = send_to(("gz", "vert"), n_gzv, s * d, pieces)
             sy_total, sx_total, core_total = sy_total + got[0], sx_total + got[1], core_total + got[2]

time: 24.5 us -> 24.5 us (level)
  no operation moved by 1% of the time
where the time goes in v24:
time: 24.5 us; the launch traced here: 24.3 us
  starting transfers between devices  7.7 us (31%)
  waiting for transfers between devices  6.13 us (25%)
  other arithmetic  3.13 us (13%)
  local copies, waits for them, and re-layouts  2.81 us (11%)
  between operations  2.29 us (9%)
  matrix products  2.23 us (9%)
    ppermute x6, starting transfers between devices, send_to(): got = lax.ppermute(flat, axes, [(i, i ^ shift) for i in range(n)])  7.7 us
    ppermute x6, waiting for transfers between devices, send_to(): got = lax.ppermute(flat, axes, [(i, i ^ shift) for i in range(n)])  6.13 us
    slice x1, local copies, waits for them, and re-layouts, shards(): factor_stream = test_streams[0]  1.34 us
    mul x1, other arithmetic, shards(): core_out * scale_core  0.72 us
    mul x1, other arithmetic, shards(): sz.reshape(cols_each, cells_z).T * scale_z  0.61 us
    dot_general x1, matrix products, shards(): jnp.dot(rows_z, phz.T, preferred_element_type=f32)  0.6 us
    mul x1, other arithmetic, shards(): sx * scale_x  0.52 us
    dot_general x1, matrix products, shards(): jnp.einsum('qxyz,qzk->xyk', field, jnp.concatenate([qz_hi, qz_lo], axis=-...  0.5 us
  transfers between devices with their start and end apart: 6, of which 4 were waited for; matrix products, arithmetic and copies ran while one was open for 6% of the time, Pallas kernels for 0%

profile of v24, /device:TPU:0, one launch (start us, length us, event | category | flops | bytes accessed | tf_op | source)
XLA Modules:
  0.0 24.3 jit_solution(12381473719413806743)
XLA Ops:
  0.6 0.0 copy-start
  0.8 1.3 %fusion.201 = (s32[1]{0:T(128)}, s32[1]{0:T(128)}) fusion(s32[2]{0:T(128)} %param.4), kind=kLoop, calls=%fused_computation.285 | loop fusion | bytes 16 | tf_op jit(solution)/shard_map/slice | solution.py:81
  2.7 0.0 copy-done
  2.8 0.6 %convolution_bitcast_fusion = f32[5120,48]{0,1:T(8,128)S(1)} fusion(bf16[5120,128]{1,0:T(8,128)(2,1)S(1)} %bitcast.100, s32[]{:T(128)} %bitcast.15, s32[128]{0:T(128)S(1)} %get-tuple-element.37, s32[48]{0:T(128)S(1)} %iota_multiply_fusion.3), kind=kOutput, calls=%fused_computation | convolution fusion | flops 63019008 | bytes 2294468 | tf_op jit(solution)/shard_map/dot_general | solution.py:120
  3.4 0.0 copy-start.1
  3.4 0.2 reshape.769
  3.5 0.1 iota_add_fusion
  3.6 0.4 %copy-done.1 = s32[2,2]{1,0:T(2,128)S(1)} copy-done((s32[2,2]{1,0:T(2,128)S(1)}, s32[2,2]{1,0:T(2,128)}, u32[]{:S(2)}) %copy-start.1) | copy-done | bytes 40
  4.0 0.1 fusion.121
  4.2 0.4 %fusion.135 = f32[2,256,48]{1,0,2:T(2,128)S(1)} fusion(f32[20,256,48]{1,0,2:T(8,128)S(1)} %reshape.769, s32[]{:T(128)} %bitcast.13, s32[20]{0:T(128)S(1)} %broadcast_multiply_fusion.2, s32[2]{0:T(128)S(1)} %iota_multiply_fusion.4), kind=kOutput, calls=%fused_computation.209 | convolution fusion | flops 2949800 | bytes 1081436 | tf_op jit(solution)/shard_map/qxyn,qe->xeyn/dot_general | solution.py:122
  4.5 0.3 %convolution_bitcast_fusion.2 = f32[1,2,48,48]{2,3,1,0:T(8,128)S(1)} fusion(f32[2,256,48]{1,0,2:T(2,128)S(1)} %fusion.135, s32[]{:T(128)} %bitcast.18, s32[256]{0:T(256)S(1)} %iota_multiply_fusion, s32[48]{0:T(128)S(1)} %iota_multiply_fusion.3), kind=kOutput, calls=%fused_computation.12 | convolution fusion | flops 7286784 | bytes 117956 | tf_op jit(solution)/shard_map/my,xeyn->xemn/dot_general | solution.py:123
  4.8 0.1 copy.15
  4.9 0.1 reshape.770
  5.0 0.1 reshape_reshape.16
  5.8 0.1 fusion.61
  5.9 0.1 broadcast_multiply_fusion.1
  6.0 0.3 %multiply_convert_fusion = (bf16[20,128,128]{2,1,0:T(8,128)(2,1)S(1)}, bf16[20,128,128]{2,1,0:T(8,128)(2,1)S(1)}) fusion(f32[128,128]{1,0:T(8,128)S(1)} %fusion.61, f32[20,128]{1,0:T(8,128)S(1)} %get-tuple-element.34), kind=kLoop, calls=%fused_computation.2 | loop fusion | flops 1638400 | bytes 1386496 | tf_op jit(solution)/shard_map/convert_element_type | solution.py:109
  6.3 0.5 %fusion.7 = f32[1,256,256]{2,1,0:T(8,128)S(1)} fusion(bf16[20,256,128]{2,1,0:T(8,128)(2,1)S(1)} %bitcast.101, bf16[20,128,128]{2,1,0:T(8,128)(2,1)S(1)} %get-tuple-element.22, bf16[20,128,128]{2,1,0:T(8,128)(2,1)S(1)} %get-tuple-element.21), kind=kOutput, calls=%fused_computation.11 | convolution fusion | flops 338165760 | bytes 2883584 | tf_op jit(solution)/shard_map/qxyz,qzk->xyk/dot_general | solution.py:111
  6.8 0.2 broadcast_multiply_fusion
  7.1 3.0 %collective-permute-start.2 = (f32[101,128]{1,0:T(8,128)S(1)}, f32[101,128]{1,0:T(8,128)S(1)}, u32[]{:S(2)}, u32[]{:S(2)}) collective-permute-start(f32[101,128]{1,0:T(8,128)S(1)} %get-tuple-element.32), channel_id=1, source_target_pairs={{0,2},{1,3},{2,0},{3,1},{4,6},{5,7},{6,4},{7,5},{8,10},{9,11},{10,... | collective-permute-start | bytes 155144 | tf_op jit(solution)/shard_map/ppermute | solution.py:54
  10.1 0.0 collective-permute-start.1
  10.1 0.5 %fusion.6 = f32[128,128]{0,1:T(8,128)S(1)} fusion(bf16[20,256,128]{2,1,0:T(8,128)(2,1)S(1)} %bitcast.102, f32[20,128]{1,0:T(8,128)S(1)} %get-tuple-element.33, s32[]{:T(128)} %bitcast.8, s32[128]{0:T(128)S(1)} %iota_multiply_fusion.5, s32[256]{0:T(256)S(1)} %iota_multiply_fusion.1), kind=kOutput, calls=%fused_computation.10 | convolution fusion | flops 168968192 | bytes 1388036 | tf_op jit(solution)/shard_map/qxyz,yk->qxzk/dot_general | solution.py:117
  10.6 0.3 %collective-permute-start = (f32[165,128]{1,0:T(8,128)S(1)}, f32[165,128]{1,0:T(8,128)S(1)}, u32[]{:S(2)}, u32[]{:S(2)}) collective-permute-start(f32[165,128]{1,0:T(8,128)S(1)} %pad_maximum_fusion), channel_id=1, source_target_pairs={{0,1},{1,0},{2,3},{3,2},{4,5},{5,4},{6,7},{7,6},{8,9},{9,8},{10,11... | collective-permute-start | bytes 253448 | tf_op jit(solution)/shard_map/ppermute | solution.py:54
  10.9 0.1 fusion.123
  11.0 0.1 reshape.780
  11.0 1.1 %collective-permute-done.2 = f32[101,128]{1,0:T(8,128)S(1)} collective-permute-done((f32[101,128]{1,0:T(8,128)S(1)}, f32[101,128]{1,0:T(8,128)S(1)}, u32[]{:S(2)}, u32[]{:S(2)}) %collective-permute-start.2) | collective-permute-done | bytes 51744 | tf_op jit(solution)/shard_map/ppermute | solution.py:54
  12.2 1.7 %collective-permute-done.1 = f32[101,128]{1,0:T(8,128)S(1)} collective-permute-done((f32[101,128]{1,0:T(8,128)S(1)}, f32[101,128]{1,0:T(8,128)S(1)}, u32[]{:S(2)}, u32[]{:S(2)}) %collective-permute-start.1) | collective-permute-done | bytes 51744 | tf_op jit(solution)/shard_map/ppermute | solution.py:54
  14.0 0.0 collective-permute-done
  14.1 0.1 dynamic-slice_reduce_fusion
  14.2 3.7 %collective-permute-start.5 = (f32[41,128]{1,0:T(8,128)S(1)}, f32[41,128]{1,0:T(8,128)S(1)}, u32[]{:S(2)}, u32[]{:S(2)}) collective-permute-start(f32[41,128]{1,0:T(8,128)S(1)} %pad_maximum_fusion.7), channel_id=1, source_target_pairs={{0,12},{4,8},{8,4},{12,0},{1,13},{5,9},{9,5},{13,1},{2,14},{6,10},... | collective-permute-start | bytes 62984 | tf_op jit(solution)/shard_map/ppermute | solution.py:54
  17.9 0.0 collective-permute-start.4
  17.9 0.8 %collective-permute-start.3 = (f32[41,128]{1,0:T(8,128)S(1)}, f32[41,128]{1,0:T(8,128)S(1)}, u32[]{:S(2)}, u32[]{:S(2)}) collective-permute-start(f32[41,128]{1,0:T(8,128)S(1)} %pad_maximum_fusion.5), channel_id=1, source_target_pairs={{0,4},{4,0},{8,12},{12,8},{1,5},{5,1},{9,13},{13,9},{2,6},{6,2},{1... | collective-permute-start | bytes 62984 | tf_op jit(solution)/shard_map/ppermute | solution.py:54
  18.7 0.5 %fusion.147 = f32[1,128]{1,0:T(1,128)} fusion(f32[101,128]{1,0:T(8,128)S(1)} %collective-permute-done.2, f32[101,128]{1,0:T(8,128)S(1)} %collective-permute-done.1, f32[165,128]{1,0:T(8,128)S(1)} %collective-permute-done, f32[128]{0:T(128)S(1)} %get-tuple-element.15), kind=kLoop, calls=%fused_computation.221 | loop fusion | flops 512 | bytes 2560 | tf_op jit(solution)/shard_map/mul | solution.py:192
  19.2 0.1 concatenate.40
  19.3 0.6 %collective-permute-done.5 = f32[41,128]{1,0:T(8,128)S(1)} collective-permute-done((f32[41,128]{1,0:T(8,128)S(1)}, f32[41,128]{1,0:T(8,128)S(1)}, u32[]{:S(2)}, u32[]{:S(2)}) %collective-permute-start.5) | collective-permute-done | bytes 21024 | tf_op jit(solution)/shard_map/ppermute | solution.py:54
  19.9 0.1 concatenate.43
  20.0 2.6 %collective-permute-done.4 = f32[41,128]{1,0:T(8,128)S(1)} collective-permute-done((f32[41,128]{1,0:T(8,128)S(1)}, f32[41,128]{1,0:T(8,128)S(1)}, u32[]{:S(2)}, u32[]{:S(2)}) %collective-permute-start.4) | collective-permute-done | bytes 21024 | tf_op jit(solution)/shard_map/ppermute | solution.py:54
  22.6 0.1 concatenate.42
  22.7 0.0 collective-permute-done.3
  22.7 0.1 concatenate.41
  22.8 0.1 multiply_reduce_fusion
  23.0 0.7 %multiply_bitcast_fusion = f32[576,2,48]{0,2,1:T(8,128)} fusion(f32[48,2,576]{2,0,1:T(8,128)S(1)} %multiply_reduce_fusion), kind=kLoop, calls=%fused_computation.14 | loop fusion | flops 55296 | bytes 442368 | tf_op jit(solution)/shard_map/mul | solution.py:195
  23.7 0.6 %fusion.110 = (f32[128,16]{0,1:T(8,128)}, f32[16,128]{1,0:T(8,128)}) fusion(f32[41,128]{1,0:T(8,128)S(1)} %collective-permute-done.5, f32[41,128]{1,0:T(8,128)S(1)} %collective-permute-done.4, f32[41,128]{1,0:T(8,128)S(1)} %collective-permute-done.3, f32[4,1,16,128]{3,2,0,1:T(8,128)S(1)} %bitcast_add_fusion, s32[]{:T(128)S(6)} %select_n.92, ...), kind=kLoop, calls=%fused_computation.146 | loop fusion | flops 16384 | bytes 81924 | tf_op jit(solution)/shard_map/mul | solution.py:194
  (39 shorter events, 0.3 us)
Async XLA Ops:
  0.6 2.1 %copy-start = (bf16[2,2,5,1,256,128]{5,4,3,2,1,0:T(8,128)(2,1)S(1)}, bf16[2,2,5,1,256,128]{5,4,3,2,1,0:T(8,128)(2,1)}, u32[]{:S(2)}) copy-start(bf16[2,2,5,1,256,128]{5,4,3,2,1,0:T(8,128)(2,1)} %param.3) | copy-start | bytes 3932164
  3.4 0.7 %copy-start.1 = (s32[2,2]{1,0:T(2,128)S(1)}, s32[2,2]{1,0:T(2,128)}, u32[]{:S(2)}) copy-start(s32[2,2]{1,0:T(2,128)} %param.5) | copy-start | bytes 52
  7.1 5.1 %collective-permute-start.2 = (f32[101,128]{1,0:T(8,128)S(1)}, f32[101,128]{1,0:T(8,128)S(1)}, u32[]{:S(2)}, u32[]{:S(2)}) collective-permute-start(f32[101,128]{1,0:T(8,128)S(1)} %get-tuple-element.32), channel_id=1, source_target_pairs={{0,2},{1,3},{2,0},{3,1},{4,6},{5,7},{6,4},{7,5},{8,10},{9,11},{10,... | collective-permute-start | bytes 155144 | tf_op jit(solution)/shard_map/ppermute | solution.py:54
  10.1 3.9 %collective-permute-start.1 = (f32[101,128]{1,0:T(8,128)S(1)}, f32[101,128]{1,0:T(8,128)S(1)}, u32[]{:S(2)}, u32[]{:S(2)}) collective-permute-start(f32[101,128]{1,0:T(8,128)S(1)} %get-tuple-element.31), channel_id=1, source_target_pairs={{0,3},{1,2},{2,1},{3,0},{4,7},{5,6},{6,5},{7,4},{8,11},{9,10},{10,... | collective-permute-start | bytes 155144 | tf_op jit(solution)/shard_map/ppermute | solution.py:54
  10.6 3.4 %collective-permute-start = (f32[165,128]{1,0:T(8,128)S(1)}, f32[165,128]{1,0:T(8,128)S(1)}, u32[]{:S(2)}, u32[]{:S(2)}) collective-permute-start(f32[165,128]{1,0:T(8,128)S(1)} %pad_maximum_fusion), channel_id=1, source_target_pairs={{0,1},{1,0},{2,3},{3,2},{4,5},{5,4},{6,7},{7,6},{8,9},{9,8},{10,11... | collective-permute-start | bytes 253448 | tf_op jit(solution)/shard_map/ppermute | solution.py:54
  14.2 5.7 %collective-permute-start.5 = (f32[41,128]{1,0:T(8,128)S(1)}, f32[41,128]{1,0:T(8,128)S(1)}, u32[]{:S(2)}, u32[]{:S(2)}) collective-permute-start(f32[41,128]{1,0:T(8,128)S(1)} %pad_maximum_fusion.7), channel_id=1, source_target_pairs={{0,12},{4,8},{8,4},{12,0},{1,13},{5,9},{9,5},{13,1},{2,14},{6,10},... | collective-permute-start | bytes 62984 | tf_op jit(solution)/shard_map/ppermute | solution.py:54
  17.9 4.7 %collective-permute-start.4 = (f32[41,128]{1,0:T(8,128)S(1)}, f32[41,128]{1,0:T(8,128)S(1)}, u32[]{:S(2)}, u32[]{:S(2)}) collective-permute-start(f32[41,128]{1,0:T(8,128)S(1)} %pad_maximum_fusion.6), channel_id=1, source_target_pairs={{0,8},{4,12},{8,0},{12,4},{1,9},{5,13},{9,1},{13,5},{2,10},{6,14},... | collective-permute-start | bytes 62984 | tf_op jit(solution)/shard_map/ppermute | solution.py:54
  17.9 4.8 %collective-permute-start.3 = (f32[41,128]{1,0:T(8,128)S(1)}, f32[41,128]{1,0:T(8,128)S(1)}, u32[]{:S(2)}, u32[]{:S(2)}) collective-permute-start(f32[41,128]{1,0:T(8,128)S(1)} %pad_maximum_fusion.5), channel_id=1, source_target_pairs={{0,4},{4,0},{8,12},{12,8},{1,5},{5,1},{9,13},{13,9},{2,6},{6,2},{1... | collective-permute-start | bytes 62984 | tf_op jit(solution)/shard_map/ppermute | solution.py:54

commit v25 on v19

--- a/solution.py
+++ b/solution.py
@@ -166,7 +166,8 @@
     src = jnp.bitwise_xor(gx_me, jnp.arange(n_gx, dtype=jnp.int32))
     x_src = (src[:, None] * cells_x + jnp.arange(cells_x, dtype=jnp.int32)[None, :]).reshape(-1)
     phx = test_table(sketch_ids, x_src, total_x, core_stream, 5).astype(f32).reshape(S, n_gx, cells_x)
-    core, phx = lax.optimization_barrier((core, phx))
+    scale_core = 9.0 / math.sqrt(total_x * cells_y * total_z * total_q)
+    core, phx = lax.optimization_barrier((core, phx * scale_core))
     for d, r in digit_steps(n_gx):
         digit = (gx_me // d) % r
         at_y = split_digit(sy, 0, r, digit)
@@ -187,12 +188,11 @@
     scale_x = 3.0**1.5 / math.sqrt(cells_y * total_z * total_q)
     scale_y = 3.0**1.5 / math.sqrt(total_x * total_z * total_q)
     scale_z = 3.0**1.5 / math.sqrt(total_x * cells_y * total_q)
-    scale_core = 9.0 / math.sqrt(total_x * cells_y * total_z * total_q)
     return (
         sx * scale_x,
         sy.reshape(rows_each, K) * scale_y,
         sz.reshape(cols_each, cells_z).T * scale_z,
-        core_out * scale_core,
+        core_out,
     )
 
 

time: 24.5 us -> 24.4 us (level)
    reduce_sum x1, other arithmetic: 0.14 us -> 0.83 us  [shards(): jnp.sum(held[:, None, :, :] * weights_x.T[:, :, None, None], axis=0)]
    mul x1, other arithmetic: 0.72 us -> 0.09 us  [shards(): core, phx = lax.optimization_barrier((core, phx * scale_core))]
where the time goes in v25:
time: 24.4 us; the launch traced here: 24.2 us
  starting transfers between devices  7.64 us (31%)
  waiting for transfers between devices  6.17 us (25%)
  other arithmetic  3.11 us (13%)
  local copies, waits for them, and re-layouts  2.81 us (12%)
  between operations  2.28 us (9%)
  matrix products  2.23 us (9%)
    ppermute x6, starting transfers between devices, send_to(): got = lax.ppermute(flat, axes, [(i, i ^ shift) for i in range(n)])  7.64 us
    ppermute x6, waiting for transfers between devices, send_to(): got = lax.ppermute(flat, axes, [(i, i ^ shift) for i in range(n)])  6.17 us
    slice x1, local copies, waits for them, and re-layouts, shards(): factor_stream = test_streams[0]  1.34 us
    reduce_sum x1, other arithmetic, shards(): jnp.sum(held[:, None, :, :] * weights_x.T[:, :, None, None], axis=0)  0.83 us
    mul x1, other arithmetic, shards(): sz.reshape(cols_each, cells_z).T * scale_z  0.61 us
    dot_general x1, matrix products, shards(): jnp.dot(rows_z, phz.T, preferred_element_type=f32)  0.6 us
    mul x1, other arithmetic, shards(): sx * scale_x  0.52 us
    dot_general x1, matrix products, shards(): jnp.einsum('qxyz,qzk->xyk', field, jnp.concatenate([qz_hi, qz_lo], axis=-...  0.5 us
  transfers between devices with their start and end apart: 6, of which 4 were waited for; matrix products, arithmetic and copies ran while one was open for 6% of the time, Pallas kernels for 0%

profile of v25, /device:TPU:0, one launch (start us, length us, event | category | flops | bytes accessed | tf_op | source)
XLA Modules:
  0.0 24.2 jit_solution(40009802309017380)
XLA Ops:
  0.6 0.0 copy-start
  0.8 1.3 %fusion.200 = (s32[1]{0:T(128)}, s32[1]{0:T(128)}) fusion(s32[2]{0:T(128)} %param.4), kind=kLoop, calls=%fused_computation.284 | loop fusion | bytes 16 | tf_op jit(solution)/shard_map/slice | solution.py:81
  2.7 0.0 copy-done
  2.8 0.6 %convolution_bitcast_fusion = f32[5120,48]{0,1:T(8,128)S(1)} fusion(bf16[5120,128]{1,0:T(8,128)(2,1)S(1)} %bitcast.99, s32[]{:T(128)} %bitcast.15, s32[128]{0:T(128)S(1)} %get-tuple-element.37, s32[48]{0:T(128)S(1)} %iota_multiply_fusion.3), kind=kOutput, calls=%fused_computation | convolution fusion | flops 63019008 | bytes 2294468 | tf_op jit(solution)/shard_map/dot_general | solution.py:120
  3.4 0.0 copy-start.1
  3.4 0.2 reshape.773
  3.5 0.1 iota_add_fusion
  3.6 0.4 %copy-done.1 = s32[2,2]{1,0:T(2,128)S(1)} copy-done((s32[2,2]{1,0:T(2,128)S(1)}, s32[2,2]{1,0:T(2,128)}, u32[]{:S(2)}) %copy-start.1) | copy-done | bytes 40
  4.0 0.1 fusion.121
  4.2 0.4 %fusion.134 = f32[2,256,48]{1,0,2:T(2,128)S(1)} fusion(f32[20,256,48]{1,0,2:T(8,128)S(1)} %reshape.773, s32[]{:T(128)} %bitcast.13, s32[20]{0:T(128)S(1)} %broadcast_multiply_fusion.2, s32[2]{0:T(128)S(1)} %iota_multiply_fusion.4), kind=kOutput, calls=%fused_computation.208 | convolution fusion | flops 2949800 | bytes 1081436 | tf_op jit(solution)/shard_map/qxyn,qe->xeyn/dot_general | solution.py:122
  4.5 0.3 %convolution_bitcast_fusion.2 = f32[1,2,48,48]{2,3,1,0:T(8,128)S(1)} fusion(f32[2,256,48]{1,0,2:T(2,128)S(1)} %fusion.134, s32[]{:T(128)} %bitcast.18, s32[256]{0:T(256)S(1)} %iota_multiply_fusion, s32[48]{0:T(128)S(1)} %iota_multiply_fusion.3), kind=kOutput, calls=%fused_computation.12 | convolution fusion | flops 7286784 | bytes 117956 | tf_op jit(solution)/shard_map/my,xeyn->xemn/dot_general | solution.py:123
  4.8 0.1 copy.15
  4.9 0.1 reshape.774
  5.0 0.1 reshape_reshape.16
  5.8 0.1 fusion.61
  5.9 0.1 broadcast_multiply_fusion.1
  6.0 0.3 %multiply_convert_fusion = (bf16[20,128,128]{2,1,0:T(8,128)(2,1)S(1)}, bf16[20,128,128]{2,1,0:T(8,128)(2,1)S(1)}) fusion(f32[128,128]{1,0:T(8,128)S(1)} %fusion.61, f32[20,128]{1,0:T(8,128)S(1)} %get-tuple-element.34), kind=kLoop, calls=%fused_computation.2 | loop fusion | flops 1638400 | bytes 1386496 | tf_op jit(solution)/shard_map/convert_element_type | solution.py:109
  6.3 0.5 %fusion.7 = f32[1,256,256]{2,1,0:T(8,128)S(1)} fusion(bf16[20,256,128]{2,1,0:T(8,128)(2,1)S(1)} %bitcast.100, bf16[20,128,128]{2,1,0:T(8,128)(2,1)S(1)} %get-tuple-element.22, bf16[20,128,128]{2,1,0:T(8,128)(2,1)S(1)} %get-tuple-element.21), kind=kOutput, calls=%fused_computation.11 | convolution fusion | flops 338165760 | bytes 2883584 | tf_op jit(solution)/shard_map/qxyz,qzk->xyk/dot_general | solution.py:111
  6.8 0.2 broadcast_multiply_fusion
  7.1 2.4 %collective-permute-start.2 = (f32[101,128]{1,0:T(8,128)S(1)}, f32[101,128]{1,0:T(8,128)S(1)}, u32[]{:S(2)}, u32[]{:S(2)}) collective-permute-start(f32[101,128]{1,0:T(8,128)S(1)} %get-tuple-element.32), channel_id=1, source_target_pairs={{0,3},{1,2},{2,1},{3,0},{4,7},{5,6},{6,5},{7,4},{8,11},{9,10},{10,... | collective-permute-start | bytes 155144 | tf_op jit(solution)/shard_map/ppermute | solution.py:54
  9.5 0.6 %collective-permute-start.1 = (f32[101,128]{1,0:T(8,128)S(1)}, f32[101,128]{1,0:T(8,128)S(1)}, u32[]{:S(2)}, u32[]{:S(2)}) collective-permute-start(f32[101,128]{1,0:T(8,128)S(1)} %get-tuple-element.31), channel_id=1, source_target_pairs={{0,2},{1,3},{2,0},{3,1},{4,6},{5,7},{6,4},{7,5},{8,10},{9,11},{10,... | collective-permute-start | bytes 155144 | tf_op jit(solution)/shard_map/ppermute | solution.py:54
  10.1 0.5 %fusion.6 = f32[128,128]{0,1:T(8,128)S(1)} fusion(bf16[20,256,128]{2,1,0:T(8,128)(2,1)S(1)} %bitcast.101, f32[20,128]{1,0:T(8,128)S(1)} %get-tuple-element.33, s32[]{:T(128)} %bitcast.8, s32[128]{0:T(128)S(1)} %iota_multiply_fusion.5, s32[256]{0:T(256)S(1)} %iota_multiply_fusion.1), kind=kOutput, calls=%fused_computation.10 | convolution fusion | flops 168968192 | bytes 1388036 | tf_op jit(solution)/shard_map/qxyz,yk->qxzk/dot_general | solution.py:117
  10.7 0.1 collective-permute-start
  10.8 0.1 convert_multiply_fusion
  10.9 0.1 reshape.784
  11.0 0.7 %collective-permute-done.2 = f32[101,128]{1,0:T(8,128)S(1)} collective-permute-done((f32[101,128]{1,0:T(8,128)S(1)}, f32[101,128]{1,0:T(8,128)S(1)}, u32[]{:S(2)}, u32[]{:S(2)}) %collective-permute-start.2) | collective-permute-done | bytes 51744 | tf_op jit(solution)/shard_map/ppermute | solution.py:54
  11.7 2.2 %collective-permute-done.1 = f32[101,128]{1,0:T(8,128)S(1)} collective-permute-done((f32[101,128]{1,0:T(8,128)S(1)}, f32[101,128]{1,0:T(8,128)S(1)}, u32[]{:S(2)}, u32[]{:S(2)}) %collective-permute-start.1) | collective-permute-done | bytes 51744 | tf_op jit(solution)/shard_map/ppermute | solution.py:54
  14.0 0.0 collective-permute-done
  14.1 0.1 dynamic-slice_reduce_fusion
  14.2 3.7 %collective-permute-start.5 = (f32[41,128]{1,0:T(8,128)S(1)}, f32[41,128]{1,0:T(8,128)S(1)}, u32[]{:S(2)}, u32[]{:S(2)}) collective-permute-start(f32[41,128]{1,0:T(8,128)S(1)} %pad_maximum_fusion.7), channel_id=1, source_target_pairs={{0,12},{4,8},{8,4},{12,0},{1,13},{5,9},{9,5},{13,1},{2,14},{6,10},... | collective-permute-start | bytes 62984 | tf_op jit(solution)/shard_map/ppermute | solution.py:54
  17.9 0.0 collective-permute-start.4
  17.9 0.8 %collective-permute-start.3 = (f32[41,128]{1,0:T(8,128)S(1)}, f32[41,128]{1,0:T(8,128)S(1)}, u32[]{:S(2)}, u32[]{:S(2)}) collective-permute-start(f32[41,128]{1,0:T(8,128)S(1)} %pad_maximum_fusion.5), channel_id=1, source_target_pairs={{0,4},{4,0},{8,12},{12,8},{1,5},{5,1},{9,13},{13,9},{2,6},{6,2},{1... | collective-permute-start | bytes 62984 | tf_op jit(solution)/shard_map/ppermute | solution.py:54
  18.7 0.5 %fusion.146 = f32[1,128]{1,0:T(1,128)} fusion(f32[101,128]{1,0:T(8,128)S(1)} %collective-permute-done.2, f32[101,128]{1,0:T(8,128)S(1)} %collective-permute-done.1, f32[165,128]{1,0:T(8,128)S(1)} %collective-permute-done, f32[128]{0:T(128)S(1)} %get-tuple-element.15), kind=kLoop, calls=%fused_computation.220 | loop fusion | flops 512 | bytes 2560 | tf_op jit(solution)/shard_map/mul | solution.py:192
  19.2 0.1 concatenate.40
  19.3 0.6 %collective-permute-done.5 = f32[41,128]{1,0:T(8,128)S(1)} collective-permute-done((f32[41,128]{1,0:T(8,128)S(1)}, f32[41,128]{1,0:T(8,128)S(1)}, u32[]{:S(2)}, u32[]{:S(2)}) %collective-permute-start.5) | collective-permute-done | bytes 21024 | tf_op jit(solution)/shard_map/ppermute | solution.py:54
  19.9 0.1 concatenate.43
  20.0 2.6 %collective-permute-done.4 = f32[41,128]{1,0:T(8,128)S(1)} collective-permute-done((f32[41,128]{1,0:T(8,128)S(1)}, f32[41,128]{1,0:T(8,128)S(1)}, u32[]{:S(2)}, u32[]{:S(2)}) %collective-permute-start.4) | collective-permute-done | bytes 21024 | tf_op jit(solution)/shard_map/ppermute | solution.py:54
  22.6 0.1 concatenate.42
  22.7 0.0 collective-permute-done.3
  22.7 0.1 concatenate.41
  22.8 0.8 %multiply_reduce_fusion = f32[48,2,576]{2,0,1:T(8,128)} fusion(f32[4,48]{1,0:T(4,128)S(1)} %bitcast.121, f32[4,2,576]{2,1,0:T(2,128)S(1)} %maximum_bitcast_fusion), kind=kLoop, calls=%fused_computation.13 | loop fusion | flops 387072 | bytes 240384 | tf_op jit(solution)/shard_map/reduce_sum | solution.py:186
  23.6 0.6 %fusion.110 = (f32[128,16]{0,1:T(8,128)}, f32[16,128]{1,0:T(8,128)}) fusion(f32[41,128]{1,0:T(8,128)S(1)} %collective-permute-done.5, f32[41,128]{1,0:T(8,128)S(1)} %collective-permute-done.4, f32[41,128]{1,0:T(8,128)S(1)} %collective-permute-done.3, f32[4,1,16,128]{3,2,0,1:T(8,128)S(1)} %bitcast_add_fusion, s32[]{:T(128)S(6)} %select_n.92, ...), kind=kLoop, calls=%fused_computation.145 | loop fusion | flops 16384 | bytes 81924 | tf_op jit(solution)/shard_map/mul | solution.py:194
  (39 shorter events, 0.3 us)
Async XLA Ops:
  0.6 2.1 %copy-start = (bf16[2,2,5,1,256,128]{5,4,3,2,1,0:T(8,128)(2,1)S(1)}, bf16[2,2,5,1,256,128]{5,4,3,2,1,0:T(8,128)(2,1)}, u32[]{:S(2)}) copy-start(bf16[2,2,5,1,256,128]{5,4,3,2,1,0:T(8,128)(2,1)} %param.3) | copy-start | bytes 3932164
  3.4 0.7 %copy-start.1 = (s32[2,2]{1,0:T(2,128)S(1)}, s32[2,2]{1,0:T(2,128)}, u32[]{:S(2)}) copy-start(s32[2,2]{1,0:T(2,128)} %param.5) | copy-start | bytes 52
  7.1 4.7 %collective-permute-start.2 = (f32[101,128]{1,0:T(8,128)S(1)}, f32[101,128]{1,0:T(8,128)S(1)}, u32[]{:S(2)}, u32[]{:S(2)}) collective-permute-start(f32[101,128]{1,0:T(8,128)S(1)} %get-tuple-element.32), channel_id=1, source_target_pairs={{0,3},{1,2},{2,1},{3,0},{4,7},{5,6},{6,5},{7,4},{8,11},{9,10},{10,... | collective-permute-start | bytes 155144 | tf_op jit(solution)/shard_map/ppermute | solution.py:54
  9.5 4.4 %collective-permute-start.1 = (f32[101,128]{1,0:T(8,128)S(1)}, f32[101,128]{1,0:T(8,128)S(1)}, u32[]{:S(2)}, u32[]{:S(2)}) collective-permute-start(f32[101,128]{1,0:T(8,128)S(1)} %get-tuple-element.31), channel_id=1, source_target_pairs={{0,2},{1,3},{2,0},{3,1},{4,6},{5,7},{6,4},{7,5},{8,10},{9,11},{10,... | collective-permute-start | bytes 155144 | tf_op jit(solution)/shard_map/ppermute | solution.py:54
  10.7 3.3 %collective-permute-start = (f32[165,128]{1,0:T(8,128)S(1)}, f32[165,128]{1,0:T(8,128)S(1)}, u32[]{:S(2)}, u32[]{:S(2)}) collective-permute-start(f32[165,128]{1,0:T(8,128)S(1)} %pad_maximum_fusion), channel_id=1, source_target_pairs={{0,1},{1,0},{2,3},{3,2},{4,5},{5,4},{6,7},{7,6},{8,9},{9,8},{10,11... | collective-permute-start | bytes 253448 | tf_op jit(solution)/shard_map/ppermute | solution.py:54
  14.2 5.7 %collective-permute-start.5 = (f32[41,128]{1,0:T(8,128)S(1)}, f32[41,128]{1,0:T(8,128)S(1)}, u32[]{:S(2)}, u32[]{:S(2)}) collective-permute-start(f32[41,128]{1,0:T(8,128)S(1)} %pad_maximum_fusion.7), channel_id=1, source_target_pairs={{0,12},{4,8},{8,4},{12,0},{1,13},{5,9},{9,5},{13,1},{2,14},{6,10},... | collective-permute-start | bytes 62984 | tf_op jit(solution)/shard_map/ppermute | solution.py:54
  17.9 4.7 %collective-permute-start.4 = (f32[41,128]{1,0:T(8,128)S(1)}, f32[41,128]{1,0:T(8,128)S(1)}, u32[]{:S(2)}, u32[]{:S(2)}) collective-permute-start(f32[41,128]{1,0:T(8,128)S(1)} %pad_maximum_fusion.6), channel_id=1, source_target_pairs={{0,8},{4,12},{8,0},{12,4},{1,9},{5,13},{9,1},{13,5},{2,10},{6,14},... | collective-permute-start | bytes 62984 | tf_op jit(solution)/shard_map/ppermute | solution.py:54
  17.9 4.8 %collective-permute-start.3 = (f32[41,128]{1,0:T(8,128)S(1)}, f32[41,128]{1,0:T(8,128)S(1)}, u32[]{:S(2)}, u32[]{:S(2)}) collective-permute-start(f32[41,128]{1,0:T(8,128)S(1)} %pad_maximum_fusion.5), channel_id=1, source_target_pairs={{0,4},{4,0},{8,12},{12,8},{1,5},{5,1},{9,13},{13,9},{2,6},{6,2},{1... | collective-permute-start | bytes 62984 | tf_op jit(solution)/shard_map/ppermute | solution.py:54

commit v26 on v19

--- a/solution.py
+++ b/solution.py
@@ -106,12 +106,9 @@
     rows_z = field.reshape(-1, cells_z)
 
     qz = aq[:, None, :] * az.astype(f32)[None, :, :]
-    qz_hi = qz.astype(bf16)
-    qz_lo = (qz - qz_hi.astype(f32)).astype(bf16)
-    both = jnp.einsum(
-        "qxyz,qzk->xyk", field, jnp.concatenate([qz_hi, qz_lo], axis=-1), preferred_element_type=f32
-    )
-    by_q = both[..., :K] + both[..., K:]
+    by_q = jnp.einsum(
+        "qxyz,qzk->xyk", field.astype(f32), qz, precision=lax.Precision.HIGH, preferred_element_type=f32
+    )
     part_y = jnp.sum(by_q * ax[:, None, :], axis=0)
     part_x = jnp.sum(by_q * ay.astype(f32)[None, :, :], axis=1)
     along_y = jnp.einsum("qxyz,yk->qxzk", field, ay, preferred_element_type=f32)

time: 24.5 us -> 24.6 us (level)
  matrix products: 2.23 us -> 2.81 us
  other arithmetic: 3.13 us -> 2.61 us
    dot_general x1, matrix products: 0.5 us -> 1.07 us  [shards(): jnp.einsum('qxyz,qzk->xyk', field.astype(f32), qz, precision=lax.Precisio...]
    convert_element_type x1 -> x0, other arithmetic: 0.34 us -> none  [shards(): qz_hi = qz.astype(bf16)]
where the time goes in v26:
time: 24.6 us; the launch traced here: 24.4 us
  starting transfers between devices  7.64 us (31%)
  waiting for transfers between devices  6.17 us (25%)
  local copies, waits for them, and re-layouts  2.9 us (12%)
  matrix products  2.81 us (11%)
  other arithmetic  2.61 us (11%)
  between operations  2.28 us (9%)
    ppermute x6, starting transfers between devices, send_to(): got = lax.ppermute(flat, axes, [(i, i ^ shift) for i in range(n)])  7.64 us
    ppermute x6, waiting for transfers between devices, send_to(): got = lax.ppermute(flat, axes, [(i, i ^ shift) for i in range(n)])  6.17 us
    slice x1, local copies, waits for them, and re-layouts, shards(): factor_stream = test_streams[0]  1.34 us
    dot_general x1, matrix products, shards(): jnp.einsum('qxyz,qzk->xyk', field.astype(f32), qz, precision=lax.Precisio...  1.07 us
    mul x1, other arithmetic, shards(): core_out * scale_core  0.72 us
    mul x1, other arithmetic, shards(): sz.reshape(cols_each, cells_z).T * scale_z  0.61 us
    dot_general x1, matrix products, shards(): jnp.dot(rows_z, phz.T, preferred_element_type=f32)  0.6 us
    mul x1, other arithmetic, shards(): sx * scale_x  0.52 us
  transfers between devices with their start and end apart: 6, of which 4 were waited for; matrix products, arithmetic and copies ran while one was open for 6% of the time, Pallas kernels for 0%

profile of v26, /device:TPU:0, one launch (start us, length us, event | category | flops | bytes accessed | tf_op | source)
XLA Modules:
  0.0 24.4 jit_solution(14270075972384601310)
XLA Ops:
  0.6 0.0 copy-start
  0.8 1.3 %fusion.178 = (s32[1]{0:T(128)}, s32[1]{0:T(128)}) fusion(s32[2]{0:T(128)} %param.4), kind=kLoop, calls=%fused_computation.256 | loop fusion | bytes 16 | tf_op jit(solution)/shard_map/slice | solution.py:81
  2.7 0.0 copy-done
  2.8 0.6 %convolution_bitcast_fusion = f32[5120,48]{0,1:T(8,128)S(1)} fusion(bf16[5120,128]{1,0:T(8,128)(2,1)S(1)} %bitcast.98, s32[]{:T(128)} %bitcast.13, s32[128]{0:T(128)S(1)} %get-tuple-element.35, s32[48]{0:T(128)S(1)} %iota_multiply_fusion.3), kind=kOutput, calls=%fused_computation | convolution fusion | flops 63019008 | bytes 2294468 | tf_op jit(solution)/shard_map/dot_general | solution.py:117
  3.4 0.0 copy-start.1
  3.4 0.2 reshape.678
  3.5 0.1 iota_add_fusion
  3.6 0.4 %copy-done.1 = s32[2,2]{1,0:T(2,128)S(1)} copy-done((s32[2,2]{1,0:T(2,128)S(1)}, s32[2,2]{1,0:T(2,128)}, u32[]{:S(2)}) %copy-start.1) | copy-done | bytes 40
  4.0 0.1 fusion.99
  4.2 0.4 %fusion.113 = f32[2,256,48]{1,0,2:T(2,128)S(1)} fusion(f32[20,256,48]{1,0,2:T(8,128)S(1)} %reshape.678, s32[]{:T(128)} %bitcast.11, s32[20]{0:T(128)S(1)} %broadcast_multiply_fusion.2, s32[2]{0:T(128)S(1)} %iota_multiply_fusion.4), kind=kOutput, calls=%fused_computation.181 | convolution fusion | flops 2949800 | bytes 1081436 | tf_op jit(solution)/shard_map/qxyn,qe->xeyn/dot_general | solution.py:119
  4.5 0.3 %convolution_bitcast_fusion.2 = f32[1,2,48,48]{2,3,1,0:T(8,128)S(1)} fusion(f32[2,256,48]{1,0,2:T(2,128)S(1)} %fusion.113, s32[]{:T(128)} %bitcast.16, s32[256]{0:T(256)S(1)} %iota_multiply_fusion, s32[48]{0:T(128)S(1)} %iota_multiply_fusion.3), kind=kOutput, calls=%fused_computation.7 | convolution fusion | flops 7286784 | bytes 117956 | tf_op jit(solution)/shard_map/my,xeyn->xemn/dot_general | solution.py:120
  4.8 0.1 copy.21
  4.9 0.1 reshape.679
  5.0 0.1 reshape_reshape.16
  5.8 0.1 fusion.39
  5.9 0.1 broadcast_multiply_fusion.1
  6.0 1.1 %broadcast_multiply_fusion = (f32[256,128]{0,1:T(8,128)S(1)}, f32[128]{0:T(128)S(1)}) fusion(f32[128]{0:T(128)S(1)} %fusion.124, s32[]{:T(128)} %bitcast.5, s32[128]{0:T(128)S(1)} %iota_multiply_fusion.5, s32[256]{0:T(256)S(1)} %iota_multiply_fusion.1, bf16[20,256,128]{2,1,0:T(8,128)(2,1)S(1)} %bitcast.99, f32[128,128]{0,1:T(8,128)S(1)} %fusion.39, ...), kind=kOutput, calls=%fused_computation.46 | convolution fusion | flops 504332160 | bytes 1520132 | tf_op jit(solution)/shard_map/qxyz,qzk->xyk/dot_general | solution.py:109
  7.0 0.1 copy.19
  7.2 2.4 %collective-permute-start.2 = (f32[101,128]{1,0:T(8,128)S(1)}, f32[101,128]{1,0:T(8,128)S(1)}, u32[]{:S(2)}, u32[]{:S(2)}) collective-permute-start(f32[101,128]{1,0:T(8,128)S(1)} %get-tuple-element.30), channel_id=1, source_target_pairs={{0,3},{1,2},{2,1},{3,0},{4,7},{5,6},{6,5},{7,4},{8,11},{9,10},{10,... | collective-permute-start | bytes 155144 | tf_op jit(solution)/shard_map/ppermute | solution.py:54
  9.6 0.6 %collective-permute-start.1 = (f32[101,128]{1,0:T(8,128)S(1)}, f32[101,128]{1,0:T(8,128)S(1)}, u32[]{:S(2)}, u32[]{:S(2)}) collective-permute-start(f32[101,128]{1,0:T(8,128)S(1)} %get-tuple-element.29), channel_id=1, source_target_pairs={{0,2},{1,3},{2,0},{3,1},{4,6},{5,7},{6,4},{7,5},{8,10},{9,11},{10,... | collective-permute-start | bytes 155144 | tf_op jit(solution)/shard_map/ppermute | solution.py:54
  10.3 0.5 %fusion.3 = f32[128,128]{0,1:T(8,128)S(1)} fusion(bf16[20,256,128]{2,1,0:T(8,128)(2,1)S(1)} %bitcast.100, f32[20,128]{1,0:T(8,128)S(1)} %get-tuple-element.31, s32[]{:T(128)} %bitcast.5, s32[128]{0:T(128)S(1)} %iota_multiply_fusion.5, s32[256]{0:T(256)S(1)} %iota_multiply_fusion.1), kind=kOutput, calls=%fused_computation.5 | convolution fusion | flops 168968192 | bytes 1388036 | tf_op jit(solution)/shard_map/qxyz,yk->qxzk/dot_general | solution.py:114
  10.8 0.1 collective-permute-start
  10.9 0.1 fusion.101
  11.0 0.1 reshape.689
  11.1 0.7 %collective-permute-done.2 = f32[101,128]{1,0:T(8,128)S(1)} collective-permute-done((f32[101,128]{1,0:T(8,128)S(1)}, f32[101,128]{1,0:T(8,128)S(1)}, u32[]{:S(2)}, u32[]{:S(2)}) %collective-permute-start.2) | collective-permute-done | bytes 51744 | tf_op jit(solution)/shard_map/ppermute | solution.py:54
  11.9 2.2 %collective-permute-done.1 = f32[101,128]{1,0:T(8,128)S(1)} collective-permute-done((f32[101,128]{1,0:T(8,128)S(1)}, f32[101,128]{1,0:T(8,128)S(1)}, u32[]{:S(2)}, u32[]{:S(2)}) %collective-permute-start.1) | collective-permute-done | bytes 51744 | tf_op jit(solution)/shard_map/ppermute | solution.py:54
  14.1 0.0 collective-permute-done
  14.3 0.1 dynamic-slice_reduce_fusion
  14.3 3.7 %collective-permute-start.5 = (f32[41,128]{1,0:T(8,128)S(1)}, f32[41,128]{1,0:T(8,128)S(1)}, u32[]{:S(2)}, u32[]{:S(2)}) collective-permute-start(f32[41,128]{1,0:T(8,128)S(1)} %pad_maximum_fusion.7), channel_id=1, source_target_pairs={{0,12},{4,8},{8,4},{12,0},{1,13},{5,9},{9,5},{13,1},{2,14},{6,10},... | collective-permute-start | bytes 62984 | tf_op jit(solution)/shard_map/ppermute | solution.py:54
  18.0 0.0 collective-permute-start.4
  18.0 0.8 %collective-permute-start.3 = (f32[41,128]{1,0:T(8,128)S(1)}, f32[41,128]{1,0:T(8,128)S(1)}, u32[]{:S(2)}, u32[]{:S(2)}) collective-permute-start(f32[41,128]{1,0:T(8,128)S(1)} %pad_maximum_fusion.5), channel_id=1, source_target_pairs={{0,4},{4,0},{8,12},{12,8},{1,5},{5,1},{9,13},{13,9},{2,6},{6,2},{1... | collective-permute-start | bytes 62984 | tf_op jit(solution)/shard_map/ppermute | solution.py:54
  18.8 0.5 %fusion.125 = f32[1,128]{1,0:T(1,128)} fusion(f32[101,128]{1,0:T(8,128)S(1)} %collective-permute-done.2, f32[101,128]{1,0:T(8,128)S(1)} %collective-permute-done.1, f32[165,128]{1,0:T(8,128)S(1)} %collective-permute-done, f32[128]{0:T(128)S(1)} %get-tuple-element.18), kind=kLoop, calls=%fused_computation.193 | loop fusion | flops 512 | bytes 2560 | tf_op jit(solution)/shard_map/mul | solution.py:189
  19.3 0.1 concatenate.36
  19.4 0.6 %collective-permute-done.5 = f32[41,128]{1,0:T(8,128)S(1)} collective-permute-done((f32[41,128]{1,0:T(8,128)S(1)}, f32[41,128]{1,0:T(8,128)S(1)}, u32[]{:S(2)}, u32[]{:S(2)}) %collective-permute-start.5) | collective-permute-done | bytes 21024 | tf_op jit(solution)/shard_map/ppermute | solution.py:54
  20.0 0.1 concatenate.39
  20.1 2.6 %collective-permute-done.4 = f32[41,128]{1,0:T(8,128)S(1)} collective-permute-done((f32[41,128]{1,0:T(8,128)S(1)}, f32[41,128]{1,0:T(8,128)S(1)}, u32[]{:S(2)}, u32[]{:S(2)}) %collective-permute-start.4) | collective-permute-done | bytes 21024 | tf_op jit(solution)/shard_map/ppermute | solution.py:54
  22.7 0.1 concatenate.38
  22.8 0.0 collective-permute-done.3
  22.8 0.1 concatenate.37
  22.9 0.1 multiply_reduce_fusion
  23.1 0.7 %multiply_bitcast_fusion = f32[576,2,48]{0,2,1:T(8,128)} fusion(f32[48,2,576]{2,0,1:T(8,128)S(1)} %multiply_reduce_fusion), kind=kLoop, calls=%fused_computation.11 | loop fusion | flops 55296 | bytes 442368 | tf_op jit(solution)/shard_map/mul | solution.py:192
  23.8 0.6 %fusion.88 = (f32[128,16]{0,1:T(8,128)}, f32[16,128]{1,0:T(8,128)}) fusion(f32[41,128]{1,0:T(8,128)S(1)} %collective-permute-done.5, f32[41,128]{1,0:T(8,128)S(1)} %collective-permute-done.4, f32[41,128]{1,0:T(8,128)S(1)} %collective-permute-done.3, f32[4,1,16,128]{3,2,0,1:T(8,128)S(1)} %bitcast_add_fusion, s32[]{:T(128)S(6)} %select_n.92, ...), kind=kLoop, calls=%fused_computation.118 | loop fusion | flops 16384 | bytes 81924 | tf_op jit(solution)/shard_map/mul | solution.py:191
  (39 shorter events, 0.3 us)
Async XLA Ops:
  0.6 2.1 %copy-start = (bf16[2,2,5,1,256,128]{5,4,3,2,1,0:T(8,128)(2,1)S(1)}, bf16[2,2,5,1,256,128]{5,4,3,2,1,0:T(8,128)(2,1)}, u32[]{:S(2)}) copy-start(bf16[2,2,5,1,256,128]{5,4,3,2,1,0:T(8,128)(2,1)} %param.3) | copy-start | bytes 3932164
  3.4 0.7 %copy-start.1 = (s32[2,2]{1,0:T(2,128)S(1)}, s32[2,2]{1,0:T(2,128)}, u32[]{:S(2)}) copy-start(s32[2,2]{1,0:T(2,128)} %param.5) | copy-start | bytes 52
  7.2 4.7 %collective-permute-start.2 = (f32[101,128]{1,0:T(8,128)S(1)}, f32[101,128]{1,0:T(8,128)S(1)}, u32[]{:S(2)}, u32[]{:S(2)}) collective-permute-start(f32[101,128]{1,0:T(8,128)S(1)} %get-tuple-element.30), channel_id=1, source_target_pairs={{0,3},{1,2},{2,1},{3,0},{4,7},{5,6},{6,5},{7,4},{8,11},{9,10},{10,... | collective-permute-start | bytes 155144 | tf_op jit(solution)/shard_map/ppermute | solution.py:54
  9.6 4.4 %collective-permute-start.1 = (f32[101,128]{1,0:T(8,128)S(1)}, f32[101,128]{1,0:T(8,128)S(1)}, u32[]{:S(2)}, u32[]{:S(2)}) collective-permute-start(f32[101,128]{1,0:T(8,128)S(1)} %get-tuple-element.29), channel_id=1, source_target_pairs={{0,2},{1,3},{2,0},{3,1},{4,6},{5,7},{6,4},{7,5},{8,10},{9,11},{10,... | collective-permute-start | bytes 155144 | tf_op jit(solution)/shard_map/ppermute | solution.py:54
  10.8 3.3 %collective-permute-start = (f32[165,128]{1,0:T(8,128)S(1)}, f32[165,128]{1,0:T(8,128)S(1)}, u32[]{:S(2)}, u32[]{:S(2)}) collective-permute-start(f32[165,128]{1,0:T(8,128)S(1)} %pad_maximum_fusion), channel_id=1, source_target_pairs={{0,1},{1,0},{2,3},{3,2},{4,5},{5,4},{6,7},{7,6},{8,9},{9,8},{10,11... | collective-permute-start | bytes 253448 | tf_op jit(solution)/shard_map/ppermute | solution.py:54
  14.3 5.7 %collective-permute-start.5 = (f32[41,128]{1,0:T(8,128)S(1)}, f32[41,128]{1,0:T(8,128)S(1)}, u32[]{:S(2)}, u32[]{:S(2)}) collective-permute-start(f32[41,128]{1,0:T(8,128)S(1)} %pad_maximum_fusion.7), channel_id=1, source_target_pairs={{0,12},{4,8},{8,4},{12,0},{1,13},{5,9},{9,5},{13,1},{2,14},{6,10},... | collective-permute-start | bytes 62984 | tf_op jit(solution)/shard_map/ppermute | solution.py:54
  18.0 4.7 %collective-permute-start.4 = (f32[41,128]{1,0:T(8,128)S(1)}, f32[41,128]{1,0:T(8,128)S(1)}, u32[]{:S(2)}, u32[]{:S(2)}) collective-permute-start(f32[41,128]{1,0:T(8,128)S(1)} %pad_maximum_fusion.6), channel_id=1, source_target_pairs={{0,8},{4,12},{8,0},{12,4},{1,9},{5,13},{9,1},{13,5},{2,10},{6,14},... | collective-permute-start | bytes 62984 | tf_op jit(solution)/shard_map/ppermute | solution.py:54
  18.0 4.8 %collective-permute-start.3 = (f32[41,128]{1,0:T(8,128)S(1)}, f32[41,128]{1,0:T(8,128)S(1)}, u32[]{:S(2)}, u32[]{:S(2)}) collective-permute-start(f32[41,128]{1,0:T(8,128)S(1)} %pad_maximum_fusion.5), channel_id=1, source_target_pairs={{0,4},{4,0},{8,12},{12,8},{1,5},{5,1},{9,13},{13,9},{2,6},{6,2},{1... | collective-permute-start | bytes 62984 | tf_op jit(solution)/shard_map/ppermute | solution.py:54

commit v27 on v19

--- a/solution.py
+++ b/solution.py
@@ -114,9 +114,9 @@
     by_q = both[..., :K] + both[..., K:]
     part_y = jnp.sum(by_q * ax[:, None, :], axis=0)
     part_x = jnp.sum(by_q * ay.astype(f32)[None, :, :], axis=1)
-    along_y = jnp.einsum("qxyz,yk->qxzk", field, ay, preferred_element_type=f32)
+    along_y = jnp.einsum("qxyz,yk->qxkz", field, ay, preferred_element_type=f32)
     weights = aq[:, None, :] * ax[None, :, :]
-    part_z = jnp.sum(along_y * weights[:, :, None, :], axis=(0, 1))
+    part_z_t = jnp.sum(along_y * weights[:, :, :, None], axis=(0, 1))
     first = jnp.dot(rows_z, phz.T, preferred_element_type=f32).reshape(n_q, cells_x, cells_y, S)
     high = lax.Precision.HIGH
     by_e = jnp.einsum("qxyn,qe->xeyn", first, phq, precision=high)
@@ -127,7 +127,7 @@
     core_rows = S * S // n_gx
     n_gzv = n_gz * n_vert
     sy = part_y.reshape(n_gx, n_gzv, rows_each, K)
-    sz = part_z.T.reshape(n_gx, n_vert, cols_each, cells_z)
+    sz = part_z_t.reshape(n_gx, n_vert, cols_each, cells_z)
     sx = part_x
     core = (
         part_core.reshape(cells_x, E, n_gx, core_rows)

time: 24.5 us -> 24.5 us (level)
  no operation moved by 1% of the time
where the time goes in v27:
time: 24.5 us; the launch traced here: 24.3 us
  starting transfers between devices  7.64 us (31%)
  waiting for transfers between devices  6.17 us (25%)
  other arithmetic  3.13 us (13%)
  local copies, waits for them, and re-layouts  2.81 us (11%)
  between operations  2.29 us (9%)
  matrix products  2.23 us (9%)
    ppermute x6, starting transfers between devices, send_to(): got = lax.ppermute(flat, axes, [(i, i ^ shift) for i in range(n)])  7.64 us
    ppermute x6, waiting for transfers between devices, send_to(): got = lax.ppermute(flat, axes, [(i, i ^ shift) for i in range(n)])  6.17 us
    slice x1, local copies, waits for them, and re-layouts, shards(): factor_stream = test_streams[0]  1.34 us
    mul x1, other arithmetic, shards(): core_out * scale_core  0.72 us
    mul x1, other arithmetic, shards(): sz.reshape(cols_each, cells_z).T * scale_z  0.61 us
    dot_general x1, matrix products, shards(): jnp.dot(rows_z, phz.T, preferred_element_type=f32)  0.6 us
    mul x1, other arithmetic, shards(): sx * scale_x  0.52 us
    dot_general x1, matrix products, shards(): jnp.einsum('qxyz,qzk->xyk', field, jnp.concatenate([qz_hi, qz_lo], axis=-...  0.5 us
  transfers between devices with their start and end apart: 6, of which 4 were waited for; matrix products, arithmetic and copies ran while one was open for 6% of the time, Pallas kernels for 0%

profile of v27, /device:TPU:0, one launch (start us, length us, event | category | flops | bytes accessed | tf_op | source)
XLA Modules:
  0.0 24.3 jit_solution(13885593374490823583)
XLA Ops:
  0.6 0.0 copy-start
  0.8 1.3 %fusion.201 = (s32[1]{0:T(128)}, s32[1]{0:T(128)}) fusion(s32[2]{0:T(128)} %param.4), kind=kLoop, calls=%fused_computation.285 | loop fusion | bytes 16 | tf_op jit(solution)/shard_map/slice | solution.py:81
  2.7 0.0 copy-done
  2.8 0.6 %convolution_bitcast_fusion = f32[5120,48]{0,1:T(8,128)S(1)} fusion(bf16[5120,128]{1,0:T(8,128)(2,1)S(1)} %bitcast.100, s32[]{:T(128)} %bitcast.15, s32[128]{0:T(128)S(1)} %get-tuple-element.37, s32[48]{0:T(128)S(1)} %iota_multiply_fusion.3), kind=kOutput, calls=%fused_computation | convolution fusion | flops 63019008 | bytes 2294468 | tf_op jit(solution)/shard_map/dot_general | solution.py:120
  3.4 0.0 copy-start.1
  3.4 0.2 reshape.779
  3.5 0.1 iota_add_fusion
  3.6 0.4 %copy-done.1 = s32[2,2]{1,0:T(2,128)S(1)} copy-done((s32[2,2]{1,0:T(2,128)S(1)}, s32[2,2]{1,0:T(2,128)}, u32[]{:S(2)}) %copy-start.1) | copy-done | bytes 40
  4.0 0.1 fusion.121
  4.2 0.4 %fusion.135 = f32[2,256,48]{1,0,2:T(2,128)S(1)} fusion(f32[20,256,48]{1,0,2:T(8,128)S(1)} %reshape.779, s32[]{:T(128)} %bitcast.13, s32[20]{0:T(128)S(1)} %broadcast_multiply_fusion.2, s32[2]{0:T(128)S(1)} %iota_multiply_fusion.4), kind=kOutput, calls=%fused_computation.209 | convolution fusion | flops 2949800 | bytes 1081436 | tf_op jit(solution)/shard_map/qxyn,qe->xeyn/dot_general | solution.py:122
  4.5 0.3 %convolution_bitcast_fusion.2 = f32[1,2,48,48]{2,3,1,0:T(8,128)S(1)} fusion(f32[2,256,48]{1,0,2:T(2,128)S(1)} %fusion.135, s32[]{:T(128)} %bitcast.18, s32[256]{0:T(256)S(1)} %iota_multiply_fusion, s32[48]{0:T(128)S(1)} %iota_multiply_fusion.3), kind=kOutput, calls=%fused_computation.12 | convolution fusion | flops 7286784 | bytes 117956 | tf_op jit(solution)/shard_map/my,xeyn->xemn/dot_general | solution.py:123
  4.8 0.1 copy.15
  4.9 0.1 reshape.780
  5.0 0.1 reshape_reshape.16
  5.8 0.1 fusion.61
  5.9 0.1 broadcast_multiply_fusion.1
  6.0 0.3 %multiply_convert_fusion = (bf16[20,128,128]{2,1,0:T(8,128)(2,1)S(1)}, bf16[20,128,128]{2,1,0:T(8,128)(2,1)S(1)}) fusion(f32[128,128]{1,0:T(8,128)S(1)} %fusion.61, f32[20,128]{1,0:T(8,128)S(1)} %get-tuple-element.34), kind=kLoop, calls=%fused_computation.2 | loop fusion | flops 1638400 | bytes 1386496 | tf_op jit(solution)/shard_map/convert_element_type | solution.py:109
  6.3 0.5 %fusion.7 = f32[1,256,256]{2,1,0:T(8,128)S(1)} fusion(bf16[20,256,128]{2,1,0:T(8,128)(2,1)S(1)} %bitcast.101, bf16[20,128,128]{2,1,0:T(8,128)(2,1)S(1)} %get-tuple-element.22, bf16[20,128,128]{2,1,0:T(8,128)(2,1)S(1)} %get-tuple-element.21), kind=kOutput, calls=%fused_computation.11 | convolution fusion | flops 338165760 | bytes 2883584 | tf_op jit(solution)/shard_map/qxyz,qzk->xyk/dot_general | solution.py:111
  6.8 0.2 broadcast_multiply_fusion
  7.1 2.4 %collective-permute-start.2 = (f32[101,128]{1,0:T(8,128)S(1)}, f32[101,128]{1,0:T(8,128)S(1)}, u32[]{:S(2)}, u32[]{:S(2)}) collective-permute-start(f32[101,128]{1,0:T(8,128)S(1)} %get-tuple-element.32), channel_id=1, source_target_pairs={{0,3},{1,2},{2,1},{3,0},{4,7},{5,6},{6,5},{7,4},{8,11},{9,10},{10,... | collective-permute-start | bytes 155144 | tf_op jit(solution)/shard_map/ppermute | solution.py:54
  9.5 0.6 %collective-permute-start.1 = (f32[101,128]{1,0:T(8,128)S(1)}, f32[101,128]{1,0:T(8,128)S(1)}, u32[]{:S(2)}, u32[]{:S(2)}) collective-permute-start(f32[101,128]{1,0:T(8,128)S(1)} %get-tuple-element.31), channel_id=1, source_target_pairs={{0,2},{1,3},{2,0},{3,1},{4,6},{5,7},{6,4},{7,5},{8,10},{9,11},{10,... | collective-permute-start | bytes 155144 | tf_op jit(solution)/shard_map/ppermute | solution.py:54
  10.1 0.5 %fusion.6 = f32[128,128]{1,0:T(8,128)S(1)} fusion(bf16[20,256,128]{2,1,0:T(8,128)(2,1)S(1)} %bitcast.102, f32[20,128]{1,0:T(8,128)S(1)} %get-tuple-element.33, s32[]{:T(128)} %bitcast.8, s32[128]{0:T(128)S(1)} %iota_multiply_fusion.5, s32[256]{0:T(256)S(1)} %iota_multiply_fusion.1), kind=kOutput, calls=%fused_computation.10 | convolution fusion | flops 168968192 | bytes 1388036 | tf_op jit(solution)/shard_map/qxyz,yk->qxkz/dot_general | solution.py:117
  10.7 0.1 collective-permute-start
  10.8 0.1 fusion.123
  10.9 0.1 reshape.790
  11.0 0.7 %collective-permute-done.2 = f32[101,128]{1,0:T(8,128)S(1)} collective-permute-done((f32[101,128]{1,0:T(8,128)S(1)}, f32[101,128]{1,0:T(8,128)S(1)}, u32[]{:S(2)}, u32[]{:S(2)}) %collective-permute-start.2) | collective-permute-done | bytes 51744 | tf_op jit(solution)/shard_map/ppermute | solution.py:54
  11.7 2.2 %collective-permute-done.1 = f32[101,128]{1,0:T(8,128)S(1)} collective-permute-done((f32[101,128]{1,0:T(8,128)S(1)}, f32[101,128]{1,0:T(8,128)S(1)}, u32[]{:S(2)}, u32[]{:S(2)}) %collective-permute-start.1) | collective-permute-done | bytes 51744 | tf_op jit(solution)/shard_map/ppermute | solution.py:54
  14.0 0.0 collective-permute-done
  14.1 0.1 dynamic-slice_reduce_fusion
  14.2 3.7 %collective-permute-start.5 = (f32[41,128]{1,0:T(8,128)S(1)}, f32[41,128]{1,0:T(8,128)S(1)}, u32[]{:S(2)}, u32[]{:S(2)}) collective-permute-start(f32[41,128]{1,0:T(8,128)S(1)} %pad_maximum_fusion.7), channel_id=1, source_target_pairs={{0,12},{4,8},{8,4},{12,0},{1,13},{5,9},{9,5},{13,1},{2,14},{6,10},... | collective-permute-start | bytes 62984 | tf_op jit(solution)/shard_map/ppermute | solution.py:54
  17.9 0.0 collective-permute-start.4
  17.9 0.8 %collective-permute-start.3 = (f32[41,128]{1,0:T(8,128)S(1)}, f32[41,128]{1,0:T(8,128)S(1)}, u32[]{:S(2)}, u32[]{:S(2)}) collective-permute-start(f32[41,128]{1,0:T(8,128)S(1)} %pad_maximum_fusion.5), channel_id=1, source_target_pairs={{0,4},{4,0},{8,12},{12,8},{1,5},{5,1},{9,13},{13,9},{2,6},{6,2},{1... | collective-permute-start | bytes 62984 | tf_op jit(solution)/shard_map/ppermute | solution.py:54
  18.7 0.5 %fusion.147 = f32[1,128]{1,0:T(1,128)} fusion(f32[101,128]{1,0:T(8,128)S(1)} %collective-permute-done.2, f32[101,128]{1,0:T(8,128)S(1)} %collective-permute-done.1, f32[165,128]{1,0:T(8,128)S(1)} %collective-permute-done, f32[128]{0:T(128)S(1)} %get-tuple-element.15), kind=kLoop, calls=%fused_computation.221 | loop fusion | flops 512 | bytes 2560 | tf_op jit(solution)/shard_map/mul | solution.py:192
  19.2 0.1 concatenate.40
  19.3 0.6 %collective-permute-done.5 = f32[41,128]{1,0:T(8,128)S(1)} collective-permute-done((f32[41,128]{1,0:T(8,128)S(1)}, f32[41,128]{1,0:T(8,128)S(1)}, u32[]{:S(2)}, u32[]{:S(2)}) %collective-permute-start.5) | collective-permute-done | bytes 21024 | tf_op jit(solution)/shard_map/ppermute | solution.py:54
  19.9 0.1 concatenate.43
  20.0 2.6 %collective-permute-done.4 = f32[41,128]{1,0:T(8,128)S(1)} collective-permute-done((f32[41,128]{1,0:T(8,128)S(1)}, f32[41,128]{1,0:T(8,128)S(1)}, u32[]{:S(2)}, u32[]{:S(2)}) %collective-permute-start.4) | collective-permute-done | bytes 21024 | tf_op jit(solution)/shard_map/ppermute | solution.py:54
  22.6 0.1 concatenate.42
  22.7 0.0 collective-permute-done.3
  22.7 0.1 concatenate.41
  22.8 0.1 multiply_reduce_fusion
  22.9 0.7 %multiply_bitcast_fusion = f32[576,2,48]{0,2,1:T(8,128)} fusion(f32[48,2,576]{2,0,1:T(8,128)S(1)} %multiply_reduce_fusion), kind=kLoop, calls=%fused_computation.14 | loop fusion | flops 55296 | bytes 442368 | tf_op jit(solution)/shard_map/mul | solution.py:195
  23.7 0.6 %fusion.110 = (f32[128,16]{0,1:T(8,128)}, f32[16,128]{1,0:T(8,128)}) fusion(f32[41,128]{1,0:T(8,128)S(1)} %collective-permute-done.5, f32[41,128]{1,0:T(8,128)S(1)} %collective-permute-done.4, f32[41,128]{1,0:T(8,128)S(1)} %collective-permute-done.3, f32[4,1,16,128]{3,2,0,1:T(8,128)S(1)} %bitcast_add_fusion, s32[]{:T(128)S(6)} %select_n.92, ...), kind=kLoop, calls=%fused_computation.146 | loop fusion | flops 16384 | bytes 81924 | tf_op jit(solution)/shard_map/mul | solution.py:194
  (39 shorter events, 0.3 us)
Async XLA Ops:
  0.6 2.1 %copy-start = (bf16[2,2,5,1,256,128]{5,4,3,2,1,0:T(8,128)(2,1)S(1)}, bf16[2,2,5,1,256,128]{5,4,3,2,1,0:T(8,128)(2,1)}, u32[]{:S(2)}) copy-start(bf16[2,2,5,1,256,128]{5,4,3,2,1,0:T(8,128)(2,1)} %param.3) | copy-start | bytes 3932164
  3.4 0.7 %copy-start.1 = (s32[2,2]{1,0:T(2,128)S(1)}, s32[2,2]{1,0:T(2,128)}, u32[]{:S(2)}) copy-start(s32[2,2]{1,0:T(2,128)} %param.5) | copy-start | bytes 52
  7.1 4.7 %collective-permute-start.2 = (f32[101,128]{1,0:T(8,128)S(1)}, f32[101,128]{1,0:T(8,128)S(1)}, u32[]{:S(2)}, u32[]{:S(2)}) collective-permute-start(f32[101,128]{1,0:T(8,128)S(1)} %get-tuple-element.32), channel_id=1, source_target_pairs={{0,3},{1,2},{2,1},{3,0},{4,7},{5,6},{6,5},{7,4},{8,11},{9,10},{10,... | collective-permute-start | bytes 155144 | tf_op jit(solution)/shard_map/ppermute | solution.py:54
  9.5 4.4 %collective-permute-start.1 = (f32[101,128]{1,0:T(8,128)S(1)}, f32[101,128]{1,0:T(8,128)S(1)}, u32[]{:S(2)}, u32[]{:S(2)}) collective-permute-start(f32[101,128]{1,0:T(8,128)S(1)} %get-tuple-element.31), channel_id=1, source_target_pairs={{0,2},{1,3},{2,0},{3,1},{4,6},{5,7},{6,4},{7,5},{8,10},{9,11},{10,... | collective-permute-start | bytes 155144 | tf_op jit(solution)/shard_map/ppermute | solution.py:54
  10.7 3.3 %collective-permute-start = (f32[165,128]{1,0:T(8,128)S(1)}, f32[165,128]{1,0:T(8,128)S(1)}, u32[]{:S(2)}, u32[]{:S(2)}) collective-permute-start(f32[165,128]{1,0:T(8,128)S(1)} %pad_maximum_fusion), channel_id=1, source_target_pairs={{0,1},{1,0},{2,3},{3,2},{4,5},{5,4},{6,7},{7,6},{8,9},{9,8},{10,11... | collective-permute-start | bytes 253448 | tf_op jit(solution)/shard_map/ppermute | solution.py:54
  14.2 5.7 %collective-permute-start.5 = (f32[41,128]{1,0:T(8,128)S(1)}, f32[41,128]{1,0:T(8,128)S(1)}, u32[]{:S(2)}, u32[]{:S(2)}) collective-permute-start(f32[41,128]{1,0:T(8,128)S(1)} %pad_maximum_fusion.7), channel_id=1, source_target_pairs={{0,12},{4,8},{8,4},{12,0},{1,13},{5,9},{9,5},{13,1},{2,14},{6,10},... | collective-permute-start | bytes 62984 | tf_op jit(solution)/shard_map/ppermute | solution.py:54
  17.9 4.7 %collective-permute-start.4 = (f32[41,128]{1,0:T(8,128)S(1)}, f32[41,128]{1,0:T(8,128)S(1)}, u32[]{:S(2)}, u32[]{:S(2)}) collective-permute-start(f32[41,128]{1,0:T(8,128)S(1)} %pad_maximum_fusion.6), channel_id=1, source_target_pairs={{0,8},{4,12},{8,0},{12,4},{1,9},{5,13},{9,1},{13,5},{2,10},{6,14},... | collective-permute-start | bytes 62984 | tf_op jit(solution)/shard_map/ppermute | solution.py:54
  17.9 4.8 %collective-permute-start.3 = (f32[41,128]{1,0:T(8,128)S(1)}, f32[41,128]{1,0:T(8,128)S(1)}, u32[]{:S(2)}, u32[]{:S(2)}) collective-permute-start(f32[41,128]{1,0:T(8,128)S(1)} %pad_maximum_fusion.5), channel_id=1, source_target_pairs={{0,4},{4,0},{8,12},{12,8},{1,5},{5,1},{9,13},{13,9},{2,6},{6,2},{1... | collective-permute-start | bytes 62984 | tf_op jit(solution)/shard_map/ppermute | solution.py:54
